TPU v7x, 32 devices: a whole 2x2x4 slice. The times are simulated.
32 devices in a mesh: grp: 2 (over y), tile: 4 (over z), freq: 4 (over x, core).
Axes of the slice: x: 2, y: 2, z: 4, core: 2. Of those that a mesh axis runs over, the one named last changes fastest.
Arguments:
- sources: bfloat16 [4, 4, 2048, 512], P('freq', 'grp', 'tile'), parts along dimension 1, may hold values from -6 to 6
- v_factors: bfloat16 [4, 4, 2, 4, 112, 512], P('freq', 'tile', None, 'grp'), parts along dimension 3, may hold values from -0.1875 to 0.1875
- u_factors: bfloat16 [4, 4, 4, 112, 1024], P('freq', None, 'grp', None, 'tile'), parts along dimension 2, may hold values from -0.1875 to 0.1875
- tile_ranks: int32 [4, 4, 4], P('freq', 'grp', 'tile'), parts along dimension 1, may hold values from 16 to 112, as said below
- window_bounds: int32 [4, 1024, 512], P('grp', ('tile', 'freq')), parts along dimension 0, may hold values from 0 to 31, as said below
Outputs:
- windowed_traces: float32 [1024, 64, 512], P(('tile', 'freq'), 'grp'), parts along dimension 1
There are 2 independent parts, one for each index of `grp`. A program takes and returns all parts, laid end to end along the dimension named above; each array names one. Nothing has to cross between parts.
Inputs may be any that keep to these rules, and one draw needn't show every extreme that they name: `tile_ranks`: each tile's rank for each frequency; rank slots at or beyond it carry no coefficients. window_bounds[1] - window_bounds[0] lies between 8 and 16 for every receiver and virtual source.
All inputs are finite; a program needn't handle non-finite values.
Results may differ from a plain program's by a relative error of at most 0.0041.
Values may be sent and summed in bfloat16 or wider, within the bound.
No kernel may reach another device: no remote copies, remote signals or barrier semaphores. Data moves between devices by JAX's collectives and lax.ppermute only.
A program may use at most 64 MiB of HBM per device.

v0:
```python
import math

import jax
import jax.numpy as jnp
from jax import lax
from jax.sharding import PartitionSpec as P

NT = 32


first_bin = 2


def inverse_tables(count_freq, count_time):
    freq_index = jnp.arange(count_freq, dtype=jnp.int32)[:, None] + first_bin
    time_index = jnp.arange(count_time, dtype=jnp.int32)[None, :]
    phase_step = freq_index * time_index % count_time
    angles = phase_step.astype(jnp.float32) * (2.0 * math.pi / count_time)
    return (jnp.cos(angles), jnp.sin(angles))


def column_products(v_local, x_local, rank_local):
    products = lax.dot_general(
        v_local, x_local, (((3,), (1,)), ((), ())), preferred_element_type=jnp.float32
    )
    coef_real = products[:, 0, :, 0] - products[:, 1, :, 1]
    coef_imag = products[:, 0, :, 1] + products[:, 1, :, 0]
    slot_index = jnp.arange(v_local.shape[2], dtype=jnp.int32)
    live_slots = slot_index[None, :, None] < rank_local[:, None, None]
    coef_real = jnp.where(live_slots, coef_real, jnp.float32(0.0)).astype(jnp.bfloat16)
    coef_imag = jnp.where(live_slots, coef_imag, jnp.float32(0.0)).astype(jnp.bfloat16)
    return (coef_real, coef_imag)


def row_products(u_part, coef_part):
    return lax.dot_general(
        u_part, coef_part, (((0, 2), (0, 2)), ((), ())), preferred_element_type=jnp.float32
    )


def finish_spectrum(products):
    real_part = products[0, :, 0] - products[1, :, 1]
    imag_part = products[0, :, 1] + products[1, :, 0]
    return jnp.stack([real_part, imag_part], axis=0).astype(jnp.bfloat16)


def per_device(sources, v_factors, u_factors, tile_ranks, window_bounds):
    v_local = v_factors[0, 0]
    u_local = u_factors[0]
    coef_real, coef_imag = column_products(v_local, sources[0], tile_ranks[0, :, 0])
    sending = jnp.repeat(jnp.stack([coef_real, coef_imag], axis=1), 2, axis=0)

    def apply_whole(received, u_local=u_local):
        return finish_spectrum(row_products(u_local, received))

    spectrum = apply_whole(lax.all_to_all(sending, "tile", split_axis=0, concat_axis=0, tiled=True))
    spectrum_list = [spectrum]
    spectra = jnp.stack(spectrum_list, axis=0)
    received = lax.all_to_all(spectra, "freq", split_axis=2, concat_axis=0, tiled=True)
    count_freq = received.shape[0]
    cosine_table, sine_table = inverse_tables(count_freq, NT)
    widened = received.astype(jnp.float32)
    traces = jnp.einsum(
        "frs,fn->rns", widened[:, 0], cosine_table, precision=lax.Precision.HIGHEST
    ) - jnp.einsum("frs,fn->rns", widened[:, 1], sine_table, precision=lax.Precision.HIGHEST)
    traces = traces * (1.0 / math.sqrt(count_freq))
    time_index = jnp.arange(traces.shape[1], dtype=jnp.int32)[None, :, None]
    inside = (time_index >= window_bounds[0][:, None, :]) & (
        time_index < window_bounds[1][:, None, :]
    )
    return jnp.where(inside, traces, jnp.float32(0.0))


def solution(mesh):
    return jax.shard_map(
        per_device,
        mesh=mesh,
        in_specs=(
            P("freq", "grp", "tile", None),
            P("freq", "tile", None, "grp", None, None),
            P("freq", None, "grp", None, "tile"),
            P("freq", "grp", "tile"),
            P("grp", ("tile", "freq"), None),
        ),
        out_specs=P(("tile", "freq"), "grp", None),
        check_vma=False,
    )
```

profile of v0, /device:TPU:0, one launch (start us, length us, event | category | flops | bytes accessed | tf_op | source)
XLA Modules:
  0.0 53.6 jit_solution(12524646599114764560)
XLA Ops:
  0.0 0.0 copy-start
  0.0 0.8 %iota_compare_fusion.2 = pred[2,112]{1,0:T(4,128)(4,1)S(1)} fusion(s32[2]{0:T(128)} %bitcast.104), kind=kLoop, calls=%fused_computation.47 | loop fusion | flops 224 | bytes 232 | tf_op jit(solution)/shard_map/lt | solution.py:29
  0.8 0.4 copy-done
  1.2 1.7 %fusion.1 = f32[2,2,112,2,512]{4,2,3,1,0:T(8,128)S(1)} fusion(bf16[1,2,512,512]{3,2,1,0:T(8,128)(2,1)S(1)} %copy-done, bf16[1,1,2,2,112,512]{5,4,3,2,1,0:T(8,128)(2,1)} %param.6), kind=kOutput, calls=%fused_computation.5 | convolution fusion | flops 469762048 | bytes 3342336 | tf_op jit(solution)/shard_map/dot_general | solution.py:23
  2.9 0.0 copy-start.2
  2.9 0.2 fusion.13
  3.2 0.1 broadcast_in_dim.29
  3.3 29.0 %all_to_all.23 = bf16[4,2,112,512]{3,2,1,0:T(8,128)(2,1)S(1)} all-to-all(bf16[4,2,112,512]{3,2,1,0:T(8,128)(2,1)S(1)} %bitcast.100), channel_id=1, replica_groups=mesh['grp'=2,'tile'=4,'freq'=4] {'tile'}, dimensions={0} | all-to-all | bytes 1835008 | tf_op jit(solution)/shard_map/all_to_all | solution.py:56
  32.3 0.0 copy-done.2
  32.3 0.0 copy-start.1
  32.3 0.7 %convolution_bitcast_fusion = f32[2,256,2,512]{1,3,0,2:T(8,128)S(1)} fusion(bf16[4,2,112,512]{3,2,1,0:T(8,128)(2,1)S(1)} %all_to_all.23, bf16[1,4,2,112,256]{4,3,2,1,0:T(8,128)(2,1)S(1)} %copy-done.2), kind=kOutput, calls=%fused_computation.4 | convolution fusion | flops 469762048 | bytes 3473408 | tf_op jit(solution)/shard_map/dot_general | solution.py:36
  33.0 0.1 fusion.18
  33.1 0.1 fusion.17
  33.2 0.1 pad_maximum_fusion
  33.2 1.2 %copy.26 = bf16[1,2,256,512]{3,1,0,2:T(2,128)(2,1)} copy(bf16[1,2,256,512]{2,3,1,0:T(8,128)(2,1)S(1)} %pad_maximum_fusion) | data formatting | bytes 1048576 | tf_op jit(solution)/shard_map/stack | solution.py:44
  34.4 3.5 %all-to-all-start.1 = ((bf16[1,2,256,512]{3,1,0,2:T(2,128)(2,1)}), bf16[1,2,256,512]{3,1,0,2:T(2,128)(2,1)S(1)}, u32[]{:S(2)}, u32[]{:S(2)}) async-start(bf16[1,2,256,512]{3,1,0,2:T(2,128)(2,1)} %copy.26), calls=%async_computation.1 | async-start | bytes 1048576 | tf_op jit(solution)/shard_map/all_to_all | solution.py:59
  37.9 0.0 copy-done.1
  37.9 8.8 %all-to-all-done.1 = bf16[1,2,256,512]{3,1,0,2:T(2,128)(2,1)S(1)} async-done(((bf16[1,2,256,512]{3,1,0,2:T(2,128)(2,1)}), bf16[1,2,256,512]{3,1,0,2:T(2,128)(2,1)S(1)}, u32[]{:S(2)}, u32[]{:S(2)}) %all-to-all-start.1) | async-done | bytes 524320 | tf_op jit(solution)/shard_map/all_to_all | solution.py:59
  46.7 0.4 copy.48
  47.1 2.0 %fusion.19 = f32[32,64,512]{2,0,1:T(8,128)S(1)} fusion(bf16[4,2,64,512]{3,0,2,1:T(4,128)(2,1)S(1)} %bitcast.101, s32[4]{0:T(128)S(1)} %iota_add_fusion), kind=kOutput, calls=%fused_computation.34 | convolution fusion | flops 50333440 | bytes 4456960 | tf_op jit(solution)/shard_map/frs,fn->rns/dot_general | solution.py:63
  49.1 4.5 %bitcast_select_fusion = f32[64,32,512]{2,1,0:T(8,128)} fusion(f32[32,64,512]{2,0,1:T(8,128)S(1)} %fusion.19, s32[64,512]{1,0:T(8,128)S(1)} %get-tuple-element.8, s32[64,512]{1,0:T(8,128)S(1)} %get-tuple-element.7, bf16[4,2,64,512]{3,0,2,1:T(4,128)(2,1)S(1)} %bitcast.102, s32[4]{0:T(128)S(1)} %iota_add_fusion), kind=kOutput, calls=%fused_computation | convolution fusion | flops 56624896 | bytes 8913408 | tf_op jit(solution)/shard_map/frs,fn->rns/dot_general | solution.py:65
  (4 shorter events, 0.1 us)
Async XLA Ops:
  0.0 1.2 %copy-start = (bf16[1,2,512,512]{3,2,1,0:T(8,128)(2,1)S(1)}, bf16[1,2,512,512]{3,2,1,0:T(8,128)(2,1)}, u32[]{:S(2)}) copy-start(bf16[1,2,512,512]{3,2,1,0:T(8,128)(2,1)} %param.5) | copy-start | bytes 3145732
  2.9 29.4 %copy-start.2 = (bf16[1,4,2,112,256]{4,3,2,1,0:T(8,128)(2,1)S(1)}, bf16[1,4,2,112,256]{4,3,2,1,0:T(8,128)(2,1)}, u32[]{:S(2)}) copy-start(bf16[1,4,2,112,256]{4,3,2,1,0:T(8,128)(2,1)} %param.7) | copy-start | bytes 1376260
  32.3 5.6 %copy-start.1 = (s32[2,64,512]{2,1,0:T(8,128)S(1)}, s32[2,64,512]{2,1,0:T(8,128)}, u32[]{:S(2)}) copy-start(s32[2,64,512]{2,1,0:T(8,128)} %param.9) | copy-start | bytes 786436
  34.4 12.3 %all-to-all-start.1 = ((bf16[1,2,256,512]{3,1,0,2:T(2,128)(2,1)}), bf16[1,2,256,512]{3,1,0,2:T(2,128)(2,1)S(1)}, u32[]{:S(2)}, u32[]{:S(2)}) async-start(bf16[1,2,256,512]{3,1,0,2:T(2,128)(2,1)} %copy.26), calls=%async_computation.1 | async-start | bytes 1048576 | tf_op jit(solution)/shard_map/all_to_all | solution.py:59
where the time goes:
time: 53.9 us; the launch traced here: 53.6 us
  blocking collectives  29 us (54%)
  matrix products  8.92 us (17%)
  waiting for transfers between devices  8.76 us (16%)
  starting transfers between devices  3.47 us (6%)
  local copies, waits for them, and re-layouts  2.15 us (4%)
  other arithmetic  1.19 us (2%)
    all_to_all x1, blocking collectives, per_device(): lax.all_to_all(sending, 'tile', split_axis=0, concat_axis=0, tiled=True)  29 us
    all_to_all x1, waiting for transfers between devices, per_device(): lax.all_to_all(spectra, 'freq', split_axis=2, concat_axis=0, tiled=True)  8.76 us
    dot_general x1, matrix products, per_device(): jnp.einsum('frs,fn->rns', widened[:, 1], sine_table, precision=lax.Precis...  4.53 us
    all_to_all x1, starting transfers between devices, per_device(): lax.all_to_all(spectra, 'freq', split_axis=2, concat_axis=0, tiled=True)  3.47 us
    dot_general x1, matrix products, per_device(): jnp.einsum('frs,fn->rns', widened[:, 0], cosine_table, precision=lax.Prec...  2.01 us
    dot_general x1, matrix products, column_products(): lax.dot_general(v_local, x_local, (((3,), (1,)), ((), ())), preferred_ele...  1.65 us
    another operation x1, local copies, waits for them, and re-layouts, finish_spectrum(): return jnp.stack([real_part, imag_part], axis=0).astype(jnp.bfloat16)  1.18 us
  transfers between devices with their start and end apart: 1, of which 1 were waited for; matrix products, arithmetic and copies ran while one was open for 0% of the time, Pallas kernels for 0%

commit v1 on v0

v1 whole, which is shorter than its diff:
```python
import math

import jax
import jax.numpy as jnp
from jax import lax
from jax.sharding import PartitionSpec as P

NT = 32
S_CHUNKS = 1


first_bin = 2


def inverse_tables(count_freq, count_time):
    freq_index = jnp.arange(count_freq, dtype=jnp.int32)[:, None] + first_bin
    time_index = jnp.arange(count_time, dtype=jnp.int32)[None, :]
    phase_step = freq_index * time_index % count_time
    angles = phase_step.astype(jnp.float32) * (2.0 * math.pi / count_time)
    return (jnp.cos(angles), jnp.sin(angles))


def column_products(v_local, x_local, rank_local):
    products = lax.dot_general(
        v_local, x_local, (((3,), (1,)), ((), ())), preferred_element_type=jnp.float32
    )
    coef_real = products[:, 0, :, 0] - products[:, 1, :, 1]
    coef_imag = products[:, 0, :, 1] + products[:, 1, :, 0]
    slot_index = jnp.arange(v_local.shape[2], dtype=jnp.int32)
    live_slots = slot_index[None, :, None] < rank_local[:, None, None]
    coef_real = jnp.where(live_slots, coef_real, jnp.float32(0.0)).astype(jnp.bfloat16)
    coef_imag = jnp.where(live_slots, coef_imag, jnp.float32(0.0)).astype(jnp.bfloat16)
    return jnp.stack([coef_real, coef_imag], axis=1)


def row_spectrum(u_local, blocks):
    products = lax.dot_general(
        u_local, blocks, (((0, 2), (0, 2)), ((), ())), preferred_element_type=jnp.float32
    )
    real_part = products[0, :, 0] - products[1, :, 1]
    imag_part = products[0, :, 1] + products[1, :, 0]
    return jnp.stack([real_part, imag_part], axis=0).astype(jnp.bfloat16)


def relay_exchange(own, u_local):
    t = lax.axis_index("tile")
    up = [(0, 1), (1, 2), (2, 3)]
    down = [(1, 0), (2, 1), (3, 2)]
    up1 = lax.ppermute(own[1], "tile", up)
    down1 = lax.ppermute(own[0], "tile", down)
    up2 = lax.ppermute(jnp.where(t == 0, own[0], up1), "tile", up)
    down2 = lax.ppermute(jnp.where(t == 3, own[1], down1), "tile", down)
    up3 = lax.ppermute(up2, "tile", [(2, 3)])
    down3 = lax.ppermute(down2, "tile", [(1, 0)])
    orders = (
        lambda: (own[0], down1, down2, down3),
        lambda: (up2, own[0], down1, down2),
        lambda: (up2, up1, own[1], down2),
        lambda: (up3, up2, up1, own[1]),
    )
    branches = [
        (lambda order: (lambda: row_spectrum(u_local, jnp.stack(order(), axis=0))))(order)
        for order in orders
    ]
    return lax.switch(t, branches)


def gather_exchange(own, u_local, n_tile):
    repeat = n_tile // own.shape[0]
    sending = jnp.repeat(own, repeat, axis=0)
    received = lax.all_to_all(sending, "tile", split_axis=0, concat_axis=0, tiled=True)
    return row_spectrum(u_local, received)


def make_per_device(n_tile):
    def per_device(sources, v_factors, u_factors, tile_ranks, window_bounds):
        v_local = v_factors[0, 0]
        u_local = u_factors[0]
        x_local = sources[0]
        rank_local = tile_ranks[0, :, 0]
        rows = v_local.shape[0]
        use_relay = n_tile == 4 and rows == 2 and u_local.shape[0] == 4
        count_s = x_local.shape[2]
        chunks = S_CHUNKS if count_s % S_CHUNKS == 0 else 1
        width = count_s // chunks
        received_parts = []
        for c in range(chunks):
            x_part = x_local[:, :, c * width:(c + 1) * width]
            own = column_products(v_local, x_part, rank_local)
            if use_relay:
                spectrum = relay_exchange(own, u_local)
            else:
                spectrum = gather_exchange(own, u_local, n_tile)
            received_parts.append(
                lax.all_to_all(spectrum[None], "freq", split_axis=2, concat_axis=0, tiled=True)
            )
        received = jnp.concatenate(received_parts, axis=3) if chunks > 1 else received_parts[0]
        count_freq = received.shape[0]
        cosine_table, sine_table = inverse_tables(count_freq, NT)
        widened = received.astype(jnp.float32)
        real_sum = 0.0
        imag_sum = 0.0
        for f in range(count_freq):
            real_sum = real_sum + widened[f, 0][:, None, :] * cosine_table[f][None, :, None]
            imag_sum = imag_sum + widened[f, 1][:, None, :] * sine_table[f][None, :, None]
        traces = (real_sum - imag_sum) * (1.0 / math.sqrt(count_freq))
        time_index = jnp.arange(NT, dtype=jnp.int32)[None, :, None]
        inside = (time_index >= window_bounds[0][:, None, :]) & (
            time_index < window_bounds[1][:, None, :]
        )
        return jnp.where(inside, traces, jnp.float32(0.0))

    return per_device


def solution(mesh):
    return jax.shard_map(
        make_per_device(mesh.shape["tile"]),
        mesh=mesh,
        in_specs=(
            P("freq", "grp", "tile", None),
            P("freq", "tile", None, "grp", None, None),
            P("freq", None, "grp", None, "tile"),
            P("freq", "grp", "tile"),
            P("grp", ("tile", "freq"), None),
        ),
        out_specs=P(("tile", "freq"), "grp", None),
        check_vma=False,
    )
```

time: 53.9 us -> 58.6 us (1.087)
  blocking collectives: 29 us -> 0 us
  waiting for transfers between devices: 8.76 us -> 28.3 us
  starting transfers between devices: 3.47 us -> 18.8 us
  matrix products: 8.92 us -> 3.33 us
  other arithmetic: 1.19 us -> 5.77 us
    all_to_all x1 -> x0, blocking collectives: 29 us -> none  [per_device(): lax.all_to_all(sending, 'tile', split_axis=0, concat_axis=0, tiled=True)]
    ppermute x0 -> x6, waiting for transfers between devices: none -> 19.5 us  [the longest x1 6.63 us: relay_exchange(): down3 = lax.ppermute(down2, 'tile', [(1, 0)])]
    ppermute x0 -> x6, starting transfers between devices: none -> 15.3 us  [the longest x1 5.7 us: relay_exchange(): up2 = lax.ppermute(jnp.where(t == 0, own[0], up1), 'tile', up)]
    dot_general x3 -> x1, matrix products: 7.27 us -> 1.68 us  [row_spectrum(): lax.dot_general(u_local, blocks, (((0, 2), (0, 2)), ((), ())), preferred_...]
    select_n x0 -> x3, other arithmetic: none -> 4.32 us  [the longest x1 4.26 us: per_device(): return jnp.where(inside, traces, jnp.float32(0.0))]
    unnamed x6 -> x8, local copies, waits for them, and re-layouts: 0.43 us -> 1.65 us
    another operation x2 -> x0, local copies, waits for them, and re-layouts: 1.21 us -> none  [the longest x1 1.18 us: finish_spectrum(): return jnp.stack([real_part, imag_part], axis=0).astype(jnp.bfloat16)]
  transfers between devices with their start and end apart: 1 -> 7, of which waited for: 1 -> 5; matrix products, arithmetic and copies ran while one was open for 0% -> 0% of each run, Pallas kernels for 0% -> 0%
where the time goes in v1:
time: 58.6 us; the launch traced here: 58.2 us
  waiting for transfers between devices  28.3 us (48%)
  starting transfers between devices  18.8 us (32%)
  other arithmetic  5.77 us (10%)
  matrix products  3.33 us (6%)
  local copies, waits for them, and re-layouts  1.82 us (3%)
    all_to_all x1, waiting for transfers between devices, per_device(): lax.all_to_all(spectrum[None], 'freq', split_axis=2, concat_axis=0, tiled...  8.76 us
    ppermute x1, waiting for transfers between devices, relay_exchange(): down3 = lax.ppermute(down2, 'tile', [(1, 0)])  6.63 us
    ppermute x1, waiting for transfers between devices, relay_exchange(): down2 = lax.ppermute(jnp.where(t == 3, own[1], down1), 'tile', down)  5.97 us
    ppermute x1, starting transfers between devices, relay_exchange(): up2 = lax.ppermute(jnp.where(t == 0, own[0], up1), 'tile', up)  5.7 us
    ppermute x1, starting transfers between devices, relay_exchange(): up1 = lax.ppermute(own[1], 'tile', up)  5.07 us
    ppermute x1, waiting for transfers between devices, relay_exchange(): up1 = lax.ppermute(own[1], 'tile', up)  4.82 us
    select_n x1, other arithmetic, per_device(): return jnp.where(inside, traces, jnp.float32(0.0))  4.26 us
    all_to_all x1, starting transfers between devices, per_device(): lax.all_to_all(spectrum[None], 'freq', split_axis=2, concat_axis=0, tiled...  3.47 us
  transfers between devices with their start and end apart: 7, of which 5 were waited for; matrix products, arithmetic and copies ran while one was open for 0% of the time, Pallas kernels for 0%

profile of v1, /device:TPU:0, one launch (start us, length us, event | category | flops | bytes accessed | tf_op | source)
XLA Modules:
  0.0 58.2 jit_solution(6450538746881997647)
XLA Ops:
  0.0 0.0 copy-start
  0.0 0.8 %iota_compare_fusion.2 = pred[2,112]{1,0:T(4,128)(4,1)S(1)} fusion(s32[2]{0:T(128)} %bitcast.225), kind=kLoop, calls=%fused_computation.116 | loop fusion | flops 224 | bytes 232 | tf_op jit(solution)/shard_map/lt | solution.py:30
  0.8 0.4 copy-done
  1.2 1.7 %fusion.45 = f32[2,2,112,2,512]{4,2,3,1,0:T(8,128)S(1)} fusion(bf16[1,2,512,512]{3,2,1,0:T(8,128)(2,1)S(1)} %copy-done, bf16[1,1,2,2,112,512]{5,4,3,2,1,0:T(8,128)(2,1)} %param.10), kind=kOutput, calls=%fused_computation.72 | convolution fusion | flops 469762048 | bytes 3342336 | tf_op jit(solution)/shard_map/dot_general | solution.py:24
  2.9 0.2 fusion.53
  3.1 0.0 copy-start.1
  3.1 5.1 %collective-permute-start.3 = (bf16[2,112,512]{2,1,0:T(8,128)(2,1)S(1)}, bf16[2,112,512]{2,1,0:T(8,128)(2,1)S(1)}, u32[]{:S(2)}, u32[]{:S(2)}) collective-permute-start(bf16[2,112,512]{2,1,0:T(8,128)(2,1)S(1)} %fusion.58), channel_id=1, source_target_pairs={{0,4},{4,8},{8,12},{1,5},{5,9},{9,13},{2,6},{6,10},{10,14},{3,7},{... | collective-permute-start | bytes 688136 | tf_op jit(solution)/shard_map/ppermute | solution.py:49
  8.2 4.8 %collective-permute-done.3 = bf16[2,112,512]{2,1,0:T(8,128)(2,1)S(1)} collective-permute-done((bf16[2,112,512]{2,1,0:T(8,128)(2,1)S(1)}, bf16[2,112,512]{2,1,0:T(8,128)(2,1)S(1)}, u32[]{:S(2)}, u32[]{:S(2)}) %collective-permute-start.3) | collective-permute-done | bytes 229408 | tf_op jit(solution)/shard_map/ppermute | solution.py:49
  13.1 1.3 %collective-permute-start = (bf16[2,112,512]{2,1,0:T(8,128)(2,1)S(1)}, bf16[2,112,512]{2,1,0:T(8,128)(2,1)S(1)}, u32[]{:S(2)}, u32[]{:S(2)}) collective-permute-start(bf16[2,112,512]{2,1,0:T(8,128)(2,1)S(1)} %get-tuple-element.73), channel_id=1, source_target_pairs={{4,0},{8,4},{12,8},{5,1},{9,5},{13,9},{6,2},{10,6},{14,10},{7,3},{... | collective-permute-start | bytes 688136 | tf_op jit(solution)/shard_map/ppermute | solution.py:50
  14.4 5.7 %collective-permute-start.4 = (bf16[2,112,512]{2,1,0:T(8,128)(2,1)S(1)}, bf16[2,112,512]{2,1,0:T(8,128)(2,1)}, u32[]{:S(2)}, u32[]{:S(2)}) collective-permute-start(bf16[2,112,512]{2,1,0:T(8,128)(2,1)S(1)} %get-tuple-element.72), channel_id=1, source_target_pairs={{0,4},{4,8},{8,12},{1,5},{5,9},{9,13},{2,6},{6,10},{10,14},{3,7},{... | collective-permute-start | bytes 688136 | tf_op jit(solution)/shard_map/ppermute | solution.py:51
  20.1 2.1 %collective-permute-done = bf16[2,112,512]{2,1,0:T(8,128)(2,1)S(1)} collective-permute-done((bf16[2,112,512]{2,1,0:T(8,128)(2,1)S(1)}, bf16[2,112,512]{2,1,0:T(8,128)(2,1)S(1)}, u32[]{:S(2)}, u32[]{:S(2)}) %collective-permute-start) | collective-permute-done | bytes 229408 | tf_op jit(solution)/shard_map/ppermute | solution.py:50
  22.2 1.3 %collective-permute-start.1 = (bf16[2,112,512]{2,1,0:T(8,128)(2,1)S(1)}, bf16[2,112,512]{2,1,0:T(8,128)(2,1)}, u32[]{:S(2)}, u32[]{:S(2)}) collective-permute-start(bf16[2,112,512]{2,1,0:T(8,128)(2,1)S(1)} %broadcast_select_fusion.1), channel_id=1, source_target_pairs={{4,0},{8,4},{12,8},{5,1},{9,5},{13,9},{6,2},{10,6},{14,10},{7,3},{... | collective-permute-start | bytes 688136 | tf_op jit(solution)/shard_map/ppermute | solution.py:52
  23.6 0.0 collective-permute-done.4
  23.6 0.7 %collective-permute-start.5 = (bf16[2,112,512]{2,1,0:T(8,128)(2,1)}, bf16[2,112,512]{2,1,0:T(8,128)(2,1)S(1)}, u32[]{:S(2)}, u32[]{:S(2)}) collective-permute-start(bf16[2,112,512]{2,1,0:T(8,128)(2,1)} %collective-permute-done.4), channel_id=1, source_target_pairs={{8,12},{9,13},{10,14},{11,15},{24,28},{25,29},{26,30},{27,31}} | collective-permute-start | bytes 688136 | tf_op jit(solution)/shard_map/ppermute | solution.py:53
  24.3 6.0 %collective-permute-done.1 = bf16[2,112,512]{2,1,0:T(8,128)(2,1)} collective-permute-done((bf16[2,112,512]{2,1,0:T(8,128)(2,1)S(1)}, bf16[2,112,512]{2,1,0:T(8,128)(2,1)}, u32[]{:S(2)}, u32[]{:S(2)}) %collective-permute-start.1) | collective-permute-done | bytes 229408 | tf_op jit(solution)/shard_map/ppermute | solution.py:52
  30.2 1.3 %collective-permute-start.2 = (bf16[2,112,512]{2,1,0:T(8,128)(2,1)}, bf16[2,112,512]{2,1,0:T(8,128)(2,1)S(1)}, u32[]{:S(2)}, u32[]{:S(2)}) collective-permute-start(bf16[2,112,512]{2,1,0:T(8,128)(2,1)} %collective-permute-done.1), channel_id=1, source_target_pairs={{4,0},{5,1},{6,2},{7,3},{20,16},{21,17},{22,18},{23,19}} | collective-permute-start | bytes 688136 | tf_op jit(solution)/shard_map/ppermute | solution.py:54
  31.6 0.1 fusion.63
  31.7 0.0 collective-permute-done.5
  31.7 6.6 %collective-permute-done.2 = bf16[2,112,512]{2,1,0:T(8,128)(2,1)S(1)} collective-permute-done((bf16[2,112,512]{2,1,0:T(8,128)(2,1)}, bf16[2,112,512]{2,1,0:T(8,128)(2,1)S(1)}, u32[]{:S(2)}, u32[]{:S(2)}) %collective-permute-start.2) | collective-permute-done | bytes 229408 | tf_op jit(solution)/shard_map/ppermute | solution.py:54
  38.3 1.9 %conditional.2 = (bf16[2,256,512]{1,2,0:T(8,128)(2,1)S(1)}) conditional(s32[]{:T(128)} %clamp.3, (bf16[2,2,112,512]{3,2,0,1:T(8,128)(2,1)S(1)}, bf16[2,112,512]{2,1,0:T(8,128)(2,1)S(1)}, bf16[2,112,512]{2,1,0:T(8,128)(2,1)}, bf16[2,112,512]{2,1,0:T(8,128)(2,1)S(1)}, bf16[4,2,112,256]{3,2,0,1:T(8,128)(2,1)S(1)}) %tuple.51, ...), branch_computations={%region_0.1_spmd, %region_1.2_spmd, %region_2.3_spmd, %region_3.4_... | conditional | flops 474218496 | bytes 7602184
  38.4 1.7 %convolution_bitcast_fusion = f32[2,256,2,512]{1,3,0,2:T(8,128)S(1)} fusion(bf16[1,2,112,512]{3,2,0,1:T(8,128)(2,1)S(1)} %bitcast.224, bf16[1,2,112,512]{3,2,0,1:T(8,128)(2,1)} %bitcast.1, bf16[1,2,112,512]{3,2,0,1:T(8,128)(2,1)S(1)} %bitcast.219, bf16[1,2,112,512]{3,2,0,1:T(8,128)(2,1)S(1)} %slice.62, bf16[4,2,112,256]{3,2,0,1:T(8,128)(2,1)S(1)} %get-tuple-element.56), kind=kOutput, calls=%fused_computation | convolution fusion | flops 473432064 | bytes 3473408 | tf_op jit(solution)/shard_map/cond/branch_0_fun/dot_general | solution.py:37
  40.0 0.1 fusion.6
  40.1 0.1 fusion.8
  40.2 0.1 pad_maximum_fusion
  40.2 0.0 copy-start.2
  40.3 1.2 %copy.67 = bf16[2,256,512]{2,0,1:T(2,128)(2,1)} copy(bf16[2,256,512]{1,2,0:T(8,128)(2,1)S(1)} %get-tuple-element.100) | data formatting | bytes 1048576
  41.4 3.5 %all-to-all-start = ((bf16[1,2,256,512]{3,1,0,2:T(2,128)(2,1)}), bf16[1,2,256,512]{3,1,0,2:T(2,128)(2,1)S(1)}, u32[]{:S(2)}, u32[]{:S(2)}) async-start(bf16[1,2,256,512]{3,1,0,2:T(2,128)(2,1)} %bitcast.62), calls=%async_computation | async-start | bytes 1048576 | tf_op jit(solution)/shard_map/all_to_all | solution.py:95
  45.0 8.8 %all-to-all-done = bf16[1,2,256,512]{3,1,0,2:T(2,128)(2,1)S(1)} async-done(((bf16[1,2,256,512]{3,1,0,2:T(2,128)(2,1)}), bf16[1,2,256,512]{3,1,0,2:T(2,128)(2,1)S(1)}, u32[]{:S(2)}, u32[]{:S(2)}) %all-to-all-start) | async-done | bytes 524320 | tf_op jit(solution)/shard_map/all_to_all | solution.py:95
  53.7 0.1 copy.45
  53.8 0.1 convert_bitcast_fusion
  53.9 0.1 slice_bitcast_fusion.17
  54.0 4.3 %multiply_select_fusion = f32[64,32,512]{2,1,0:T(8,128)} fusion(f32[32]{0:T(128)S(1)} %get-tuple-element.91, f32[64,512]{1,0:T(8,128)S(1)} %get-tuple-element.77, f32[32]{0:T(128)S(1)} %get-tuple-element.92, f32[64,512]{1,0:T(8,128)S(1)} %get-tuple-element.78, f32[32]{0:T(128)S(1)} %get-tuple-element.93, f32[64,512]{1,0:T(8,128)S(1)} %get-tuple-element.79, ...), kind=kLoop, calls=%fused_computation.68 | loop fusion | flops 20971520 | bytes 5506048 | tf_op jit(solution)/shard_map/jit(_where)/select_n | solution.py:111
  (11 shorter events, 0.2 us)
Async XLA Ops:
  0.0 1.2 %copy-start = (bf16[1,2,512,512]{3,2,1,0:T(8,128)(2,1)S(1)}, bf16[1,2,512,512]{3,2,1,0:T(8,128)(2,1)}, u32[]{:S(2)}) copy-start(bf16[1,2,512,512]{3,2,1,0:T(8,128)(2,1)} %param.9) | copy-start | bytes 3145732
  3.1 28.5 %copy-start.1 = (bf16[1,4,2,112,256]{4,3,2,1,0:T(8,128)(2,1)S(1)}, bf16[1,4,2,112,256]{4,3,2,1,0:T(8,128)(2,1)}, u32[]{:S(2)}) copy-start(bf16[1,4,2,112,256]{4,3,2,1,0:T(8,128)(2,1)} %param.11) | copy-start | bytes 1376260
  3.1 9.9 %collective-permute-start.3 = (bf16[2,112,512]{2,1,0:T(8,128)(2,1)S(1)}, bf16[2,112,512]{2,1,0:T(8,128)(2,1)S(1)}, u32[]{:S(2)}, u32[]{:S(2)}) collective-permute-start(bf16[2,112,512]{2,1,0:T(8,128)(2,1)S(1)} %fusion.58), channel_id=1, source_target_pairs={{0,4},{4,8},{8,12},{1,5},{5,9},{9,13},{2,6},{6,10},{10,14},{3,7},{... | collective-permute-start | bytes 688136 | tf_op jit(solution)/shard_map/ppermute | solution.py:49
  13.1 9.1 %collective-permute-start = (bf16[2,112,512]{2,1,0:T(8,128)(2,1)S(1)}, bf16[2,112,512]{2,1,0:T(8,128)(2,1)S(1)}, u32[]{:S(2)}, u32[]{:S(2)}) collective-permute-start(bf16[2,112,512]{2,1,0:T(8,128)(2,1)S(1)} %get-tuple-element.73), channel_id=1, source_target_pairs={{4,0},{8,4},{12,8},{5,1},{9,5},{13,9},{6,2},{10,6},{14,10},{7,3},{... | collective-permute-start | bytes 688136 | tf_op jit(solution)/shard_map/ppermute | solution.py:50
  14.4 9.2 %collective-permute-start.4 = (bf16[2,112,512]{2,1,0:T(8,128)(2,1)S(1)}, bf16[2,112,512]{2,1,0:T(8,128)(2,1)}, u32[]{:S(2)}, u32[]{:S(2)}) collective-permute-start(bf16[2,112,512]{2,1,0:T(8,128)(2,1)S(1)} %get-tuple-element.72), channel_id=1, source_target_pairs={{0,4},{4,8},{8,12},{1,5},{5,9},{9,13},{2,6},{6,10},{10,14},{3,7},{... | collective-permute-start | bytes 688136 | tf_op jit(solution)/shard_map/ppermute | solution.py:51
  22.2 8.0 %collective-permute-start.1 = (bf16[2,112,512]{2,1,0:T(8,128)(2,1)S(1)}, bf16[2,112,512]{2,1,0:T(8,128)(2,1)}, u32[]{:S(2)}, u32[]{:S(2)}) collective-permute-start(bf16[2,112,512]{2,1,0:T(8,128)(2,1)S(1)} %broadcast_select_fusion.1), channel_id=1, source_target_pairs={{4,0},{8,4},{12,8},{5,1},{9,5},{13,9},{6,2},{10,6},{14,10},{7,3},{... | collective-permute-start | bytes 688136 | tf_op jit(solution)/shard_map/ppermute | solution.py:52
  23.6 8.1 %collective-permute-start.5 = (bf16[2,112,512]{2,1,0:T(8,128)(2,1)}, bf16[2,112,512]{2,1,0:T(8,128)(2,1)S(1)}, u32[]{:S(2)}, u32[]{:S(2)}) collective-permute-start(bf16[2,112,512]{2,1,0:T(8,128)(2,1)} %collective-permute-done.4), channel_id=1, source_target_pairs={{8,12},{9,13},{10,14},{11,15},{24,28},{25,29},{26,30},{27,31}} | collective-permute-start | bytes 688136 | tf_op jit(solution)/shard_map/ppermute | solution.py:53
  30.2 8.1 %collective-permute-start.2 = (bf16[2,112,512]{2,1,0:T(8,128)(2,1)}, bf16[2,112,512]{2,1,0:T(8,128)(2,1)S(1)}, u32[]{:S(2)}, u32[]{:S(2)}) collective-permute-start(bf16[2,112,512]{2,1,0:T(8,128)(2,1)} %collective-permute-done.1), channel_id=1, source_target_pairs={{4,0},{5,1},{6,2},{7,3},{20,16},{21,17},{22,18},{23,19}} | collective-permute-start | bytes 688136 | tf_op jit(solution)/shard_map/ppermute | solution.py:54
  40.2 4.7 %copy-start.2 = (s32[2,64,512]{2,1,0:T(8,128)S(1)}, s32[2,64,512]{2,1,0:T(8,128)}, u32[]{:S(2)}) copy-start(s32[2,64,512]{2,1,0:T(8,128)} %param.13) | copy-start | bytes 786436
  41.4 12.3 %all-to-all-start = ((bf16[1,2,256,512]{3,1,0,2:T(2,128)(2,1)}), bf16[1,2,256,512]{3,1,0,2:T(2,128)(2,1)S(1)}, u32[]{:S(2)}, u32[]{:S(2)}) async-start(bf16[1,2,256,512]{3,1,0,2:T(2,128)(2,1)} %bitcast.62), calls=%async_computation | async-start | bytes 1048576 | tf_op jit(solution)/shard_map/all_to_all | solution.py:95

commit v2 on v1

--- a/solution.py
+++ b/solution.py
@@ -6,7 +6,7 @@
 from jax.sharding import PartitionSpec as P
 
 NT = 32
-S_CHUNKS = 1
+S_CHUNKS = 2
 
 
 first_bin = 2

time: 58.6 us -> 70.3 us (1.20)
  starting transfers between devices: 18.8 us -> 33.8 us
  waiting for transfers between devices: 28.3 us -> 22.8 us
  local copies, waits for them, and re-layouts: 1.82 us -> 2.97 us
    ppermute x1 -> x2, waiting for transfers between devices: 5.97 us -> 0.04 us  [relay_exchange(): down2 = lax.ppermute(jnp.where(t == 3, own[1], down1), 'tile', down)]
    ppermute x1 -> x2, starting transfers between devices: 5.7 us -> 9.53 us  [relay_exchange(): up2 = lax.ppermute(jnp.where(t == 0, own[0], up1), 'tile', up)]
    ppermute x1 -> x2, waiting for transfers between devices: 6.63 us -> 10.1 us  [relay_exchange(): down3 = lax.ppermute(down2, 'tile', [(1, 0)])]
    ppermute x1 -> x2, starting transfers between devices: 5.07 us -> 8.42 us  [relay_exchange(): up1 = lax.ppermute(own[1], 'tile', up)]
    all_to_all x1 -> x2, starting transfers between devices: 3.47 us -> 6.81 us  [per_device(): lax.all_to_all(spectrum[None], 'freq', split_axis=2, concat_axis=0, tiled...]
    all_to_all x1 -> x2, waiting for transfers between devices: 8.76 us -> 5.95 us  [per_device(): lax.all_to_all(spectrum[None], 'freq', split_axis=2, concat_axis=0, tiled...]
    ppermute x1 -> x2, waiting for transfers between devices: 4.82 us -> 2.3 us  [relay_exchange(): up1 = lax.ppermute(own[1], 'tile', up)]
    ppermute x1 -> x2, waiting for transfers between devices: 2.11 us -> 4.4 us  [relay_exchange(): down1 = lax.ppermute(own[0], 'tile', down)]
  transfers between devices with their start and end apart: 7 -> 14, of which waited for: 5 -> 5; matrix products, arithmetic and copies ran while one was open for 0% -> 5% of each run, Pallas kernels for 0% -> 0%
where the time goes in v2:
time: 70.3 us; the launch traced here: 69.7 us
  starting transfers between devices  33.8 us (48%)
  waiting for transfers between devices  22.8 us (32%)
  other arithmetic  5.77 us (8%)
  matrix products  3.87 us (6%)
  local copies, waits for them, and re-layouts  2.97 us (4%)
    ppermute x2, waiting for transfers between devices, relay_exchange(): down3 = lax.ppermute(down2, 'tile', [(1, 0)])  10.1 us
    ppermute x2, starting transfers between devices, relay_exchange(): up2 = lax.ppermute(jnp.where(t == 0, own[0], up1), 'tile', up)  9.53 us
    ppermute x2, starting transfers between devices, relay_exchange(): up1 = lax.ppermute(own[1], 'tile', up)  8.42 us
    all_to_all x2, starting transfers between devices, per_device(): lax.all_to_all(spectrum[None], 'freq', split_axis=2, concat_axis=0, tiled...  6.81 us
    all_to_all x2, waiting for transfers between devices, per_device(): lax.all_to_all(spectrum[None], 'freq', split_axis=2, concat_axis=0, tiled...  5.95 us
    ppermute x2, waiting for transfers between devices, relay_exchange(): down1 = lax.ppermute(own[0], 'tile', down)  4.4 us
    select_n x1, other arithmetic, per_device(): return jnp.where(inside, traces, jnp.float32(0.0))  4.26 us
    dot_general x2, matrix products, column_products(): lax.dot_general(v_local, x_local, (((3,), (1,)), ((), ())), preferred_ele...  2.94 us
  transfers between devices with their start and end apart: 14, of which 5 were waited for; matrix products, arithmetic and copies ran while one was open for 5% of the time, Pallas kernels for 0%

profile of v2, /device:TPU:0, one launch (start us, length us, event | category | flops | bytes accessed | tf_op | source)
XLA Modules:
  0.0 69.7 jit_solution(6855587100608741447)
XLA Ops:
  0.0 1.0 %copy-done = bf16[1,1,2,2,112,512]{5,4,3,2,1,0:T(8,128)(2,1)S(1)} copy-done((bf16[1,1,2,2,112,512]{5,4,3,2,1,0:T(8,128)(2,1)S(1)}, bf16[1,1,2,2,112,512]{5,4,3,2,1,0:T(8,128)(2,1)}, u32[]{:S(2)}) %copy-start) | copy-done | bytes 458776
  1.0 1.5 %fusion.90 = f32[2,2,112,2,256]{4,2,3,1,0:T(8,128)S(1)} fusion(bf16[2,512,512]{2,1,0:T(8,128)(2,1)} %bitcast.377, bf16[1,1,2,2,112,512]{5,4,3,2,1,0:T(8,128)(2,1)S(1)} %copy-done), kind=kOutput, calls=%fused_computation.143 | convolution fusion | flops 234881024 | bytes 1900544 | tf_op jit(solution)/shard_map/dot_general | solution.py:24
  2.5 1.4 %fusion.89 = f32[2,2,112,2,256]{4,2,0,3,1:T(8,128)S(1)} fusion(bf16[2,512,512]{2,1,0:T(8,128)(2,1)} %bitcast.378, bf16[1,1,2,2,112,512]{5,4,3,2,1,0:T(8,128)(2,1)S(1)} %copy-done), kind=kOutput, calls=%fused_computation.141 | convolution fusion | flops 234881024 | bytes 1900544 | tf_op jit(solution)/shard_map/dot_general | solution.py:24
  4.0 0.7 %iota_compare_fusion.2 = pred[2,112]{1,0:T(4,128)(4,1)S(1)} fusion(s32[2]{0:T(128)} %bitcast.408), kind=kLoop, calls=%fused_computation.207 | loop fusion | flops 224 | bytes 232 | tf_op jit(solution)/shard_map/lt | solution.py:30
  4.8 0.1 fusion.98
  5.0 4.9 %collective-permute-start.3 = (bf16[2,112,256]{2,1,0:T(8,128)(2,1)S(1)}, bf16[2,112,256]{2,1,0:T(8,128)(2,1)S(1)}, u32[]{:S(2)}, u32[]{:S(2)}) collective-permute-start(bf16[2,112,256]{2,1,0:T(8,128)(2,1)S(1)} %fusion.114), channel_id=1, source_target_pairs={{0,4},{4,8},{8,12},{1,5},{5,9},{9,13},{2,6},{6,10},{10,14},{3,7},{... | collective-permute-start | bytes 344072 | tf_op jit(solution)/shard_map/ppermute | solution.py:49
  9.9 3.5 %collective-permute-start.9 = (bf16[2,112,256]{2,1,0:T(8,128)(2,1)S(1)}, bf16[2,112,256]{2,1,0:T(8,128)(2,1)S(1)}, u32[]{:S(2)}, u32[]{:S(2)}) collective-permute-start(bf16[2,112,256]{2,1,0:T(8,128)(2,1)S(1)} %fusion.110), channel_id=1, source_target_pairs={{0,4},{4,8},{8,12},{1,5},{5,9},{9,13},{2,6},{6,10},{10,14},{3,7},{... | collective-permute-start | bytes 344072 | tf_op jit(solution)/shard_map/ppermute | solution.py:49
  13.5 2.3 %collective-permute-done.9 = bf16[2,112,256]{2,1,0:T(8,128)(2,1)S(1)} collective-permute-done((bf16[2,112,256]{2,1,0:T(8,128)(2,1)S(1)}, bf16[2,112,256]{2,1,0:T(8,128)(2,1)S(1)}, u32[]{:S(2)}, u32[]{:S(2)}) %collective-permute-start.9) | collective-permute-done | bytes 114720 | tf_op jit(solution)/shard_map/ppermute | solution.py:49
  15.8 5.0 %collective-permute-start.10 = (bf16[2,112,256]{2,1,0:T(8,128)(2,1)S(1)}, bf16[2,112,256]{2,1,0:T(8,128)(2,1)}, u32[]{:S(2)}, u32[]{:S(2)}) collective-permute-start(bf16[2,112,256]{2,1,0:T(8,128)(2,1)S(1)} %get-tuple-element.201), channel_id=1, source_target_pairs={{0,4},{4,8},{8,12},{1,5},{5,9},{9,13},{2,6},{6,10},{10,14},{3,7},{... | collective-permute-start | bytes 344072 | tf_op jit(solution)/shard_map/ppermute | solution.py:51
  20.8 1.3 %collective-permute-start.6 = (bf16[2,112,256]{2,1,0:T(8,128)(2,1)S(1)}, bf16[2,112,256]{2,1,0:T(8,128)(2,1)S(1)}, u32[]{:S(2)}, u32[]{:S(2)}) collective-permute-start(bf16[2,112,256]{2,1,0:T(8,128)(2,1)S(1)} %get-tuple-element.202), channel_id=1, source_target_pairs={{4,0},{8,4},{12,8},{5,1},{9,5},{13,9},{6,2},{10,6},{14,10},{7,3},{... | collective-permute-start | bytes 344072 | tf_op jit(solution)/shard_map/ppermute | solution.py:50
  22.1 1.3 %collective-permute-start = (bf16[2,112,256]{2,1,0:T(8,128)(2,1)S(1)}, bf16[2,112,256]{2,1,0:T(8,128)(2,1)S(1)}, u32[]{:S(2)}, u32[]{:S(2)}) collective-permute-start(bf16[2,112,256]{2,1,0:T(8,128)(2,1)S(1)} %get-tuple-element.200), channel_id=1, source_target_pairs={{4,0},{8,4},{12,8},{5,1},{9,5},{13,9},{6,2},{10,6},{14,10},{7,3},{... | collective-permute-start | bytes 344072 | tf_op jit(solution)/shard_map/ppermute | solution.py:50
  23.4 4.4 %collective-permute-done.6 = bf16[2,112,256]{2,1,0:T(8,128)(2,1)S(1)} collective-permute-done((bf16[2,112,256]{2,1,0:T(8,128)(2,1)S(1)}, bf16[2,112,256]{2,1,0:T(8,128)(2,1)S(1)}, u32[]{:S(2)}, u32[]{:S(2)}) %collective-permute-start.6) | collective-permute-done | bytes 114720 | tf_op jit(solution)/shard_map/ppermute | solution.py:50
  27.8 1.3 %collective-permute-start.7 = (bf16[2,112,256]{2,1,0:T(8,128)(2,1)S(1)}, bf16[2,112,256]{2,1,0:T(8,128)(2,1)S(1)}, u32[]{:S(2)}, u32[]{:S(2)}) collective-permute-start(bf16[2,112,256]{2,1,0:T(8,128)(2,1)S(1)} %broadcast_select_fusion.2), channel_id=1, source_target_pairs={{4,0},{8,4},{12,8},{5,1},{9,5},{13,9},{6,2},{10,6},{14,10},{7,3},{... | collective-permute-start | bytes 344072 | tf_op jit(solution)/shard_map/ppermute | solution.py:52
  29.2 4.6 %collective-permute-start.4 = (bf16[2,112,256]{2,1,0:T(8,128)(2,1)S(1)}, bf16[2,112,256]{2,1,0:T(8,128)(2,1)S(1)}, u32[]{:S(2)}, u32[]{:S(2)}) collective-permute-start(bf16[2,112,256]{2,1,0:T(8,128)(2,1)S(1)} %get-tuple-element.199), channel_id=1, source_target_pairs={{0,4},{4,8},{8,12},{1,5},{5,9},{9,13},{2,6},{6,10},{10,14},{3,7},{... | collective-permute-start | bytes 344072 | tf_op jit(solution)/shard_map/ppermute | solution.py:51
  33.8 0.7 collective-permute-start.11
  34.5 1.3 %collective-permute-start.8 = (bf16[2,112,256]{2,1,0:T(8,128)(2,1)S(1)}, bf16[2,112,256]{2,1,0:T(8,128)(2,1)S(1)}, u32[]{:S(2)}, u32[]{:S(2)}) collective-permute-start(bf16[2,112,256]{2,1,0:T(8,128)(2,1)S(1)} %collective-permute-done.7), channel_id=1, source_target_pairs={{4,0},{5,1},{6,2},{7,3},{20,16},{21,17},{22,18},{23,19}} | collective-permute-start | bytes 344072 | tf_op jit(solution)/shard_map/ppermute | solution.py:54
  35.8 1.3 %collective-permute-start.1 = (bf16[2,112,256]{2,1,0:T(8,128)(2,1)S(1)}, bf16[2,112,256]{2,1,0:T(8,128)(2,1)S(1)}, u32[]{:S(2)}, u32[]{:S(2)}) collective-permute-start(bf16[2,112,256]{2,1,0:T(8,128)(2,1)S(1)} %broadcast_select_fusion.3), channel_id=1, source_target_pairs={{4,0},{8,4},{12,8},{5,1},{9,5},{13,9},{6,2},{10,6},{14,10},{7,3},{... | collective-permute-start | bytes 344072 | tf_op jit(solution)/shard_map/ppermute | solution.py:52
  37.1 4.0 %collective-permute-done.8 = bf16[2,112,256]{2,1,0:T(8,128)(2,1)S(1)} collective-permute-done((bf16[2,112,256]{2,1,0:T(8,128)(2,1)S(1)}, bf16[2,112,256]{2,1,0:T(8,128)(2,1)S(1)}, u32[]{:S(2)}, u32[]{:S(2)}) %collective-permute-start.8) | collective-permute-done | bytes 114720 | tf_op jit(solution)/shard_map/ppermute | solution.py:54
  41.2 0.6 conditional.5
  41.2 0.5 convolution_bitcast_fusion.4
  41.8 0.9 %copy.148 = bf16[2,256,256]{2,0,1:T(2,128)(2,1)} copy(bf16[2,256,256]{1,2,0:T(8,128)(2,1)S(1)} %get-tuple-element.231) | data formatting | bytes 524288
  42.7 3.4 %all-to-all-start.1 = ((bf16[1,2,256,256]{3,1,0,2:T(2,128)(2,1)}), bf16[1,2,256,256]{3,1,0,2:T(2,128)(2,1)S(1)}, u32[]{:S(2)}, u32[]{:S(2)}) async-start(bf16[1,2,256,256]{3,1,0,2:T(2,128)(2,1)} %bitcast.124), calls=%async_computation.1 | async-start | bytes 524288 | tf_op jit(solution)/shard_map/all_to_all | solution.py:95
  46.1 0.1 fusion.119
  46.2 0.7 collective-permute-start.5
  46.9 1.3 %collective-permute-start.2 = (bf16[2,112,256]{2,1,0:T(8,128)(2,1)S(1)}, bf16[2,112,256]{2,1,0:T(8,128)(2,1)S(1)}, u32[]{:S(2)}, u32[]{:S(2)}) collective-permute-start(bf16[2,112,256]{2,1,0:T(8,128)(2,1)S(1)} %collective-permute-done.1), channel_id=1, source_target_pairs={{4,0},{5,1},{6,2},{7,3},{20,16},{21,17},{22,18},{23,19}} | collective-permute-start | bytes 344072 | tf_op jit(solution)/shard_map/ppermute | solution.py:54
  48.2 6.1 %collective-permute-done.2 = bf16[2,112,256]{2,1,0:T(8,128)(2,1)S(1)} collective-permute-done((bf16[2,112,256]{2,1,0:T(8,128)(2,1)S(1)}, bf16[2,112,256]{2,1,0:T(8,128)(2,1)S(1)}, u32[]{:S(2)}, u32[]{:S(2)}) %collective-permute-start.2) | collective-permute-done | bytes 114720 | tf_op jit(solution)/shard_map/ppermute | solution.py:54
  54.3 0.6 conditional.4
  54.3 0.5 convolution_bitcast_fusion
  54.9 0.9 %copy.147 = bf16[2,256,256]{2,0,1:T(2,128)(2,1)} copy(bf16[2,256,256]{1,2,0:T(8,128)(2,1)S(1)} %get-tuple-element.230) | data formatting | bytes 524288
  55.8 3.4 %all-to-all-start = ((bf16[1,2,256,256]{3,1,0,2:T(2,128)(2,1)}), bf16[1,2,256,256]{3,1,0,2:T(2,128)(2,1)S(1)}, u32[]{:S(2)}, u32[]{:S(2)}) async-start(bf16[1,2,256,256]{3,1,0,2:T(2,128)(2,1)} %bitcast.113), calls=%async_computation | async-start | bytes 524288 | tf_op jit(solution)/shard_map/all_to_all | solution.py:95
  59.2 5.9 %all-to-all-done = bf16[1,2,256,256]{3,1,0,2:T(2,128)(2,1)S(1)} async-done(((bf16[1,2,256,256]{3,1,0,2:T(2,128)(2,1)}), bf16[1,2,256,256]{3,1,0,2:T(2,128)(2,1)S(1)}, u32[]{:S(2)}, u32[]{:S(2)}) %all-to-all-start) | async-done | bytes 262176 | tf_op jit(solution)/shard_map/all_to_all | solution.py:95
  65.4 4.3 %multiply_select_fusion = f32[64,32,512]{2,1,0:T(8,128)} fusion(f32[32]{0:T(128)S(1)} %get-tuple-element.220, f32[64,512]{1,0:T(8,128)S(1)} %get-tuple-element.204, f32[32]{0:T(128)S(1)} %get-tuple-element.221, f32[64,512]{1,0:T(8,128)S(1)} %get-tuple-element.205, f32[32]{0:T(128)S(1)} %get-tuple-element.222, f32[64,512]{1,0:T(8,128)S(1)} %get-tuple-element.206, ...), kind=kLoop, calls=%fused_computation.136 | loop fusion | flops 20971520 | bytes 5506048 | tf_op jit(solution)/shard_map/jit(_where)/select_n | solution.py:111
  (40 shorter events, 0.8 us)
Async XLA Ops:
  0.0 1.0 %copy-start = (bf16[1,1,2,2,112,512]{5,4,3,2,1,0:T(8,128)(2,1)S(1)}, bf16[1,1,2,2,112,512]{5,4,3,2,1,0:T(8,128)(2,1)}, u32[]{:S(2)}) copy-start(bf16[1,1,2,2,112,512]{5,4,3,2,1,0:T(8,128)(2,1)} %param.14) | copy-start | bytes 1376260
  0.0 13.4 %copy-start.2 = (s32[2,64,512]{2,1,0:T(8,128)S(1)}, s32[2,64,512]{2,1,0:T(8,128)}, u32[]{:S(2)}) copy-start(s32[2,64,512]{2,1,0:T(8,128)} %param.17) | copy-start | bytes 786436
  1.0 28.1 %copy-start.1 = (bf16[1,4,2,112,256]{4,3,2,1,0:T(8,128)(2,1)S(1)}, bf16[1,4,2,112,256]{4,3,2,1,0:T(8,128)(2,1)}, u32[]{:S(2)}) copy-start(bf16[1,4,2,112,256]{4,3,2,1,0:T(8,128)(2,1)} %param.15) | copy-start | bytes 1376260
  5.0 17.1 %collective-permute-start.3 = (bf16[2,112,256]{2,1,0:T(8,128)(2,1)S(1)}, bf16[2,112,256]{2,1,0:T(8,128)(2,1)S(1)}, u32[]{:S(2)}, u32[]{:S(2)}) collective-permute-start(bf16[2,112,256]{2,1,0:T(8,128)(2,1)S(1)} %fusion.114), channel_id=1, source_target_pairs={{0,4},{4,8},{8,12},{1,5},{5,9},{9,13},{2,6},{6,10},{10,14},{3,7},{... | collective-permute-start | bytes 344072 | tf_op jit(solution)/shard_map/ppermute | solution.py:49
  9.9 5.8 %collective-permute-start.9 = (bf16[2,112,256]{2,1,0:T(8,128)(2,1)S(1)}, bf16[2,112,256]{2,1,0:T(8,128)(2,1)S(1)}, u32[]{:S(2)}, u32[]{:S(2)}) collective-permute-start(bf16[2,112,256]{2,1,0:T(8,128)(2,1)S(1)} %fusion.110), channel_id=1, source_target_pairs={{0,4},{4,8},{8,12},{1,5},{5,9},{9,13},{2,6},{6,10},{10,14},{3,7},{... | collective-permute-start | bytes 344072 | tf_op jit(solution)/shard_map/ppermute | solution.py:49
  15.8 18.0 %collective-permute-start.10 = (bf16[2,112,256]{2,1,0:T(8,128)(2,1)S(1)}, bf16[2,112,256]{2,1,0:T(8,128)(2,1)}, u32[]{:S(2)}, u32[]{:S(2)}) collective-permute-start(bf16[2,112,256]{2,1,0:T(8,128)(2,1)S(1)} %get-tuple-element.201), channel_id=1, source_target_pairs={{0,4},{4,8},{8,12},{1,5},{5,9},{9,13},{2,6},{6,10},{10,14},{3,7},{... | collective-permute-start | bytes 344072 | tf_op jit(solution)/shard_map/ppermute | solution.py:51
  20.8 7.0 %collective-permute-start.6 = (bf16[2,112,256]{2,1,0:T(8,128)(2,1)S(1)}, bf16[2,112,256]{2,1,0:T(8,128)(2,1)S(1)}, u32[]{:S(2)}, u32[]{:S(2)}) collective-permute-start(bf16[2,112,256]{2,1,0:T(8,128)(2,1)S(1)} %get-tuple-element.202), channel_id=1, source_target_pairs={{4,0},{8,4},{12,8},{5,1},{9,5},{13,9},{6,2},{10,6},{14,10},{7,3},{... | collective-permute-start | bytes 344072 | tf_op jit(solution)/shard_map/ppermute | solution.py:50
  22.1 13.7 %collective-permute-start = (bf16[2,112,256]{2,1,0:T(8,128)(2,1)S(1)}, bf16[2,112,256]{2,1,0:T(8,128)(2,1)S(1)}, u32[]{:S(2)}, u32[]{:S(2)}) collective-permute-start(bf16[2,112,256]{2,1,0:T(8,128)(2,1)S(1)} %get-tuple-element.200), channel_id=1, source_target_pairs={{4,0},{8,4},{12,8},{5,1},{9,5},{13,9},{6,2},{10,6},{14,10},{7,3},{... | collective-permute-start | bytes 344072 | tf_op jit(solution)/shard_map/ppermute | solution.py:50
  27.8 6.7 %collective-permute-start.7 = (bf16[2,112,256]{2,1,0:T(8,128)(2,1)S(1)}, bf16[2,112,256]{2,1,0:T(8,128)(2,1)S(1)}, u32[]{:S(2)}, u32[]{:S(2)}) collective-permute-start(bf16[2,112,256]{2,1,0:T(8,128)(2,1)S(1)} %broadcast_select_fusion.2), channel_id=1, source_target_pairs={{4,0},{8,4},{12,8},{5,1},{9,5},{13,9},{6,2},{10,6},{14,10},{7,3},{... | collective-permute-start | bytes 344072 | tf_op jit(solution)/shard_map/ppermute | solution.py:52
  29.2 17.0 %collective-permute-start.4 = (bf16[2,112,256]{2,1,0:T(8,128)(2,1)S(1)}, bf16[2,112,256]{2,1,0:T(8,128)(2,1)S(1)}, u32[]{:S(2)}, u32[]{:S(2)}) collective-permute-start(bf16[2,112,256]{2,1,0:T(8,128)(2,1)S(1)} %get-tuple-element.199), channel_id=1, source_target_pairs={{0,4},{4,8},{8,12},{1,5},{5,9},{9,13},{2,6},{6,10},{10,14},{3,7},{... | collective-permute-start | bytes 344072 | tf_op jit(solution)/shard_map/ppermute | solution.py:51
  33.8 3.3 %collective-permute-start.11 = (bf16[2,112,256]{2,1,0:T(8,128)(2,1)}, bf16[2,112,256]{2,1,0:T(8,128)(2,1)S(1)}, u32[]{:S(2)}, u32[]{:S(2)}) collective-permute-start(bf16[2,112,256]{2,1,0:T(8,128)(2,1)} %collective-permute-done.10), channel_id=1, source_target_pairs={{8,12},{9,13},{10,14},{11,15},{24,28},{25,29},{26,30},{27,31}} | collective-permute-start | bytes 344072 | tf_op jit(solution)/shard_map/ppermute | solution.py:53
  34.5 6.7 %collective-permute-start.8 = (bf16[2,112,256]{2,1,0:T(8,128)(2,1)S(1)}, bf16[2,112,256]{2,1,0:T(8,128)(2,1)S(1)}, u32[]{:S(2)}, u32[]{:S(2)}) collective-permute-start(bf16[2,112,256]{2,1,0:T(8,128)(2,1)S(1)} %collective-permute-done.7), channel_id=1, source_target_pairs={{4,0},{5,1},{6,2},{7,3},{20,16},{21,17},{22,18},{23,19}} | collective-permute-start | bytes 344072 | tf_op jit(solution)/shard_map/ppermute | solution.py:54
  35.8 11.1 %collective-permute-start.1 = (bf16[2,112,256]{2,1,0:T(8,128)(2,1)S(1)}, bf16[2,112,256]{2,1,0:T(8,128)(2,1)S(1)}, u32[]{:S(2)}, u32[]{:S(2)}) collective-permute-start(bf16[2,112,256]{2,1,0:T(8,128)(2,1)S(1)} %broadcast_select_fusion.3), channel_id=1, source_target_pairs={{4,0},{8,4},{12,8},{5,1},{9,5},{13,9},{6,2},{10,6},{14,10},{7,3},{... | collective-permute-start | bytes 344072 | tf_op jit(solution)/shard_map/ppermute | solution.py:52
  42.7 13.1 %all-to-all-start.1 = ((bf16[1,2,256,256]{3,1,0,2:T(2,128)(2,1)}), bf16[1,2,256,256]{3,1,0,2:T(2,128)(2,1)S(1)}, u32[]{:S(2)}, u32[]{:S(2)}) async-start(bf16[1,2,256,256]{3,1,0,2:T(2,128)(2,1)} %bitcast.124), calls=%async_computation.1 | async-start | bytes 524288 | tf_op jit(solution)/shard_map/all_to_all | solution.py:95
  46.2 2.0 %collective-permute-start.5 = (bf16[2,112,256]{2,1,0:T(8,128)(2,1)S(1)}, bf16[2,112,256]{2,1,0:T(8,128)(2,1)S(1)}, u32[]{:S(2)}, u32[]{:S(2)}) collective-permute-start(bf16[2,112,256]{2,1,0:T(8,128)(2,1)S(1)} %collective-permute-done.4), channel_id=1, source_target_pairs={{8,12},{9,13},{10,14},{11,15},{24,28},{25,29},{26,30},{27,31}} | collective-permute-start | bytes 344072 | tf_op jit(solution)/shard_map/ppermute | solution.py:53
  46.9 7.4 %collective-permute-start.2 = (bf16[2,112,256]{2,1,0:T(8,128)(2,1)S(1)}, bf16[2,112,256]{2,1,0:T(8,128)(2,1)S(1)}, u32[]{:S(2)}, u32[]{:S(2)}) collective-permute-start(bf16[2,112,256]{2,1,0:T(8,128)(2,1)S(1)} %collective-permute-done.1), channel_id=1, source_target_pairs={{4,0},{5,1},{6,2},{7,3},{20,16},{21,17},{22,18},{23,19}} | collective-permute-start | bytes 344072 | tf_op jit(solution)/shard_map/ppermute | solution.py:54
  55.8 9.4 %all-to-all-start = ((bf16[1,2,256,256]{3,1,0,2:T(2,128)(2,1)}), bf16[1,2,256,256]{3,1,0,2:T(2,128)(2,1)S(1)}, u32[]{:S(2)}, u32[]{:S(2)}) async-start(bf16[1,2,256,256]{3,1,0,2:T(2,128)(2,1)} %bitcast.113), calls=%async_computation | async-start | bytes 524288 | tf_op jit(solution)/shard_map/all_to_all | solution.py:95

commit v3 on v1

--- a/solution.py
+++ b/solution.py
@@ -44,25 +44,19 @@
 
 def relay_exchange(own, u_local):
     t = lax.axis_index("tile")
-    up = [(0, 1), (1, 2), (2, 3)]
-    down = [(1, 0), (2, 1), (3, 2)]
-    up1 = lax.ppermute(own[1], "tile", up)
-    down1 = lax.ppermute(own[0], "tile", down)
-    up2 = lax.ppermute(jnp.where(t == 0, own[0], up1), "tile", up)
-    down2 = lax.ppermute(jnp.where(t == 3, own[1], down1), "tile", down)
-    up3 = lax.ppermute(up2, "tile", [(2, 3)])
-    down3 = lax.ppermute(down2, "tile", [(1, 0)])
-    orders = (
-        lambda: (own[0], down1, down2, down3),
-        lambda: (up2, own[0], down1, down2),
-        lambda: (up2, up1, own[1], down2),
-        lambda: (up3, up2, up1, own[1]),
+    row = t // 2
+    mine = lax.dynamic_index_in_dim(own, row, 0, keepdims=False)
+    other = lax.dynamic_index_in_dim(own, 1 - row, 0, keepdims=False)
+    across = lax.ppermute(other, "tile", [(0, 2), (2, 0), (1, 3), (3, 1)])
+    swapped = lax.ppermute(
+        jnp.stack([mine, across], axis=0), "tile", [(0, 1), (1, 0), (2, 3), (3, 2)]
     )
-    branches = [
-        (lambda order: (lambda: row_spectrum(u_local, jnp.stack(order(), axis=0))))(order)
-        for order in orders
-    ]
-    return lax.switch(t, branches)
+    columns = (t, t ^ 2, t ^ 1, t ^ 3)
+    u_order = jnp.stack(
+        [lax.dynamic_index_in_dim(u_local, j, 0, keepdims=False) for j in columns], axis=0
+    )
+    blocks = jnp.concatenate([mine[None], across[None], swapped], axis=0)
+    return row_spectrum(u_order, blocks)
 
 
 def gather_exchange(own, u_local, n_tile):

time: 58.6 us -> 49.9 us (0.85)
  starting transfers between devices: 18.8 us -> 8.36 us
  waiting for transfers between devices: 28.3 us -> 30.1 us
  matrix products: 3.33 us -> 2.38 us
  local copies, waits for them, and re-layouts: 1.82 us -> 2.69 us
    ppermute x6 -> x2, starting transfers between devices: 15.3 us -> 4.89 us  [the longest x1 4.1 us: relay_exchange(): across = lax.ppermute(other, 'tile', [(0, 2), (2, 0), (1, 3), (3, 1)])]
    ppermute x6 -> x2, waiting for transfers between devices: 19.5 us -> 21.3 us  [the longest x1 10.8 us: relay_exchange(): lax.ppermute(jnp.stack([mine, across], axis=0), 'tile', [(0, 1), (1, 0),...]
    another operation x0 -> x1, local copies, waits for them, and re-layouts: none -> 1.33 us  [row_spectrum(): return jnp.stack([real_part, imag_part], axis=0).astype(jnp.bfloat16)]
    unnamed x8 -> x10, local copies, waits for them, and re-layouts: 1.65 us -> 0.48 us
    dot_general x1, matrix products: 1.68 us -> 0.72 us  [row_spectrum(): lax.dot_general(u_local, blocks, (((0, 2), (0, 2)), ((), ())), preferred_...]
    slice x1, local copies, waits for them, and re-layouts: 0.02 us -> 0.81 us  [per_device(): widened[f, 0][:, None, :] * cosine_table[f][None, :, None]]
  transfers between devices with their start and end apart: 7 -> 3, of which waited for: 5 -> 3; matrix products, arithmetic and copies ran while one was open for 0% -> 0% of each run, Pallas kernels for 0% -> 0%
where the time goes in v3:
time: 49.9 us; the launch traced here: 49.7 us
  waiting for transfers between devices  30.1 us (60%)
  starting transfers between devices  8.36 us (17%)
  other arithmetic  6.05 us (12%)
  local copies, waits for them, and re-layouts  2.69 us (5%)
  matrix products  2.38 us (5%)
    ppermute x1, waiting for transfers between devices, relay_exchange(): lax.ppermute(jnp.stack([mine, across], axis=0), 'tile', [(0, 1), (1, 0),...  10.8 us
    ppermute x1, waiting for transfers between devices, relay_exchange(): across = lax.ppermute(other, 'tile', [(0, 2), (2, 0), (1, 3), (3, 1)])  10.5 us
    all_to_all x1, waiting for transfers between devices, per_device(): lax.all_to_all(spectrum[None], 'freq', split_axis=2, concat_axis=0, tiled...  8.76 us
    select_n x1, other arithmetic, per_device(): return jnp.where(inside, traces, jnp.float32(0.0))  4.26 us
    ppermute x1, starting transfers between devices, relay_exchange(): across = lax.ppermute(other, 'tile', [(0, 2), (2, 0), (1, 3), (3, 1)])  4.1 us
    all_to_all x1, starting transfers between devices, per_device(): lax.all_to_all(spectrum[None], 'freq', split_axis=2, concat_axis=0, tiled...  3.47 us
    dot_general x1, matrix products, column_products(): lax.dot_general(v_local, x_local, (((3,), (1,)), ((), ())), preferred_ele...  1.65 us
    another operation x1, local copies, waits for them, and re-layouts, row_spectrum(): return jnp.stack([real_part, imag_part], axis=0).astype(jnp.bfloat16)  1.33 us
  transfers between devices with their start and end apart: 3, of which 3 were waited for; matrix products, arithmetic and copies ran while one was open for 0% of the time, Pallas kernels for 0%

profile of v3, /device:TPU:0, one launch (start us, length us, event | category | flops | bytes accessed | tf_op | source)
XLA Modules:
  0.0 49.7 jit_solution(17756140355296025773)
XLA Ops:
  0.0 0.0 copy-start
  0.0 0.0 copy-start.1
  0.0 0.8 %iota_compare_fusion.2 = pred[2,112]{1,0:T(4,128)(4,1)S(1)} fusion(s32[2]{0:T(128)} %bitcast.112), kind=kLoop, calls=%fused_computation.68 | loop fusion | flops 224 | bytes 232 | tf_op jit(solution)/shard_map/lt | solution.py:30
  0.8 0.4 copy-done
  1.2 1.7 %fusion.1 = f32[2,2,112,2,512]{4,2,3,1,0:T(8,128)S(1)} fusion(bf16[1,2,512,512]{3,2,1,0:T(8,128)(2,1)S(1)} %copy-done, bf16[1,1,2,2,112,512]{5,4,3,2,1,0:T(8,128)(2,1)} %param.6), kind=kOutput, calls=%fused_computation.5 | convolution fusion | flops 469762048 | bytes 3342336 | tf_op jit(solution)/shard_map/dot_general | solution.py:24
  2.9 0.2 fusion.11
  3.1 0.1 fusion.27
  3.1 4.1 %collective-permute-start = (bf16[2,112,512]{2,1,0:T(8,128)(2,1)S(1)}, bf16[2,112,512]{2,1,0:T(8,128)(2,1)S(1)}, u32[]{:S(2)}, u32[]{:S(2)}) collective-permute-start(bf16[2,112,512]{2,1,0:T(8,128)(2,1)S(1)} %get-tuple-element.22), channel_id=1, source_target_pairs={{0,8},{8,0},{4,12},{12,4},{1,9},{9,1},{5,13},{13,5},{2,10},{10,2},... | collective-permute-start | bytes 688136 | tf_op jit(solution)/shard_map/ppermute | solution.py:50
  7.2 10.5 %collective-permute-done = bf16[2,112,512]{2,1,0:T(8,128)(2,1)S(1)} collective-permute-done((bf16[2,112,512]{2,1,0:T(8,128)(2,1)S(1)}, bf16[2,112,512]{2,1,0:T(8,128)(2,1)S(1)}, u32[]{:S(2)}, u32[]{:S(2)}) %collective-permute-start) | collective-permute-done | bytes 229408 | tf_op jit(solution)/shard_map/ppermute | solution.py:50
  17.8 0.8 %collective-permute-start.1 = (bf16[2,2,112,512]{3,2,0,1:T(8,128)(2,1)S(1)}, bf16[2,2,112,512]{3,2,0,1:T(8,128)(2,1)S(1)}, u32[]{:S(2)}, u32[]{:S(2)}) collective-permute-start(bf16[2,2,112,512]{3,2,0,1:T(8,128)(2,1)S(1)} %pad_maximum_fusion.1), channel_id=1, source_target_pairs={{0,4},{4,0},{8,12},{12,8},{1,5},{5,1},{9,13},{13,9},{2,6},{6,2},{1... | collective-permute-start | bytes 1376264 | tf_op jit(solution)/shard_map/ppermute | solution.py:51
  18.6 0.0 copy-done.1
  18.6 0.1 fusion.32
  18.7 10.8 %collective-permute-done.1 = bf16[2,2,112,512]{3,2,0,1:T(8,128)(2,1)S(1)} collective-permute-done((bf16[2,2,112,512]{3,2,0,1:T(8,128)(2,1)S(1)}, bf16[2,2,112,512]{3,2,0,1:T(8,128)(2,1)S(1)}, u32[]{:S(2)}, u32[]{:S(2)}) %collective-permute-start.1) | collective-permute-done | bytes 458784 | tf_op jit(solution)/shard_map/ppermute | solution.py:51
  29.6 0.7 %convolution_bitcast_fusion = f32[2,256,2,512]{3,1,2,0:T(8,128)S(1)} fusion(bf16[2,2,112,512]{3,2,0,1:T(8,128)(2,1)S(1)} %collective-permute-done.1, bf16[1,2,112,512]{3,2,0,1:T(8,128)(2,1)S(1)} %bitcast.111, bf16[1,2,112,512]{3,2,0,1:T(8,128)(2,1)S(1)} %get-tuple-element.21, bf16[1,2,112,256]{3,2,0,1:T(8,128)(2,1)S(1)} %get-tuple-element.19, ...), kind=kOutput, calls=%fused_computation.4 | convolution fusion | flops 474349568 | bytes 3473408 | tf_op jit(solution)/shard_map/dot_general | solution.py:37
  30.3 0.0 copy-start.2
  30.3 0.2 fusion.23
  30.5 0.1 pad_maximum_fusion
  30.5 1.3 %copy.10 = bf16[1,2,256,512]{3,1,0,2:T(2,128)(2,1)} copy(bf16[1,2,256,512]{3,2,1,0:T(8,128)(2,1)S(1)} %pad_maximum_fusion) | data formatting | bytes 1048576 | tf_op jit(solution)/shard_map/stack | solution.py:42
  31.9 3.5 %all-to-all-start = ((bf16[1,2,256,512]{3,1,0,2:T(2,128)(2,1)}), bf16[1,2,256,512]{3,1,0,2:T(2,128)(2,1)S(1)}, u32[]{:S(2)}, u32[]{:S(2)}) async-start(bf16[1,2,256,512]{3,1,0,2:T(2,128)(2,1)} %copy.10), calls=%async_computation | async-start | bytes 1048576 | tf_op jit(solution)/shard_map/all_to_all | solution.py:89
  35.4 0.0 copy-done.2
  35.4 8.8 %all-to-all-done = bf16[1,2,256,512]{3,1,0,2:T(2,128)(2,1)S(1)} async-done(((bf16[1,2,256,512]{3,1,0,2:T(2,128)(2,1)}), bf16[1,2,256,512]{3,1,0,2:T(2,128)(2,1)S(1)}, u32[]{:S(2)}, u32[]{:S(2)}) %all-to-all-start) | async-done | bytes 524320 | tf_op jit(solution)/shard_map/all_to_all | solution.py:89
  44.2 0.4 convert_bitcast_fusion
  44.5 0.8 %fusion.34 = (f32[1,1,64,512]{3,1,2,0:T(1,128)S(1)}, f32[1,1,64,512]{3,1,2,0:T(1,128)S(1)}, f32[1,1,64,512]{3,1,2,0:T(1,128)S(1)}, f32[1,1,64,512]{3,1,2,0:T(1,1...) fusion(f32[4,2,64,512]{3,1,2,0:T(2,128)S(1)} %convert_bitcast_f, ...), kind=kLoop, calls=%fused_computation.79 | loop fusion | bytes 2097152 | tf_op jit(solution)/shard_map/slice | solution.py:98
  45.5 4.3 %multiply_select_fusion = f32[64,32,512]{2,1,0:T(8,128)} fusion(f32[32]{0:T(128)S(1)} %get-tuple-element.30, f32[64,512]{1,0:T(8,128)S(1)} %get-tuple-element.39, f32[32]{0:T(128)S(1)} %get-tuple-element.31, f32[64,512]{1,0:T(8,128)S(1)} %get-tuple-element.40, f32[32]{0:T(128)S(1)} %get-tuple-element.32, f32[64,512]{1,0:T(8,128)S(1)} %get-tuple-element.41, ...), kind=kLoop, calls=%fused_computation | loop fusion | flops 20971520 | bytes 5506048 | tf_op jit(solution)/shard_map/jit(_where)/select_n | solution.py:105
  (9 shorter events, 0.2 us)
Async XLA Ops:
  0.0 1.2 %copy-start = (bf16[1,2,512,512]{3,2,1,0:T(8,128)(2,1)S(1)}, bf16[1,2,512,512]{3,2,1,0:T(8,128)(2,1)}, u32[]{:S(2)}) copy-start(bf16[1,2,512,512]{3,2,1,0:T(8,128)(2,1)} %param.5) | copy-start | bytes 3145732
  0.0 18.6 %copy-start.1 = (bf16[1,4,2,112,256]{4,3,2,1,0:T(8,128)(2,1)S(1)}, bf16[1,4,2,112,256]{4,3,2,1,0:T(8,128)(2,1)}, u32[]{:S(2)}) copy-start(bf16[1,4,2,112,256]{4,3,2,1,0:T(8,128)(2,1)} %param.7) | copy-start | bytes 1376260
  3.1 14.6 %collective-permute-start = (bf16[2,112,512]{2,1,0:T(8,128)(2,1)S(1)}, bf16[2,112,512]{2,1,0:T(8,128)(2,1)S(1)}, u32[]{:S(2)}, u32[]{:S(2)}) collective-permute-start(bf16[2,112,512]{2,1,0:T(8,128)(2,1)S(1)} %get-tuple-element.22), channel_id=1, source_target_pairs={{0,8},{8,0},{4,12},{12,4},{1,9},{9,1},{5,13},{13,5},{2,10},{10,2},... | collective-permute-start | bytes 688136 | tf_op jit(solution)/shard_map/ppermute | solution.py:50
  17.8 11.8 %collective-permute-start.1 = (bf16[2,2,112,512]{3,2,0,1:T(8,128)(2,1)S(1)}, bf16[2,2,112,512]{3,2,0,1:T(8,128)(2,1)S(1)}, u32[]{:S(2)}, u32[]{:S(2)}) collective-permute-start(bf16[2,2,112,512]{3,2,0,1:T(8,128)(2,1)S(1)} %pad_maximum_fusion.1), channel_id=1, source_target_pairs={{0,4},{4,0},{8,12},{12,8},{1,5},{5,1},{9,13},{13,9},{2,6},{6,2},{1... | collective-permute-start | bytes 1376264 | tf_op jit(solution)/shard_map/ppermute | solution.py:51
  30.3 5.1 %copy-start.2 = (s32[2,64,512]{2,1,0:T(8,128)S(1)}, s32[2,64,512]{2,1,0:T(8,128)}, u32[]{:S(2)}) copy-start(s32[2,64,512]{2,1,0:T(8,128)} %param.9) | copy-start | bytes 786436
  31.9 12.3 %all-to-all-start = ((bf16[1,2,256,512]{3,1,0,2:T(2,128)(2,1)}), bf16[1,2,256,512]{3,1,0,2:T(2,128)(2,1)S(1)}, u32[]{:S(2)}, u32[]{:S(2)}) async-start(bf16[1,2,256,512]{3,1,0,2:T(2,128)(2,1)} %copy.10), calls=%async_computation | async-start | bytes 1048576 | tf_op jit(solution)/shard_map/all_to_all | solution.py:89

commit v4 on v3

--- a/solution.py
+++ b/solution.py
@@ -47,15 +47,15 @@
     row = t // 2
     mine = lax.dynamic_index_in_dim(own, row, 0, keepdims=False)
     other = lax.dynamic_index_in_dim(own, 1 - row, 0, keepdims=False)
+    pairs = [(0, 1), (1, 0), (2, 3), (3, 2)]
     across = lax.ppermute(other, "tile", [(0, 2), (2, 0), (1, 3), (3, 1)])
-    swapped = lax.ppermute(
-        jnp.stack([mine, across], axis=0), "tile", [(0, 1), (1, 0), (2, 3), (3, 2)]
-    )
+    partner = lax.ppermute(mine, "tile", pairs)
+    passed = lax.ppermute(across, "tile", pairs)
     columns = (t, t ^ 2, t ^ 1, t ^ 3)
     u_order = jnp.stack(
         [lax.dynamic_index_in_dim(u_local, j, 0, keepdims=False) for j in columns], axis=0
     )
-    blocks = jnp.concatenate([mine[None], across[None], swapped], axis=0)
+    blocks = jnp.stack([mine, across, partner, passed], axis=0)
     return row_spectrum(u_order, blocks)
 
 

time: 49.9 us -> 44.9 us (0.90)
  waiting for transfers between devices: 30.1 us -> 23.8 us
  starting transfers between devices: 8.36 us -> 9.76 us
    ppermute x1 -> x2, waiting for transfers between devices: 10.8 us -> 5.98 us  [the longest x1 5.98 us: relay_exchange(): passed = lax.ppermute(across, 'tile', pairs)]
    ppermute x1, waiting for transfers between devices: 10.5 us -> 9.01 us  [relay_exchange(): across = lax.ppermute(other, 'tile', [(0, 2), (2, 0), (1, 3), (3, 1)])]
    ppermute x1 -> x2, starting transfers between devices: 0.79 us -> 2.19 us  [the longest x1 1.58 us: relay_exchange(): partner = lax.ppermute(mine, 'tile', pairs)]
  transfers between devices with their start and end apart: 3 -> 4, of which waited for: 3 -> 3; matrix products, arithmetic and copies ran while one was open for 0% -> 0% of each run, Pallas kernels for 0% -> 0%
where the time goes in v4:
time: 44.9 us; the launch traced here: 44.7 us
  waiting for transfers between devices  23.8 us (53%)
  starting transfers between devices  9.76 us (22%)
  other arithmetic  6.01 us (13%)
  local copies, waits for them, and re-layouts  2.69 us (6%)
  matrix products  2.38 us (5%)
    ppermute x1, waiting for transfers between devices, relay_exchange(): across = lax.ppermute(other, 'tile', [(0, 2), (2, 0), (1, 3), (3, 1)])  9.01 us
    all_to_all x1, waiting for transfers between devices, per_device(): lax.all_to_all(spectrum[None], 'freq', split_axis=2, concat_axis=0, tiled...  8.76 us
    ppermute x1, waiting for transfers between devices, relay_exchange(): passed = lax.ppermute(across, 'tile', pairs)  5.98 us
    select_n x1, other arithmetic, per_device(): return jnp.where(inside, traces, jnp.float32(0.0))  4.26 us
    ppermute x1, starting transfers between devices, relay_exchange(): across = lax.ppermute(other, 'tile', [(0, 2), (2, 0), (1, 3), (3, 1)])  4.1 us
    all_to_all x1, starting transfers between devices, per_device(): lax.all_to_all(spectrum[None], 'freq', split_axis=2, concat_axis=0, tiled...  3.47 us
    dot_general x1, matrix products, column_products(): lax.dot_general(v_local, x_local, (((3,), (1,)), ((), ())), preferred_ele...  1.65 us
    ppermute x1, starting transfers between devices, relay_exchange(): partner = lax.ppermute(mine, 'tile', pairs)  1.58 us
  transfers between devices with their start and end apart: 4, of which 3 were waited for; matrix products, arithmetic and copies ran while one was open for 0% of the time, Pallas kernels for 0%

profile of v4, /device:TPU:0, one launch (start us, length us, event | category | flops | bytes accessed | tf_op | source)
XLA Modules:
  0.0 44.7 jit_solution(3401966437951291425)
XLA Ops:
  0.0 0.0 copy-start
  0.0 0.0 copy-start.1
  0.0 0.8 %iota_compare_fusion.2 = pred[2,112]{1,0:T(4,128)(4,1)S(1)} fusion(s32[2]{0:T(128)} %bitcast.119), kind=kLoop, calls=%fused_computation.69 | loop fusion | flops 224 | bytes 232 | tf_op jit(solution)/shard_map/lt | solution.py:30
  0.8 0.4 copy-done
  1.2 1.7 %fusion.1 = f32[2,2,112,2,512]{4,2,3,1,0:T(8,128)S(1)} fusion(bf16[1,2,512,512]{3,2,1,0:T(8,128)(2,1)S(1)} %copy-done, bf16[1,1,2,2,112,512]{5,4,3,2,1,0:T(8,128)(2,1)} %param.6), kind=kOutput, calls=%fused_computation.5 | convolution fusion | flops 469762048 | bytes 3342336 | tf_op jit(solution)/shard_map/dot_general | solution.py:24
  2.9 0.2 fusion.13
  3.1 0.1 fusion.29
  3.1 4.1 %collective-permute-start = (bf16[2,112,512]{2,1,0:T(8,128)(2,1)S(1)}, bf16[2,112,512]{2,1,0:T(8,128)(2,1)S(1)}, u32[]{:S(2)}, u32[]{:S(2)}) collective-permute-start(bf16[2,112,512]{2,1,0:T(8,128)(2,1)S(1)} %get-tuple-element.22), channel_id=1, source_target_pairs={{0,8},{8,0},{4,12},{12,4},{1,9},{9,1},{5,13},{13,5},{2,10},{10,2},... | collective-permute-start | bytes 688136 | tf_op jit(solution)/shard_map/ppermute | solution.py:51
  7.2 1.6 %collective-permute-start.1 = (bf16[2,112,512]{2,1,0:T(8,128)(2,1)S(1)}, bf16[2,112,512]{2,1,0:T(8,128)(2,1)S(1)}, u32[]{:S(2)}, u32[]{:S(2)}) collective-permute-start(bf16[2,112,512]{2,1,0:T(8,128)(2,1)S(1)} %bitcast.115), channel_id=1, source_target_pairs={{0,4},{4,0},{8,12},{12,8},{1,5},{5,1},{9,13},{13,9},{2,6},{6,2},{1... | collective-permute-start | bytes 688136 | tf_op jit(solution)/shard_map/ppermute | solution.py:52
  8.8 0.0 copy-done.1
  8.8 9.0 %collective-permute-done = bf16[2,112,512]{2,1,0:T(8,128)(2,1)S(1)} collective-permute-done((bf16[2,112,512]{2,1,0:T(8,128)(2,1)S(1)}, bf16[2,112,512]{2,1,0:T(8,128)(2,1)S(1)}, u32[]{:S(2)}, u32[]{:S(2)}) %collective-permute-start) | collective-permute-done | bytes 229408 | tf_op jit(solution)/shard_map/ppermute | solution.py:51
  17.9 0.6 %collective-permute-start.2 = (bf16[2,112,512]{2,1,0:T(8,128)(2,1)S(1)}, bf16[2,112,512]{2,1,0:T(8,128)(2,1)S(1)}, u32[]{:S(2)}, u32[]{:S(2)}) collective-permute-start(bf16[2,112,512]{2,1,0:T(8,128)(2,1)S(1)} %collective-permute-done), channel_id=1, source_target_pairs={{0,4},{4,0},{8,12},{12,8},{1,5},{5,1},{9,13},{13,9},{2,6},{6,2},{1... | collective-permute-start | bytes 688136 | tf_op jit(solution)/shard_map/ppermute | solution.py:53
  18.5 0.1 fusion.34
  18.6 0.0 collective-permute-done.1
  18.6 6.0 %collective-permute-done.2 = bf16[2,112,512]{2,1,0:T(8,128)(2,1)S(1)} collective-permute-done((bf16[2,112,512]{2,1,0:T(8,128)(2,1)S(1)}, bf16[2,112,512]{2,1,0:T(8,128)(2,1)S(1)}, u32[]{:S(2)}, u32[]{:S(2)}) %collective-permute-start.2) | collective-permute-done | bytes 229408 | tf_op jit(solution)/shard_map/ppermute | solution.py:53
  24.6 0.7 %convolution_bitcast_fusion = f32[2,256,2,512]{3,1,2,0:T(8,128)S(1)} fusion(bf16[1,2,112,512]{3,2,0,1:T(8,128)(2,1)S(1)} %bitcast.118, bf16[1,2,112,512]{3,2,0,1:T(8,128)(2,1)S(1)} %bitcast.117, bf16[1,2,112,512]{3,2,0,1:T(8,128)(2,1)S(1)} %bitcast.116, bf16[1,2,112,512]{3,2,0,1:T(8,128)(2,1)S(1)} %get-tuple-element.21, ...), kind=kOutput, calls=%fused_computation.4 | convolution fusion | flops 475267072 | bytes 3473408 | tf_op jit(solution)/shard_map/dot_general | solution.py:37
  25.3 0.0 copy-start.2
  25.3 0.2 fusion.25
  25.5 0.1 pad_maximum_fusion
  25.5 1.3 %copy.12 = bf16[1,2,256,512]{3,1,0,2:T(2,128)(2,1)} copy(bf16[1,2,256,512]{3,2,1,0:T(8,128)(2,1)S(1)} %pad_maximum_fusion) | data formatting | bytes 1048576 | tf_op jit(solution)/shard_map/stack | solution.py:42
  26.9 3.5 %all-to-all-start = ((bf16[1,2,256,512]{3,1,0,2:T(2,128)(2,1)}), bf16[1,2,256,512]{3,1,0,2:T(2,128)(2,1)S(1)}, u32[]{:S(2)}, u32[]{:S(2)}) async-start(bf16[1,2,256,512]{3,1,0,2:T(2,128)(2,1)} %copy.12), calls=%async_computation | async-start | bytes 1048576 | tf_op jit(solution)/shard_map/all_to_all | solution.py:89
  30.4 0.0 copy-done.2
  30.4 8.8 %all-to-all-done = bf16[1,2,256,512]{3,1,0,2:T(2,128)(2,1)S(1)} async-done(((bf16[1,2,256,512]{3,1,0,2:T(2,128)(2,1)}), bf16[1,2,256,512]{3,1,0,2:T(2,128)(2,1)S(1)}, u32[]{:S(2)}, u32[]{:S(2)}) %all-to-all-start) | async-done | bytes 524320 | tf_op jit(solution)/shard_map/all_to_all | solution.py:89
  39.2 0.4 convert_bitcast_fusion
  39.5 0.8 %fusion.36 = (f32[1,1,64,512]{3,1,2,0:T(1,128)S(1)}, f32[1,1,64,512]{3,1,2,0:T(1,128)S(1)}, f32[1,1,64,512]{3,1,2,0:T(1,128)S(1)}, f32[1,1,64,512]{3,1,2,0:T(1,1...) fusion(f32[4,2,64,512]{3,1,2,0:T(2,128)S(1)} %convert_bitcast_f, ...), kind=kLoop, calls=%fused_computation.80 | loop fusion | bytes 2097152 | tf_op jit(solution)/shard_map/slice | solution.py:98
  40.5 4.3 %multiply_select_fusion = f32[64,32,512]{2,1,0:T(8,128)} fusion(f32[32]{0:T(128)S(1)} %get-tuple-element.30, f32[64,512]{1,0:T(8,128)S(1)} %get-tuple-element.39, f32[32]{0:T(128)S(1)} %get-tuple-element.31, f32[64,512]{1,0:T(8,128)S(1)} %get-tuple-element.40, f32[32]{0:T(128)S(1)} %get-tuple-element.32, f32[64,512]{1,0:T(8,128)S(1)} %get-tuple-element.41, ...), kind=kLoop, calls=%fused_computation | loop fusion | flops 20971520 | bytes 5506048 | tf_op jit(solution)/shard_map/jit(_where)/select_n | solution.py:105
  (8 shorter events, 0.1 us)
Async XLA Ops:
  0.0 1.2 %copy-start = (bf16[1,2,512,512]{3,2,1,0:T(8,128)(2,1)S(1)}, bf16[1,2,512,512]{3,2,1,0:T(8,128)(2,1)}, u32[]{:S(2)}) copy-start(bf16[1,2,512,512]{3,2,1,0:T(8,128)(2,1)} %param.5) | copy-start | bytes 3145732
  0.0 8.8 %copy-start.1 = (bf16[1,4,2,112,256]{4,3,2,1,0:T(8,128)(2,1)S(1)}, bf16[1,4,2,112,256]{4,3,2,1,0:T(8,128)(2,1)}, u32[]{:S(2)}) copy-start(bf16[1,4,2,112,256]{4,3,2,1,0:T(8,128)(2,1)} %param.7) | copy-start | bytes 1376260
  3.1 14.7 %collective-permute-start = (bf16[2,112,512]{2,1,0:T(8,128)(2,1)S(1)}, bf16[2,112,512]{2,1,0:T(8,128)(2,1)S(1)}, u32[]{:S(2)}, u32[]{:S(2)}) collective-permute-start(bf16[2,112,512]{2,1,0:T(8,128)(2,1)S(1)} %get-tuple-element.22), channel_id=1, source_target_pairs={{0,8},{8,0},{4,12},{12,4},{1,9},{9,1},{5,13},{13,5},{2,10},{10,2},... | collective-permute-start | bytes 688136 | tf_op jit(solution)/shard_map/ppermute | solution.py:51
  7.2 11.4 %collective-permute-start.1 = (bf16[2,112,512]{2,1,0:T(8,128)(2,1)S(1)}, bf16[2,112,512]{2,1,0:T(8,128)(2,1)S(1)}, u32[]{:S(2)}, u32[]{:S(2)}) collective-permute-start(bf16[2,112,512]{2,1,0:T(8,128)(2,1)S(1)} %bitcast.115), channel_id=1, source_target_pairs={{0,4},{4,0},{8,12},{12,8},{1,5},{5,1},{9,13},{13,9},{2,6},{6,2},{1... | collective-permute-start | bytes 688136 | tf_op jit(solution)/shard_map/ppermute | solution.py:52
  17.9 6.7 %collective-permute-start.2 = (bf16[2,112,512]{2,1,0:T(8,128)(2,1)S(1)}, bf16[2,112,512]{2,1,0:T(8,128)(2,1)S(1)}, u32[]{:S(2)}, u32[]{:S(2)}) collective-permute-start(bf16[2,112,512]{2,1,0:T(8,128)(2,1)S(1)} %collective-permute-done), channel_id=1, source_target_pairs={{0,4},{4,0},{8,12},{12,8},{1,5},{5,1},{9,13},{13,9},{2,6},{6,2},{1... | collective-permute-start | bytes 688136 | tf_op jit(solution)/shard_map/ppermute | solution.py:53
  25.3 5.1 %copy-start.2 = (s32[2,64,512]{2,1,0:T(8,128)S(1)}, s32[2,64,512]{2,1,0:T(8,128)}, u32[]{:S(2)}) copy-start(s32[2,64,512]{2,1,0:T(8,128)} %param.9) | copy-start | bytes 786436
  26.9 12.3 %all-to-all-start = ((bf16[1,2,256,512]{3,1,0,2:T(2,128)(2,1)}), bf16[1,2,256,512]{3,1,0,2:T(2,128)(2,1)S(1)}, u32[]{:S(2)}, u32[]{:S(2)}) async-start(bf16[1,2,256,512]{3,1,0,2:T(2,128)(2,1)} %copy.12), calls=%async_computation | async-start | bytes 1048576 | tf_op jit(solution)/shard_map/all_to_all | solution.py:89

commit v5 on v4

--- a/solution.py
+++ b/solution.py
@@ -6,7 +6,7 @@
 from jax.sharding import PartitionSpec as P
 
 NT = 32
-S_CHUNKS = 1
+S_CHUNKS = 2
 
 
 first_bin = 2

time: 44.9 us -> 52.4 us (1.17)
  starting transfers between devices: 9.76 us -> 15.1 us
  matrix products: 2.38 us -> 3.8 us
  local copies, waits for them, and re-layouts: 2.69 us -> 3.91 us
  waiting for transfers between devices: 23.8 us -> 23.1 us
    all_to_all x1 -> x2, starting transfers between devices: 3.47 us -> 6.81 us  [per_device(): lax.all_to_all(spectrum[None], 'freq', split_axis=2, concat_axis=0, tiled...]
    ppermute x1 -> x2, waiting for transfers between devices: 5.98 us -> 2.65 us  [relay_exchange(): passed = lax.ppermute(across, 'tile', pairs)]
    all_to_all x1 -> x2, waiting for transfers between devices: 8.76 us -> 10.4 us  [per_device(): lax.all_to_all(spectrum[None], 'freq', split_axis=2, concat_axis=0, tiled...]
    ppermute x1 -> x2, starting transfers between devices: 1.58 us -> 3.18 us  [relay_exchange(): partner = lax.ppermute(mine, 'tile', pairs)]
    ppermute x1 -> x2, starting transfers between devices: 0.62 us -> 2.09 us  [relay_exchange(): passed = lax.ppermute(across, 'tile', pairs)]
    dot_general x1 -> x2, matrix products: 1.65 us -> 2.88 us  [column_products(): lax.dot_general(v_local, x_local, (((3,), (1,)), ((), ())), preferred_ele...]
    ppermute x1 -> x2, starting transfers between devices: 4.1 us -> 3.05 us  [relay_exchange(): across = lax.ppermute(other, 'tile', [(0, 2), (2, 0), (1, 3), (3, 1)])]
    ppermute x1 -> x2, waiting for transfers between devices: 9.01 us -> 9.98 us  [relay_exchange(): across = lax.ppermute(other, 'tile', [(0, 2), (2, 0), (1, 3), (3, 1)])]
  transfers between devices with their start and end apart: 4 -> 8, of which waited for: 3 -> 4; matrix products, arithmetic and copies ran while one was open for 0% -> 6% of each run, Pallas kernels for 0% -> 0%
where the time goes in v5:
time: 52.4 us; the launch traced here: 52.1 us
  waiting for transfers between devices  23.1 us (44%)
  starting transfers between devices  15.1 us (29%)
  other arithmetic  5.95 us (11%)
  local copies, waits for them, and re-layouts  3.91 us (7%)
  matrix products  3.8 us (7%)
    all_to_all x2, waiting for transfers between devices, per_device(): lax.all_to_all(spectrum[None], 'freq', split_axis=2, concat_axis=0, tiled...  10.4 us
    ppermute x2, waiting for transfers between devices, relay_exchange(): across = lax.ppermute(other, 'tile', [(0, 2), (2, 0), (1, 3), (3, 1)])  9.98 us
    all_to_all x2, starting transfers between devices, per_device(): lax.all_to_all(spectrum[None], 'freq', split_axis=2, concat_axis=0, tiled...  6.81 us
    select_n x1, other arithmetic, per_device(): return jnp.where(inside, traces, jnp.float32(0.0))  4.26 us
    ppermute x2, starting transfers between devices, relay_exchange(): partner = lax.ppermute(mine, 'tile', pairs)  3.18 us
    ppermute x2, starting transfers between devices, relay_exchange(): across = lax.ppermute(other, 'tile', [(0, 2), (2, 0), (1, 3), (3, 1)])  3.05 us
    dot_general x2, matrix products, column_products(): lax.dot_general(v_local, x_local, (((3,), (1,)), ((), ())), preferred_ele...  2.88 us
    ppermute x2, waiting for transfers between devices, relay_exchange(): passed = lax.ppermute(across, 'tile', pairs)  2.65 us
  transfers between devices with their start and end apart: 8, of which 4 were waited for; matrix products, arithmetic and copies ran while one was open for 6% of the time, Pallas kernels for 0%

profile of v5, /device:TPU:0, one launch (start us, length us, event | category | flops | bytes accessed | tf_op | source)
XLA Modules:
  0.0 52.1 jit_solution(3606053379729875305)
XLA Ops:
  0.0 0.0 copy-start
  0.0 1.0 %copy-done = bf16[1,1,2,2,112,512]{5,4,3,2,1,0:T(8,128)(2,1)S(1)} copy-done((bf16[1,1,2,2,112,512]{5,4,3,2,1,0:T(8,128)(2,1)S(1)}, bf16[1,1,2,2,112,512]{5,4,3,2,1,0:T(8,128)(2,1)}, u32[]{:S(2)}) %copy-start) | copy-done | bytes 458776
  1.0 1.4 %fusion.1 = f32[2,2,112,2,256]{4,2,0,3,1:T(8,128)S(1)} fusion(bf16[2,512,512]{2,1,0:T(8,128)(2,1)} %bitcast.158, bf16[1,1,2,2,112,512]{5,4,3,2,1,0:T(8,128)(2,1)S(1)} %copy-done), kind=kOutput, calls=%fused_computation.7 | convolution fusion | flops 234881024 | bytes 1900544 | tf_op jit(solution)/shard_map/dot_general | solution.py:24
  2.5 1.4 %fusion.2 = f32[2,2,112,2,256]{4,2,3,1,0:T(8,128)S(1)} fusion(bf16[2,512,512]{2,1,0:T(8,128)(2,1)} %bitcast.159, bf16[1,1,2,2,112,512]{5,4,3,2,1,0:T(8,128)(2,1)S(1)} %copy-done), kind=kOutput, calls=%fused_computation.9 | convolution fusion | flops 234881024 | bytes 1900544 | tf_op jit(solution)/shard_map/dot_general | solution.py:24
  3.9 0.7 %iota_compare_fusion.2 = pred[2,112]{1,0:T(4,128)(4,1)S(1)} fusion(s32[2]{0:T(128)} %bitcast.168), kind=kLoop, calls=%fused_computation.96 | loop fusion | flops 224 | bytes 232 | tf_op jit(solution)/shard_map/lt | solution.py:30
  4.6 0.2 fusion.29
  4.9 3.1 %collective-permute-start.4 = (bf16[2,112,256]{2,1,0:T(8,128)(2,1)S(1)}, bf16[2,112,256]{2,1,0:T(8,128)(2,1)S(1)}, u32[]{:S(2)}, u32[]{:S(2)}) collective-permute-start(bf16[2,112,256]{2,1,0:T(8,128)(2,1)S(1)} %bitcast.161), channel_id=1, source_target_pairs={{0,4},{4,0},{8,12},{12,8},{1,5},{5,1},{9,13},{13,9},{2,6},{6,2},{1... | collective-permute-start | bytes 344072 | tf_op jit(solution)/shard_map/ppermute | solution.py:52
  8.0 0.1 collective-permute-start.1
  8.1 3.0 %collective-permute-start = (bf16[2,112,256]{2,1,0:T(8,128)(2,1)S(1)}, bf16[2,112,256]{2,1,0:T(8,128)(2,1)S(1)}, u32[]{:S(2)}, u32[]{:S(2)}) collective-permute-start(bf16[2,112,256]{2,1,0:T(8,128)(2,1)S(1)} %get-tuple-element.28), channel_id=1, source_target_pairs={{0,8},{8,0},{4,12},{12,4},{1,9},{9,1},{5,13},{13,5},{2,10},{10,2},... | collective-permute-start | bytes 344072 | tf_op jit(solution)/shard_map/ppermute | solution.py:51
  11.1 0.0 collective-permute-start.3
  11.2 0.1 fusion.48
  11.3 10.0 %collective-permute-done.3 = bf16[2,112,256]{2,1,0:T(8,128)(2,1)S(1)} collective-permute-done((bf16[2,112,256]{2,1,0:T(8,128)(2,1)S(1)}, bf16[2,112,256]{2,1,0:T(8,128)(2,1)S(1)}, u32[]{:S(2)}, u32[]{:S(2)}) %collective-permute-start.3) | collective-permute-done | bytes 114720 | tf_op jit(solution)/shard_map/ppermute | solution.py:51
  21.3 0.7 %collective-permute-start.5 = (bf16[2,112,256]{2,1,0:T(8,128)(2,1)S(1)}, bf16[2,112,256]{2,1,0:T(8,128)(2,1)S(1)}, u32[]{:S(2)}, u32[]{:S(2)}) collective-permute-start(bf16[2,112,256]{2,1,0:T(8,128)(2,1)S(1)} %collective-permute-done.3), channel_id=1, source_target_pairs={{0,4},{4,0},{8,12},{12,8},{1,5},{5,1},{9,13},{13,9},{2,6},{6,2},{1... | collective-permute-start | bytes 344072 | tf_op jit(solution)/shard_map/ppermute | solution.py:53
  22.0 0.0 collective-permute-done
  22.0 1.4 %collective-permute-start.2 = (bf16[2,112,256]{2,1,0:T(8,128)(2,1)S(1)}, bf16[2,112,256]{2,1,0:T(8,128)(2,1)S(1)}, u32[]{:S(2)}, u32[]{:S(2)}) collective-permute-start(bf16[2,112,256]{2,1,0:T(8,128)(2,1)S(1)} %collective-permute-done), channel_id=1, source_target_pairs={{0,4},{4,0},{8,12},{12,8},{1,5},{5,1},{9,13},{13,9},{2,6},{6,2},{1... | collective-permute-start | bytes 344072 | tf_op jit(solution)/shard_map/ppermute | solution.py:53
  23.4 0.0 collective-permute-done.4
  23.4 2.6 %collective-permute-done.5 = bf16[2,112,256]{2,1,0:T(8,128)(2,1)S(1)} collective-permute-done((bf16[2,112,256]{2,1,0:T(8,128)(2,1)S(1)}, bf16[2,112,256]{2,1,0:T(8,128)(2,1)S(1)}, u32[]{:S(2)}, u32[]{:S(2)}) %collective-permute-start.5) | collective-permute-done | bytes 114720 | tf_op jit(solution)/shard_map/ppermute | solution.py:53
  26.0 0.5 convolution_bitcast_fusion
  26.5 0.1 fusion.36
  26.6 1.0 %copy.23 = bf16[1,2,256,256]{3,1,0,2:T(2,128)(2,1)} copy(bf16[1,2,256,256]{3,2,1,0:T(8,128)(2,1)S(1)} %pad_maximum_fusion.1) | data formatting | bytes 524288 | tf_op jit(solution)/shard_map/stack | solution.py:42
  27.6 3.4 %all-to-all-start.1 = ((bf16[1,2,256,256]{3,1,0,2:T(2,128)(2,1)}), bf16[1,2,256,256]{3,1,0,2:T(2,128)(2,1)S(1)}, u32[]{:S(2)}, u32[]{:S(2)}) async-start(bf16[1,2,256,256]{3,1,0,2:T(2,128)(2,1)} %copy.23), calls=%async_computation.1 | async-start | bytes 524288 | tf_op jit(solution)/shard_map/all_to_all | solution.py:89
  31.0 0.0 collective-permute-done.1
  31.0 0.0 collective-permute-done.2
  31.0 0.5 convolution_bitcast_fusion.1
  31.5 0.1 fusion.34
  31.6 1.0 %copy.17 = bf16[1,2,256,256]{3,1,0,2:T(2,128)(2,1)} copy(bf16[1,2,256,256]{3,2,1,0:T(8,128)(2,1)S(1)} %pad_maximum_fusion) | data formatting | bytes 524288 | tf_op jit(solution)/shard_map/stack | solution.py:42
  32.5 4.4 %all-to-all-done.1 = bf16[1,2,256,256]{3,1,0,2:T(2,128)(2,1)S(1)} async-done(((bf16[1,2,256,256]{3,1,0,2:T(2,128)(2,1)}), bf16[1,2,256,256]{3,1,0,2:T(2,128)(2,1)S(1)}, u32[]{:S(2)}, u32[]{:S(2)}) %all-to-all-start.1) | async-done | bytes 262176 | tf_op jit(solution)/shard_map/all_to_all | solution.py:89
  37.0 3.4 %all-to-all-start = ((bf16[1,2,256,256]{3,1,0,2:T(2,128)(2,1)}), bf16[1,2,256,256]{3,1,0,2:T(2,128)(2,1)S(1)}, u32[]{:S(2)}, u32[]{:S(2)}) async-start(bf16[1,2,256,256]{3,1,0,2:T(2,128)(2,1)} %copy.17), calls=%async_computation | async-start | bytes 524288 | tf_op jit(solution)/shard_map/all_to_all | solution.py:89
  40.4 6.0 %all-to-all-done = bf16[1,2,256,256]{3,1,0,2:T(2,128)(2,1)S(1)} async-done(((bf16[1,2,256,256]{3,1,0,2:T(2,128)(2,1)}), bf16[1,2,256,256]{3,1,0,2:T(2,128)(2,1)S(1)}, u32[]{:S(2)}, u32[]{:S(2)}) %all-to-all-start) | async-done | bytes 262176 | tf_op jit(solution)/shard_map/all_to_all | solution.py:89
  46.4 0.5 maximum_convert_fusion
  46.9 0.8 %fusion.51 = (f32[1,1,64,512]{3,1,2,0:T(1,128)S(1)}, f32[1,1,64,512]{3,1,2,0:T(1,128)S(1)}, f32[1,1,64,512]{3,1,2,0:T(1,128)S(1)}, f32[1,1,64,512]{3,1,2,0:T(1,1...) fusion(f32[4,2,64,512]{3,1,2,0:T(2,128)S(1)} %maximum_convert_f, ...), kind=kLoop, calls=%fused_computation.108 | loop fusion | bytes 2097152 | tf_op jit(solution)/shard_map/slice | solution.py:98
  47.8 4.3 %multiply_select_fusion = f32[64,32,512]{2,1,0:T(8,128)} fusion(f32[32]{0:T(128)S(1)} %get-tuple-element.36, f32[64,512]{1,0:T(8,128)S(1)} %get-tuple-element.47, f32[32]{0:T(128)S(1)} %get-tuple-element.37, f32[64,512]{1,0:T(8,128)S(1)} %get-tuple-element.48, f32[32]{0:T(128)S(1)} %get-tuple-element.38, f32[64,512]{1,0:T(8,128)S(1)} %get-tuple-element.49, ...), kind=kLoop, calls=%fused_computation | loop fusion | flops 20971520 | bytes 5506048 | tf_op jit(solution)/shard_map/jit(_where)/select_n | solution.py:105
  (16 shorter events, 0.3 us)
Async XLA Ops:
  0.0 1.0 %copy-start = (bf16[1,1,2,2,112,512]{5,4,3,2,1,0:T(8,128)(2,1)S(1)}, bf16[1,1,2,2,112,512]{5,4,3,2,1,0:T(8,128)(2,1)}, u32[]{:S(2)}) copy-start(bf16[1,1,2,2,112,512]{5,4,3,2,1,0:T(8,128)(2,1)} %param.6) | copy-start | bytes 1376260
  0.0 11.1 %copy-start.2 = (s32[2,64,512]{2,1,0:T(8,128)S(1)}, s32[2,64,512]{2,1,0:T(8,128)}, u32[]{:S(2)}) copy-start(s32[2,64,512]{2,1,0:T(8,128)} %param.9) | copy-start | bytes 786436
  0.0 21.9 %copy-start.1 = (bf16[1,4,2,112,256]{4,3,2,1,0:T(8,128)(2,1)S(1)}, bf16[1,4,2,112,256]{4,3,2,1,0:T(8,128)(2,1)}, u32[]{:S(2)}) copy-start(bf16[1,4,2,112,256]{4,3,2,1,0:T(8,128)(2,1)} %param.7) | copy-start | bytes 1376260
  4.9 18.5 %collective-permute-start.4 = (bf16[2,112,256]{2,1,0:T(8,128)(2,1)S(1)}, bf16[2,112,256]{2,1,0:T(8,128)(2,1)S(1)}, u32[]{:S(2)}, u32[]{:S(2)}) collective-permute-start(bf16[2,112,256]{2,1,0:T(8,128)(2,1)S(1)} %bitcast.161), channel_id=1, source_target_pairs={{0,4},{4,0},{8,12},{12,8},{1,5},{5,1},{9,13},{13,9},{2,6},{6,2},{1... | collective-permute-start | bytes 344072 | tf_op jit(solution)/shard_map/ppermute | solution.py:52
  8.0 23.0 %collective-permute-start.1 = (bf16[2,112,256]{2,1,0:T(8,128)(2,1)S(1)}, bf16[2,112,256]{2,1,0:T(8,128)(2,1)S(1)}, u32[]{:S(2)}, u32[]{:S(2)}) collective-permute-start(bf16[2,112,256]{2,1,0:T(8,128)(2,1)S(1)} %bitcast.160), channel_id=1, source_target_pairs={{0,4},{4,0},{8,12},{12,8},{1,5},{5,1},{9,13},{13,9},{2,6},{6,2},{1... | collective-permute-start | bytes 344072 | tf_op jit(solution)/shard_map/ppermute | solution.py:52
  8.1 13.9 %collective-permute-start = (bf16[2,112,256]{2,1,0:T(8,128)(2,1)S(1)}, bf16[2,112,256]{2,1,0:T(8,128)(2,1)S(1)}, u32[]{:S(2)}, u32[]{:S(2)}) collective-permute-start(bf16[2,112,256]{2,1,0:T(8,128)(2,1)S(1)} %get-tuple-element.28), channel_id=1, source_target_pairs={{0,8},{8,0},{4,12},{12,4},{1,9},{9,1},{5,13},{13,5},{2,10},{10,2},... | collective-permute-start | bytes 344072 | tf_op jit(solution)/shard_map/ppermute | solution.py:51
  11.1 10.2 %collective-permute-start.3 = (bf16[2,112,256]{2,1,0:T(8,128)(2,1)S(1)}, bf16[2,112,256]{2,1,0:T(8,128)(2,1)S(1)}, u32[]{:S(2)}, u32[]{:S(2)}) collective-permute-start(bf16[2,112,256]{2,1,0:T(8,128)(2,1)S(1)} %get-tuple-element.30), channel_id=1, source_target_pairs={{0,8},{8,0},{4,12},{12,4},{1,9},{9,1},{5,13},{13,5},{2,10},{10,2},... | collective-permute-start | bytes 344072 | tf_op jit(solution)/shard_map/ppermute | solution.py:51
  21.3 4.8 %collective-permute-start.5 = (bf16[2,112,256]{2,1,0:T(8,128)(2,1)S(1)}, bf16[2,112,256]{2,1,0:T(8,128)(2,1)S(1)}, u32[]{:S(2)}, u32[]{:S(2)}) collective-permute-start(bf16[2,112,256]{2,1,0:T(8,128)(2,1)S(1)} %collective-permute-done.3), channel_id=1, source_target_pairs={{0,4},{4,0},{8,12},{12,8},{1,5},{5,1},{9,13},{13,9},{2,6},{6,2},{1... | collective-permute-start | bytes 344072 | tf_op jit(solution)/shard_map/ppermute | solution.py:53
  22.0 9.0 %collective-permute-start.2 = (bf16[2,112,256]{2,1,0:T(8,128)(2,1)S(1)}, bf16[2,112,256]{2,1,0:T(8,128)(2,1)S(1)}, u32[]{:S(2)}, u32[]{:S(2)}) collective-permute-start(bf16[2,112,256]{2,1,0:T(8,128)(2,1)S(1)} %collective-permute-done), channel_id=1, source_target_pairs={{0,4},{4,0},{8,12},{12,8},{1,5},{5,1},{9,13},{13,9},{2,6},{6,2},{1... | collective-permute-start | bytes 344072 | tf_op jit(solution)/shard_map/ppermute | solution.py:53
  27.6 9.4 %all-to-all-start.1 = ((bf16[1,2,256,256]{3,1,0,2:T(2,128)(2,1)}), bf16[1,2,256,256]{3,1,0,2:T(2,128)(2,1)S(1)}, u32[]{:S(2)}, u32[]{:S(2)}) async-start(bf16[1,2,256,256]{3,1,0,2:T(2,128)(2,1)} %copy.23), calls=%async_computation.1 | async-start | bytes 524288 | tf_op jit(solution)/shard_map/all_to_all | solution.py:89
  37.0 9.4 %all-to-all-start = ((bf16[1,2,256,256]{3,1,0,2:T(2,128)(2,1)}), bf16[1,2,256,256]{3,1,0,2:T(2,128)(2,1)S(1)}, u32[]{:S(2)}, u32[]{:S(2)}) async-start(bf16[1,2,256,256]{3,1,0,2:T(2,128)(2,1)} %copy.17), calls=%async_computation | async-start | bytes 524288 | tf_op jit(solution)/shard_map/all_to_all | solution.py:89

commit v6 on v4

--- a/solution.py
+++ b/solution.py
@@ -66,7 +66,18 @@
     return row_spectrum(u_local, received)
 
 
-def make_per_device(n_tile):
+def freq_exchange(spectrum, n_freq):
+    f = lax.axis_index("freq")
+    width = spectrum.shape[1] // n_freq
+    pieces = [(f, lax.dynamic_slice_in_dim(spectrum, f * width, width, axis=1))]
+    for d in range(1, n_freq):
+        part = lax.dynamic_slice_in_dim(spectrum, (f ^ d) * width, width, axis=1)
+        pairs = [(i, i ^ d) for i in range(n_freq)]
+        pieces.append((f ^ d, lax.ppermute(part, "freq", pairs)))
+    return pieces
+
+
+def make_per_device(n_tile, n_freq):
     def per_device(sources, v_factors, u_factors, tile_ranks, window_bounds):
         v_local = v_factors[0, 0]
         u_local = u_factors[0]
@@ -74,6 +85,7 @@
         rank_local = tile_ranks[0, :, 0]
         rows = v_local.shape[0]
         use_relay = n_tile == 4 and rows == 2 and u_local.shape[0] == 4
+        use_swaps = n_freq & (n_freq - 1) == 0
         count_s = x_local.shape[2]
         chunks = S_CHUNKS if count_s % S_CHUNKS == 0 else 1
         width = count_s // chunks
@@ -85,19 +97,34 @@
                 spectrum = relay_exchange(own, u_local)
             else:
                 spectrum = gather_exchange(own, u_local, n_tile)
-            received_parts.append(
-                lax.all_to_all(spectrum[None], "freq", split_axis=2, concat_axis=0, tiled=True)
+            if use_swaps:
+                received_parts.append(freq_exchange(spectrum, n_freq))
+            else:
+                received = lax.all_to_all(
+                    spectrum[None], "freq", split_axis=2, concat_axis=0, tiled=True
+                )
+                received_parts.append([(f, received[f]) for f in range(n_freq)])
+        pieces = [
+            (
+                index,
+                jnp.concatenate([part[k][1] for part in received_parts], axis=2)
+                if chunks > 1
+                else piece,
             )
-        received = jnp.concatenate(received_parts, axis=3) if chunks > 1 else received_parts[0]
-        count_freq = received.shape[0]
-        cosine_table, sine_table = inverse_tables(count_freq, NT)
-        widened = received.astype(jnp.float32)
-        real_sum = 0.0
-        imag_sum = 0.0
-        for f in range(count_freq):
-            real_sum = real_sum + widened[f, 0][:, None, :] * cosine_table[f][None, :, None]
-            imag_sum = imag_sum + widened[f, 1][:, None, :] * sine_table[f][None, :, None]
-        traces = (real_sum - imag_sum) * (1.0 / math.sqrt(count_freq))
+            for k, (index, piece) in enumerate(received_parts[0])
+        ]
+        cosine_table, sine_table = inverse_tables(n_freq, NT)
+        scale = 1.0 / math.sqrt(n_freq)
+        traces = 0.0
+        for index, piece in pieces:
+            cosine = lax.dynamic_index_in_dim(cosine_table, index, 0, keepdims=False) * scale
+            sine = lax.dynamic_index_in_dim(sine_table, index, 0, keepdims=False) * scale
+            widened = piece.astype(jnp.float32)
+            traces = (
+                traces
+                + widened[0][:, None, :] * cosine[None, :, None]
+                - widened[1][:, None, :] * sine[None, :, None]
+            )
         time_index = jnp.arange(NT, dtype=jnp.int32)[None, :, None]
         inside = (time_index >= window_bounds[0][:, None, :]) & (
             time_index < window_bounds[1][:, None, :]
@@ -109,7 +136,7 @@
 
 def solution(mesh):
     return jax.shard_map(
-        make_per_device(mesh.shape["tile"]),
+        make_per_device(mesh.shape["tile"], mesh.shape["freq"]),
         mesh=mesh,
         in_specs=(
             P("freq", "grp", "tile", None),

time: 44.9 us -> 38.8 us (0.86)
  local copies, waits for them, and re-layouts: 2.69 us -> 0.52 us
  waiting for transfers between devices: 23.8 us -> 21.9 us
  starting transfers between devices: 9.76 us -> 8.06 us
    all_to_all x1 -> x0, waiting for transfers between devices: 8.76 us -> none  [per_device(): lax.all_to_all(spectrum[None], 'freq', split_axis=2, concat_axis=0, tiled...]
    ppermute x0 -> x3, waiting for transfers between devices: none -> 6.27 us  [freq_exchange(): pieces.append((f ^ d, lax.ppermute(part, 'freq', pairs)))]
    all_to_all x1 -> x0, starting transfers between devices: 3.47 us -> none  [per_device(): lax.all_to_all(spectrum[None], 'freq', split_axis=2, concat_axis=0, tiled...]
    ppermute x0 -> x3, starting transfers between devices: none -> 1.93 us  [freq_exchange(): pieces.append((f ^ d, lax.ppermute(part, 'freq', pairs)))]
    ppermute x1, starting transfers between devices: 1.58 us -> 3.09 us  [relay_exchange(): partner = lax.ppermute(mine, 'tile', pairs)]
    ppermute x1, starting transfers between devices: 4.1 us -> 2.59 us  [relay_exchange(): across = lax.ppermute(other, 'tile', [(0, 2), (2, 0), (1, 3), (3, 1)])]
    another operation x1 -> x0, local copies, waits for them, and re-layouts: 1.33 us -> none  [row_spectrum(): return jnp.stack([real_part, imag_part], axis=0).astype(jnp.bfloat16)]
    ppermute x1, waiting for transfers between devices: 9.01 us -> 10.1 us  [relay_exchange(): across = lax.ppermute(other, 'tile', [(0, 2), (2, 0), (1, 3), (3, 1)])]
  transfers between devices with their start and end apart: 4 -> 6, of which waited for: 3 -> 4; matrix products, arithmetic and copies ran while one was open for 0% -> 1% of each run, Pallas kernels for 0% -> 0%
where the time goes in v6:
time: 38.8 us; the launch traced here: 38.6 us
  waiting for transfers between devices  21.9 us (56%)
  starting transfers between devices  8.06 us (21%)
  other arithmetic  5.57 us (14%)
  matrix products  2.38 us (6%)
  local copies, waits for them, and re-layouts  0.52 us (1%)
    ppermute x1, waiting for transfers between devices, relay_exchange(): across = lax.ppermute(other, 'tile', [(0, 2), (2, 0), (1, 3), (3, 1)])  10.1 us
    ppermute x3, waiting for transfers between devices, freq_exchange(): pieces.append((f ^ d, lax.ppermute(part, 'freq', pairs)))  6.27 us
    ppermute x1, waiting for transfers between devices, relay_exchange(): passed = lax.ppermute(across, 'tile', pairs)  5.54 us
    select_n x1, other arithmetic, per_device(): return jnp.where(inside, traces, jnp.float32(0.0))  4.07 us
    ppermute x1, starting transfers between devices, relay_exchange(): partner = lax.ppermute(mine, 'tile', pairs)  3.09 us
    ppermute x1, starting transfers between devices, relay_exchange(): across = lax.ppermute(other, 'tile', [(0, 2), (2, 0), (1, 3), (3, 1)])  2.59 us
    ppermute x3, starting transfers between devices, freq_exchange(): pieces.append((f ^ d, lax.ppermute(part, 'freq', pairs)))  1.93 us
    dot_general x1, matrix products, column_products(): lax.dot_general(v_local, x_local, (((3,), (1,)), ((), ())), preferred_ele...  1.65 us
  transfers between devices with their start and end apart: 6, of which 4 were waited for; matrix products, arithmetic and copies ran while one was open for 1% of the time, Pallas kernels for 0%

profile of v6, /device:TPU:0, one launch (start us, length us, event | category | flops | bytes accessed | tf_op | source)
XLA Modules:
  0.0 38.6 jit_solution(9069207482808832269)
XLA Ops:
  0.0 0.0 copy-start
  0.0 0.0 copy-start.1
  0.0 0.0 copy-start.2
  0.0 0.9 %iota_compare_fusion.2 = pred[2,112]{1,0:T(4,128)(4,1)S(1)} fusion(s32[2]{0:T(128)} %bitcast.112), kind=kLoop, calls=%fused_computation.88 | loop fusion | flops 224 | bytes 232 | tf_op jit(solution)/shard_map/lt | solution.py:30
  0.9 0.4 copy-done
  1.2 1.7 %fusion.1 = f32[2,2,112,2,512]{4,2,3,1,0:T(8,128)S(1)} fusion(bf16[1,2,512,512]{3,2,1,0:T(8,128)(2,1)S(1)} %copy-done, bf16[1,1,2,2,112,512]{5,4,3,2,1,0:T(8,128)(2,1)} %param.6), kind=kOutput, calls=%fused_computation.5 | convolution fusion | flops 469762048 | bytes 3342336 | tf_op jit(solution)/shard_map/dot_general | solution.py:24
  2.9 0.2 fusion.13
  3.1 0.1 fusion.29
  3.1 3.1 %collective-permute-start.1 = (bf16[2,112,512]{2,1,0:T(8,128)(2,1)S(1)}, bf16[2,112,512]{2,1,0:T(8,128)(2,1)S(1)}, u32[]{:S(2)}, u32[]{:S(2)}) collective-permute-start(bf16[2,112,512]{2,1,0:T(8,128)(2,1)S(1)} %bitcast.108), channel_id=1, source_target_pairs={{0,4},{4,0},{8,12},{12,8},{1,5},{5,1},{9,13},{13,9},{2,6},{6,2},{1... | collective-permute-start | bytes 688136 | tf_op jit(solution)/shard_map/ppermute | solution.py:52
  6.2 2.6 %collective-permute-start = (bf16[2,112,512]{2,1,0:T(8,128)(2,1)S(1)}, bf16[2,112,512]{2,1,0:T(8,128)(2,1)S(1)}, u32[]{:S(2)}, u32[]{:S(2)}) collective-permute-start(bf16[2,112,512]{2,1,0:T(8,128)(2,1)S(1)} %get-tuple-element.18), channel_id=1, source_target_pairs={{0,8},{8,0},{4,12},{12,4},{1,9},{9,1},{5,13},{13,5},{2,10},{10,2},... | collective-permute-start | bytes 688136 | tf_op jit(solution)/shard_map/ppermute | solution.py:51
  8.8 0.1 fusion.39
  9.0 0.0 copy-done.1
  9.1 10.1 %collective-permute-done = bf16[2,112,512]{2,1,0:T(8,128)(2,1)S(1)} collective-permute-done((bf16[2,112,512]{2,1,0:T(8,128)(2,1)S(1)}, bf16[2,112,512]{2,1,0:T(8,128)(2,1)S(1)}, u32[]{:S(2)}, u32[]{:S(2)}) %collective-permute-start) | collective-permute-done | bytes 229408 | tf_op jit(solution)/shard_map/ppermute | solution.py:51
  19.1 0.4 %collective-permute-start.2 = (bf16[2,112,512]{2,1,0:T(8,128)(2,1)S(1)}, bf16[2,112,512]{2,1,0:T(8,128)(2,1)S(1)}, u32[]{:S(2)}, u32[]{:S(2)}) collective-permute-start(bf16[2,112,512]{2,1,0:T(8,128)(2,1)S(1)} %collective-permute-done), channel_id=1, source_target_pairs={{0,4},{4,0},{8,12},{12,8},{1,5},{5,1},{9,13},{13,9},{2,6},{6,2},{1... | collective-permute-start | bytes 688136 | tf_op jit(solution)/shard_map/ppermute | solution.py:53
  19.6 0.0 copy-done.2
  19.6 0.0 collective-permute-done.1
  19.6 5.5 %collective-permute-done.2 = bf16[2,112,512]{2,1,0:T(8,128)(2,1)S(1)} collective-permute-done((bf16[2,112,512]{2,1,0:T(8,128)(2,1)S(1)}, bf16[2,112,512]{2,1,0:T(8,128)(2,1)S(1)}, u32[]{:S(2)}, u32[]{:S(2)}) %collective-permute-start.2) | collective-permute-done | bytes 229408 | tf_op jit(solution)/shard_map/ppermute | solution.py:53
  25.2 0.7 %convolution_bitcast_fusion = f32[2,256,2,512]{3,1,2,0:T(8,128)S(1)} fusion(bf16[1,2,112,512]{3,2,0,1:T(8,128)(2,1)S(1)} %bitcast.111, bf16[1,2,112,512]{3,2,0,1:T(8,128)(2,1)S(1)} %bitcast.109, bf16[1,2,112,512]{3,2,0,1:T(8,128)(2,1)S(1)} %bitcast.110, bf16[1,2,112,512]{3,2,0,1:T(8,128)(2,1)S(1)} %get-tuple-element.17, ...), kind=kOutput, calls=%fused_computation.4 | convolution fusion | flops 475267072 | bytes 3473408 | tf_op jit(solution)/shard_map/dot_general | solution.py:37
  25.9 0.2 fusion.26
  26.1 0.1 fusion.32
  26.1 0.1 collective-permute-start.3
  26.2 1.6 %collective-permute-start.4 = (bf16[2,64,512]{2,1,0:T(8,128)(2,1)S(1)}, bf16[2,64,512]{2,1,0:T(8,128)(2,1)S(1)}, u32[]{:S(2)}, u32[]{:S(2)}) collective-permute-start(bf16[2,64,512]{2,1,0:T(8,128)(2,1)S(1)} %get-tuple-element.11), channel_id=1, source_target_pairs={{0,2},{1,3},{2,0},{3,1},{4,6},{5,7},{6,4},{7,5},{8,10},{9,11},{10,... | collective-permute-start | bytes 393224 | tf_op jit(solution)/shard_map/ppermute | solution.py:76
  27.8 0.3 collective-permute-start.5
  28.1 0.0 collective-permute-done.3
  28.2 4.4 %collective-permute-done.4 = bf16[2,64,512]{2,1,0:T(8,128)(2,1)S(1)} collective-permute-done((bf16[2,64,512]{2,1,0:T(8,128)(2,1)S(1)}, bf16[2,64,512]{2,1,0:T(8,128)(2,1)S(1)}, u32[]{:S(2)}, u32[]{:S(2)}) %collective-permute-start.4) | collective-permute-done | bytes 131104 | tf_op jit(solution)/shard_map/ppermute | solution.py:76
  32.6 1.9 %collective-permute-done.5 = bf16[2,64,512]{2,1,0:T(8,128)(2,1)S(1)} collective-permute-done((bf16[2,64,512]{2,1,0:T(8,128)(2,1)S(1)}, bf16[2,64,512]{2,1,0:T(8,128)(2,1)S(1)}, u32[]{:S(2)}, u32[]{:S(2)}) %collective-permute-start.5) | collective-permute-done | bytes 131104 | tf_op jit(solution)/shard_map/ppermute | solution.py:76
  34.5 4.1 %subtract_select_fusion = f32[64,32,512]{2,1,0:T(8,128)} fusion(f32[32]{0:T(128)S(1)} %get-tuple-element.41, f32[64,512]{1,0:T(8,128)S(1)} %get-tuple-element.28, f32[32]{0:T(128)S(1)} %get-tuple-element.30, f32[64,512]{1,0:T(8,128)S(1)} %get-tuple-element.27, f32[32]{0:T(128)S(1)} %get-tuple-element.40, f32[64,512]{1,0:T(8,128)S(1)} %get-tuple-element.26, ...), kind=kLoop, calls=%fused_computation | loop fusion | flops 19922944 | bytes 5506048 | tf_op jit(solution)/shard_map/jit(_where)/select_n | solution.py:132
  (11 shorter events, 0.2 us)
Async XLA Ops:
  0.0 1.2 %copy-start = (bf16[1,2,512,512]{3,2,1,0:T(8,128)(2,1)S(1)}, bf16[1,2,512,512]{3,2,1,0:T(8,128)(2,1)}, u32[]{:S(2)}) copy-start(bf16[1,2,512,512]{3,2,1,0:T(8,128)(2,1)} %param.5) | copy-start | bytes 3145732
  0.0 9.0 %copy-start.1 = (bf16[1,4,2,112,256]{4,3,2,1,0:T(8,128)(2,1)S(1)}, bf16[1,4,2,112,256]{4,3,2,1,0:T(8,128)(2,1)}, u32[]{:S(2)}) copy-start(bf16[1,4,2,112,256]{4,3,2,1,0:T(8,128)(2,1)} %param.7) | copy-start | bytes 1376260
  0.0 19.6 %copy-start.2 = (s32[2,64,512]{2,1,0:T(8,128)S(1)}, s32[2,64,512]{2,1,0:T(8,128)}, u32[]{:S(2)}) copy-start(s32[2,64,512]{2,1,0:T(8,128)} %param.9) | copy-start | bytes 786436
  3.1 16.5 %collective-permute-start.1 = (bf16[2,112,512]{2,1,0:T(8,128)(2,1)S(1)}, bf16[2,112,512]{2,1,0:T(8,128)(2,1)S(1)}, u32[]{:S(2)}, u32[]{:S(2)}) collective-permute-start(bf16[2,112,512]{2,1,0:T(8,128)(2,1)S(1)} %bitcast.108), channel_id=1, source_target_pairs={{0,4},{4,0},{8,12},{12,8},{1,5},{5,1},{9,13},{13,9},{2,6},{6,2},{1... | collective-permute-start | bytes 688136 | tf_op jit(solution)/shard_map/ppermute | solution.py:52
  6.2 12.9 %collective-permute-start = (bf16[2,112,512]{2,1,0:T(8,128)(2,1)S(1)}, bf16[2,112,512]{2,1,0:T(8,128)(2,1)S(1)}, u32[]{:S(2)}, u32[]{:S(2)}) collective-permute-start(bf16[2,112,512]{2,1,0:T(8,128)(2,1)S(1)} %get-tuple-element.18), channel_id=1, source_target_pairs={{0,8},{8,0},{4,12},{12,4},{1,9},{9,1},{5,13},{13,5},{2,10},{10,2},... | collective-permute-start | bytes 688136 | tf_op jit(solution)/shard_map/ppermute | solution.py:51
  19.1 6.0 %collective-permute-start.2 = (bf16[2,112,512]{2,1,0:T(8,128)(2,1)S(1)}, bf16[2,112,512]{2,1,0:T(8,128)(2,1)S(1)}, u32[]{:S(2)}, u32[]{:S(2)}) collective-permute-start(bf16[2,112,512]{2,1,0:T(8,128)(2,1)S(1)} %collective-permute-done), channel_id=1, source_target_pairs={{0,4},{4,0},{8,12},{12,8},{1,5},{5,1},{9,13},{13,9},{2,6},{6,2},{1... | collective-permute-start | bytes 688136 | tf_op jit(solution)/shard_map/ppermute | solution.py:53
  26.1 2.0 %collective-permute-start.3 = (bf16[2,64,512]{2,1,0:T(8,128)(2,1)S(1)}, bf16[2,64,512]{2,1,0:T(8,128)(2,1)S(1)}, u32[]{:S(2)}, u32[]{:S(2)}) collective-permute-start(bf16[2,64,512]{2,1,0:T(8,128)(2,1)S(1)} %get-tuple-element.10), channel_id=1, source_target_pairs={{0,1},{1,0},{2,3},{3,2},{4,5},{5,4},{6,7},{7,6},{8,9},{9,8},{10,11... | collective-permute-start | bytes 393224 | tf_op jit(solution)/shard_map/ppermute | solution.py:76
  26.2 6.4 %collective-permute-start.4 = (bf16[2,64,512]{2,1,0:T(8,128)(2,1)S(1)}, bf16[2,64,512]{2,1,0:T(8,128)(2,1)S(1)}, u32[]{:S(2)}, u32[]{:S(2)}) collective-permute-start(bf16[2,64,512]{2,1,0:T(8,128)(2,1)S(1)} %get-tuple-element.11), channel_id=1, source_target_pairs={{0,2},{1,3},{2,0},{3,1},{4,6},{5,7},{6,4},{7,5},{8,10},{9,11},{10,... | collective-permute-start | bytes 393224 | tf_op jit(solution)/shard_map/ppermute | solution.py:76
  27.8 6.7 %collective-permute-start.5 = (bf16[2,64,512]{2,1,0:T(8,128)(2,1)S(1)}, bf16[2,64,512]{2,1,0:T(8,128)(2,1)S(1)}, u32[]{:S(2)}, u32[]{:S(2)}) collective-permute-start(bf16[2,64,512]{2,1,0:T(8,128)(2,1)S(1)} %get-tuple-element.12), channel_id=1, source_target_pairs={{0,3},{1,2},{2,1},{3,0},{4,7},{5,6},{6,5},{7,4},{8,11},{9,10},{10,... | collective-permute-start | bytes 393224 | tf_op jit(solution)/shard_map/ppermute | solution.py:76

commit v7 on v6

--- a/solution.py
+++ b/solution.py
@@ -6,7 +6,7 @@
 from jax.sharding import PartitionSpec as P
 
 NT = 32
-S_CHUNKS = 1
+S_CHUNKS = 2
 
 
 first_bin = 2

time: 38.8 us -> 41.8 us (1.077)
  starting transfers between devices: 8.06 us -> 13.6 us
  waiting for transfers between devices: 21.9 us -> 17.4 us
  matrix products: 2.38 us -> 3.81 us
  local copies, waits for them, and re-layouts: 0.52 us -> 1.15 us
    ppermute x3 -> x6, starting transfers between devices: 1.93 us -> 5.26 us  [freq_exchange(): pieces.append((f ^ d, lax.ppermute(part, 'freq', pairs)))]
    ppermute x1 -> x2, waiting for transfers between devices: 5.54 us -> 2.59 us  [relay_exchange(): passed = lax.ppermute(across, 'tile', pairs)]
    ppermute x1 -> x2, starting transfers between devices: 0.45 us -> 2.09 us  [relay_exchange(): passed = lax.ppermute(across, 'tile', pairs)]
    ppermute x3 -> x6, waiting for transfers between devices: 6.27 us -> 4.83 us  [freq_exchange(): pieces.append((f ^ d, lax.ppermute(part, 'freq', pairs)))]
    dot_general x1 -> x2, matrix products: 1.65 us -> 2.88 us  [column_products(): lax.dot_general(v_local, x_local, (((3,), (1,)), ((), ())), preferred_ele...]
    unnamed x6, local copies, waits for them, and re-layouts: 0.39 us -> 1.02 us
    ppermute x1 -> x2, starting transfers between devices: 2.59 us -> 3.05 us  [relay_exchange(): across = lax.ppermute(other, 'tile', [(0, 2), (2, 0), (1, 3), (3, 1)])]
    dot_general x1 -> x2, matrix products: 0.72 us -> 0.93 us  [row_spectrum(): lax.dot_general(u_local, blocks, (((0, 2), (0, 2)), ((), ())), preferred_...]
  transfers between devices with their start and end apart: 6 -> 12, of which waited for: 4 -> 5; matrix products, arithmetic and copies ran while one was open for 1% -> 3% of each run, Pallas kernels for 0% -> 0%
where the time goes in v7:
time: 41.8 us; the launch traced here: 41.6 us
  waiting for transfers between devices  17.4 us (42%)
  starting transfers between devices  13.6 us (33%)
  other arithmetic  5.41 us (13%)
  matrix products  3.81 us (9%)
  local copies, waits for them, and re-layouts  1.15 us (3%)
    ppermute x2, waiting for transfers between devices, relay_exchange(): across = lax.ppermute(other, 'tile', [(0, 2), (2, 0), (1, 3), (3, 1)])  9.98 us
    ppermute x6, starting transfers between devices, freq_exchange(): pieces.append((f ^ d, lax.ppermute(part, 'freq', pairs)))  5.26 us
    ppermute x6, waiting for transfers between devices, freq_exchange(): pieces.append((f ^ d, lax.ppermute(part, 'freq', pairs)))  4.83 us
    select_n x1, other arithmetic, per_device(): return jnp.where(inside, traces, jnp.float32(0.0))  4.07 us
    ppermute x2, starting transfers between devices, relay_exchange(): partner = lax.ppermute(mine, 'tile', pairs)  3.18 us
    ppermute x2, starting transfers between devices, relay_exchange(): across = lax.ppermute(other, 'tile', [(0, 2), (2, 0), (1, 3), (3, 1)])  3.05 us
    dot_general x2, matrix products, column_products(): lax.dot_general(v_local, x_local, (((3,), (1,)), ((), ())), preferred_ele...  2.88 us
    ppermute x2, waiting for transfers between devices, relay_exchange(): passed = lax.ppermute(across, 'tile', pairs)  2.59 us
  transfers between devices with their start and end apart: 12, of which 5 were waited for; matrix products, arithmetic and copies ran while one was open for 3% of the time, Pallas kernels for 0%

profile of v7, /device:TPU:0, one launch (start us, length us, event | category | flops | bytes accessed | tf_op | source)
XLA Modules:
  0.0 41.6 jit_solution(2599636814201029612)
XLA Ops:
  0.0 1.0 %copy-done = bf16[1,1,2,2,112,512]{5,4,3,2,1,0:T(8,128)(2,1)S(1)} copy-done((bf16[1,1,2,2,112,512]{5,4,3,2,1,0:T(8,128)(2,1)S(1)}, bf16[1,1,2,2,112,512]{5,4,3,2,1,0:T(8,128)(2,1)}, u32[]{:S(2)}) %copy-start) | copy-done | bytes 458776
  1.0 1.4 %fusion.1 = f32[2,2,112,2,256]{4,2,0,3,1:T(8,128)S(1)} fusion(bf16[2,512,512]{2,1,0:T(8,128)(2,1)} %bitcast.146, bf16[1,1,2,2,112,512]{5,4,3,2,1,0:T(8,128)(2,1)S(1)} %copy-done), kind=kOutput, calls=%fused_computation.7 | convolution fusion | flops 234881024 | bytes 1900544 | tf_op jit(solution)/shard_map/dot_general | solution.py:24
  2.5 1.4 %fusion.2 = f32[2,2,112,2,256]{4,2,3,1,0:T(8,128)S(1)} fusion(bf16[2,512,512]{2,1,0:T(8,128)(2,1)} %bitcast.147, bf16[1,1,2,2,112,512]{5,4,3,2,1,0:T(8,128)(2,1)S(1)} %copy-done), kind=kOutput, calls=%fused_computation.9 | convolution fusion | flops 234881024 | bytes 1900544 | tf_op jit(solution)/shard_map/dot_general | solution.py:24
  3.9 0.7 %iota_compare_fusion.2 = pred[2,112]{1,0:T(4,128)(4,1)S(1)} fusion(s32[2]{0:T(128)} %bitcast.156), kind=kLoop, calls=%fused_computation.129 | loop fusion | flops 224 | bytes 232 | tf_op jit(solution)/shard_map/lt | solution.py:30
  4.6 0.2 fusion.29
  4.9 3.1 %collective-permute-start.4 = (bf16[2,112,256]{2,1,0:T(8,128)(2,1)S(1)}, bf16[2,112,256]{2,1,0:T(8,128)(2,1)S(1)}, u32[]{:S(2)}, u32[]{:S(2)}) collective-permute-start(bf16[2,112,256]{2,1,0:T(8,128)(2,1)S(1)} %bitcast.149), channel_id=1, source_target_pairs={{0,4},{4,0},{8,12},{12,8},{1,5},{5,1},{9,13},{13,9},{2,6},{6,2},{1... | collective-permute-start | bytes 344072 | tf_op jit(solution)/shard_map/ppermute | solution.py:52
  8.0 0.1 collective-permute-start.1
  8.1 3.0 %collective-permute-start = (bf16[2,112,256]{2,1,0:T(8,128)(2,1)S(1)}, bf16[2,112,256]{2,1,0:T(8,128)(2,1)S(1)}, u32[]{:S(2)}, u32[]{:S(2)}) collective-permute-start(bf16[2,112,256]{2,1,0:T(8,128)(2,1)S(1)} %get-tuple-element.36), channel_id=1, source_target_pairs={{0,8},{8,0},{4,12},{12,4},{1,9},{9,1},{5,13},{13,5},{2,10},{10,2},... | collective-permute-start | bytes 344072 | tf_op jit(solution)/shard_map/ppermute | solution.py:51
  11.1 0.0 collective-permute-start.3
  11.2 0.1 fusion.56
  11.3 10.0 %collective-permute-done.3 = bf16[2,112,256]{2,1,0:T(8,128)(2,1)S(1)} collective-permute-done((bf16[2,112,256]{2,1,0:T(8,128)(2,1)S(1)}, bf16[2,112,256]{2,1,0:T(8,128)(2,1)S(1)}, u32[]{:S(2)}, u32[]{:S(2)}) %collective-permute-start.3) | collective-permute-done | bytes 114720 | tf_op jit(solution)/shard_map/ppermute | solution.py:51
  21.3 0.7 %collective-permute-start.5 = (bf16[2,112,256]{2,1,0:T(8,128)(2,1)S(1)}, bf16[2,112,256]{2,1,0:T(8,128)(2,1)S(1)}, u32[]{:S(2)}, u32[]{:S(2)}) collective-permute-start(bf16[2,112,256]{2,1,0:T(8,128)(2,1)S(1)} %collective-permute-done.3), channel_id=1, source_target_pairs={{0,4},{4,0},{8,12},{12,8},{1,5},{5,1},{9,13},{13,9},{2,6},{6,2},{1... | collective-permute-start | bytes 344072 | tf_op jit(solution)/shard_map/ppermute | solution.py:53
  22.0 0.0 collective-permute-done
  22.0 1.4 %collective-permute-start.2 = (bf16[2,112,256]{2,1,0:T(8,128)(2,1)S(1)}, bf16[2,112,256]{2,1,0:T(8,128)(2,1)S(1)}, u32[]{:S(2)}, u32[]{:S(2)}) collective-permute-start(bf16[2,112,256]{2,1,0:T(8,128)(2,1)S(1)} %collective-permute-done), channel_id=1, source_target_pairs={{0,4},{4,0},{8,12},{12,8},{1,5},{5,1},{9,13},{13,9},{2,6},{6,2},{1... | collective-permute-start | bytes 344072 | tf_op jit(solution)/shard_map/ppermute | solution.py:53
  23.5 2.6 %collective-permute-done.5 = bf16[2,112,256]{2,1,0:T(8,128)(2,1)S(1)} collective-permute-done((bf16[2,112,256]{2,1,0:T(8,128)(2,1)S(1)}, bf16[2,112,256]{2,1,0:T(8,128)(2,1)S(1)}, u32[]{:S(2)}, u32[]{:S(2)}) %collective-permute-start.5) | collective-permute-done | bytes 114720 | tf_op jit(solution)/shard_map/ppermute | solution.py:53
  26.0 0.5 %convolution_bitcast_fusion = f32[2,256,2,256]{3,1,2,0:T(8,128)S(1)} fusion(bf16[1,2,112,256]{3,2,0,1:T(8,128)(2,1)S(1)} %bitcast.154, bf16[1,2,112,256]{3,2,0,1:T(8,128)(2,1)S(1)} %bitcast.152, bf16[1,2,112,256]{3,2,0,1:T(8,128)(2,1)S(1)} %bitcast.153, bf16[1,2,112,256]{3,2,0,1:T(8,128)(2,1)S(1)} %get-tuple-element.37, ...), kind=kOutput, calls=%fused_computation.4 | convolution fusion | flops 238551040 | bytes 1966080 | tf_op jit(solution)/shard_map/dot_general | solution.py:37
  26.5 0.1 fusion.37
  26.6 0.1 collective-permute-start.7
  26.7 1.9 %collective-permute-start.9 = (bf16[2,64,256]{2,1,0:T(8,128)(2,1)S(1)}, bf16[2,64,256]{2,1,0:T(8,128)(2,1)S(1)}, u32[]{:S(2)}, u32[]{:S(2)}) collective-permute-start(bf16[2,64,256]{2,1,0:T(8,128)(2,1)S(1)} %get-tuple-element.27), channel_id=1, source_target_pairs={{0,2},{1,3},{2,0},{3,1},{4,6},{5,7},{6,4},{7,5},{8,10},{9,11},{10,... | collective-permute-start | bytes 196616 | tf_op jit(solution)/shard_map/ppermute | solution.py:76
  28.6 0.1 collective-permute-start.11
  28.6 0.5 %convolution_bitcast_fusion.1 = f32[2,256,2,256]{3,1,2,0:T(8,128)S(1)} fusion(bf16[1,2,112,256]{3,2,0,1:T(8,128)(2,1)S(1)} %bitcast.155, bf16[1,2,112,256]{3,2,0,1:T(8,128)(2,1)S(1)} %bitcast.150, bf16[1,2,112,256]{3,2,0,1:T(8,128)(2,1)S(1)} %bitcast.151, bf16[1,2,112,256]{3,2,0,1:T(8,128)(2,1)S(1)} %get-tuple-element.35, ...), kind=kOutput, calls=%fused_computation.5 | convolution fusion | flops 238551040 | bytes 1966080 | tf_op jit(solution)/shard_map/dot_general | solution.py:37
  29.1 0.1 fusion.35
  29.2 0.3 collective-permute-start.6
  29.5 1.6 %collective-permute-start.10 = (bf16[2,64,256]{2,1,0:T(8,128)(2,1)S(1)}, bf16[2,64,256]{2,1,0:T(8,128)(2,1)S(1)}, u32[]{:S(2)}, u32[]{:S(2)}) collective-permute-start(bf16[2,64,256]{2,1,0:T(8,128)(2,1)S(1)} %get-tuple-element.24), channel_id=1, source_target_pairs={{0,3},{1,2},{2,1},{3,0},{4,7},{5,6},{6,5},{7,4},{8,11},{9,10},{10,... | collective-permute-start | bytes 196616 | tf_op jit(solution)/shard_map/ppermute | solution.py:76
  31.2 1.4 %collective-permute-done.11 = bf16[2,64,256]{2,1,0:T(8,128)(2,1)S(1)} collective-permute-done((bf16[2,64,256]{2,1,0:T(8,128)(2,1)S(1)}, bf16[2,64,256]{2,1,0:T(8,128)(2,1)S(1)}, u32[]{:S(2)}, u32[]{:S(2)}) %collective-permute-start.11) | collective-permute-done | bytes 65568 | tf_op jit(solution)/shard_map/ppermute | solution.py:76
  32.6 1.3 %collective-permute-start.8 = (bf16[2,64,256]{2,1,0:T(8,128)(2,1)S(1)}, bf16[2,64,256]{2,1,0:T(8,128)(2,1)S(1)}, u32[]{:S(2)}, u32[]{:S(2)}) collective-permute-start(bf16[2,64,256]{2,1,0:T(8,128)(2,1)S(1)} %get-tuple-element.23), channel_id=1, source_target_pairs={{0,2},{1,3},{2,0},{3,1},{4,6},{5,7},{6,4},{7,5},{8,10},{9,11},{10,... | collective-permute-start | bytes 196616 | tf_op jit(solution)/shard_map/ppermute | solution.py:76
  33.9 0.1 collective-permute-done.10
  34.1 0.0 collective-permute-done.9
  34.1 3.3 %collective-permute-done.8 = bf16[2,64,256]{2,1,0:T(8,128)(2,1)S(1)} collective-permute-done((bf16[2,64,256]{2,1,0:T(8,128)(2,1)S(1)}, bf16[2,64,256]{2,1,0:T(8,128)(2,1)S(1)}, u32[]{:S(2)}, u32[]{:S(2)}) %collective-permute-start.8) | collective-permute-done | bytes 65568 | tf_op jit(solution)/shard_map/ppermute | solution.py:76
  37.5 0.0 collective-permute-done.7
  37.5 0.0 collective-permute-done.6
  37.5 4.1 %subtract_select_fusion = f32[64,32,512]{2,1,0:T(8,128)} fusion(f32[32]{0:T(128)S(1)} %get-tuple-element.53, f32[64,512]{1,0:T(8,128)S(1)} %get-tuple-element.34, f32[32]{0:T(128)S(1)} %get-tuple-element.40, f32[64,512]{1,0:T(8,128)S(1)} %get-tuple-element.33, f32[32]{0:T(128)S(1)} %get-tuple-element.52, f32[64,512]{1,0:T(8,128)S(1)} %get-tuple-element.32, ...), kind=kLoop, calls=%fused_computation | loop fusion | flops 19922944 | bytes 5506048 | tf_op jit(solution)/shard_map/jit(_where)/select_n | solution.py:132
  (24 shorter events, 0.4 us)
Async XLA Ops:
  0.0 1.0 %copy-start = (bf16[1,1,2,2,112,512]{5,4,3,2,1,0:T(8,128)(2,1)S(1)}, bf16[1,1,2,2,112,512]{5,4,3,2,1,0:T(8,128)(2,1)}, u32[]{:S(2)}) copy-start(bf16[1,1,2,2,112,512]{5,4,3,2,1,0:T(8,128)(2,1)} %param.6) | copy-start | bytes 1376260
  0.0 11.1 %copy-start.2 = (s32[2,64,512]{2,1,0:T(8,128)S(1)}, s32[2,64,512]{2,1,0:T(8,128)}, u32[]{:S(2)}) copy-start(s32[2,64,512]{2,1,0:T(8,128)} %param.9) | copy-start | bytes 786436
  0.0 21.9 %copy-start.1 = (bf16[1,4,2,112,256]{4,3,2,1,0:T(8,128)(2,1)S(1)}, bf16[1,4,2,112,256]{4,3,2,1,0:T(8,128)(2,1)}, u32[]{:S(2)}) copy-start(bf16[1,4,2,112,256]{4,3,2,1,0:T(8,128)(2,1)} %param.7) | copy-start | bytes 1376260
  4.9 18.6 %collective-permute-start.4 = (bf16[2,112,256]{2,1,0:T(8,128)(2,1)S(1)}, bf16[2,112,256]{2,1,0:T(8,128)(2,1)S(1)}, u32[]{:S(2)}, u32[]{:S(2)}) collective-permute-start(bf16[2,112,256]{2,1,0:T(8,128)(2,1)S(1)} %bitcast.149), channel_id=1, source_target_pairs={{0,4},{4,0},{8,12},{12,8},{1,5},{5,1},{9,13},{13,9},{2,6},{6,2},{1... | collective-permute-start | bytes 344072 | tf_op jit(solution)/shard_map/ppermute | solution.py:52
  8.0 20.7 %collective-permute-start.1 = (bf16[2,112,256]{2,1,0:T(8,128)(2,1)S(1)}, bf16[2,112,256]{2,1,0:T(8,128)(2,1)S(1)}, u32[]{:S(2)}, u32[]{:S(2)}) collective-permute-start(bf16[2,112,256]{2,1,0:T(8,128)(2,1)S(1)} %bitcast.148), channel_id=1, source_target_pairs={{0,4},{4,0},{8,12},{12,8},{1,5},{5,1},{9,13},{13,9},{2,6},{6,2},{1... | collective-permute-start | bytes 344072 | tf_op jit(solution)/shard_map/ppermute | solution.py:52
  8.1 14.0 %collective-permute-start = (bf16[2,112,256]{2,1,0:T(8,128)(2,1)S(1)}, bf16[2,112,256]{2,1,0:T(8,128)(2,1)S(1)}, u32[]{:S(2)}, u32[]{:S(2)}) collective-permute-start(bf16[2,112,256]{2,1,0:T(8,128)(2,1)S(1)} %get-tuple-element.36), channel_id=1, source_target_pairs={{0,8},{8,0},{4,12},{12,4},{1,9},{9,1},{5,13},{13,5},{2,10},{10,2},... | collective-permute-start | bytes 344072 | tf_op jit(solution)/shard_map/ppermute | solution.py:51
  11.1 10.2 %collective-permute-start.3 = (bf16[2,112,256]{2,1,0:T(8,128)(2,1)S(1)}, bf16[2,112,256]{2,1,0:T(8,128)(2,1)S(1)}, u32[]{:S(2)}, u32[]{:S(2)}) collective-permute-start(bf16[2,112,256]{2,1,0:T(8,128)(2,1)S(1)} %get-tuple-element.38), channel_id=1, source_target_pairs={{0,8},{8,0},{4,12},{12,4},{1,9},{9,1},{5,13},{13,5},{2,10},{10,2},... | collective-permute-start | bytes 344072 | tf_op jit(solution)/shard_map/ppermute | solution.py:51
  21.3 4.8 %collective-permute-start.5 = (bf16[2,112,256]{2,1,0:T(8,128)(2,1)S(1)}, bf16[2,112,256]{2,1,0:T(8,128)(2,1)S(1)}, u32[]{:S(2)}, u32[]{:S(2)}) collective-permute-start(bf16[2,112,256]{2,1,0:T(8,128)(2,1)S(1)} %collective-permute-done.3), channel_id=1, source_target_pairs={{0,4},{4,0},{8,12},{12,8},{1,5},{5,1},{9,13},{13,9},{2,6},{6,2},{1... | collective-permute-start | bytes 344072 | tf_op jit(solution)/shard_map/ppermute | solution.py:53
  22.0 6.6 %collective-permute-start.2 = (bf16[2,112,256]{2,1,0:T(8,128)(2,1)S(1)}, bf16[2,112,256]{2,1,0:T(8,128)(2,1)S(1)}, u32[]{:S(2)}, u32[]{:S(2)}) collective-permute-start(bf16[2,112,256]{2,1,0:T(8,128)(2,1)S(1)} %collective-permute-done), channel_id=1, source_target_pairs={{0,4},{4,0},{8,12},{12,8},{1,5},{5,1},{9,13},{13,9},{2,6},{6,2},{1... | collective-permute-start | bytes 344072 | tf_op jit(solution)/shard_map/ppermute | solution.py:53
  26.6 10.8 %collective-permute-start.7 = (bf16[2,64,256]{2,1,0:T(8,128)(2,1)S(1)}, bf16[2,64,256]{2,1,0:T(8,128)(2,1)S(1)}, u32[]{:S(2)}, u32[]{:S(2)}) collective-permute-start(bf16[2,64,256]{2,1,0:T(8,128)(2,1)S(1)} %get-tuple-element.26), channel_id=1, source_target_pairs={{0,1},{1,0},{2,3},{3,2},{4,5},{5,4},{6,7},{7,6},{8,9},{9,8},{10,11... | collective-permute-start | bytes 196616 | tf_op jit(solution)/shard_map/ppermute | solution.py:76
  26.7 7.4 %collective-permute-start.9 = (bf16[2,64,256]{2,1,0:T(8,128)(2,1)S(1)}, bf16[2,64,256]{2,1,0:T(8,128)(2,1)S(1)}, u32[]{:S(2)}, u32[]{:S(2)}) collective-permute-start(bf16[2,64,256]{2,1,0:T(8,128)(2,1)S(1)} %get-tuple-element.27), channel_id=1, source_target_pairs={{0,2},{1,3},{2,0},{3,1},{4,6},{5,7},{6,4},{7,5},{8,10},{9,11},{10,... | collective-permute-start | bytes 196616 | tf_op jit(solution)/shard_map/ppermute | solution.py:76
  28.6 4.0 %collective-permute-start.11 = (bf16[2,64,256]{2,1,0:T(8,128)(2,1)S(1)}, bf16[2,64,256]{2,1,0:T(8,128)(2,1)S(1)}, u32[]{:S(2)}, u32[]{:S(2)}) collective-permute-start(bf16[2,64,256]{2,1,0:T(8,128)(2,1)S(1)} %get-tuple-element.28), channel_id=1, source_target_pairs={{0,3},{1,2},{2,1},{3,0},{4,7},{5,6},{6,5},{7,4},{8,11},{9,10},{10,... | collective-permute-start | bytes 196616 | tf_op jit(solution)/shard_map/ppermute | solution.py:76
  29.2 8.3 %collective-permute-start.6 = (bf16[2,64,256]{2,1,0:T(8,128)(2,1)S(1)}, bf16[2,64,256]{2,1,0:T(8,128)(2,1)S(1)}, u32[]{:S(2)}, u32[]{:S(2)}) collective-permute-start(bf16[2,64,256]{2,1,0:T(8,128)(2,1)S(1)} %get-tuple-element.22), channel_id=1, source_target_pairs={{0,1},{1,0},{2,3},{3,2},{4,5},{5,4},{6,7},{7,6},{8,9},{9,8},{10,11... | collective-permute-start | bytes 196616 | tf_op jit(solution)/shard_map/ppermute | solution.py:76
  29.5 4.5 %collective-permute-start.10 = (bf16[2,64,256]{2,1,0:T(8,128)(2,1)S(1)}, bf16[2,64,256]{2,1,0:T(8,128)(2,1)S(1)}, u32[]{:S(2)}, u32[]{:S(2)}) collective-permute-start(bf16[2,64,256]{2,1,0:T(8,128)(2,1)S(1)} %get-tuple-element.24), channel_id=1, source_target_pairs={{0,3},{1,2},{2,1},{3,0},{4,7},{5,6},{6,5},{7,4},{8,11},{9,10},{10,... | collective-permute-start | bytes 196616 | tf_op jit(solution)/shard_map/ppermute | solution.py:76
  32.6 4.8 %collective-permute-start.8 = (bf16[2,64,256]{2,1,0:T(8,128)(2,1)S(1)}, bf16[2,64,256]{2,1,0:T(8,128)(2,1)S(1)}, u32[]{:S(2)}, u32[]{:S(2)}) collective-permute-start(bf16[2,64,256]{2,1,0:T(8,128)(2,1)S(1)} %get-tuple-element.23), channel_id=1, source_target_pairs={{0,2},{1,3},{2,0},{3,1},{4,6},{5,7},{6,4},{7,5},{8,10},{9,11},{10,... | collective-permute-start | bytes 196616 | tf_op jit(solution)/shard_map/ppermute | solution.py:76

commit v8 on v6

--- a/solution.py
+++ b/solution.py
@@ -3,6 +3,7 @@
 import jax
 import jax.numpy as jnp
 from jax import lax
+from jax.experimental import pallas as pl
 from jax.sharding import PartitionSpec as P
 
 NT = 32
@@ -77,6 +78,61 @@
     return pieces
 
 
+def traces_kernel(table_ref, *refs):
+    piece_refs = refs[:-2]
+    bounds_ref, out_ref = refs[-2], refs[-1]
+    half = table_ref.shape[1]
+    count = len(piece_refs)
+    time_index = lax.broadcasted_iota(jnp.int32, (half, table_ref.shape[2]), 0)
+    for i in range(out_ref.shape[0]):
+        sums = [None, None]
+        for k, piece_ref in enumerate(piece_refs):
+            real = piece_ref[0, i:i + 1, :]
+            imag = piece_ref[1, i:i + 1, :]
+            term = real * table_ref[2 * k] - imag * table_ref[2 * k + 1]
+            sums[k % 2] = term if sums[k % 2] is None else sums[k % 2] + term
+        even = sums[0]
+        odd = sums[1] if sums[1] is not None else jnp.zeros_like(even)
+        first = bounds_ref[0, i:i + 1, :]
+        last = bounds_ref[1, i:i + 1, :]
+        low = even + odd
+        out_ref[i, 0:half, :] = jnp.where(
+            (time_index >= first) & (time_index < last), low, jnp.float32(0.0)
+        )
+        high = (even - odd) * table_ref[2 * count]
+        later = time_index + half
+        out_ref[i, half:2 * half, :] = jnp.where(
+            (later >= first) & (later < last), high, jnp.float32(0.0)
+        )
+
+
+def windowed_traces(pieces, window_bounds, n_freq):
+    cosine_table, sine_table = inverse_tables(n_freq, NT)
+    scale = 1.0 / math.sqrt(n_freq)
+    half = NT // 2
+    count_m, count_s = window_bounds.shape[1], window_bounds.shape[2]
+    rows = []
+    for index, _ in pieces:
+        for table in (cosine_table, sine_table):
+            row = lax.dynamic_index_in_dim(table, index, 0, keepdims=False)[:half] * scale
+            rows.append(jnp.broadcast_to(row[:, None], (half, count_s)))
+    parity = (pieces[0][0] + first_bin) % 2
+    sign = jnp.asarray(1 - 2 * parity, jnp.float32)
+    rows.append(jnp.full((half, count_s), sign, jnp.float32))
+    table = jnp.stack(rows, axis=0)
+    block_m = 8 if count_m % 8 == 0 else count_m
+    piece_spec = pl.BlockSpec((2, block_m, count_s), lambda g: (0, g, 0))
+    return pl.pallas_call(
+        traces_kernel,
+        grid=(count_m // block_m,),
+        in_specs=[pl.BlockSpec(table.shape, lambda g: (0, 0, 0))]
+        + [piece_spec] * len(pieces)
+        + [piece_spec],
+        out_specs=pl.BlockSpec((block_m, NT, count_s), lambda g: (g, 0, 0)),
+        out_shape=jax.ShapeDtypeStruct((count_m, NT, count_s), jnp.float32),
+    )(table, *[piece.astype(jnp.float32) for _, piece in pieces], window_bounds)
+
+
 def make_per_device(n_tile, n_freq):
     def per_device(sources, v_factors, u_factors, tile_ranks, window_bounds):
         v_local = v_factors[0, 0]
@@ -113,23 +169,7 @@
             )
             for k, (index, piece) in enumerate(received_parts[0])
         ]
-        cosine_table, sine_table = inverse_tables(n_freq, NT)
-        scale = 1.0 / math.sqrt(n_freq)
-        traces = 0.0
-        for index, piece in pieces:
-            cosine = lax.dynamic_index_in_dim(cosine_table, index, 0, keepdims=False) * scale
-            sine = lax.dynamic_index_in_dim(sine_table, index, 0, keepdims=False) * scale
-            widened = piece.astype(jnp.float32)
-            traces = (
-                traces
-                + widened[0][:, None, :] * cosine[None, :, None]
-                - widened[1][:, None, :] * sine[None, :, None]
-            )
-        time_index = jnp.arange(NT, dtype=jnp.int32)[None, :, None]
-        inside = (time_index >= window_bounds[0][:, None, :]) & (
-            time_index < window_bounds[1][:, None, :]
-        )
-        return jnp.where(inside, traces, jnp.float32(0.0))
+        return windowed_traces(pieces, window_bounds, n_freq)
 
     return per_device
 

time: 38.8 us -> 43.5 us (1.12); the launches traced: 38.6 us -> 42.8 us
  Pallas kernels: 0 us -> 6.65 us
  waiting for transfers between devices: 21.9 us -> 20 us
  other arithmetic: 5.57 us -> 4.32 us
  local copies, waits for them, and re-layouts: 0.52 us -> 1.05 us
    pallas_call x0 -> x1, Pallas kernels: none -> 6.65 us  [windowed_traces(): pl.pallas_call(traces_kernel, grid=(count_m // block_m,), in_specs=[pl.Bl...]
    select_n x1 -> x0, other arithmetic: 4.07 us -> none  [per_device(): return jnp.where(inside, traces, jnp.float32(0.0))]
    convert_element_type x4 -> x3, other arithmetic: 0.12 us -> 2.22 us  [windowed_traces(): piece.astype(jnp.float32)]
    ppermute x3, waiting for transfers between devices: 6.27 us -> 4.91 us  [freq_exchange(): pieces.append((f ^ d, lax.ppermute(part, 'freq', pairs)))]
    another operation x0 -> x1, other arithmetic: none -> 0.76 us  [row_spectrum(): return jnp.stack([real_part, imag_part], axis=0).astype(jnp.bfloat16)]
    unnamed x6 -> x14, local copies, waits for them, and re-layouts: 0.39 us -> 1 us
  transfers between devices with their start and end apart: 6 -> 6, of which waited for: 4 -> 4; matrix products, arithmetic and copies ran while one was open for 1% -> 5% of each run, Pallas kernels for 0% -> 0%
where the time goes in v8:
time: 43.5 us; the launch traced here: 42.8 us
  waiting for transfers between devices  20 us (46%)
  starting transfers between devices  8.27 us (19%)
  Pallas kernels  6.65 us (15%)
  other arithmetic  4.32 us (10%)
  matrix products  2.38 us (5%)
  local copies, waits for them, and re-layouts  1.05 us (2%)
    ppermute x1, waiting for transfers between devices, relay_exchange(): across = lax.ppermute(other, 'tile', [(0, 2), (2, 0), (1, 3), (3, 1)])  9.67 us
    pallas_call x1, Pallas kernels, windowed_traces(): pl.pallas_call(traces_kernel, grid=(count_m // block_m,), in_specs=[pl.Bl...  6.65 us
    ppermute x1, waiting for transfers between devices, relay_exchange(): passed = lax.ppermute(across, 'tile', pairs)  5.43 us
    ppermute x3, waiting for transfers between devices, freq_exchange(): pieces.append((f ^ d, lax.ppermute(part, 'freq', pairs)))  4.91 us
    ppermute x1, starting transfers between devices, relay_exchange(): partner = lax.ppermute(mine, 'tile', pairs)  3.09 us
    ppermute x1, starting transfers between devices, relay_exchange(): across = lax.ppermute(other, 'tile', [(0, 2), (2, 0), (1, 3), (3, 1)])  2.59 us
    convert_element_type x3, other arithmetic, windowed_traces(): piece.astype(jnp.float32)  2.22 us
    ppermute x3, starting transfers between devices, freq_exchange(): pieces.append((f ^ d, lax.ppermute(part, 'freq', pairs)))  2.14 us
  transfers between devices with their start and end apart: 6, of which 4 were waited for; matrix products, arithmetic and copies ran while one was open for 5% of the time, Pallas kernels for 0%

profile of v8, /device:TPU:0, one launch (start us, length us, event | category | flops | bytes accessed | tf_op | source)
XLA Modules:
  0.0 42.8 jit_solution(7613654658274528169)
XLA Ops:
  0.0 0.8 %iota_compare_fusion = pred[2,112]{1,0:T(4,128)(4,1)S(1)} fusion(s32[2]{0:T(128)} %bitcast.92), kind=kLoop, calls=%fused_computation.81 | loop fusion | flops 224 | bytes 232 | tf_op jit(solution)/shard_map/lt | solution.py:31
  0.8 0.4 copy-done
  1.2 1.7 %fusion = f32[2,2,112,2,512]{4,2,3,1,0:T(8,128)S(1)} fusion(bf16[1,2,512,512]{3,2,1,0:T(8,128)(2,1)S(1)} %copy-done, bf16[1,1,2,2,112,512]{5,4,3,2,1,0:T(8,128)(2,1)} %param.6), kind=kOutput, calls=%fused_computation.1 | convolution fusion | flops 469762048 | bytes 3342336 | tf_op jit(solution)/shard_map/dot_general | solution.py:25
  2.9 0.0 copy-start.1
  2.9 0.2 fusion.12
  3.1 0.1 fusion.28
  3.1 3.1 %collective-permute-start.1 = (bf16[2,112,512]{2,1,0:T(8,128)(2,1)S(1)}, bf16[2,112,512]{2,1,0:T(8,128)(2,1)S(1)}, u32[]{:S(2)}, u32[]{:S(2)}) collective-permute-start(bf16[2,112,512]{2,1,0:T(8,128)(2,1)S(1)} %bitcast.88), channel_id=1, source_target_pairs={{0,4},{4,0},{8,12},{12,8},{1,5},{5,1},{9,13},{13,9},{2,6},{6,2},{1... | collective-permute-start | bytes 688136 | tf_op jit(solution)/shard_map/ppermute | solution.py:53
  6.2 2.6 %collective-permute-start = (bf16[2,112,512]{2,1,0:T(8,128)(2,1)S(1)}, bf16[2,112,512]{2,1,0:T(8,128)(2,1)S(1)}, u32[]{:S(2)}, u32[]{:S(2)}) collective-permute-start(bf16[2,112,512]{2,1,0:T(8,128)(2,1)S(1)} %get-tuple-element.18), channel_id=1, source_target_pairs={{0,8},{8,0},{4,12},{12,4},{1,9},{9,1},{5,13},{13,5},{2,10},{10,2},... | collective-permute-start | bytes 688136 | tf_op jit(solution)/shard_map/ppermute | solution.py:52
  8.8 0.1 fusion.37
  9.1 0.1 constant_dynamic-update-slice_fusion.8
  9.1 0.1 constant_dynamic-update-slice_fusion.7
  9.2 0.1 constant_dynamic-update-slice_fusion.6
  9.3 0.1 constant_dynamic-update-slice_fusion.5
  9.3 0.1 constant_dynamic-update-slice_fusion.4
  9.4 0.1 constant_dynamic-update-slice_fusion.3
  9.5 9.7 %collective-permute-done = bf16[2,112,512]{2,1,0:T(8,128)(2,1)S(1)} collective-permute-done((bf16[2,112,512]{2,1,0:T(8,128)(2,1)S(1)}, bf16[2,112,512]{2,1,0:T(8,128)(2,1)S(1)}, u32[]{:S(2)}, u32[]{:S(2)}) %collective-permute-start) | collective-permute-done | bytes 229408 | tf_op jit(solution)/shard_map/ppermute | solution.py:52
  19.2 0.4 %collective-permute-start.2 = (bf16[2,112,512]{2,1,0:T(8,128)(2,1)S(1)}, bf16[2,112,512]{2,1,0:T(8,128)(2,1)S(1)}, u32[]{:S(2)}, u32[]{:S(2)}) collective-permute-start(bf16[2,112,512]{2,1,0:T(8,128)(2,1)S(1)} %collective-permute-done), channel_id=1, source_target_pairs={{0,4},{4,0},{8,12},{12,8},{1,5},{5,1},{9,13},{13,9},{2,6},{6,2},{1... | collective-permute-start | bytes 688136 | tf_op jit(solution)/shard_map/ppermute | solution.py:54
  19.7 0.1 constant_dynamic-update-slice_fusion.2
  19.7 0.0 collective-permute-done.1
  19.7 5.4 %collective-permute-done.2 = bf16[2,112,512]{2,1,0:T(8,128)(2,1)S(1)} collective-permute-done((bf16[2,112,512]{2,1,0:T(8,128)(2,1)S(1)}, bf16[2,112,512]{2,1,0:T(8,128)(2,1)S(1)}, u32[]{:S(2)}, u32[]{:S(2)}) %collective-permute-start.2) | collective-permute-done | bytes 229408 | tf_op jit(solution)/shard_map/ppermute | solution.py:54
  25.2 0.7 %convolution_bitcast_fusion = f32[2,256,2,512]{3,1,2,0:T(8,128)S(1)} fusion(bf16[1,2,112,512]{3,2,0,1:T(8,128)(2,1)S(1)} %bitcast.91, bf16[1,2,112,512]{3,2,0,1:T(8,128)(2,1)S(1)} %bitcast.89, bf16[1,2,112,512]{3,2,0,1:T(8,128)(2,1)S(1)} %bitcast.90, bf16[1,2,112,512]{3,2,0,1:T(8,128)(2,1)S(1)} %get-tuple-element.17, ...), kind=kOutput, calls=%fused_computation | convolution fusion | flops 475267072 | bytes 3473408 | tf_op jit(solution)/shard_map/dot_general | solution.py:38
  25.9 0.2 fusion.25
  26.1 0.8 %fusion.29 = (bf16[2,64,512]{2,1,0:T(8,128)(2,1)S(1)}, f32[2,64,512]{2,1,0:T(8,128)}, bf16[2,64,512]{2,1,0:T(8,128)(2,1)S(1)}, bf16[2,64,512]{2,1,0:T(8,128)(2,1)S(1)}) fusion(s32[]{:T(128)S(6)} %select_n.119, bf16[1,256,512]{2,1,0:T(8,128)(2,1)S(1)} %get-tuple-element.6, bf16[1,256,512]{2,1,0:T(8,128)(2,1)S(1)} %get-tuple-element.5, s32[]{:T(128)S(6)} %select_n.116, ...), kind=kLoop, calls=%fused_computation.49 | loop fusion | flops 1048576 | bytes 1179664 | tf_op jit(solution)/shard_map/stack | solution.py:43
  26.8 1.6 %collective-permute-start.3 = (bf16[2,64,512]{2,1,0:T(8,128)(2,1)S(1)}, bf16[2,64,512]{2,1,0:T(8,128)(2,1)S(1)}, u32[]{:S(2)}, u32[]{:S(2)}) collective-permute-start(bf16[2,64,512]{2,1,0:T(8,128)(2,1)S(1)} %get-tuple-element.11), channel_id=1, source_target_pairs={{0,1},{1,0},{2,3},{3,2},{4,5},{5,4},{6,7},{7,6},{8,9},{9,8},{10,11... | collective-permute-start | bytes 393224 | tf_op jit(solution)/shard_map/ppermute | solution.py:77
  28.4 0.5 %collective-permute-start.4 = (bf16[2,64,512]{2,1,0:T(8,128)(2,1)S(1)}, bf16[2,64,512]{2,1,0:T(8,128)(2,1)S(1)}, u32[]{:S(2)}, u32[]{:S(2)}) collective-permute-start(bf16[2,64,512]{2,1,0:T(8,128)(2,1)S(1)} %get-tuple-element.12), channel_id=1, source_target_pairs={{0,2},{1,3},{2,0},{3,1},{4,6},{5,7},{6,4},{7,5},{8,10},{9,11},{10,... | collective-permute-start | bytes 393224 | tf_op jit(solution)/shard_map/ppermute | solution.py:77
  29.0 0.1 constant_dynamic-update-slice_fusion.1
  29.1 3.5 %collective-permute-done.5 = bf16[2,64,512]{2,1,0:T(8,128)(2,1)S(1)} collective-permute-done((bf16[2,64,512]{2,1,0:T(8,128)(2,1)S(1)}, bf16[2,64,512]{2,1,0:T(8,128)(2,1)S(1)}, u32[]{:S(2)}, u32[]{:S(2)}) %collective-permute-start.5) | collective-permute-done | bytes 131104 | tf_op jit(solution)/shard_map/ppermute | solution.py:77
  32.6 0.7 %convert_element_type.60.refs_3_ = f32[2,64,512]{2,1,0:T(8,128)} convert(bf16[2,64,512]{2,1,0:T(8,128)(2,1)S(1)} %collective-permute-done.5) | non-fusion elementwise | flops 65536 | bytes 393216 | tf_op jit(solution)/shard_map/convert_element_type | solution.py:133
  33.3 0.7 %convert_element_type.58.refs_1_ = f32[2,64,512]{2,1,0:T(8,128)} convert(bf16[2,64,512]{2,1,0:T(8,128)(2,1)S(1)} %collective-permute-done.3) | non-fusion elementwise | flops 65536 | bytes 393216 | tf_op jit(solution)/shard_map/convert_element_type | solution.py:133
  34.1 1.4 %collective-permute-done.4 = bf16[2,64,512]{2,1,0:T(8,128)(2,1)S(1)} collective-permute-done((bf16[2,64,512]{2,1,0:T(8,128)(2,1)S(1)}, bf16[2,64,512]{2,1,0:T(8,128)(2,1)S(1)}, u32[]{:S(2)}, u32[]{:S(2)}) %collective-permute-start.4) | collective-permute-done | bytes 131104 | tf_op jit(solution)/shard_map/ppermute | solution.py:77
  35.4 0.7 %convert_element_type.59.refs_2_ = f32[2,64,512]{2,1,0:T(8,128)} convert(bf16[2,64,512]{2,1,0:T(8,128)(2,1)S(1)} %collective-permute-done.4) | non-fusion elementwise | flops 65536 | bytes 393216 | tf_op jit(solution)/shard_map/convert_element_type | solution.py:133
  36.2 6.7 %shard_map.55 = f32[64,32,512]{2,1,0:T(8,128)} custom-call(f32[9,16,512]{2,1,0:T(8,128)} %copy-done.2, f32[2,64,512]{2,1,0:T(8,128)} %get-tuple-element.10.refs_0_, f32[2,64,512]{2,1,0:T(8,128)} %convert_element_type.58.refs_1_, f32[2,64,512]{2,1,0:T(8,128)} %convert_element_type.59.refs_2_, f32[2,64,512]{2,1,0:T(8,128)} %convert_element_type.60.refs_3_, ...), custom_call_target="tpu_custom_call" | custom-call | tf_op jit(solution)/shard_map/pallas_call | solution.py:125
  (18 shorter events, 0.1 us)
Async XLA Ops:
  0.0 1.2 %copy-start = (bf16[1,2,512,512]{3,2,1,0:T(8,128)(2,1)S(1)}, bf16[1,2,512,512]{3,2,1,0:T(8,128)(2,1)}, u32[]{:S(2)}) copy-start(bf16[1,2,512,512]{3,2,1,0:T(8,128)(2,1)} %param.5) | copy-start | bytes 3145732
  2.9 16.7 %copy-start.1 = (bf16[1,4,2,112,256]{4,3,2,1,0:T(8,128)(2,1)S(1)}, bf16[1,4,2,112,256]{4,3,2,1,0:T(8,128)(2,1)}, u32[]{:S(2)}) copy-start(bf16[1,4,2,112,256]{4,3,2,1,0:T(8,128)(2,1)} %param.7) | copy-start | bytes 1376260
  3.1 16.6 %collective-permute-start.1 = (bf16[2,112,512]{2,1,0:T(8,128)(2,1)S(1)}, bf16[2,112,512]{2,1,0:T(8,128)(2,1)S(1)}, u32[]{:S(2)}, u32[]{:S(2)}) collective-permute-start(bf16[2,112,512]{2,1,0:T(8,128)(2,1)S(1)} %bitcast.88), channel_id=1, source_target_pairs={{0,4},{4,0},{8,12},{12,8},{1,5},{5,1},{9,13},{13,9},{2,6},{6,2},{1... | collective-permute-start | bytes 688136 | tf_op jit(solution)/shard_map/ppermute | solution.py:53
  6.2 12.9 %collective-permute-start = (bf16[2,112,512]{2,1,0:T(8,128)(2,1)S(1)}, bf16[2,112,512]{2,1,0:T(8,128)(2,1)S(1)}, u32[]{:S(2)}, u32[]{:S(2)}) collective-permute-start(bf16[2,112,512]{2,1,0:T(8,128)(2,1)S(1)} %get-tuple-element.18), channel_id=1, source_target_pairs={{0,8},{8,0},{4,12},{12,4},{1,9},{9,1},{5,13},{13,5},{2,10},{10,2},... | collective-permute-start | bytes 688136 | tf_op jit(solution)/shard_map/ppermute | solution.py:52
  19.2 6.0 %collective-permute-start.2 = (bf16[2,112,512]{2,1,0:T(8,128)(2,1)S(1)}, bf16[2,112,512]{2,1,0:T(8,128)(2,1)S(1)}, u32[]{:S(2)}, u32[]{:S(2)}) collective-permute-start(bf16[2,112,512]{2,1,0:T(8,128)(2,1)S(1)} %collective-permute-done), channel_id=1, source_target_pairs={{0,4},{4,0},{8,12},{12,8},{1,5},{5,1},{9,13},{13,9},{2,6},{6,2},{1... | collective-permute-start | bytes 688136 | tf_op jit(solution)/shard_map/ppermute | solution.py:54
  26.8 5.8 %collective-permute-start.5 = (bf16[2,64,512]{2,1,0:T(8,128)(2,1)S(1)}, bf16[2,64,512]{2,1,0:T(8,128)(2,1)S(1)}, u32[]{:S(2)}, u32[]{:S(2)}) collective-permute-start(bf16[2,64,512]{2,1,0:T(8,128)(2,1)S(1)} %get-tuple-element.9), channel_id=1, source_target_pairs={{0,3},{1,2},{2,1},{3,0},{4,7},{5,6},{6,5},{7,4},{8,11},{9,10},{10,... | collective-permute-start | bytes 393224 | tf_op jit(solution)/shard_map/ppermute | solution.py:77
  26.8 6.5 %collective-permute-start.3 = (bf16[2,64,512]{2,1,0:T(8,128)(2,1)S(1)}, bf16[2,64,512]{2,1,0:T(8,128)(2,1)S(1)}, u32[]{:S(2)}, u32[]{:S(2)}) collective-permute-start(bf16[2,64,512]{2,1,0:T(8,128)(2,1)S(1)} %get-tuple-element.11), channel_id=1, source_target_pairs={{0,1},{1,0},{2,3},{3,2},{4,5},{5,4},{6,7},{7,6},{8,9},{9,8},{10,11... | collective-permute-start | bytes 393224 | tf_op jit(solution)/shard_map/ppermute | solution.py:77
  28.4 7.0 %collective-permute-start.4 = (bf16[2,64,512]{2,1,0:T(8,128)(2,1)S(1)}, bf16[2,64,512]{2,1,0:T(8,128)(2,1)S(1)}, u32[]{:S(2)}, u32[]{:S(2)}) collective-permute-start(bf16[2,64,512]{2,1,0:T(8,128)(2,1)S(1)} %get-tuple-element.12), channel_id=1, source_target_pairs={{0,2},{1,3},{2,0},{3,1},{4,6},{5,7},{6,4},{7,5},{8,10},{9,11},{10,... | collective-permute-start | bytes 393224 | tf_op jit(solution)/shard_map/ppermute | solution.py:77
  29.1 7.1 %copy-start.2 = (f32[9,16,512]{2,1,0:T(8,128)}, f32[9,16,512]{2,1,0:T(8,128)S(1)}, u32[]{:S(2)}) copy-start(f32[9,16,512]{2,1,0:T(8,128)S(1)} %constant_dynamic-update-slice_fusion.table_ref) | copy-start | bytes 884740

commit v9 on v6

--- a/solution.py
+++ b/solution.py
@@ -115,15 +115,20 @@
         ]
         cosine_table, sine_table = inverse_tables(n_freq, NT)
         scale = 1.0 / math.sqrt(n_freq)
+        count_s = window_bounds.shape[2]
+        rows = []
+        for index, _ in pieces:
+            for table in (cosine_table, sine_table):
+                row = lax.dynamic_index_in_dim(table, index, 0, keepdims=False) * scale
+                rows.append(jnp.broadcast_to(row[:, None], (NT, count_s)))
+        rows = lax.optimization_barrier(rows)
         traces = 0.0
-        for index, piece in pieces:
-            cosine = lax.dynamic_index_in_dim(cosine_table, index, 0, keepdims=False) * scale
-            sine = lax.dynamic_index_in_dim(sine_table, index, 0, keepdims=False) * scale
+        for k, (_, piece) in enumerate(pieces):
             widened = piece.astype(jnp.float32)
             traces = (
                 traces
-                + widened[0][:, None, :] * cosine[None, :, None]
-                - widened[1][:, None, :] * sine[None, :, None]
+                + widened[0][:, None, :] * rows[2 * k][None]
+                - widened[1][:, None, :] * rows[2 * k + 1][None]
             )
         time_index = jnp.arange(NT, dtype=jnp.int32)[None, :, None]
         inside = (time_index >= window_bounds[0][:, None, :]) & (

time: 38.8 us -> 38.6 us (level)
  local copies, waits for them, and re-layouts: 0.52 us -> 1.09 us
  waiting for transfers between devices: 21.9 us -> 21.4 us
    broadcast_in_dim x0 -> x8, local copies, waits for them, and re-layouts: none -> 0.57 us  [per_device(): rows.append(jnp.broadcast_to(row[:, None], (NT, count_s)))]
    ppermute x1, waiting for transfers between devices: 10.1 us -> 9.55 us  [relay_exchange(): across = lax.ppermute(other, 'tile', [(0, 2), (2, 0), (1, 3), (3, 1)])]
  transfers between devices with their start and end apart: 6 -> 6, of which waited for: 4 -> 4; matrix products, arithmetic and copies ran while one was open for 1% -> 2% of each run, Pallas kernels for 0% -> 0%
where the time goes in v9:
time: 38.6 us; the launch traced here: 38.5 us
  waiting for transfers between devices  21.4 us (55%)
  starting transfers between devices  8.06 us (21%)
  other arithmetic  5.45 us (14%)
  matrix products  2.38 us (6%)
  local copies, waits for them, and re-layouts  1.09 us (3%)
    ppermute x1, waiting for transfers between devices, relay_exchange(): across = lax.ppermute(other, 'tile', [(0, 2), (2, 0), (1, 3), (3, 1)])  9.55 us
    ppermute x3, waiting for transfers between devices, freq_exchange(): pieces.append((f ^ d, lax.ppermute(part, 'freq', pairs)))  6.27 us
    ppermute x1, waiting for transfers between devices, relay_exchange(): passed = lax.ppermute(across, 'tile', pairs)  5.54 us
    select_n x1, other arithmetic, per_device(): return jnp.where(inside, traces, jnp.float32(0.0))  3.96 us
    ppermute x1, starting transfers between devices, relay_exchange(): partner = lax.ppermute(mine, 'tile', pairs)  3.09 us
    ppermute x1, starting transfers between devices, relay_exchange(): across = lax.ppermute(other, 'tile', [(0, 2), (2, 0), (1, 3), (3, 1)])  2.59 us
    ppermute x3, starting transfers between devices, freq_exchange(): pieces.append((f ^ d, lax.ppermute(part, 'freq', pairs)))  1.93 us
    dot_general x1, matrix products, column_products(): lax.dot_general(v_local, x_local, (((3,), (1,)), ((), ())), preferred_ele...  1.65 us
  transfers between devices with their start and end apart: 6, of which 4 were waited for; matrix products, arithmetic and copies ran while one was open for 2% of the time, Pallas kernels for 0%

profile of v9, /device:TPU:0, one launch (start us, length us, event | category | flops | bytes accessed | tf_op | source)
XLA Modules:
  0.0 38.5 jit_solution(17588947249147235481)
XLA Ops:
  0.0 0.0 copy-start
  0.0 0.9 %iota_compare_fusion.2 = pred[2,112]{1,0:T(4,128)(4,1)S(1)} fusion(s32[2]{0:T(128)} %bitcast.112), kind=kLoop, calls=%fused_computation.88 | loop fusion | flops 224 | bytes 232 | tf_op jit(solution)/shard_map/lt | solution.py:30
  0.9 0.4 copy-done
  1.2 1.7 %fusion.1 = f32[2,2,112,2,512]{4,2,3,1,0:T(8,128)S(1)} fusion(bf16[1,2,512,512]{3,2,1,0:T(8,128)(2,1)S(1)} %copy-done, bf16[1,1,2,2,112,512]{5,4,3,2,1,0:T(8,128)(2,1)} %param.6), kind=kOutput, calls=%fused_computation.5 | convolution fusion | flops 469762048 | bytes 3342336 | tf_op jit(solution)/shard_map/dot_general | solution.py:24
  2.9 0.2 fusion.13
  3.1 0.1 fusion.29
  3.1 3.1 %collective-permute-start.1 = (bf16[2,112,512]{2,1,0:T(8,128)(2,1)S(1)}, bf16[2,112,512]{2,1,0:T(8,128)(2,1)S(1)}, u32[]{:S(2)}, u32[]{:S(2)}) collective-permute-start(bf16[2,112,512]{2,1,0:T(8,128)(2,1)S(1)} %bitcast.108), channel_id=1, source_target_pairs={{0,4},{4,0},{8,12},{12,8},{1,5},{5,1},{9,13},{13,9},{2,6},{6,2},{1... | collective-permute-start | bytes 688136 | tf_op jit(solution)/shard_map/ppermute | solution.py:52
  6.2 2.6 %collective-permute-start = (bf16[2,112,512]{2,1,0:T(8,128)(2,1)S(1)}, bf16[2,112,512]{2,1,0:T(8,128)(2,1)S(1)}, u32[]{:S(2)}, u32[]{:S(2)}) collective-permute-start(bf16[2,112,512]{2,1,0:T(8,128)(2,1)S(1)} %get-tuple-element.34), channel_id=1, source_target_pairs={{0,8},{8,0},{4,12},{12,4},{1,9},{9,1},{5,13},{13,5},{2,10},{10,2},... | collective-permute-start | bytes 688136 | tf_op jit(solution)/shard_map/ppermute | solution.py:51
  8.8 0.1 fusion.38
  9.0 0.1 broadcast_in_dim.43
  9.0 0.1 broadcast_in_dim.41
  9.1 0.1 broadcast_in_dim.39
  9.2 0.1 broadcast_in_dim.37
  9.3 0.1 broadcast_in_dim.38
  9.3 0.1 broadcast_in_dim.40
  9.4 0.1 broadcast_in_dim.42
  9.5 0.1 broadcast_in_dim.44
  9.5 0.0 copy-done.1
  9.6 9.6 %collective-permute-done = bf16[2,112,512]{2,1,0:T(8,128)(2,1)S(1)} collective-permute-done((bf16[2,112,512]{2,1,0:T(8,128)(2,1)S(1)}, bf16[2,112,512]{2,1,0:T(8,128)(2,1)S(1)}, u32[]{:S(2)}, u32[]{:S(2)}) %collective-permute-start) | collective-permute-done | bytes 229408 | tf_op jit(solution)/shard_map/ppermute | solution.py:51
  19.1 0.4 %collective-permute-start.2 = (bf16[2,112,512]{2,1,0:T(8,128)(2,1)S(1)}, bf16[2,112,512]{2,1,0:T(8,128)(2,1)S(1)}, u32[]{:S(2)}, u32[]{:S(2)}) collective-permute-start(bf16[2,112,512]{2,1,0:T(8,128)(2,1)S(1)} %collective-permute-done), channel_id=1, source_target_pairs={{0,4},{4,0},{8,12},{12,8},{1,5},{5,1},{9,13},{13,9},{2,6},{6,2},{1... | collective-permute-start | bytes 688136 | tf_op jit(solution)/shard_map/ppermute | solution.py:53
  19.6 0.0 collective-permute-done.1
  19.6 5.5 %collective-permute-done.2 = bf16[2,112,512]{2,1,0:T(8,128)(2,1)S(1)} collective-permute-done((bf16[2,112,512]{2,1,0:T(8,128)(2,1)S(1)}, bf16[2,112,512]{2,1,0:T(8,128)(2,1)S(1)}, u32[]{:S(2)}, u32[]{:S(2)}) %collective-permute-start.2) | collective-permute-done | bytes 229408 | tf_op jit(solution)/shard_map/ppermute | solution.py:53
  25.2 0.7 %convolution_bitcast_fusion = f32[2,256,2,512]{3,1,2,0:T(8,128)S(1)} fusion(bf16[1,2,112,512]{3,2,0,1:T(8,128)(2,1)S(1)} %bitcast.111, bf16[1,2,112,512]{3,2,0,1:T(8,128)(2,1)S(1)} %bitcast.109, bf16[1,2,112,512]{3,2,0,1:T(8,128)(2,1)S(1)} %bitcast.110, bf16[1,2,112,512]{3,2,0,1:T(8,128)(2,1)S(1)} %get-tuple-element.33, ...), kind=kOutput, calls=%fused_computation.4 | convolution fusion | flops 475267072 | bytes 3473408 | tf_op jit(solution)/shard_map/dot_general | solution.py:37
  25.9 0.2 fusion.26
  26.1 0.1 fusion.32
  26.1 0.1 collective-permute-start.3
  26.2 1.6 %collective-permute-start.4 = (bf16[2,64,512]{2,1,0:T(8,128)(2,1)S(1)}, bf16[2,64,512]{2,1,0:T(8,128)(2,1)S(1)}, u32[]{:S(2)}, u32[]{:S(2)}) collective-permute-start(bf16[2,64,512]{2,1,0:T(8,128)(2,1)S(1)} %get-tuple-element.27), channel_id=1, source_target_pairs={{0,2},{1,3},{2,0},{3,1},{4,6},{5,7},{6,4},{7,5},{8,10},{9,11},{10,... | collective-permute-start | bytes 393224 | tf_op jit(solution)/shard_map/ppermute | solution.py:76
  27.8 0.3 collective-permute-start.5
  28.1 0.0 collective-permute-done.3
  28.2 4.4 %collective-permute-done.4 = bf16[2,64,512]{2,1,0:T(8,128)(2,1)S(1)} collective-permute-done((bf16[2,64,512]{2,1,0:T(8,128)(2,1)S(1)}, bf16[2,64,512]{2,1,0:T(8,128)(2,1)S(1)}, u32[]{:S(2)}, u32[]{:S(2)}) %collective-permute-start.4) | collective-permute-done | bytes 131104 | tf_op jit(solution)/shard_map/ppermute | solution.py:76
  32.6 1.9 %collective-permute-done.5 = bf16[2,64,512]{2,1,0:T(8,128)(2,1)S(1)} collective-permute-done((bf16[2,64,512]{2,1,0:T(8,128)(2,1)S(1)}, bf16[2,64,512]{2,1,0:T(8,128)(2,1)S(1)}, u32[]{:S(2)}, u32[]{:S(2)}) %collective-permute-start.5) | collective-permute-done | bytes 131104 | tf_op jit(solution)/shard_map/ppermute | solution.py:76
  34.5 4.0 %subtract_select_fusion = f32[64,32,512]{2,1,0:T(8,128)} fusion(f32[32,512]{1,0:T(8,128)S(1)} %broadcast_in_dim.44, f32[64,512]{1,0:T(8,128)S(1)} %get-tuple-element.44, f32[32,512]{1,0:T(8,128)S(1)} %broadcast_in_dim.43, f32[64,512]{1,0:T(8,128)S(1)} %get-tuple-element.43, f32[32,512]{1,0:T(8,128)S(1)} %broadcast_in_dim.42, ...), kind=kLoop, calls=%fused_computation | loop fusion | flops 19922944 | bytes 6029312 | tf_op jit(solution)/shard_map/jit(_where)/select_n | solution.py:137
  (14 shorter events, 0.2 us)
Async XLA Ops:
  0.0 1.2 %copy-start = (bf16[1,2,512,512]{3,2,1,0:T(8,128)(2,1)S(1)}, bf16[1,2,512,512]{3,2,1,0:T(8,128)(2,1)}, u32[]{:S(2)}) copy-start(bf16[1,2,512,512]{3,2,1,0:T(8,128)(2,1)} %param.5) | copy-start | bytes 3145732
  0.0 9.5 %copy-start.1 = (bf16[1,4,2,112,256]{4,3,2,1,0:T(8,128)(2,1)S(1)}, bf16[1,4,2,112,256]{4,3,2,1,0:T(8,128)(2,1)}, u32[]{:S(2)}) copy-start(bf16[1,4,2,112,256]{4,3,2,1,0:T(8,128)(2,1)} %param.7) | copy-start | bytes 1376260
  0.0 19.6 %copy-start.2 = (s32[2,64,512]{2,1,0:T(8,128)S(1)}, s32[2,64,512]{2,1,0:T(8,128)}, u32[]{:S(2)}) copy-start(s32[2,64,512]{2,1,0:T(8,128)} %param.9) | copy-start | bytes 786436
  3.1 16.5 %collective-permute-start.1 = (bf16[2,112,512]{2,1,0:T(8,128)(2,1)S(1)}, bf16[2,112,512]{2,1,0:T(8,128)(2,1)S(1)}, u32[]{:S(2)}, u32[]{:S(2)}) collective-permute-start(bf16[2,112,512]{2,1,0:T(8,128)(2,1)S(1)} %bitcast.108), channel_id=1, source_target_pairs={{0,4},{4,0},{8,12},{12,8},{1,5},{5,1},{9,13},{13,9},{2,6},{6,2},{1... | collective-permute-start | bytes 688136 | tf_op jit(solution)/shard_map/ppermute | solution.py:52
  6.2 12.9 %collective-permute-start = (bf16[2,112,512]{2,1,0:T(8,128)(2,1)S(1)}, bf16[2,112,512]{2,1,0:T(8,128)(2,1)S(1)}, u32[]{:S(2)}, u32[]{:S(2)}) collective-permute-start(bf16[2,112,512]{2,1,0:T(8,128)(2,1)S(1)} %get-tuple-element.34), channel_id=1, source_target_pairs={{0,8},{8,0},{4,12},{12,4},{1,9},{9,1},{5,13},{13,5},{2,10},{10,2},... | collective-permute-start | bytes 688136 | tf_op jit(solution)/shard_map/ppermute | solution.py:51
  19.1 6.0 %collective-permute-start.2 = (bf16[2,112,512]{2,1,0:T(8,128)(2,1)S(1)}, bf16[2,112,512]{2,1,0:T(8,128)(2,1)S(1)}, u32[]{:S(2)}, u32[]{:S(2)}) collective-permute-start(bf16[2,112,512]{2,1,0:T(8,128)(2,1)S(1)} %collective-permute-done), channel_id=1, source_target_pairs={{0,4},{4,0},{8,12},{12,8},{1,5},{5,1},{9,13},{13,9},{2,6},{6,2},{1... | collective-permute-start | bytes 688136 | tf_op jit(solution)/shard_map/ppermute | solution.py:53
  26.1 2.0 %collective-permute-start.3 = (bf16[2,64,512]{2,1,0:T(8,128)(2,1)S(1)}, bf16[2,64,512]{2,1,0:T(8,128)(2,1)S(1)}, u32[]{:S(2)}, u32[]{:S(2)}) collective-permute-start(bf16[2,64,512]{2,1,0:T(8,128)(2,1)S(1)} %get-tuple-element.26), channel_id=1, source_target_pairs={{0,1},{1,0},{2,3},{3,2},{4,5},{5,4},{6,7},{7,6},{8,9},{9,8},{10,11... | collective-permute-start | bytes 393224 | tf_op jit(solution)/shard_map/ppermute | solution.py:76
  26.2 6.4 %collective-permute-start.4 = (bf16[2,64,512]{2,1,0:T(8,128)(2,1)S(1)}, bf16[2,64,512]{2,1,0:T(8,128)(2,1)S(1)}, u32[]{:S(2)}, u32[]{:S(2)}) collective-permute-start(bf16[2,64,512]{2,1,0:T(8,128)(2,1)S(1)} %get-tuple-element.27), channel_id=1, source_target_pairs={{0,2},{1,3},{2,0},{3,1},{4,6},{5,7},{6,4},{7,5},{8,10},{9,11},{10,... | collective-permute-start | bytes 393224 | tf_op jit(solution)/shard_map/ppermute | solution.py:76
  27.8 6.7 %collective-permute-start.5 = (bf16[2,64,512]{2,1,0:T(8,128)(2,1)S(1)}, bf16[2,64,512]{2,1,0:T(8,128)(2,1)S(1)}, u32[]{:S(2)}, u32[]{:S(2)}) collective-permute-start(bf16[2,64,512]{2,1,0:T(8,128)(2,1)S(1)} %get-tuple-element.28), channel_id=1, source_target_pairs={{0,3},{1,2},{2,1},{3,0},{4,7},{5,6},{6,5},{7,4},{8,11},{9,10},{10,... | collective-permute-start | bytes 393224 | tf_op jit(solution)/shard_map/ppermute | solution.py:76

commit v10 on v9

--- a/solution.py
+++ b/solution.py
@@ -6,7 +6,7 @@
 from jax.sharding import PartitionSpec as P
 
 NT = 32
-S_CHUNKS = 1
+S_CHUNKS = 2
 
 
 first_bin = 2
@@ -42,11 +42,13 @@
     return jnp.stack([real_part, imag_part], axis=0).astype(jnp.bfloat16)
 
 
-def relay_exchange(own, u_local):
+def relay_exchange(own, u_local, after=None):
     t = lax.axis_index("tile")
     row = t // 2
     mine = lax.dynamic_index_in_dim(own, row, 0, keepdims=False)
     other = lax.dynamic_index_in_dim(own, 1 - row, 0, keepdims=False)
+    if after is not None:
+        mine, other, _ = lax.optimization_barrier((mine, other, after))
     pairs = [(0, 1), (1, 0), (2, 3), (3, 2)]
     across = lax.ppermute(other, "tile", [(0, 2), (2, 0), (1, 3), (3, 1)])
     partner = lax.ppermute(mine, "tile", pairs)
@@ -56,7 +58,7 @@
         [lax.dynamic_index_in_dim(u_local, j, 0, keepdims=False) for j in columns], axis=0
     )
     blocks = jnp.stack([mine, across, partner, passed], axis=0)
-    return row_spectrum(u_order, blocks)
+    return row_spectrum(u_order, blocks), across
 
 
 def gather_exchange(own, u_local, n_tile):
@@ -90,11 +92,12 @@
         chunks = S_CHUNKS if count_s % S_CHUNKS == 0 else 1
         width = count_s // chunks
         received_parts = []
+        after = None
         for c in range(chunks):
             x_part = x_local[:, :, c * width:(c + 1) * width]
             own = column_products(v_local, x_part, rank_local)
             if use_relay:
-                spectrum = relay_exchange(own, u_local)
+                spectrum, after = relay_exchange(own, u_local, after)
             else:
                 spectrum = gather_exchange(own, u_local, n_tile)
             if use_swaps:

time: 38.6 us -> 39.9 us (1.034)
  waiting for transfers between devices: 21.4 us -> 15.2 us
  starting transfers between devices: 8.06 us -> 13.4 us
  matrix products: 2.38 us -> 3.81 us
  local copies, waits for them, and re-layouts: 1.09 us -> 1.74 us
    ppermute x1 -> x2, waiting for transfers between devices: 9.55 us -> 4.56 us  [relay_exchange(): across = lax.ppermute(other, 'tile', [(0, 2), (2, 0), (1, 3), (3, 1)])]
    ppermute x1 -> x2, starting transfers between devices: 2.59 us -> 5.24 us  [relay_exchange(): across = lax.ppermute(other, 'tile', [(0, 2), (2, 0), (1, 3), (3, 1)])]
    ppermute x3 -> x6, waiting for transfers between devices: 6.27 us -> 3.66 us  [freq_exchange(): pieces.append((f ^ d, lax.ppermute(part, 'freq', pairs)))]
    ppermute x3 -> x6, starting transfers between devices: 1.93 us -> 4.21 us  [freq_exchange(): pieces.append((f ^ d, lax.ppermute(part, 'freq', pairs)))]
    ppermute x1 -> x2, waiting for transfers between devices: 5.54 us -> 6.97 us  [relay_exchange(): passed = lax.ppermute(across, 'tile', pairs)]
    dot_general x1 -> x2, matrix products: 1.65 us -> 2.88 us  [column_products(): lax.dot_general(v_local, x_local, (((3,), (1,)), ((), ())), preferred_ele...]
    unnamed x6, local copies, waits for them, and re-layouts: 0.39 us -> 1.02 us
    ppermute x1 -> x2, starting transfers between devices: 0.45 us -> 0.89 us  [relay_exchange(): passed = lax.ppermute(across, 'tile', pairs)]
  transfers between devices with their start and end apart: 6 -> 12, of which waited for: 4 -> 5; matrix products, arithmetic and copies ran while one was open for 2% -> 5% of each run, Pallas kernels for 0% -> 0%
where the time goes in v10:
time: 39.9 us; the launch traced here: 39.7 us
  waiting for transfers between devices  15.2 us (38%)
  starting transfers between devices  13.4 us (34%)
  other arithmetic  5.28 us (13%)
  matrix products  3.81 us (10%)
  local copies, waits for them, and re-layouts  1.74 us (4%)
    ppermute x2, waiting for transfers between devices, relay_exchange(): passed = lax.ppermute(across, 'tile', pairs)  6.97 us
    ppermute x2, starting transfers between devices, relay_exchange(): across = lax.ppermute(other, 'tile', [(0, 2), (2, 0), (1, 3), (3, 1)])  5.24 us
    ppermute x2, waiting for transfers between devices, relay_exchange(): across = lax.ppermute(other, 'tile', [(0, 2), (2, 0), (1, 3), (3, 1)])  4.56 us
    ppermute x6, starting transfers between devices, freq_exchange(): pieces.append((f ^ d, lax.ppermute(part, 'freq', pairs)))  4.21 us
    select_n x1, other arithmetic, per_device(): return jnp.where(inside, traces, jnp.float32(0.0))  3.96 us
    ppermute x6, waiting for transfers between devices, freq_exchange(): pieces.append((f ^ d, lax.ppermute(part, 'freq', pairs)))  3.66 us
    ppermute x2, starting transfers between devices, relay_exchange(): partner = lax.ppermute(mine, 'tile', pairs)  3.09 us
    dot_general x2, matrix products, column_products(): lax.dot_general(v_local, x_local, (((3,), (1,)), ((), ())), preferred_ele...  2.88 us
  transfers between devices with their start and end apart: 12, of which 5 were waited for; matrix products, arithmetic and copies ran while one was open for 5% of the time, Pallas kernels for 0%

profile of v10, /device:TPU:0, one launch (start us, length us, event | category | flops | bytes accessed | tf_op | source)
XLA Modules:
  0.0 39.7 jit_solution(12940330208639852103)
XLA Ops:
  0.0 1.0 %copy-done = bf16[1,1,2,2,112,512]{5,4,3,2,1,0:T(8,128)(2,1)S(1)} copy-done((bf16[1,1,2,2,112,512]{5,4,3,2,1,0:T(8,128)(2,1)S(1)}, bf16[1,1,2,2,112,512]{5,4,3,2,1,0:T(8,128)(2,1)}, u32[]{:S(2)}) %copy-start) | copy-done | bytes 458776
  1.0 1.4 %fusion.1 = f32[2,2,112,2,256]{4,2,0,3,1:T(8,128)S(1)} fusion(bf16[2,512,512]{2,1,0:T(8,128)(2,1)} %bitcast.150, bf16[1,1,2,2,112,512]{5,4,3,2,1,0:T(8,128)(2,1)S(1)} %copy-done), kind=kOutput, calls=%fused_computation.7 | convolution fusion | flops 234881024 | bytes 1900544 | tf_op jit(solution)/shard_map/dot_general | solution.py:24
  2.5 1.4 %fusion.2 = f32[2,2,112,2,256]{4,2,3,1,0:T(8,128)S(1)} fusion(bf16[2,512,512]{2,1,0:T(8,128)(2,1)} %bitcast.151, bf16[1,1,2,2,112,512]{5,4,3,2,1,0:T(8,128)(2,1)S(1)} %copy-done), kind=kOutput, calls=%fused_computation.9 | convolution fusion | flops 234881024 | bytes 1900544 | tf_op jit(solution)/shard_map/dot_general | solution.py:24
  3.9 0.7 %iota_compare_fusion.2 = pred[2,112]{1,0:T(4,128)(4,1)S(1)} fusion(s32[2]{0:T(128)} %bitcast.160), kind=kLoop, calls=%fused_computation.130 | loop fusion | flops 224 | bytes 232 | tf_op jit(solution)/shard_map/lt | solution.py:30
  4.6 0.2 fusion.29
  4.9 3.1 %collective-permute-start.1 = (bf16[2,112,256]{2,1,0:T(8,128)(2,1)S(1)}, bf16[2,112,256]{2,1,0:T(8,128)(2,1)S(1)}, u32[]{:S(2)}, u32[]{:S(2)}) collective-permute-start(bf16[2,112,256]{2,1,0:T(8,128)(2,1)S(1)} %bitcast.152), channel_id=1, source_target_pairs={{0,4},{4,0},{8,12},{12,8},{1,5},{5,1},{9,13},{13,9},{2,6},{6,2},{1... | collective-permute-start | bytes 344072 | tf_op jit(solution)/shard_map/ppermute | solution.py:54
  7.9 2.6 %collective-permute-start = (bf16[2,112,256]{2,1,0:T(8,128)(2,1)S(1)}, bf16[2,112,256]{2,1,0:T(8,128)(2,1)S(1)}, u32[]{:S(2)}, u32[]{:S(2)}) collective-permute-start(bf16[2,112,256]{2,1,0:T(8,128)(2,1)S(1)} %get-tuple-element.56), channel_id=1, source_target_pairs={{0,8},{8,0},{4,12},{12,4},{1,9},{9,1},{5,13},{13,5},{2,10},{10,2},... | collective-permute-start | bytes 344072 | tf_op jit(solution)/shard_map/ppermute | solution.py:53
  10.5 0.1 fusion.56
  10.7 0.1 broadcast_in_dim.51
  10.8 0.1 broadcast_in_dim.49
  10.8 0.1 broadcast_in_dim.47
  10.9 0.1 broadcast_in_dim.45
  11.1 0.1 broadcast_in_dim.48
  11.1 0.1 broadcast_in_dim.50
  11.2 0.1 broadcast_in_dim.52
  11.4 4.6 %collective-permute-done = bf16[2,112,256]{2,1,0:T(8,128)(2,1)S(1)} collective-permute-done((bf16[2,112,256]{2,1,0:T(8,128)(2,1)S(1)}, bf16[2,112,256]{2,1,0:T(8,128)(2,1)S(1)}, u32[]{:S(2)}, u32[]{:S(2)}) %collective-permute-start) | collective-permute-done | bytes 114720 | tf_op jit(solution)/shard_map/ppermute | solution.py:53
  16.0 0.4 %collective-permute-start.2 = (bf16[2,112,256]{2,1,0:T(8,128)(2,1)S(1)}, bf16[2,112,256]{2,1,0:T(8,128)(2,1)S(1)}, u32[]{:S(2)}, u32[]{:S(2)}) collective-permute-start(bf16[2,112,256]{2,1,0:T(8,128)(2,1)S(1)} %collective-permute-done), channel_id=1, source_target_pairs={{0,4},{4,0},{8,12},{12,8},{1,5},{5,1},{9,13},{13,9},{2,6},{6,2},{1... | collective-permute-start | bytes 344072 | tf_op jit(solution)/shard_map/ppermute | solution.py:55
  16.4 2.7 %collective-permute-start.3 = (bf16[2,112,256]{2,1,0:T(8,128)(2,1)S(1)}, bf16[2,112,256]{2,1,0:T(8,128)(2,1)S(1)}, u32[]{:S(2)}, u32[]{:S(2)}) collective-permute-start(bf16[2,112,256]{2,1,0:T(8,128)(2,1)S(1)} %get-tuple-element.16), channel_id=1, source_target_pairs={{0,8},{8,0},{4,12},{12,4},{1,9},{9,1},{5,13},{13,5},{2,10},{10,2},... | collective-permute-start | bytes 344072 | tf_op jit(solution)/shard_map/ppermute | solution.py:53
  19.1 4.5 %collective-permute-done.2 = bf16[2,112,256]{2,1,0:T(8,128)(2,1)S(1)} collective-permute-done((bf16[2,112,256]{2,1,0:T(8,128)(2,1)S(1)}, bf16[2,112,256]{2,1,0:T(8,128)(2,1)S(1)}, u32[]{:S(2)}, u32[]{:S(2)}) %collective-permute-start.2) | collective-permute-done | bytes 114720 | tf_op jit(solution)/shard_map/ppermute | solution.py:55
  23.6 0.5 %convolution_bitcast_fusion.1 = f32[2,256,2,256]{3,1,2,0:T(8,128)S(1)} fusion(bf16[1,2,112,256]{3,2,0,1:T(8,128)(2,1)S(1)} %bitcast.159, bf16[1,2,112,256]{3,2,0,1:T(8,128)(2,1)S(1)} %bitcast.154, bf16[1,2,112,256]{3,2,0,1:T(8,128)(2,1)S(1)} %bitcast.155, bf16[1,2,112,256]{3,2,0,1:T(8,128)(2,1)S(1)} %get-tuple-element.55, ...), kind=kOutput, calls=%fused_computation.5 | convolution fusion | flops 238551040 | bytes 1966080 | tf_op jit(solution)/shard_map/dot_general | solution.py:37
  24.2 0.4 %collective-permute-start.5 = (bf16[2,112,256]{2,1,0:T(8,128)(2,1)S(1)}, bf16[2,112,256]{2,1,0:T(8,128)(2,1)S(1)}, u32[]{:S(2)}, u32[]{:S(2)}) collective-permute-start(bf16[2,112,256]{2,1,0:T(8,128)(2,1)S(1)} %collective-permute-done.3), channel_id=1, source_target_pairs={{0,4},{4,0},{8,12},{12,8},{1,5},{5,1},{9,13},{13,9},{2,6},{6,2},{1... | collective-permute-start | bytes 344072 | tf_op jit(solution)/shard_map/ppermute | solution.py:55
  24.6 0.1 collective-permute-start.6
  24.7 1.6 %collective-permute-start.8 = (bf16[2,64,256]{2,1,0:T(8,128)(2,1)S(1)}, bf16[2,64,256]{2,1,0:T(8,128)(2,1)S(1)}, u32[]{:S(2)}, u32[]{:S(2)}) collective-permute-start(bf16[2,64,256]{2,1,0:T(8,128)(2,1)S(1)} %get-tuple-element.43), channel_id=1, source_target_pairs={{0,2},{1,3},{2,0},{3,1},{4,6},{5,7},{6,4},{7,5},{8,10},{9,11},{10,... | collective-permute-start | bytes 196616 | tf_op jit(solution)/shard_map/ppermute | solution.py:78
  26.3 0.3 collective-permute-start.10
  26.6 2.4 %collective-permute-done.5 = bf16[2,112,256]{2,1,0:T(8,128)(2,1)S(1)} collective-permute-done((bf16[2,112,256]{2,1,0:T(8,128)(2,1)S(1)}, bf16[2,112,256]{2,1,0:T(8,128)(2,1)S(1)}, u32[]{:S(2)}, u32[]{:S(2)}) %collective-permute-start.5) | collective-permute-done | bytes 114720 | tf_op jit(solution)/shard_map/ppermute | solution.py:55
  29.0 0.5 %convolution_bitcast_fusion = f32[2,256,2,256]{3,1,2,0:T(8,128)S(1)} fusion(bf16[1,2,112,256]{3,2,0,1:T(8,128)(2,1)S(1)} %bitcast.158, bf16[1,2,112,256]{3,2,0,1:T(8,128)(2,1)S(1)} %bitcast.157, bf16[1,2,112,256]{3,2,0,1:T(8,128)(2,1)S(1)} %bitcast.156, bf16[1,2,112,256]{3,2,0,1:T(8,128)(2,1)S(1)} %bitcast.153, ...), kind=kOutput, calls=%fused_computation.4 | convolution fusion | flops 238551040 | bytes 1966080 | tf_op jit(solution)/shard_map/dot_general | solution.py:37
  29.6 0.1 collective-permute-start.7
  29.7 1.6 %collective-permute-start.11 = (bf16[2,64,256]{2,1,0:T(8,128)(2,1)S(1)}, bf16[2,64,256]{2,1,0:T(8,128)(2,1)S(1)}, u32[]{:S(2)}, u32[]{:S(2)}) collective-permute-start(bf16[2,64,256]{2,1,0:T(8,128)(2,1)S(1)} %get-tuple-element.48), channel_id=1, source_target_pairs={{0,3},{1,2},{2,1},{3,0},{4,7},{5,6},{6,5},{7,4},{8,11},{9,10},{10,... | collective-permute-start | bytes 196616 | tf_op jit(solution)/shard_map/ppermute | solution.py:78
  31.3 0.6 %collective-permute-start.9 = (bf16[2,64,256]{2,1,0:T(8,128)(2,1)S(1)}, bf16[2,64,256]{2,1,0:T(8,128)(2,1)S(1)}, u32[]{:S(2)}, u32[]{:S(2)}) collective-permute-start(bf16[2,64,256]{2,1,0:T(8,128)(2,1)S(1)} %get-tuple-element.47), channel_id=1, source_target_pairs={{0,2},{1,3},{2,0},{3,1},{4,6},{5,7},{6,4},{7,5},{8,10},{9,11},{10,... | collective-permute-start | bytes 196616 | tf_op jit(solution)/shard_map/ppermute | solution.py:78
  31.9 1.7 %collective-permute-done.11 = bf16[2,64,256]{2,1,0:T(8,128)(2,1)S(1)} collective-permute-done((bf16[2,64,256]{2,1,0:T(8,128)(2,1)S(1)}, bf16[2,64,256]{2,1,0:T(8,128)(2,1)S(1)}, u32[]{:S(2)}, u32[]{:S(2)}) %collective-permute-start.11) | collective-permute-done | bytes 65568 | tf_op jit(solution)/shard_map/ppermute | solution.py:78
  33.7 1.9 %collective-permute-done.9 = bf16[2,64,256]{2,1,0:T(8,128)(2,1)S(1)} collective-permute-done((bf16[2,64,256]{2,1,0:T(8,128)(2,1)S(1)}, bf16[2,64,256]{2,1,0:T(8,128)(2,1)S(1)}, u32[]{:S(2)}, u32[]{:S(2)}) %collective-permute-start.9) | collective-permute-done | bytes 65568 | tf_op jit(solution)/shard_map/ppermute | solution.py:78
  35.8 4.0 %subtract_select_fusion = f32[64,32,512]{2,1,0:T(8,128)} fusion(f32[32,512]{1,0:T(8,128)S(1)} %broadcast_in_dim.52, f32[64,512]{1,0:T(8,128)S(1)} %get-tuple-element.54, f32[32,512]{1,0:T(8,128)S(1)} %broadcast_in_dim.51, f32[64,512]{1,0:T(8,128)S(1)} %get-tuple-element.53, f32[32,512]{1,0:T(8,128)S(1)} %broadcast_in_dim.50, ...), kind=kLoop, calls=%fused_computation | loop fusion | flops 19922944 | bytes 6029312 | tf_op jit(solution)/shard_map/jit(_where)/select_n | solution.py:140
  (32 shorter events, 0.6 us)
Async XLA Ops:
  0.0 1.0 %copy-start = (bf16[1,1,2,2,112,512]{5,4,3,2,1,0:T(8,128)(2,1)S(1)}, bf16[1,1,2,2,112,512]{5,4,3,2,1,0:T(8,128)(2,1)}, u32[]{:S(2)}) copy-start(bf16[1,1,2,2,112,512]{5,4,3,2,1,0:T(8,128)(2,1)} %param.6) | copy-start | bytes 1376260
  0.0 11.3 %copy-start.2 = (s32[2,64,512]{2,1,0:T(8,128)S(1)}, s32[2,64,512]{2,1,0:T(8,128)}, u32[]{:S(2)}) copy-start(s32[2,64,512]{2,1,0:T(8,128)} %param.9) | copy-start | bytes 786436
  0.0 11.3 %copy-start.1 = (bf16[1,4,2,112,256]{4,3,2,1,0:T(8,128)(2,1)S(1)}, bf16[1,4,2,112,256]{4,3,2,1,0:T(8,128)(2,1)}, u32[]{:S(2)}) copy-start(bf16[1,4,2,112,256]{4,3,2,1,0:T(8,128)(2,1)} %param.7) | copy-start | bytes 1376260
  4.9 14.2 %collective-permute-start.1 = (bf16[2,112,256]{2,1,0:T(8,128)(2,1)S(1)}, bf16[2,112,256]{2,1,0:T(8,128)(2,1)S(1)}, u32[]{:S(2)}, u32[]{:S(2)}) collective-permute-start(bf16[2,112,256]{2,1,0:T(8,128)(2,1)S(1)} %bitcast.152), channel_id=1, source_target_pairs={{0,4},{4,0},{8,12},{12,8},{1,5},{5,1},{9,13},{13,9},{2,6},{6,2},{1... | collective-permute-start | bytes 344072 | tf_op jit(solution)/shard_map/ppermute | solution.py:54
  7.9 8.0 %collective-permute-start = (bf16[2,112,256]{2,1,0:T(8,128)(2,1)S(1)}, bf16[2,112,256]{2,1,0:T(8,128)(2,1)S(1)}, u32[]{:S(2)}, u32[]{:S(2)}) collective-permute-start(bf16[2,112,256]{2,1,0:T(8,128)(2,1)S(1)} %get-tuple-element.56), channel_id=1, source_target_pairs={{0,8},{8,0},{4,12},{12,4},{1,9},{9,1},{5,13},{13,5},{2,10},{10,2},... | collective-permute-start | bytes 344072 | tf_op jit(solution)/shard_map/ppermute | solution.py:53
  16.0 7.7 %collective-permute-start.2 = (bf16[2,112,256]{2,1,0:T(8,128)(2,1)S(1)}, bf16[2,112,256]{2,1,0:T(8,128)(2,1)S(1)}, u32[]{:S(2)}, u32[]{:S(2)}) collective-permute-start(bf16[2,112,256]{2,1,0:T(8,128)(2,1)S(1)} %collective-permute-done), channel_id=1, source_target_pairs={{0,4},{4,0},{8,12},{12,8},{1,5},{5,1},{9,13},{13,9},{2,6},{6,2},{1... | collective-permute-start | bytes 344072 | tf_op jit(solution)/shard_map/ppermute | solution.py:55
  16.4 7.7 %collective-permute-start.3 = (bf16[2,112,256]{2,1,0:T(8,128)(2,1)S(1)}, bf16[2,112,256]{2,1,0:T(8,128)(2,1)S(1)}, u32[]{:S(2)}, u32[]{:S(2)}) collective-permute-start(bf16[2,112,256]{2,1,0:T(8,128)(2,1)S(1)} %get-tuple-element.16), channel_id=1, source_target_pairs={{0,8},{8,0},{4,12},{12,4},{1,9},{9,1},{5,13},{13,5},{2,10},{10,2},... | collective-permute-start | bytes 344072 | tf_op jit(solution)/shard_map/ppermute | solution.py:53
  19.1 7.5 %collective-permute-start.4 = (bf16[2,112,256]{2,1,0:T(8,128)(2,1)S(1)}, bf16[2,112,256]{2,1,0:T(8,128)(2,1)S(1)}, u32[]{:S(2)}, u32[]{:S(2)}) collective-permute-start(bf16[2,112,256]{2,1,0:T(8,128)(2,1)S(1)} %get-tuple-element.15), channel_id=1, source_target_pairs={{0,4},{4,0},{8,12},{12,8},{1,5},{5,1},{9,13},{13,9},{2,6},{6,2},{1... | collective-permute-start | bytes 344072 | tf_op jit(solution)/shard_map/ppermute | solution.py:54
  24.2 4.9 %collective-permute-start.5 = (bf16[2,112,256]{2,1,0:T(8,128)(2,1)S(1)}, bf16[2,112,256]{2,1,0:T(8,128)(2,1)S(1)}, u32[]{:S(2)}, u32[]{:S(2)}) collective-permute-start(bf16[2,112,256]{2,1,0:T(8,128)(2,1)S(1)} %collective-permute-done.3), channel_id=1, source_target_pairs={{0,4},{4,0},{8,12},{12,8},{1,5},{5,1},{9,13},{13,9},{2,6},{6,2},{1... | collective-permute-start | bytes 344072 | tf_op jit(solution)/shard_map/ppermute | solution.py:55
  24.6 11.1 %collective-permute-start.6 = (bf16[2,64,256]{2,1,0:T(8,128)(2,1)S(1)}, bf16[2,64,256]{2,1,0:T(8,128)(2,1)S(1)}, u32[]{:S(2)}, u32[]{:S(2)}) collective-permute-start(bf16[2,64,256]{2,1,0:T(8,128)(2,1)S(1)} %get-tuple-element.42), channel_id=1, source_target_pairs={{0,1},{1,0},{2,3},{3,2},{4,5},{5,4},{6,7},{7,6},{8,9},{9,8},{10,11... | collective-permute-start | bytes 196616 | tf_op jit(solution)/shard_map/ppermute | solution.py:78
  24.7 9.0 %collective-permute-start.8 = (bf16[2,64,256]{2,1,0:T(8,128)(2,1)S(1)}, bf16[2,64,256]{2,1,0:T(8,128)(2,1)S(1)}, u32[]{:S(2)}, u32[]{:S(2)}) collective-permute-start(bf16[2,64,256]{2,1,0:T(8,128)(2,1)S(1)} %get-tuple-element.43), channel_id=1, source_target_pairs={{0,2},{1,3},{2,0},{3,1},{4,6},{5,7},{6,4},{7,5},{8,10},{9,11},{10,... | collective-permute-start | bytes 196616 | tf_op jit(solution)/shard_map/ppermute | solution.py:78
  26.3 5.1 %collective-permute-start.10 = (bf16[2,64,256]{2,1,0:T(8,128)(2,1)S(1)}, bf16[2,64,256]{2,1,0:T(8,128)(2,1)S(1)}, u32[]{:S(2)}, u32[]{:S(2)}) collective-permute-start(bf16[2,64,256]{2,1,0:T(8,128)(2,1)S(1)} %get-tuple-element.44), channel_id=1, source_target_pairs={{0,3},{1,2},{2,1},{3,0},{4,7},{5,6},{6,5},{7,4},{8,11},{9,10},{10,... | collective-permute-start | bytes 196616 | tf_op jit(solution)/shard_map/ppermute | solution.py:78
  29.6 6.1 %collective-permute-start.7 = (bf16[2,64,256]{2,1,0:T(8,128)(2,1)S(1)}, bf16[2,64,256]{2,1,0:T(8,128)(2,1)S(1)}, u32[]{:S(2)}, u32[]{:S(2)}) collective-permute-start(bf16[2,64,256]{2,1,0:T(8,128)(2,1)S(1)} %get-tuple-element.46), channel_id=1, source_target_pairs={{0,1},{1,0},{2,3},{3,2},{4,5},{5,4},{6,7},{7,6},{8,9},{9,8},{10,11... | collective-permute-start | bytes 196616 | tf_op jit(solution)/shard_map/ppermute | solution.py:78
  29.7 4.0 %collective-permute-start.11 = (bf16[2,64,256]{2,1,0:T(8,128)(2,1)S(1)}, bf16[2,64,256]{2,1,0:T(8,128)(2,1)S(1)}, u32[]{:S(2)}, u32[]{:S(2)}) collective-permute-start(bf16[2,64,256]{2,1,0:T(8,128)(2,1)S(1)} %get-tuple-element.48), channel_id=1, source_target_pairs={{0,3},{1,2},{2,1},{3,0},{4,7},{5,6},{6,5},{7,4},{8,11},{9,10},{10,... | collective-permute-start | bytes 196616 | tf_op jit(solution)/shard_map/ppermute | solution.py:78
  31.3 4.3 %collective-permute-start.9 = (bf16[2,64,256]{2,1,0:T(8,128)(2,1)S(1)}, bf16[2,64,256]{2,1,0:T(8,128)(2,1)S(1)}, u32[]{:S(2)}, u32[]{:S(2)}) collective-permute-start(bf16[2,64,256]{2,1,0:T(8,128)(2,1)S(1)} %get-tuple-element.47), channel_id=1, source_target_pairs={{0,2},{1,3},{2,0},{3,1},{4,6},{5,7},{6,4},{7,5},{8,10},{9,11},{10,... | collective-permute-start | bytes 196616 | tf_op jit(solution)/shard_map/ppermute | solution.py:78

commit v11 on v9

--- a/solution.py
+++ b/solution.py
@@ -42,21 +42,37 @@
     return jnp.stack([real_part, imag_part], axis=0).astype(jnp.bfloat16)
 
 
-def relay_exchange(own, u_local):
+def row_products(u_part, blocks):
+    return lax.dot_general(
+        u_part, blocks, (((0, 2), (0, 2)), ((), ())), preferred_element_type=jnp.float32
+    )
+
+
+def finish_spectrum(products):
+    real_part = products[0, :, 0] - products[1, :, 1]
+    imag_part = products[0, :, 1] + products[1, :, 0]
+    return jnp.stack([real_part, imag_part], axis=0).astype(jnp.bfloat16)
+
+
+def relay_exchange(v_local, x_local, rank_local, u_local):
     t = lax.axis_index("tile")
     row = t // 2
-    mine = lax.dynamic_index_in_dim(own, row, 0, keepdims=False)
-    other = lax.dynamic_index_in_dim(own, 1 - row, 0, keepdims=False)
+
+    def block_of(r):
+        v_row = lax.dynamic_index_in_dim(v_local, r, 0, keepdims=True)
+        rank_row = lax.dynamic_index_in_dim(rank_local, r, 0, keepdims=True)
+        return column_products(v_row, x_local, rank_row)[0]
+
     pairs = [(0, 1), (1, 0), (2, 3), (3, 2)]
-    across = lax.ppermute(other, "tile", [(0, 2), (2, 0), (1, 3), (3, 1)])
+    across = lax.ppermute(block_of(1 - row), "tile", [(0, 2), (2, 0), (1, 3), (3, 1)])
+    mine = block_of(row)
     partner = lax.ppermute(mine, "tile", pairs)
     passed = lax.ppermute(across, "tile", pairs)
     columns = (t, t ^ 2, t ^ 1, t ^ 3)
-    u_order = jnp.stack(
-        [lax.dynamic_index_in_dim(u_local, j, 0, keepdims=False) for j in columns], axis=0
-    )
-    blocks = jnp.stack([mine, across, partner, passed], axis=0)
-    return row_spectrum(u_order, blocks)
+    u_order = [lax.dynamic_index_in_dim(u_local, j, 0, keepdims=False) for j in columns]
+    early = row_products(jnp.stack(u_order[:3], axis=0), jnp.stack([mine, across, partner], axis=0))
+    late = row_products(u_order[3][None], passed[None])
+    return finish_spectrum(early + late)
 
 
 def gather_exchange(own, u_local, n_tile):
@@ -92,10 +108,10 @@
         received_parts = []
         for c in range(chunks):
             x_part = x_local[:, :, c * width:(c + 1) * width]
-            own = column_products(v_local, x_part, rank_local)
             if use_relay:
-                spectrum = relay_exchange(own, u_local)
+                spectrum = relay_exchange(v_local, x_part, rank_local, u_local)
             else:
+                own = column_products(v_local, x_part, rank_local)
                 spectrum = gather_exchange(own, u_local, n_tile)
             if use_swaps:
                 received_parts.append(freq_exchange(spectrum, n_freq))

time: 38.6 us -> 41.3 us (1.070)
  matrix products: 2.38 us -> 3.91 us
  local copies, waits for them, and re-layouts: 1.09 us -> 2.07 us
  other arithmetic: 5.45 us -> 5.92 us
    dynamic_slice x0 -> x1, local copies, waits for them, and re-layouts: none -> 1.37 us  [block_of(): rank_row = lax.dynamic_index_in_dim(rank_local, r, 0, keepdims=True)]
    dot_general x1 -> x2, matrix products: 1.65 us -> 2.73 us  [column_products(): lax.dot_general(v_local, x_local, (((3,), (1,)), ((), ())), preferred_ele...]
    dot_general x1 -> x2, matrix products: 0.72 us -> 1.18 us  [row_products(): lax.dot_general(u_part, blocks, (((0, 2), (0, 2)), ((), ())), preferred_e...]
    ppermute x1, starting transfers between devices: 0.45 us -> 0.01 us  [relay_exchange(): passed = lax.ppermute(across, 'tile', pairs)]
    lt x1 -> x2, other arithmetic: 0.86 us -> 1.28 us  [column_products(): live_slots = slot_index[None, :, None] < rank_local[:, None, None]]
  transfers between devices with their start and end apart: 6 -> 6, of which waited for: 4 -> 4; matrix products, arithmetic and copies ran while one was open for 2% -> 9% of each run, Pallas kernels for 0% -> 0%
where the time goes in v11:
time: 41.3 us; the launch traced here: 41.1 us
  waiting for transfers between devices  21.3 us (52%)
  starting transfers between devices  7.68 us (19%)
  other arithmetic  5.92 us (14%)
  matrix products  3.91 us (9%)
  local copies, waits for them, and re-layouts  2.07 us (5%)
    ppermute x1, waiting for transfers between devices, relay_exchange(): lax.ppermute(block_of(1 - row), 'tile', [(0, 2), (2, 0), (1, 3), (3, 1)])  9.57 us
    ppermute x3, waiting for transfers between devices, freq_exchange(): pieces.append((f ^ d, lax.ppermute(part, 'freq', pairs)))  6.27 us
    ppermute x1, waiting for transfers between devices, relay_exchange(): passed = lax.ppermute(across, 'tile', pairs)  5.43 us
    select_n x1, other arithmetic, per_device(): return jnp.where(inside, traces, jnp.float32(0.0))  3.96 us
    ppermute x1, starting transfers between devices, relay_exchange(): partner = lax.ppermute(mine, 'tile', pairs)  3.09 us
    dot_general x2, matrix products, column_products(): lax.dot_general(v_local, x_local, (((3,), (1,)), ((), ())), preferred_ele...  2.73 us
    ppermute x1, starting transfers between devices, relay_exchange(): lax.ppermute(block_of(1 - row), 'tile', [(0, 2), (2, 0), (1, 3), (3, 1)])  2.66 us
    ppermute x3, starting transfers between devices, freq_exchange(): pieces.append((f ^ d, lax.ppermute(part, 'freq', pairs)))  1.93 us
  transfers between devices with their start and end apart: 6, of which 4 were waited for; matrix products, arithmetic and copies ran while one was open for 9% of the time, Pallas kernels for 0%

profile of v11, /device:TPU:0, one launch (start us, length us, event | category | flops | bytes accessed | tf_op | source)
XLA Modules:
  0.0 41.1 jit_solution(6830844413011859866)
XLA Ops:
  0.0 1.4 %constant_dynamic-slice_fusion.8 = (s32[1,1,1]{1,2,0:T(1,128)}, s32[1,1,1]{1,2,0:T(1,128)}) fusion(s32[1,2,1]{1,2,0:T(1,128)} %param.8, s32[]{:T(128)S(6)} %select_n.137, s32[]{:T(128)S(6)} %select_n.134), kind=kLoop, calls=%fused_computation.85 | loop fusion | bytes 24 | tf_op jit(solution)/shard_map/jit(dynamic_index_in_dim)/dynamic_slice | solution.py:63
  1.4 0.6 %iota_compare_fusion.3 = pred[112]{0:T(512)(128)(4,1)S(1)} fusion(s32[]{:T(128)} %bitcast.7), kind=kLoop, calls=%fused_computation.114 | loop fusion | flops 112 | bytes 116 | tf_op jit(solution)/shard_map/lt | solution.py:30
  2.0 0.0 copy-start.1
  2.0 1.4 %convolution_bitcast_fusion.1 = f32[1,2,112,2,512]{4,2,3,1,0:T(8,128)S(1)} fusion(bf16[1,2,512,512]{3,2,1,0:T(8,128)(2,1)S(1)} %copy-done, bf16[1,1,2,2,112,512]{5,4,3,2,1,0:T(8,128)(2,1)} %param.6, s32[]{:T(128)S(6)} %select_n.134), kind=kOutput, calls=%fused_computation.6 | convolution fusion | flops 234881024 | bytes 2195460 | tf_op jit(solution)/shard_map/dot_general | solution.py:24
  3.4 0.1 fusion.25
  3.6 3.1 %collective-permute-start.1 = (bf16[2,112,512]{2,1,0:T(8,128)(2,1)S(1)}, bf16[2,112,512]{2,1,0:T(8,128)(2,1)S(1)}, u32[]{:S(2)}, u32[]{:S(2)}) collective-permute-start(bf16[2,112,512]{2,1,0:T(8,128)(2,1)S(1)} %maximum_bitcast_fusion.2), channel_id=1, source_target_pairs={{0,4},{4,0},{8,12},{12,8},{1,5},{5,1},{9,13},{13,9},{2,6},{6,2},{1... | collective-permute-start | bytes 688136 | tf_op jit(solution)/shard_map/ppermute | solution.py:69
  6.7 1.3 %convolution_bitcast_fusion = f32[1,2,112,2,512]{4,2,3,1,0:T(8,128)S(1)} fusion(bf16[1,2,512,512]{3,2,1,0:T(8,128)(2,1)S(1)} %copy-done, bf16[1,1,2,2,112,512]{5,4,3,2,1,0:T(8,128)(2,1)} %param.6, s32[]{:T(128)S(6)} %select_n.137), kind=kOutput, calls=%fused_computation.5 | convolution fusion | flops 234881024 | bytes 2195460 | tf_op jit(solution)/shard_map/dot_general | solution.py:24
  8.0 0.7 %iota_compare_fusion.2 = pred[112]{0:T(512)(128)(4,1)S(1)} fusion(s32[]{:T(128)} %bitcast.16), kind=kLoop, calls=%fused_computation.113 | loop fusion | flops 112 | bytes 116 | tf_op jit(solution)/shard_map/lt | solution.py:30
  8.7 0.1 fusion.19
  8.8 2.7 %collective-permute-start = (bf16[2,112,512]{2,1,0:T(8,128)(2,1)S(1)}, bf16[2,112,512]{2,1,0:T(8,128)(2,1)S(1)}, u32[]{:S(2)}, u32[]{:S(2)}) collective-permute-start(bf16[2,112,512]{2,1,0:T(8,128)(2,1)S(1)} %maximum_bitcast_fusion.3), channel_id=1, source_target_pairs={{0,8},{8,0},{4,12},{12,4},{1,9},{9,1},{5,13},{13,5},{2,10},{10,2},... | collective-permute-start | bytes 688136 | tf_op jit(solution)/shard_map/ppermute | solution.py:67
  11.5 0.1 fusion.44
  11.6 0.1 broadcast_in_dim.54
  11.7 0.1 broadcast_in_dim.52
  11.8 0.1 broadcast_in_dim.50
  11.9 0.1 broadcast_in_dim.48
  11.9 0.1 broadcast_in_dim.49
  12.0 0.1 broadcast_in_dim.51
  12.1 0.1 broadcast_in_dim.53
  12.1 0.1 broadcast_in_dim.55
  12.2 9.6 %collective-permute-done = bf16[2,112,512]{2,1,0:T(8,128)(2,1)S(1)} collective-permute-done((bf16[2,112,512]{2,1,0:T(8,128)(2,1)S(1)}, bf16[2,112,512]{2,1,0:T(8,128)(2,1)S(1)}, u32[]{:S(2)}, u32[]{:S(2)}) %collective-permute-start) | collective-permute-done | bytes 229408 | tf_op jit(solution)/shard_map/ppermute | solution.py:67
  21.8 0.0 collective-permute-start.2
  21.8 0.7 %fusion.3 = f32[2,256,2,512,1]{3,1,4,2,0:T(8,128)S(1)} fusion(bf16[1,2,112,256]{3,2,0,1:T(8,128)(2,1)S(1)} %get-tuple-element.33, bf16[1,2,112,256]{3,2,0,1:T(8,128)(2,1)S(1)} %get-tuple-element.32, bf16[1,2,112,256]{3,2,0,1:T(8,128)(2,1)S(1)} %get-tuple-element.31, bf16[1,2,112,512]{3,2,1,0:T(8,128)(2,1)S(1)} %bitcast.123, ...), kind=kOutput, calls=%fused_computation.18 | convolution fusion | flops 354385920 | bytes 3129344 | tf_op jit(solution)/shard_map/dot_general | solution.py:46
  22.6 5.4 %collective-permute-done.2 = bf16[2,112,512]{2,1,0:T(8,128)(2,1)S(1)} collective-permute-done((bf16[2,112,512]{2,1,0:T(8,128)(2,1)S(1)}, bf16[2,112,512]{2,1,0:T(8,128)(2,1)S(1)}, u32[]{:S(2)}, u32[]{:S(2)}) %collective-permute-start.2) | collective-permute-done | bytes 229408 | tf_op jit(solution)/shard_map/ppermute | solution.py:70
  28.0 0.5 %bitcast_add_fusion = f32[2,256,2,512]{3,1,2,0:T(8,128)S(1)} fusion(f32[2,256,2,512,1]{3,1,4,2,0:T(8,128)S(1)} %fusion.3, bf16[2,112,512]{2,1,0:T(8,128)(2,1)S(1)} %collective-permute-done.2, bf16[1,4,2,112,256]{4,3,2,1,0:T(8,128)(2,1)S(1)} %copy-done.1, s32[]{:T(128)S(6)} %select_n.140), kind=kOutput, calls=%fused_computation.4 | convolution fusion | flops 117964800 | bytes 4538372 | tf_op jit(solution)/shard_map/dot_general | solution.py:46
  28.5 0.2 fusion.13
  28.6 0.1 fusion.33
  28.7 0.1 collective-permute-start.3
  28.8 1.6 %collective-permute-start.4 = (bf16[2,64,512]{2,1,0:T(8,128)(2,1)S(1)}, bf16[2,64,512]{2,1,0:T(8,128)(2,1)S(1)}, u32[]{:S(2)}, u32[]{:S(2)}) collective-permute-start(bf16[2,64,512]{2,1,0:T(8,128)(2,1)S(1)} %get-tuple-element.29), channel_id=1, source_target_pairs={{0,2},{1,3},{2,0},{3,1},{4,6},{5,7},{6,4},{7,5},{8,10},{9,11},{10,... | collective-permute-start | bytes 393224 | tf_op jit(solution)/shard_map/ppermute | solution.py:92
  30.3 0.3 collective-permute-start.5
  30.7 4.4 %collective-permute-done.4 = bf16[2,64,512]{2,1,0:T(8,128)(2,1)S(1)} collective-permute-done((bf16[2,64,512]{2,1,0:T(8,128)(2,1)S(1)}, bf16[2,64,512]{2,1,0:T(8,128)(2,1)S(1)}, u32[]{:S(2)}, u32[]{:S(2)}) %collective-permute-start.4) | collective-permute-done | bytes 131104 | tf_op jit(solution)/shard_map/ppermute | solution.py:92
  35.2 1.9 %collective-permute-done.5 = bf16[2,64,512]{2,1,0:T(8,128)(2,1)S(1)} collective-permute-done((bf16[2,64,512]{2,1,0:T(8,128)(2,1)S(1)}, bf16[2,64,512]{2,1,0:T(8,128)(2,1)S(1)}, u32[]{:S(2)}, u32[]{:S(2)}) %collective-permute-start.5) | collective-permute-done | bytes 131104 | tf_op jit(solution)/shard_map/ppermute | solution.py:92
  37.1 4.0 %subtract_select_fusion = f32[64,32,512]{2,1,0:T(8,128)} fusion(f32[32,512]{1,0:T(8,128)S(1)} %broadcast_in_dim.55, f32[64,512]{1,0:T(8,128)S(1)} %get-tuple-element.43, f32[32,512]{1,0:T(8,128)S(1)} %broadcast_in_dim.54, f32[64,512]{1,0:T(8,128)S(1)} %get-tuple-element.42, f32[32,512]{1,0:T(8,128)S(1)} %broadcast_in_dim.53, ...), kind=kLoop, calls=%fused_computation | loop fusion | flops 19922944 | bytes 6029312 | tf_op jit(solution)/shard_map/jit(_where)/select_n | solution.py:153
  (20 shorter events, 0.3 us)
Async XLA Ops:
  0.0 2.0 %copy-start = (bf16[1,2,512,512]{3,2,1,0:T(8,128)(2,1)S(1)}, bf16[1,2,512,512]{3,2,1,0:T(8,128)(2,1)}, u32[]{:S(2)}) copy-start(bf16[1,2,512,512]{3,2,1,0:T(8,128)(2,1)} %param.5) | copy-start | bytes 3145732
  0.0 11.5 %copy-start.2 = (s32[2,64,512]{2,1,0:T(8,128)S(1)}, s32[2,64,512]{2,1,0:T(8,128)}, u32[]{:S(2)}) copy-start(s32[2,64,512]{2,1,0:T(8,128)} %param.9) | copy-start | bytes 786436
  2.0 19.8 %copy-start.1 = (bf16[1,4,2,112,256]{4,3,2,1,0:T(8,128)(2,1)S(1)}, bf16[1,4,2,112,256]{4,3,2,1,0:T(8,128)(2,1)}, u32[]{:S(2)}) copy-start(bf16[1,4,2,112,256]{4,3,2,1,0:T(8,128)(2,1)} %param.7) | copy-start | bytes 1376260
  3.6 18.3 %collective-permute-start.1 = (bf16[2,112,512]{2,1,0:T(8,128)(2,1)S(1)}, bf16[2,112,512]{2,1,0:T(8,128)(2,1)S(1)}, u32[]{:S(2)}, u32[]{:S(2)}) collective-permute-start(bf16[2,112,512]{2,1,0:T(8,128)(2,1)S(1)} %maximum_bitcast_fusion.2), channel_id=1, source_target_pairs={{0,4},{4,0},{8,12},{12,8},{1,5},{5,1},{9,13},{13,9},{2,6},{6,2},{1... | collective-permute-start | bytes 688136 | tf_op jit(solution)/shard_map/ppermute | solution.py:69
  8.8 13.0 %collective-permute-start = (bf16[2,112,512]{2,1,0:T(8,128)(2,1)S(1)}, bf16[2,112,512]{2,1,0:T(8,128)(2,1)S(1)}, u32[]{:S(2)}, u32[]{:S(2)}) collective-permute-start(bf16[2,112,512]{2,1,0:T(8,128)(2,1)S(1)} %maximum_bitcast_fusion.3), channel_id=1, source_target_pairs={{0,8},{8,0},{4,12},{12,4},{1,9},{9,1},{5,13},{13,5},{2,10},{10,2},... | collective-permute-start | bytes 688136 | tf_op jit(solution)/shard_map/ppermute | solution.py:67
  21.8 6.2 %collective-permute-start.2 = (bf16[2,112,512]{2,1,0:T(8,128)(2,1)S(1)}, bf16[2,112,512]{2,1,0:T(8,128)(2,1)S(1)}, u32[]{:S(2)}, u32[]{:S(2)}) collective-permute-start(bf16[2,112,512]{2,1,0:T(8,128)(2,1)S(1)} %collective-permute-done), channel_id=1, source_target_pairs={{0,4},{4,0},{8,12},{12,8},{1,5},{5,1},{9,13},{13,9},{2,6},{6,2},{1... | collective-permute-start | bytes 688136 | tf_op jit(solution)/shard_map/ppermute | solution.py:70
  28.7 2.0 %collective-permute-start.3 = (bf16[2,64,512]{2,1,0:T(8,128)(2,1)S(1)}, bf16[2,64,512]{2,1,0:T(8,128)(2,1)S(1)}, u32[]{:S(2)}, u32[]{:S(2)}) collective-permute-start(bf16[2,64,512]{2,1,0:T(8,128)(2,1)S(1)} %get-tuple-element.28), channel_id=1, source_target_pairs={{0,1},{1,0},{2,3},{3,2},{4,5},{5,4},{6,7},{7,6},{8,9},{9,8},{10,11... | collective-permute-start | bytes 393224 | tf_op jit(solution)/shard_map/ppermute | solution.py:92
  28.8 6.4 %collective-permute-start.4 = (bf16[2,64,512]{2,1,0:T(8,128)(2,1)S(1)}, bf16[2,64,512]{2,1,0:T(8,128)(2,1)S(1)}, u32[]{:S(2)}, u32[]{:S(2)}) collective-permute-start(bf16[2,64,512]{2,1,0:T(8,128)(2,1)S(1)} %get-tuple-element.29), channel_id=1, source_target_pairs={{0,2},{1,3},{2,0},{3,1},{4,6},{5,7},{6,4},{7,5},{8,10},{9,11},{10,... | collective-permute-start | bytes 393224 | tf_op jit(solution)/shard_map/ppermute | solution.py:92
  30.3 6.7 %collective-permute-start.5 = (bf16[2,64,512]{2,1,0:T(8,128)(2,1)S(1)}, bf16[2,64,512]{2,1,0:T(8,128)(2,1)S(1)}, u32[]{:S(2)}, u32[]{:S(2)}) collective-permute-start(bf16[2,64,512]{2,1,0:T(8,128)(2,1)S(1)} %get-tuple-element.30), channel_id=1, source_target_pairs={{0,3},{1,2},{2,1},{3,0},{4,7},{5,6},{6,5},{7,4},{8,11},{9,10},{10,... | collective-permute-start | bytes 393224 | tf_op jit(solution)/shard_map/ppermute | solution.py:92

commit v12 on v6

--- a/solution.py
+++ b/solution.py
@@ -77,6 +77,44 @@
     return pieces
 
 
+def windowed_traces(pieces, window_bounds, n_freq):
+    cosine_table, sine_table = inverse_tables(n_freq, NT)
+    scale = 1.0 / math.sqrt(n_freq)
+    half = NT // 2
+    count_m, count_s = window_bounds.shape[1], window_bounds.shape[2]
+    rows = []
+    for index, _ in pieces:
+        for table in (cosine_table, sine_table):
+            row = lax.dynamic_index_in_dim(table, index, 0, keepdims=False)[:half] * scale
+            rows.append(jnp.broadcast_to(row[:, None], (half, count_s)))
+    rows = lax.optimization_barrier(rows)
+    sums = [0.0, 0.0]
+    for k, (_, piece) in enumerate(pieces):
+        widened = piece.astype(jnp.float32)
+        sums[k % 2] = (
+            sums[k % 2]
+            + widened[0][:, None, :] * rows[2 * k][None]
+            - widened[1][:, None, :] * rows[2 * k + 1][None]
+        )
+    even, odd = sums
+    if len(pieces) < 2:
+        odd = jnp.zeros_like(even)
+    even, odd = lax.optimization_barrier((even, odd))
+    parity = (pieces[0][0] + first_bin) % 2
+    sign = jnp.asarray(1 - 2 * parity, jnp.float32)
+    even_weight = jnp.stack([jnp.float32(1.0), sign])[None, :, None, None]
+    odd_weight = jnp.stack([jnp.float32(1.0), -sign])[None, :, None, None]
+    traces = even[:, None] * even_weight + odd[:, None] * odd_weight
+    time_index = (
+        jnp.arange(2, dtype=jnp.int32)[:, None] * half + jnp.arange(half, dtype=jnp.int32)[None, :]
+    )[None, :, :, None]
+    first = window_bounds[0][:, None, None, :]
+    last = window_bounds[1][:, None, None, :]
+    inside = (time_index >= first) & (time_index < last)
+    windowed = jnp.where(inside, traces, jnp.float32(0.0))
+    return windowed.reshape(count_m, NT, count_s)
+
+
 def make_per_device(n_tile, n_freq):
     def per_device(sources, v_factors, u_factors, tile_ranks, window_bounds):
         v_local = v_factors[0, 0]
@@ -113,23 +151,7 @@
             )
             for k, (index, piece) in enumerate(received_parts[0])
         ]
-        cosine_table, sine_table = inverse_tables(n_freq, NT)
-        scale = 1.0 / math.sqrt(n_freq)
-        traces = 0.0
-        for index, piece in pieces:
-            cosine = lax.dynamic_index_in_dim(cosine_table, index, 0, keepdims=False) * scale
-            sine = lax.dynamic_index_in_dim(sine_table, index, 0, keepdims=False) * scale
-            widened = piece.astype(jnp.float32)
-            traces = (
-                traces
-                + widened[0][:, None, :] * cosine[None, :, None]
-                - widened[1][:, None, :] * sine[None, :, None]
-            )
-        time_index = jnp.arange(NT, dtype=jnp.int32)[None, :, None]
-        inside = (time_index >= window_bounds[0][:, None, :]) & (
-            time_index < window_bounds[1][:, None, :]
-        )
-        return jnp.where(inside, traces, jnp.float32(0.0))
+        return windowed_traces(pieces, window_bounds, n_freq)
 
     return per_device
 

time: 38.8 us -> 39.3 us (1.013)
  waiting for transfers between devices: 21.9 us -> 20.7 us
  local copies, waits for them, and re-layouts: 0.52 us -> 1.54 us
  other arithmetic: 5.57 us -> 6.18 us
    ppermute x1, waiting for transfers between devices: 10.1 us -> 8.93 us  [relay_exchange(): across = lax.ppermute(other, 'tile', [(0, 2), (2, 0), (1, 3), (3, 1)])]
    sub x0 -> x2, other arithmetic: none -> 0.96 us  [windowed_traces(): sums[k % 2] + widened[0][:, None, :] * rows[2 * k][None]]
    broadcast_in_dim x0 -> x8, local copies, waits for them, and re-layouts: none -> 0.56 us  [windowed_traces(): rows.append(jnp.broadcast_to(row[:, None], (half, count_s)))]
    select_n x1, other arithmetic: 4.07 us -> 3.61 us  [windowed_traces(): windowed = jnp.where(inside, traces, jnp.float32(0.0))]
  transfers between devices with their start and end apart: 6 -> 6, of which waited for: 4 -> 4; matrix products, arithmetic and copies ran while one was open for 1% -> 4% of each run, Pallas kernels for 0% -> 0%
where the time goes in v12:
time: 39.3 us; the launch traced here: 39.1 us
  waiting for transfers between devices  20.7 us (53%)
  starting transfers between devices  8.06 us (21%)
  other arithmetic  6.18 us (16%)
  matrix products  2.38 us (6%)
  local copies, waits for them, and re-layouts  1.54 us (4%)
    ppermute x1, waiting for transfers between devices, relay_exchange(): across = lax.ppermute(other, 'tile', [(0, 2), (2, 0), (1, 3), (3, 1)])  8.93 us
    ppermute x3, waiting for transfers between devices, freq_exchange(): pieces.append((f ^ d, lax.ppermute(part, 'freq', pairs)))  6.27 us
    ppermute x1, waiting for transfers between devices, relay_exchange(): passed = lax.ppermute(across, 'tile', pairs)  5.54 us
    select_n x1, other arithmetic, windowed_traces(): windowed = jnp.where(inside, traces, jnp.float32(0.0))  3.61 us
    ppermute x1, starting transfers between devices, relay_exchange(): partner = lax.ppermute(mine, 'tile', pairs)  3.09 us
    ppermute x1, starting transfers between devices, relay_exchange(): across = lax.ppermute(other, 'tile', [(0, 2), (2, 0), (1, 3), (3, 1)])  2.59 us
    ppermute x3, starting transfers between devices, freq_exchange(): pieces.append((f ^ d, lax.ppermute(part, 'freq', pairs)))  1.93 us
    dot_general x1, matrix products, column_products(): lax.dot_general(v_local, x_local, (((3,), (1,)), ((), ())), preferred_ele...  1.65 us
  transfers between devices with their start and end apart: 6, of which 4 were waited for; matrix products, arithmetic and copies ran while one was open for 4% of the time, Pallas kernels for 0%

profile of v12, /device:TPU:0, one launch (start us, length us, event | category | flops | bytes accessed | tf_op | source)
XLA Modules:
  0.0 39.1 jit_solution(8249519081493598778)
XLA Ops:
  0.0 0.8 %iota_compare_fusion = pred[2,112]{1,0:T(4,128)(4,1)S(1)} fusion(s32[2]{0:T(128)} %bitcast.124), kind=kLoop, calls=%fused_computation.90 | loop fusion | flops 224 | bytes 232 | tf_op jit(solution)/shard_map/lt | solution.py:30
  0.8 0.4 %copy-done = bf16[1,2,512,512]{3,2,1,0:T(8,128)(2,1)S(1)} copy-done((bf16[1,2,512,512]{3,2,1,0:T(8,128)(2,1)S(1)}, bf16[1,2,512,512]{3,2,1,0:T(8,128)(2,1)}, u32[]{:S(2)}) %copy-start) | copy-done | bytes 1048600
  1.2 1.7 %fusion.2 = f32[2,2,112,2,512]{4,2,3,1,0:T(8,128)S(1)} fusion(bf16[1,2,512,512]{3,2,1,0:T(8,128)(2,1)S(1)} %copy-done, bf16[1,1,2,2,112,512]{5,4,3,2,1,0:T(8,128)(2,1)} %param.6), kind=kOutput, calls=%fused_computation.7 | convolution fusion | flops 469762048 | bytes 3342336 | tf_op jit(solution)/shard_map/dot_general | solution.py:24
  2.9 0.2 fusion.14
  3.1 3.1 %collective-permute-start.1 = (bf16[2,112,512]{2,1,0:T(8,128)(2,1)S(1)}, bf16[2,112,512]{2,1,0:T(8,128)(2,1)S(1)}, u32[]{:S(2)}, u32[]{:S(2)}) collective-permute-start(bf16[2,112,512]{2,1,0:T(8,128)(2,1)S(1)} %bitcast.120), channel_id=1, source_target_pairs={{0,4},{4,0},{8,12},{12,8},{1,5},{5,1},{9,13},{13,9},{2,6},{6,2},{1... | collective-permute-start | bytes 688136 | tf_op jit(solution)/shard_map/ppermute | solution.py:52
  6.2 2.6 %collective-permute-start = (bf16[2,112,512]{2,1,0:T(8,128)(2,1)S(1)}, bf16[2,112,512]{2,1,0:T(8,128)(2,1)S(1)}, u32[]{:S(2)}, u32[]{:S(2)}) collective-permute-start(bf16[2,112,512]{2,1,0:T(8,128)(2,1)S(1)} %get-tuple-element.38), channel_id=1, source_target_pairs={{0,8},{8,0},{4,12},{12,4},{1,9},{9,1},{5,13},{13,5},{2,10},{10,2},... | collective-permute-start | bytes 688136 | tf_op jit(solution)/shard_map/ppermute | solution.py:51
  8.8 0.1 iota_add_fusion
  8.9 0.1 fusion.39
  9.1 0.1 pad_maximum_fusion
  9.2 0.1 mul.407
  9.3 0.1 mul.408
  9.4 0.1 add.167
  9.5 0.1 mul.402
  9.6 0.1 broadcast_in_dim.43
  9.7 0.1 broadcast_in_dim.41
  9.8 0.1 broadcast_in_dim.39
  9.8 0.1 broadcast_in_dim.37
  9.9 0.1 broadcast_in_dim.38
  10.0 0.1 broadcast_in_dim.40
  10.2 8.9 %collective-permute-done = bf16[2,112,512]{2,1,0:T(8,128)(2,1)S(1)} collective-permute-done((bf16[2,112,512]{2,1,0:T(8,128)(2,1)S(1)}, bf16[2,112,512]{2,1,0:T(8,128)(2,1)S(1)}, u32[]{:S(2)}, u32[]{:S(2)}) %collective-permute-start) | collective-permute-done | bytes 229408 | tf_op jit(solution)/shard_map/ppermute | solution.py:51
  19.2 0.4 %collective-permute-start.2 = (bf16[2,112,512]{2,1,0:T(8,128)(2,1)S(1)}, bf16[2,112,512]{2,1,0:T(8,128)(2,1)S(1)}, u32[]{:S(2)}, u32[]{:S(2)}) collective-permute-start(bf16[2,112,512]{2,1,0:T(8,128)(2,1)S(1)} %collective-permute-done), channel_id=1, source_target_pairs={{0,4},{4,0},{8,12},{12,8},{1,5},{5,1},{9,13},{13,9},{2,6},{6,2},{1... | collective-permute-start | bytes 688136 | tf_op jit(solution)/shard_map/ppermute | solution.py:53
  19.6 5.5 %collective-permute-done.2 = bf16[2,112,512]{2,1,0:T(8,128)(2,1)S(1)} collective-permute-done((bf16[2,112,512]{2,1,0:T(8,128)(2,1)S(1)}, bf16[2,112,512]{2,1,0:T(8,128)(2,1)S(1)}, u32[]{:S(2)}, u32[]{:S(2)}) %collective-permute-start.2) | collective-permute-done | bytes 229408 | tf_op jit(solution)/shard_map/ppermute | solution.py:53
  25.2 0.7 %convolution_bitcast_fusion = f32[2,256,2,512]{3,1,2,0:T(8,128)S(1)} fusion(bf16[1,2,112,512]{3,2,0,1:T(8,128)(2,1)S(1)} %bitcast.123, bf16[1,2,112,512]{3,2,0,1:T(8,128)(2,1)S(1)} %bitcast.121, bf16[1,2,112,512]{3,2,0,1:T(8,128)(2,1)S(1)} %bitcast.122, bf16[1,2,112,512]{3,2,0,1:T(8,128)(2,1)S(1)} %get-tuple-element.37, ...), kind=kOutput, calls=%fused_computation.6 | convolution fusion | flops 475267072 | bytes 3473408 | tf_op jit(solution)/shard_map/dot_general | solution.py:37
  25.9 0.2 fusion.27
  26.2 0.1 collective-permute-start.4
  26.2 1.6 %collective-permute-start.3 = (bf16[2,64,512]{2,1,0:T(8,128)(2,1)S(1)}, bf16[2,64,512]{2,1,0:T(8,128)(2,1)S(1)}, u32[]{:S(2)}, u32[]{:S(2)}) collective-permute-start(bf16[2,64,512]{2,1,0:T(8,128)(2,1)S(1)} %get-tuple-element.31), channel_id=1, source_target_pairs={{0,2},{1,3},{2,0},{3,1},{4,6},{5,7},{6,4},{7,5},{8,10},{9,11},{10,... | collective-permute-start | bytes 393224 | tf_op jit(solution)/shard_map/ppermute | solution.py:76
  27.8 0.3 collective-permute-start.5
  28.2 4.4 %collective-permute-done.3 = bf16[2,64,512]{2,1,0:T(8,128)(2,1)S(1)} collective-permute-done((bf16[2,64,512]{2,1,0:T(8,128)(2,1)S(1)}, bf16[2,64,512]{2,1,0:T(8,128)(2,1)S(1)}, u32[]{:S(2)}, u32[]{:S(2)}) %collective-permute-start.3) | collective-permute-done | bytes 131104 | tf_op jit(solution)/shard_map/ppermute | solution.py:76
  32.7 1.9 %collective-permute-done.5 = bf16[2,64,512]{2,1,0:T(8,128)(2,1)S(1)} collective-permute-done((bf16[2,64,512]{2,1,0:T(8,128)(2,1)S(1)}, bf16[2,64,512]{2,1,0:T(8,128)(2,1)S(1)}, u32[]{:S(2)}, u32[]{:S(2)}) %collective-permute-start.5) | collective-permute-done | bytes 131104 | tf_op jit(solution)/shard_map/ppermute | solution.py:76
  34.6 0.5 %multiply_subtract_fusion.1 = f32[64,16,512]{2,1,0:T(8,128)S(1)} fusion(f32[16,512]{1,0:T(8,128)S(1)} %broadcast_in_dim.42, f32[64,512]{1,0:T(8,128)S(1)} %get-tuple-element.48, f32[16,512]{1,0:T(8,128)S(1)} %broadcast_in_dim.41, f32[64,512]{1,0:T(8,128)S(1)} %get-tuple-element.47, f32[16,512]{1,0:T(8,128)S(1)} %broadcast_in_dim.38, ...), kind=kLoop, calls=%fused_computation.5 | loop fusion | flops 3670016 | bytes 2752512 | tf_op jit(solution)/shard_map/sub | solution.py:95
  35.0 0.5 %multiply_subtract_fusion = f32[64,16,512]{2,1,0:T(8,128)S(1)} fusion(f32[16,512]{1,0:T(8,128)S(1)} %broadcast_in_dim.44, f32[64,512]{1,0:T(8,128)S(1)} %get-tuple-element.44, f32[16,512]{1,0:T(8,128)S(1)} %broadcast_in_dim.43, f32[64,512]{1,0:T(8,128)S(1)} %get-tuple-element.43, f32[16,512]{1,0:T(8,128)S(1)} %broadcast_in_dim.40, ...), kind=kLoop, calls=%fused_computation.4 | loop fusion | flops 3670016 | bytes 2752512 | tf_op jit(solution)/shard_map/sub | solution.py:95
  35.5 3.6 %fusion.1 = f32[64,32,512]{2,1,0:T(8,128)} fusion(f32[32]{0:T(128)S(1)} %mul.408, f32[64,16,512]{2,1,0:T(8,128)S(1)} %multiply_subtract_fusion, f32[32]{0:T(128)S(1)} %mul.402, f32[64,16,512]{2,1,0:T(8,128)S(1)} %multiply_subtract_fusion.1, s32[64,512]{1,0:T(8,128)S(1)} %get-tuple-element.40, s32[64,512]{1,0:T(8,128)S(1)} %get-tuple-element.39, s32[32]{0:T(128)S(1)} %add.167), kind=kLoop, calls=%fused_computation.2 | loop fusion | flops 7340032 | bytes 8651136 | tf_op jit(solution)/shard_map/jit(_where)/select_n | solution.py:114
  (32 shorter events, 0.6 us)
Async XLA Ops:
  0.0 1.2 %copy-start = (bf16[1,2,512,512]{3,2,1,0:T(8,128)(2,1)S(1)}, bf16[1,2,512,512]{3,2,1,0:T(8,128)(2,1)}, u32[]{:S(2)}) copy-start(bf16[1,2,512,512]{3,2,1,0:T(8,128)(2,1)} %param.5) | copy-start | bytes 3145732
  2.9 7.3 %copy-start.1 = (bf16[1,4,2,112,256]{4,3,2,1,0:T(8,128)(2,1)S(1)}, bf16[1,4,2,112,256]{4,3,2,1,0:T(8,128)(2,1)}, u32[]{:S(2)}) copy-start(bf16[1,4,2,112,256]{4,3,2,1,0:T(8,128)(2,1)} %param.7) | copy-start | bytes 1376260
  2.9 16.7 %copy-start.2 = (s32[2,64,512]{2,1,0:T(8,128)S(1)}, s32[2,64,512]{2,1,0:T(8,128)}, u32[]{:S(2)}) copy-start(s32[2,64,512]{2,1,0:T(8,128)} %param.9) | copy-start | bytes 786436
  3.1 16.5 %collective-permute-start.1 = (bf16[2,112,512]{2,1,0:T(8,128)(2,1)S(1)}, bf16[2,112,512]{2,1,0:T(8,128)(2,1)S(1)}, u32[]{:S(2)}, u32[]{:S(2)}) collective-permute-start(bf16[2,112,512]{2,1,0:T(8,128)(2,1)S(1)} %bitcast.120), channel_id=1, source_target_pairs={{0,4},{4,0},{8,12},{12,8},{1,5},{5,1},{9,13},{13,9},{2,6},{6,2},{1... | collective-permute-start | bytes 688136 | tf_op jit(solution)/shard_map/ppermute | solution.py:52
  6.2 12.9 %collective-permute-start = (bf16[2,112,512]{2,1,0:T(8,128)(2,1)S(1)}, bf16[2,112,512]{2,1,0:T(8,128)(2,1)S(1)}, u32[]{:S(2)}, u32[]{:S(2)}) collective-permute-start(bf16[2,112,512]{2,1,0:T(8,128)(2,1)S(1)} %get-tuple-element.38), channel_id=1, source_target_pairs={{0,8},{8,0},{4,12},{12,4},{1,9},{9,1},{5,13},{13,5},{2,10},{10,2},... | collective-permute-start | bytes 688136 | tf_op jit(solution)/shard_map/ppermute | solution.py:51
  19.2 6.0 %collective-permute-start.2 = (bf16[2,112,512]{2,1,0:T(8,128)(2,1)S(1)}, bf16[2,112,512]{2,1,0:T(8,128)(2,1)S(1)}, u32[]{:S(2)}, u32[]{:S(2)}) collective-permute-start(bf16[2,112,512]{2,1,0:T(8,128)(2,1)S(1)} %collective-permute-done), channel_id=1, source_target_pairs={{0,4},{4,0},{8,12},{12,8},{1,5},{5,1},{9,13},{13,9},{2,6},{6,2},{1... | collective-permute-start | bytes 688136 | tf_op jit(solution)/shard_map/ppermute | solution.py:53
  26.2 2.0 %collective-permute-start.4 = (bf16[2,64,512]{2,1,0:T(8,128)(2,1)S(1)}, bf16[2,64,512]{2,1,0:T(8,128)(2,1)S(1)}, u32[]{:S(2)}, u32[]{:S(2)}) collective-permute-start(bf16[2,64,512]{2,1,0:T(8,128)(2,1)S(1)} %get-tuple-element.29), channel_id=1, source_target_pairs={{0,1},{1,0},{2,3},{3,2},{4,5},{5,4},{6,7},{7,6},{8,9},{9,8},{10,11... | collective-permute-start | bytes 393224 | tf_op jit(solution)/shard_map/ppermute | solution.py:76
  26.2 6.4 %collective-permute-start.3 = (bf16[2,64,512]{2,1,0:T(8,128)(2,1)S(1)}, bf16[2,64,512]{2,1,0:T(8,128)(2,1)S(1)}, u32[]{:S(2)}, u32[]{:S(2)}) collective-permute-start(bf16[2,64,512]{2,1,0:T(8,128)(2,1)S(1)} %get-tuple-element.31), channel_id=1, source_target_pairs={{0,2},{1,3},{2,0},{3,1},{4,6},{5,7},{6,4},{7,5},{8,10},{9,11},{10,... | collective-permute-start | bytes 393224 | tf_op jit(solution)/shard_map/ppermute | solution.py:76
  27.8 6.7 %collective-permute-start.5 = (bf16[2,64,512]{2,1,0:T(8,128)(2,1)S(1)}, bf16[2,64,512]{2,1,0:T(8,128)(2,1)S(1)}, u32[]{:S(2)}, u32[]{:S(2)}) collective-permute-start(bf16[2,64,512]{2,1,0:T(8,128)(2,1)S(1)} %get-tuple-element.32), channel_id=1, source_target_pairs={{0,3},{1,2},{2,1},{3,0},{4,7},{5,6},{6,5},{7,4},{8,11},{9,10},{10,... | collective-permute-start | bytes 393224 | tf_op jit(solution)/shard_map/ppermute | solution.py:76

commit v13 on v9

--- a/solution.py
+++ b/solution.py
@@ -42,6 +42,18 @@
     return jnp.stack([real_part, imag_part], axis=0).astype(jnp.bfloat16)
 
 
+def row_products(u_part, blocks):
+    return lax.dot_general(
+        u_part, blocks, (((0, 2), (0, 2)), ((), ())), preferred_element_type=jnp.float32
+    )
+
+
+def finish_spectrum(products):
+    real_part = products[0, :, 0] - products[1, :, 1]
+    imag_part = products[0, :, 1] + products[1, :, 0]
+    return jnp.stack([real_part, imag_part], axis=0).astype(jnp.bfloat16)
+
+
 def relay_exchange(own, u_local):
     t = lax.axis_index("tile")
     row = t // 2
@@ -52,11 +64,12 @@
     partner = lax.ppermute(mine, "tile", pairs)
     passed = lax.ppermute(across, "tile", pairs)
     columns = (t, t ^ 2, t ^ 1, t ^ 3)
-    u_order = jnp.stack(
-        [lax.dynamic_index_in_dim(u_local, j, 0, keepdims=False) for j in columns], axis=0
+    u_order = [lax.dynamic_index_in_dim(u_local, j, 0, keepdims=False) for j in columns]
+    early = row_products(
+        jnp.stack(u_order[:3], axis=0), jnp.stack([mine, across, partner], axis=0)
     )
-    blocks = jnp.stack([mine, across, partner, passed], axis=0)
-    return row_spectrum(u_order, blocks)
+    late = row_products(u_order[3][None], passed[None])
+    return finish_spectrum(early + late)
 
 
 def gather_exchange(own, u_local, n_tile):

time: 38.6 us -> 38.4 us (level)
  waiting for transfers between devices: 21.4 us -> 20.6 us
  matrix products: 2.38 us -> 2.84 us
    ppermute x1, waiting for transfers between devices: 5.54 us -> 4.8 us  [relay_exchange(): passed = lax.ppermute(across, 'tile', pairs)]
    dot_general x1 -> x2, matrix products: 0.72 us -> 1.18 us  [row_products(): lax.dot_general(u_part, blocks, (((0, 2), (0, 2)), ((), ())), preferred_e...]
  transfers between devices with their start and end apart: 6 -> 6, of which waited for: 4 -> 4; matrix products, arithmetic and copies ran while one was open for 2% -> 4% of each run, Pallas kernels for 0% -> 0%
where the time goes in v13:
time: 38.4 us; the launch traced here: 38.2 us
  waiting for transfers between devices  20.6 us (54%)
  starting transfers between devices  8.06 us (21%)
  other arithmetic  5.45 us (14%)
  matrix products  2.84 us (7%)
  local copies, waits for them, and re-layouts  1.07 us (3%)
    ppermute x1, waiting for transfers between devices, relay_exchange(): across = lax.ppermute(other, 'tile', [(0, 2), (2, 0), (1, 3), (3, 1)])  9.58 us
    ppermute x3, waiting for transfers between devices, freq_exchange(): pieces.append((f ^ d, lax.ppermute(part, 'freq', pairs)))  6.27 us
    ppermute x1, waiting for transfers between devices, relay_exchange(): passed = lax.ppermute(across, 'tile', pairs)  4.8 us
    select_n x1, other arithmetic, per_device(): return jnp.where(inside, traces, jnp.float32(0.0))  3.96 us
    ppermute x1, starting transfers between devices, relay_exchange(): partner = lax.ppermute(mine, 'tile', pairs)  3.09 us
    ppermute x1, starting transfers between devices, relay_exchange(): across = lax.ppermute(other, 'tile', [(0, 2), (2, 0), (1, 3), (3, 1)])  2.59 us
    ppermute x3, starting transfers between devices, freq_exchange(): pieces.append((f ^ d, lax.ppermute(part, 'freq', pairs)))  1.93 us
    dot_general x1, matrix products, column_products(): lax.dot_general(v_local, x_local, (((3,), (1,)), ((), ())), preferred_ele...  1.65 us
  transfers between devices with their start and end apart: 6, of which 4 were waited for; matrix products, arithmetic and copies ran while one was open for 4% of the time, Pallas kernels for 0%

profile of v13, /device:TPU:0, one launch (start us, length us, event | category | flops | bytes accessed | tf_op | source)
XLA Modules:
  0.0 38.2 jit_solution(7946751757615396889)
XLA Ops:
  0.0 0.0 copy-start
  0.0 0.9 %iota_compare_fusion.2 = pred[2,112]{1,0:T(4,128)(4,1)S(1)} fusion(s32[2]{0:T(128)} %bitcast.116), kind=kLoop, calls=%fused_computation.88 | loop fusion | flops 224 | bytes 232 | tf_op jit(solution)/shard_map/lt | solution.py:30
  0.9 0.4 copy-done
  1.2 1.7 %fusion.1 = f32[2,2,112,2,512]{4,2,3,1,0:T(8,128)S(1)} fusion(bf16[1,2,512,512]{3,2,1,0:T(8,128)(2,1)S(1)} %copy-done, bf16[1,1,2,2,112,512]{5,4,3,2,1,0:T(8,128)(2,1)} %param.6), kind=kOutput, calls=%fused_computation.5 | convolution fusion | flops 469762048 | bytes 3342336 | tf_op jit(solution)/shard_map/dot_general | solution.py:24
  2.9 0.2 fusion.12
  3.1 0.1 fusion.25
  3.1 3.1 %collective-permute-start.1 = (bf16[2,112,512]{2,1,0:T(8,128)(2,1)S(1)}, bf16[2,112,512]{2,1,0:T(8,128)(2,1)S(1)}, u32[]{:S(2)}, u32[]{:S(2)}) collective-permute-start(bf16[2,112,512]{2,1,0:T(8,128)(2,1)S(1)} %bitcast.113), channel_id=1, source_target_pairs={{0,4},{4,0},{8,12},{12,8},{1,5},{5,1},{9,13},{13,9},{2,6},{6,2},{1... | collective-permute-start | bytes 688136 | tf_op jit(solution)/shard_map/ppermute | solution.py:64
  6.2 2.6 %collective-permute-start = (bf16[2,112,512]{2,1,0:T(8,128)(2,1)S(1)}, bf16[2,112,512]{2,1,0:T(8,128)(2,1)S(1)}, u32[]{:S(2)}, u32[]{:S(2)}) collective-permute-start(bf16[2,112,512]{2,1,0:T(8,128)(2,1)S(1)} %get-tuple-element.32), channel_id=1, source_target_pairs={{0,8},{8,0},{4,12},{12,4},{1,9},{9,1},{5,13},{13,5},{2,10},{10,2},... | collective-permute-start | bytes 688136 | tf_op jit(solution)/shard_map/ppermute | solution.py:63
  8.8 0.1 fusion.39
  9.0 0.1 broadcast_in_dim.43
  9.1 0.1 broadcast_in_dim.41
  9.1 0.1 broadcast_in_dim.39
  9.2 0.1 broadcast_in_dim.37
  9.3 0.1 broadcast_in_dim.38
  9.4 0.1 broadcast_in_dim.40
  9.4 0.1 broadcast_in_dim.42
  9.5 0.1 broadcast_in_dim.44
  9.6 9.6 %collective-permute-done = bf16[2,112,512]{2,1,0:T(8,128)(2,1)S(1)} collective-permute-done((bf16[2,112,512]{2,1,0:T(8,128)(2,1)S(1)}, bf16[2,112,512]{2,1,0:T(8,128)(2,1)S(1)}, u32[]{:S(2)}, u32[]{:S(2)}) %collective-permute-start) | collective-permute-done | bytes 229408 | tf_op jit(solution)/shard_map/ppermute | solution.py:63
  19.1 0.4 %collective-permute-start.2 = (bf16[2,112,512]{2,1,0:T(8,128)(2,1)S(1)}, bf16[2,112,512]{2,1,0:T(8,128)(2,1)S(1)}, u32[]{:S(2)}, u32[]{:S(2)}) collective-permute-start(bf16[2,112,512]{2,1,0:T(8,128)(2,1)S(1)} %collective-permute-done), channel_id=1, source_target_pairs={{0,4},{4,0},{8,12},{12,8},{1,5},{5,1},{9,13},{13,9},{2,6},{6,2},{1... | collective-permute-start | bytes 688136 | tf_op jit(solution)/shard_map/ppermute | solution.py:65
  19.6 0.0 collective-permute-done.1
  19.6 0.7 %fusion.3 = f32[2,256,2,512,1]{3,1,4,2,0:T(8,128)S(1)} fusion(bf16[1,2,112,512]{3,2,0,1:T(8,128)(2,1)S(1)} %bitcast.114, bf16[1,2,112,512]{3,2,0,1:T(8,128)(2,1)S(1)} %bitcast.115, bf16[1,2,112,512]{3,2,0,1:T(8,128)(2,1)S(1)} %get-tuple-element.33, bf16[1,2,112,256]{3,2,0,1:T(8,128)(2,1)S(1)} %get-tuple-element.31, ...), kind=kOutput, calls=%fused_computation.16 | convolution fusion | flops 355418112 | bytes 3129344 | tf_op jit(solution)/shard_map/dot_general | solution.py:46
  20.4 4.8 %collective-permute-done.2 = bf16[2,112,512]{2,1,0:T(8,128)(2,1)S(1)} collective-permute-done((bf16[2,112,512]{2,1,0:T(8,128)(2,1)S(1)}, bf16[2,112,512]{2,1,0:T(8,128)(2,1)S(1)}, u32[]{:S(2)}, u32[]{:S(2)}) %collective-permute-start.2) | collective-permute-done | bytes 229408 | tf_op jit(solution)/shard_map/ppermute | solution.py:65
  25.2 0.5 %bitcast_add_fusion = f32[2,256,2,512]{3,1,2,0:T(8,128)S(1)} fusion(f32[2,256,2,512,1]{3,1,4,2,0:T(8,128)S(1)} %fusion.3, bf16[2,112,512]{2,1,0:T(8,128)(2,1)S(1)} %collective-permute-done.2, bf16[1,4,2,112,256]{4,3,2,1,0:T(8,128)(2,1)S(1)} %copy-done.1, s32[]{:T(128)S(6)} %select_n.107), kind=kOutput, calls=%fused_computation.4 | convolution fusion | flops 117964800 | bytes 4538372 | tf_op jit(solution)/shard_map/dot_general | solution.py:46
  25.6 0.2 fusion.23
  25.8 0.1 fusion.30
  25.9 0.1 collective-permute-start.3
  25.9 1.6 %collective-permute-start.4 = (bf16[2,64,512]{2,1,0:T(8,128)(2,1)S(1)}, bf16[2,64,512]{2,1,0:T(8,128)(2,1)S(1)}, u32[]{:S(2)}, u32[]{:S(2)}) collective-permute-start(bf16[2,64,512]{2,1,0:T(8,128)(2,1)S(1)} %get-tuple-element.27), channel_id=1, source_target_pairs={{0,2},{1,3},{2,0},{3,1},{4,6},{5,7},{6,4},{7,5},{8,10},{9,11},{10,... | collective-permute-start | bytes 393224 | tf_op jit(solution)/shard_map/ppermute | solution.py:89
  27.5 0.3 collective-permute-start.5
  27.8 0.0 collective-permute-done.3
  27.9 4.4 %collective-permute-done.4 = bf16[2,64,512]{2,1,0:T(8,128)(2,1)S(1)} collective-permute-done((bf16[2,64,512]{2,1,0:T(8,128)(2,1)S(1)}, bf16[2,64,512]{2,1,0:T(8,128)(2,1)S(1)}, u32[]{:S(2)}, u32[]{:S(2)}) %collective-permute-start.4) | collective-permute-done | bytes 131104 | tf_op jit(solution)/shard_map/ppermute | solution.py:89
  32.4 1.9 %collective-permute-done.5 = bf16[2,64,512]{2,1,0:T(8,128)(2,1)S(1)} collective-permute-done((bf16[2,64,512]{2,1,0:T(8,128)(2,1)S(1)}, bf16[2,64,512]{2,1,0:T(8,128)(2,1)S(1)}, u32[]{:S(2)}, u32[]{:S(2)}) %collective-permute-start.5) | collective-permute-done | bytes 131104 | tf_op jit(solution)/shard_map/ppermute | solution.py:89
  34.3 4.0 %subtract_select_fusion = f32[64,32,512]{2,1,0:T(8,128)} fusion(f32[32,512]{1,0:T(8,128)S(1)} %broadcast_in_dim.44, f32[64,512]{1,0:T(8,128)S(1)} %get-tuple-element.43, f32[32,512]{1,0:T(8,128)S(1)} %broadcast_in_dim.43, f32[64,512]{1,0:T(8,128)S(1)} %get-tuple-element.42, f32[32,512]{1,0:T(8,128)S(1)} %broadcast_in_dim.42, ...), kind=kLoop, calls=%fused_computation | loop fusion | flops 19922944 | bytes 6029312 | tf_op jit(solution)/shard_map/jit(_where)/select_n | solution.py:150
  (15 shorter events, 0.2 us)
Async XLA Ops:
  0.0 1.2 %copy-start = (bf16[1,2,512,512]{3,2,1,0:T(8,128)(2,1)S(1)}, bf16[1,2,512,512]{3,2,1,0:T(8,128)(2,1)}, u32[]{:S(2)}) copy-start(bf16[1,2,512,512]{3,2,1,0:T(8,128)(2,1)} %param.5) | copy-start | bytes 3145732
  0.0 8.8 %copy-start.2 = (s32[2,64,512]{2,1,0:T(8,128)S(1)}, s32[2,64,512]{2,1,0:T(8,128)}, u32[]{:S(2)}) copy-start(s32[2,64,512]{2,1,0:T(8,128)} %param.9) | copy-start | bytes 786436
  0.0 19.6 %copy-start.1 = (bf16[1,4,2,112,256]{4,3,2,1,0:T(8,128)(2,1)S(1)}, bf16[1,4,2,112,256]{4,3,2,1,0:T(8,128)(2,1)}, u32[]{:S(2)}) copy-start(bf16[1,4,2,112,256]{4,3,2,1,0:T(8,128)(2,1)} %param.7) | copy-start | bytes 1376260
  3.1 16.5 %collective-permute-start.1 = (bf16[2,112,512]{2,1,0:T(8,128)(2,1)S(1)}, bf16[2,112,512]{2,1,0:T(8,128)(2,1)S(1)}, u32[]{:S(2)}, u32[]{:S(2)}) collective-permute-start(bf16[2,112,512]{2,1,0:T(8,128)(2,1)S(1)} %bitcast.113), channel_id=1, source_target_pairs={{0,4},{4,0},{8,12},{12,8},{1,5},{5,1},{9,13},{13,9},{2,6},{6,2},{1... | collective-permute-start | bytes 688136 | tf_op jit(solution)/shard_map/ppermute | solution.py:64
  6.2 12.9 %collective-permute-start = (bf16[2,112,512]{2,1,0:T(8,128)(2,1)S(1)}, bf16[2,112,512]{2,1,0:T(8,128)(2,1)S(1)}, u32[]{:S(2)}, u32[]{:S(2)}) collective-permute-start(bf16[2,112,512]{2,1,0:T(8,128)(2,1)S(1)} %get-tuple-element.32), channel_id=1, source_target_pairs={{0,8},{8,0},{4,12},{12,4},{1,9},{9,1},{5,13},{13,5},{2,10},{10,2},... | collective-permute-start | bytes 688136 | tf_op jit(solution)/shard_map/ppermute | solution.py:63
  19.1 6.0 %collective-permute-start.2 = (bf16[2,112,512]{2,1,0:T(8,128)(2,1)S(1)}, bf16[2,112,512]{2,1,0:T(8,128)(2,1)S(1)}, u32[]{:S(2)}, u32[]{:S(2)}) collective-permute-start(bf16[2,112,512]{2,1,0:T(8,128)(2,1)S(1)} %collective-permute-done), channel_id=1, source_target_pairs={{0,4},{4,0},{8,12},{12,8},{1,5},{5,1},{9,13},{13,9},{2,6},{6,2},{1... | collective-permute-start | bytes 688136 | tf_op jit(solution)/shard_map/ppermute | solution.py:65
  25.9 2.0 %collective-permute-start.3 = (bf16[2,64,512]{2,1,0:T(8,128)(2,1)S(1)}, bf16[2,64,512]{2,1,0:T(8,128)(2,1)S(1)}, u32[]{:S(2)}, u32[]{:S(2)}) collective-permute-start(bf16[2,64,512]{2,1,0:T(8,128)(2,1)S(1)} %get-tuple-element.26), channel_id=1, source_target_pairs={{0,1},{1,0},{2,3},{3,2},{4,5},{5,4},{6,7},{7,6},{8,9},{9,8},{10,11... | collective-permute-start | bytes 393224 | tf_op jit(solution)/shard_map/ppermute | solution.py:89
  25.9 6.4 %collective-permute-start.4 = (bf16[2,64,512]{2,1,0:T(8,128)(2,1)S(1)}, bf16[2,64,512]{2,1,0:T(8,128)(2,1)S(1)}, u32[]{:S(2)}, u32[]{:S(2)}) collective-permute-start(bf16[2,64,512]{2,1,0:T(8,128)(2,1)S(1)} %get-tuple-element.27), channel_id=1, source_target_pairs={{0,2},{1,3},{2,0},{3,1},{4,6},{5,7},{6,4},{7,5},{8,10},{9,11},{10,... | collective-permute-start | bytes 393224 | tf_op jit(solution)/shard_map/ppermute | solution.py:89
  27.5 6.7 %collective-permute-start.5 = (bf16[2,64,512]{2,1,0:T(8,128)(2,1)S(1)}, bf16[2,64,512]{2,1,0:T(8,128)(2,1)S(1)}, u32[]{:S(2)}, u32[]{:S(2)}) collective-permute-start(bf16[2,64,512]{2,1,0:T(8,128)(2,1)S(1)} %get-tuple-element.28), channel_id=1, source_target_pairs={{0,3},{1,2},{2,1},{3,0},{4,7},{5,6},{6,5},{7,4},{8,11},{9,10},{10,... | collective-permute-start | bytes 393224 | tf_op jit(solution)/shard_map/ppermute | solution.py:89

commit v14 on v13

--- a/solution.py
+++ b/solution.py
@@ -21,16 +21,21 @@
 
 
 def column_products(v_local, x_local, rank_local):
+    v_real, v_imag = v_local[:, 0], v_local[:, 1]
+    stacked = jnp.stack(
+        [
+            jnp.concatenate([v_real, -v_imag], axis=-1),
+            jnp.concatenate([v_imag, v_real], axis=-1),
+        ],
+        axis=1,
+    )
+    x_both = x_local.reshape(x_local.shape[0] * x_local.shape[1], x_local.shape[2])
     products = lax.dot_general(
-        v_local, x_local, (((3,), (1,)), ((), ())), preferred_element_type=jnp.float32
+        stacked, x_both, (((3,), (0,)), ((), ())), preferred_element_type=jnp.float32
     )
-    coef_real = products[:, 0, :, 0] - products[:, 1, :, 1]
-    coef_imag = products[:, 0, :, 1] + products[:, 1, :, 0]
     slot_index = jnp.arange(v_local.shape[2], dtype=jnp.int32)
-    live_slots = slot_index[None, :, None] < rank_local[:, None, None]
-    coef_real = jnp.where(live_slots, coef_real, jnp.float32(0.0)).astype(jnp.bfloat16)
-    coef_imag = jnp.where(live_slots, coef_imag, jnp.float32(0.0)).astype(jnp.bfloat16)
-    return jnp.stack([coef_real, coef_imag], axis=1)
+    live_slots = slot_index[None, None, :, None] < rank_local[:, None, None, None]
+    return jnp.where(live_slots, products, jnp.float32(0.0)).astype(jnp.bfloat16)
 
 
 def row_spectrum(u_local, blocks):

time: 38.4 us -> 38.1 us (level)
  matrix products: 2.84 us -> 1.82 us
  local copies, waits for them, and re-layouts: 1.07 us -> 1.91 us
    dot_general x1, matrix products: 1.65 us -> 0.64 us  [column_products(): lax.dot_general(stacked, x_both, (((3,), (0,)), ((), ())), preferred_elem...]
    unnamed x6 -> x7, local copies, waits for them, and re-layouts: 0.39 us -> 1.15 us
where the time goes in v14:
time: 38.1 us; the launch traced here: 37.9 us
  waiting for transfers between devices  20.6 us (54%)
  starting transfers between devices  8.06 us (21%)
  other arithmetic  5.26 us (14%)
  local copies, waits for them, and re-layouts  1.91 us (5%)
  matrix products  1.82 us (5%)
    ppermute x1, waiting for transfers between devices, relay_exchange(): across = lax.ppermute(other, 'tile', [(0, 2), (2, 0), (1, 3), (3, 1)])  9.58 us
    ppermute x3, waiting for transfers between devices, freq_exchange(): pieces.append((f ^ d, lax.ppermute(part, 'freq', pairs)))  6.27 us
    ppermute x1, waiting for transfers between devices, relay_exchange(): passed = lax.ppermute(across, 'tile', pairs)  4.8 us
    select_n x1, other arithmetic, per_device(): return jnp.where(inside, traces, jnp.float32(0.0))  3.96 us
    ppermute x1, starting transfers between devices, relay_exchange(): partner = lax.ppermute(mine, 'tile', pairs)  3.09 us
    ppermute x1, starting transfers between devices, relay_exchange(): across = lax.ppermute(other, 'tile', [(0, 2), (2, 0), (1, 3), (3, 1)])  2.59 us
    ppermute x3, starting transfers between devices, freq_exchange(): pieces.append((f ^ d, lax.ppermute(part, 'freq', pairs)))  1.93 us
    dot_general x2, matrix products, row_products(): lax.dot_general(u_part, blocks, (((0, 2), (0, 2)), ((), ())), preferred_e...  1.18 us
  transfers between devices with their start and end apart: 6, of which 4 were waited for; matrix products, arithmetic and copies ran while one was open for 4% of the time, Pallas kernels for 0%

profile of v14, /device:TPU:0, one launch (start us, length us, event | category | flops | bytes accessed | tf_op | source)
XLA Modules:
  0.0 37.9 jit_solution(11914899700206926673)
XLA Ops:
  0.0 1.1 %copy.18 = bf16[1,1,2,2,112,512]{5,4,2,3,1,0:T(8,128)(2,1)S(1)} copy(bf16[1,1,2,2,112,512]{5,4,3,2,1,0:T(8,128)(2,1)} %param.6) | data formatting | bytes 917504 | tf_op args[1]
  1.1 0.0 copy-start.2
  1.2 0.0 copy-start.1
  1.2 0.8 %iota_compare_fusion.2 = pred[2,112]{1,0:T(4,128)(4,1)S(1)} fusion(s32[2]{0:T(128)} %bitcast.100), kind=kLoop, calls=%fused_computation.78 | loop fusion | flops 224 | bytes 232 | tf_op jit(solution)/shard_map/lt | solution.py:37
  2.0 0.1 maximum_bitcast_fusion
  2.1 0.6 %fusion.1 = bf16[2,2,112,512]{3,2,1,0:T(8,128)(2,1)S(1)} fusion(bf16[1024,512,1,1]{1,0,3,2:T(8,128)(2,1)S(1)} %bitcast.94, bf16[2,1,112,1024]{3,2,1,0:T(8,128)(2,1)S(1)} %get-tuple-element.45, bf16[2,1,112,1024]{3,2,1,0:T(8,128)(2,1)S(1)} %get-tuple-element.44, pred[2,112]{1,0:T(4,128)(4,1)S(1)} %iota_compare_fusion.2), kind=kOutput, calls=%fused_computation.6 | convolution fusion | flops 470679552 | bytes 2425056 | tf_op jit(solution)/shard_map/dot_general | solution.py:33
  2.8 3.1 %collective-permute-start.1 = (bf16[2,112,512]{2,1,0:T(8,128)(2,1)S(1)}, bf16[2,112,512]{2,1,0:T(8,128)(2,1)S(1)}, u32[]{:S(2)}, u32[]{:S(2)}) collective-permute-start(bf16[2,112,512]{2,1,0:T(8,128)(2,1)S(1)} %bitcast.97), channel_id=1, source_target_pairs={{0,4},{4,0},{8,12},{12,8},{1,5},{5,1},{9,13},{13,9},{2,6},{6,2},{1... | collective-permute-start | bytes 688136 | tf_op jit(solution)/shard_map/ppermute | solution.py:69
  5.9 2.6 %collective-permute-start = (bf16[2,112,512]{2,1,0:T(8,128)(2,1)S(1)}, bf16[2,112,512]{2,1,0:T(8,128)(2,1)S(1)}, u32[]{:S(2)}, u32[]{:S(2)}) collective-permute-start(bf16[2,112,512]{2,1,0:T(8,128)(2,1)S(1)} %get-tuple-element.30), channel_id=1, source_target_pairs={{0,8},{8,0},{4,12},{12,4},{1,9},{9,1},{5,13},{13,5},{2,10},{10,2},... | collective-permute-start | bytes 688136 | tf_op jit(solution)/shard_map/ppermute | solution.py:68
  8.5 0.1 fusion.28
  8.7 0.1 broadcast_in_dim.39
  8.8 0.1 broadcast_in_dim.37
  8.8 0.1 broadcast_in_dim.35
  8.9 0.1 broadcast_in_dim.33
  9.0 0.1 broadcast_in_dim.34
  9.0 0.1 broadcast_in_dim.36
  9.1 0.1 broadcast_in_dim.38
  9.2 0.1 broadcast_in_dim.40
  9.3 9.6 %collective-permute-done = bf16[2,112,512]{2,1,0:T(8,128)(2,1)S(1)} collective-permute-done((bf16[2,112,512]{2,1,0:T(8,128)(2,1)S(1)}, bf16[2,112,512]{2,1,0:T(8,128)(2,1)S(1)}, u32[]{:S(2)}, u32[]{:S(2)}) %collective-permute-start) | collective-permute-done | bytes 229408 | tf_op jit(solution)/shard_map/ppermute | solution.py:68
  18.8 0.4 %collective-permute-start.2 = (bf16[2,112,512]{2,1,0:T(8,128)(2,1)S(1)}, bf16[2,112,512]{2,1,0:T(8,128)(2,1)S(1)}, u32[]{:S(2)}, u32[]{:S(2)}) collective-permute-start(bf16[2,112,512]{2,1,0:T(8,128)(2,1)S(1)} %collective-permute-done), channel_id=1, source_target_pairs={{0,4},{4,0},{8,12},{12,8},{1,5},{5,1},{9,13},{13,9},{2,6},{6,2},{1... | collective-permute-start | bytes 688136 | tf_op jit(solution)/shard_map/ppermute | solution.py:70
  19.3 0.0 collective-permute-done.1
  19.3 0.7 %fusion.5 = f32[2,256,2,512,1]{3,1,4,2,0:T(8,128)S(1)} fusion(bf16[1,2,112,256]{3,2,0,1:T(8,128)(2,1)S(1)} %get-tuple-element.29, bf16[1,2,112,256]{3,2,0,1:T(8,128)(2,1)S(1)} %get-tuple-element.28, bf16[1,2,112,256]{3,2,0,1:T(8,128)(2,1)S(1)} %get-tuple-element.27, bf16[1,2,112,512]{3,2,1,0:T(8,128)(2,1)S(1)} %bitcast.98, ...), kind=kOutput, calls=%fused_computation.19 | convolution fusion | flops 354041856 | bytes 3129344 | tf_op jit(solution)/shard_map/dot_general | solution.py:51
  20.1 4.8 %collective-permute-done.2 = bf16[2,112,512]{2,1,0:T(8,128)(2,1)S(1)} collective-permute-done((bf16[2,112,512]{2,1,0:T(8,128)(2,1)S(1)}, bf16[2,112,512]{2,1,0:T(8,128)(2,1)S(1)}, u32[]{:S(2)}, u32[]{:S(2)}) %collective-permute-start.2) | collective-permute-done | bytes 229408 | tf_op jit(solution)/shard_map/ppermute | solution.py:70
  24.9 0.5 %bitcast_add_fusion = f32[2,256,2,512]{3,1,2,0:T(8,128)S(1)} fusion(f32[2,256,2,512,1]{3,1,4,2,0:T(8,128)S(1)} %fusion.5, bf16[2,112,512]{2,1,0:T(8,128)(2,1)S(1)} %collective-permute-done.2, bf16[1,4,2,112,256]{4,3,2,1,0:T(8,128)(2,1)S(1)} %copy-done.1, s32[]{:T(128)S(6)} %select_n.89), kind=kOutput, calls=%fused_computation.4 | convolution fusion | flops 117964800 | bytes 4538372 | tf_op jit(solution)/shard_map/dot_general | solution.py:51
  25.3 0.2 fusion.15
  25.5 0.1 fusion.19
  25.6 0.1 collective-permute-start.3
  25.6 1.6 %collective-permute-start.4 = (bf16[2,64,512]{2,1,0:T(8,128)(2,1)S(1)}, bf16[2,64,512]{2,1,0:T(8,128)(2,1)S(1)}, u32[]{:S(2)}, u32[]{:S(2)}) collective-permute-start(bf16[2,64,512]{2,1,0:T(8,128)(2,1)S(1)} %get-tuple-element.25), channel_id=1, source_target_pairs={{0,2},{1,3},{2,0},{3,1},{4,6},{5,7},{6,4},{7,5},{8,10},{9,11},{10,... | collective-permute-start | bytes 393224 | tf_op jit(solution)/shard_map/ppermute | solution.py:94
  27.2 0.3 collective-permute-start.5
  27.5 0.0 collective-permute-done.3
  27.6 4.4 %collective-permute-done.4 = bf16[2,64,512]{2,1,0:T(8,128)(2,1)S(1)} collective-permute-done((bf16[2,64,512]{2,1,0:T(8,128)(2,1)S(1)}, bf16[2,64,512]{2,1,0:T(8,128)(2,1)S(1)}, u32[]{:S(2)}, u32[]{:S(2)}) %collective-permute-start.4) | collective-permute-done | bytes 131104 | tf_op jit(solution)/shard_map/ppermute | solution.py:94
  32.1 1.9 %collective-permute-done.5 = bf16[2,64,512]{2,1,0:T(8,128)(2,1)S(1)} collective-permute-done((bf16[2,64,512]{2,1,0:T(8,128)(2,1)S(1)}, bf16[2,64,512]{2,1,0:T(8,128)(2,1)S(1)}, u32[]{:S(2)}, u32[]{:S(2)}) %collective-permute-start.5) | collective-permute-done | bytes 131104 | tf_op jit(solution)/shard_map/ppermute | solution.py:94
  34.0 4.0 %subtract_select_fusion = f32[64,32,512]{2,1,0:T(8,128)} fusion(f32[32,512]{1,0:T(8,128)S(1)} %broadcast_in_dim.40, f32[64,512]{1,0:T(8,128)S(1)} %get-tuple-element.43, f32[32,512]{1,0:T(8,128)S(1)} %broadcast_in_dim.39, f32[64,512]{1,0:T(8,128)S(1)} %get-tuple-element.42, f32[32,512]{1,0:T(8,128)S(1)} %broadcast_in_dim.38, ...), kind=kLoop, calls=%fused_computation | loop fusion | flops 19922944 | bytes 6029312 | tf_op jit(solution)/shard_map/jit(_where)/select_n | solution.py:155
  (18 shorter events, 0.3 us)
Async XLA Ops:
  0.0 2.1 %copy-start = (bf16[1,2,512,512]{3,2,1,0:T(8,128)(2,1)S(1)}, bf16[1,2,512,512]{3,2,1,0:T(8,128)(2,1)}, u32[]{:S(2)}) copy-start(bf16[1,2,512,512]{3,2,1,0:T(8,128)(2,1)} %param.5) | copy-start | bytes 3145732
  1.1 7.4 %copy-start.2 = (s32[2,64,512]{2,1,0:T(8,128)S(1)}, s32[2,64,512]{2,1,0:T(8,128)}, u32[]{:S(2)}) copy-start(s32[2,64,512]{2,1,0:T(8,128)} %param.9) | copy-start | bytes 786436
  1.2 18.1 %copy-start.1 = (bf16[1,4,2,112,256]{4,3,2,1,0:T(8,128)(2,1)S(1)}, bf16[1,4,2,112,256]{4,3,2,1,0:T(8,128)(2,1)}, u32[]{:S(2)}) copy-start(bf16[1,4,2,112,256]{4,3,2,1,0:T(8,128)(2,1)} %param.7) | copy-start | bytes 1376260
  2.8 16.5 %collective-permute-start.1 = (bf16[2,112,512]{2,1,0:T(8,128)(2,1)S(1)}, bf16[2,112,512]{2,1,0:T(8,128)(2,1)S(1)}, u32[]{:S(2)}, u32[]{:S(2)}) collective-permute-start(bf16[2,112,512]{2,1,0:T(8,128)(2,1)S(1)} %bitcast.97), channel_id=1, source_target_pairs={{0,4},{4,0},{8,12},{12,8},{1,5},{5,1},{9,13},{13,9},{2,6},{6,2},{1... | collective-permute-start | bytes 688136 | tf_op jit(solution)/shard_map/ppermute | solution.py:69
  5.9 12.9 %collective-permute-start = (bf16[2,112,512]{2,1,0:T(8,128)(2,1)S(1)}, bf16[2,112,512]{2,1,0:T(8,128)(2,1)S(1)}, u32[]{:S(2)}, u32[]{:S(2)}) collective-permute-start(bf16[2,112,512]{2,1,0:T(8,128)(2,1)S(1)} %get-tuple-element.30), channel_id=1, source_target_pairs={{0,8},{8,0},{4,12},{12,4},{1,9},{9,1},{5,13},{13,5},{2,10},{10,2},... | collective-permute-start | bytes 688136 | tf_op jit(solution)/shard_map/ppermute | solution.py:68
  18.8 6.0 %collective-permute-start.2 = (bf16[2,112,512]{2,1,0:T(8,128)(2,1)S(1)}, bf16[2,112,512]{2,1,0:T(8,128)(2,1)S(1)}, u32[]{:S(2)}, u32[]{:S(2)}) collective-permute-start(bf16[2,112,512]{2,1,0:T(8,128)(2,1)S(1)} %collective-permute-done), channel_id=1, source_target_pairs={{0,4},{4,0},{8,12},{12,8},{1,5},{5,1},{9,13},{13,9},{2,6},{6,2},{1... | collective-permute-start | bytes 688136 | tf_op jit(solution)/shard_map/ppermute | solution.py:70
  25.6 2.0 %collective-permute-start.3 = (bf16[2,64,512]{2,1,0:T(8,128)(2,1)S(1)}, bf16[2,64,512]{2,1,0:T(8,128)(2,1)S(1)}, u32[]{:S(2)}, u32[]{:S(2)}) collective-permute-start(bf16[2,64,512]{2,1,0:T(8,128)(2,1)S(1)} %get-tuple-element.24), channel_id=1, source_target_pairs={{0,1},{1,0},{2,3},{3,2},{4,5},{5,4},{6,7},{7,6},{8,9},{9,8},{10,11... | collective-permute-start | bytes 393224 | tf_op jit(solution)/shard_map/ppermute | solution.py:94
  25.6 6.4 %collective-permute-start.4 = (bf16[2,64,512]{2,1,0:T(8,128)(2,1)S(1)}, bf16[2,64,512]{2,1,0:T(8,128)(2,1)S(1)}, u32[]{:S(2)}, u32[]{:S(2)}) collective-permute-start(bf16[2,64,512]{2,1,0:T(8,128)(2,1)S(1)} %get-tuple-element.25), channel_id=1, source_target_pairs={{0,2},{1,3},{2,0},{3,1},{4,6},{5,7},{6,4},{7,5},{8,10},{9,11},{10,... | collective-permute-start | bytes 393224 | tf_op jit(solution)/shard_map/ppermute | solution.py:94
  27.2 6.7 %collective-permute-start.5 = (bf16[2,64,512]{2,1,0:T(8,128)(2,1)S(1)}, bf16[2,64,512]{2,1,0:T(8,128)(2,1)S(1)}, u32[]{:S(2)}, u32[]{:S(2)}) collective-permute-start(bf16[2,64,512]{2,1,0:T(8,128)(2,1)S(1)} %get-tuple-element.26), channel_id=1, source_target_pairs={{0,3},{1,2},{2,1},{3,0},{4,7},{5,6},{6,5},{7,4},{8,11},{9,10},{10,... | collective-permute-start | bytes 393224 | tf_op jit(solution)/shard_map/ppermute | solution.py:94

commit v15 on v14

--- a/solution.py
+++ b/solution.py
@@ -21,18 +21,14 @@
 
 
 def column_products(v_local, x_local, rank_local):
-    v_real, v_imag = v_local[:, 0], v_local[:, 1]
-    stacked = jnp.stack(
-        [
-            jnp.concatenate([v_real, -v_imag], axis=-1),
-            jnp.concatenate([v_imag, v_real], axis=-1),
-        ],
-        axis=1,
+    x_real, x_imag = x_local[0], x_local[1]
+    x_both = jnp.stack(
+        [jnp.stack([x_real, x_imag], axis=1), jnp.stack([-x_imag, x_real], axis=1)], axis=0
     )
-    x_both = x_local.reshape(x_local.shape[0] * x_local.shape[1], x_local.shape[2])
     products = lax.dot_general(
-        stacked, x_both, (((3,), (0,)), ((), ())), preferred_element_type=jnp.float32
+        v_local, x_both, (((1, 3), (0, 1)), ((), ())), preferred_element_type=jnp.float32
     )
+    products = products.transpose(0, 2, 1, 3)
     slot_index = jnp.arange(v_local.shape[2], dtype=jnp.int32)
     live_slots = slot_index[None, None, :, None] < rank_local[:, None, None, None]
     return jnp.where(live_slots, products, jnp.float32(0.0)).astype(jnp.bfloat16)

time: 38.1 us -> 38.8 us (1.018)
  other arithmetic: 5.26 us -> 6.42 us
  waiting for transfers between devices: 20.6 us -> 19.9 us
    ppermute x1, starting transfers between devices: 2.59 us -> 4.1 us  [relay_exchange(): across = lax.ppermute(other, 'tile', [(0, 2), (2, 0), (1, 3), (3, 1)])]
    ppermute x1, starting transfers between devices: 3.09 us -> 1.58 us  [relay_exchange(): partner = lax.ppermute(mine, 'tile', pairs)]
    ppermute x1, waiting for transfers between devices: 9.58 us -> 8.29 us  [relay_exchange(): across = lax.ppermute(other, 'tile', [(0, 2), (2, 0), (1, 3), (3, 1)])]
    another operation x0 -> x1, local copies, waits for them, and re-layouts: none -> 1.27 us  [column_products(): jnp.stack([x_real, x_imag], axis=1)]
    unnamed x7 -> x6, local copies, waits for them, and re-layouts: 1.15 us -> 0.02 us
    neg x1, other arithmetic: 0.02 us -> 1.13 us  [column_products(): -x_imag]
    ppermute x1, waiting for transfers between devices: 4.8 us -> 5.34 us  [relay_exchange(): passed = lax.ppermute(across, 'tile', pairs)]
where the time goes in v15:
time: 38.8 us; the launch traced here: 38.6 us
  waiting for transfers between devices  19.9 us (51%)
  starting transfers between devices  8.23 us (21%)
  other arithmetic  6.42 us (17%)
  local copies, waits for them, and re-layouts  2.04 us (5%)
  matrix products  1.82 us (5%)
    ppermute x1, waiting for transfers between devices, relay_exchange(): across = lax.ppermute(other, 'tile', [(0, 2), (2, 0), (1, 3), (3, 1)])  8.29 us
    ppermute x3, waiting for transfers between devices, freq_exchange(): pieces.append((f ^ d, lax.ppermute(part, 'freq', pairs)))  6.27 us
    ppermute x1, waiting for transfers between devices, relay_exchange(): passed = lax.ppermute(across, 'tile', pairs)  5.34 us
    ppermute x1, starting transfers between devices, relay_exchange(): across = lax.ppermute(other, 'tile', [(0, 2), (2, 0), (1, 3), (3, 1)])  4.1 us
    select_n x1, other arithmetic, per_device(): return jnp.where(inside, traces, jnp.float32(0.0))  3.96 us
    ppermute x3, starting transfers between devices, freq_exchange(): pieces.append((f ^ d, lax.ppermute(part, 'freq', pairs)))  1.93 us
    ppermute x1, starting transfers between devices, relay_exchange(): partner = lax.ppermute(mine, 'tile', pairs)  1.58 us
    another operation x1, local copies, waits for them, and re-layouts, column_products(): jnp.stack([x_real, x_imag], axis=1)  1.27 us
  transfers between devices with their start and end apart: 6, of which 4 were waited for; matrix products, arithmetic and copies ran while one was open for 4% of the time, Pallas kernels for 0%

profile of v15, /device:TPU:0, one launch (start us, length us, event | category | flops | bytes accessed | tf_op | source)
XLA Modules:
  0.0 38.6 jit_solution(5902307347447928263)
XLA Ops:
  0.0 1.1 %fusion.51 = bf16[512,1,512]{2,0,1:T(8,128)(2,1)S(1)} fusion(bf16[1,2,512,512]{3,2,1,0:T(8,128)(2,1)} %param.5), kind=kLoop, calls=%fused_computation.101 | loop fusion | flops 262144 | bytes 1048576 | tf_op jit(solution)/shard_map/neg | solution.py:26
  1.1 1.3 %slice_bitcast_fusion = (bf16[512,1,512]{2,0,1:T(8,128)(2,1)S(1)}, bf16[512,1,512]{2,0,1:T(8,128)(2,1)S(1)}) fusion(bf16[1,2,512,512]{3,2,1,0:T(8,128)(2,1)} %param.5), kind=kLoop, calls=%fused_computation.30 | loop fusion | bytes 2097152 | tf_op jit(solution)/shard_map/stack;squeeze | solution.py:26
  2.4 0.7 %iota_compare_fusion.2 = pred[2,112]{1,0:T(4,128)(4,1)S(1)} fusion(s32[2]{0:T(128)} %bitcast.119), kind=kLoop, calls=%fused_computation.81 | loop fusion | flops 224 | bytes 232 | tf_op jit(solution)/shard_map/lt | solution.py:33
  3.1 0.2 maximum_bitcast_fusion.8
  3.3 0.0 copy-start.2
  3.3 0.0 copy-start.1
  3.4 0.6 %fusion.6 = bf16[2,512,2,112]{1,3,2,0:T(8,128)(2,1)S(1)} fusion(bf16[1,512,2,512]{3,1,0,2:T(8,128)(2,1)S(1)} %get-tuple-element.30, bf16[1,512,2,512]{3,1,0,2:T(8,128)(2,1)S(1)} %get-tuple-element.29, bf16[1,1,2,2,112,512]{5,4,3,2,1,0:T(8,128)(2,1)S(1)} %copy-done, pred[2,112]{1,0:T(4,128)(4,1)S(1)} %iota_compare_fusion.2), kind=kOutput, calls=%fused_computation.11 | convolution fusion | flops 474415104 | bytes 3014880 | tf_op jit(solution)/shard_map/dot_general | solution.py:28
  4.0 0.1 dynamic-slice_bitcast_fusion.1
  4.1 4.1 %collective-permute-start = (bf16[2,112,512]{2,1,0:T(8,128)(2,1)S(1)}, bf16[2,112,512]{2,1,0:T(8,128)(2,1)S(1)}, u32[]{:S(2)}, u32[]{:S(2)}) collective-permute-start(bf16[2,112,512]{2,1,0:T(8,128)(2,1)S(1)} %get-tuple-element.35), channel_id=1, source_target_pairs={{0,8},{8,0},{4,12},{12,4},{1,9},{9,1},{5,13},{13,5},{2,10},{10,2},... | collective-permute-start | bytes 688136 | tf_op jit(solution)/shard_map/ppermute | solution.py:64
  8.2 1.6 %collective-permute-start.1 = (bf16[2,112,512]{2,1,0:T(8,128)(2,1)S(1)}, bf16[2,112,512]{2,1,0:T(8,128)(2,1)S(1)}, u32[]{:S(2)}, u32[]{:S(2)}) collective-permute-start(bf16[2,112,512]{2,1,0:T(8,128)(2,1)S(1)} %get-tuple-element.36), channel_id=1, source_target_pairs={{0,4},{4,0},{8,12},{12,8},{1,5},{5,1},{9,13},{13,9},{2,6},{6,2},{1... | collective-permute-start | bytes 688136 | tf_op jit(solution)/shard_map/ppermute | solution.py:65
  9.8 0.1 fusion.31
  10.0 0.1 broadcast_in_dim.39
  10.0 0.1 broadcast_in_dim.37
  10.1 0.1 broadcast_in_dim.35
  10.2 0.1 broadcast_in_dim.33
  10.2 0.1 broadcast_in_dim.34
  10.3 0.1 broadcast_in_dim.36
  10.4 0.1 broadcast_in_dim.38
  10.5 0.1 broadcast_in_dim.40
  10.5 8.3 %collective-permute-done = bf16[2,112,512]{2,1,0:T(8,128)(2,1)S(1)} collective-permute-done((bf16[2,112,512]{2,1,0:T(8,128)(2,1)S(1)}, bf16[2,112,512]{2,1,0:T(8,128)(2,1)S(1)}, u32[]{:S(2)}, u32[]{:S(2)}) %collective-permute-start) | collective-permute-done | bytes 229408 | tf_op jit(solution)/shard_map/ppermute | solution.py:64
  18.8 0.6 %collective-permute-start.2 = (bf16[2,112,512]{2,1,0:T(8,128)(2,1)S(1)}, bf16[2,112,512]{2,1,0:T(8,128)(2,1)S(1)}, u32[]{:S(2)}, u32[]{:S(2)}) collective-permute-start(bf16[2,112,512]{2,1,0:T(8,128)(2,1)S(1)} %collective-permute-done), channel_id=1, source_target_pairs={{0,4},{4,0},{8,12},{12,8},{1,5},{5,1},{9,13},{13,9},{2,6},{6,2},{1... | collective-permute-start | bytes 688136 | tf_op jit(solution)/shard_map/ppermute | solution.py:66
  19.5 0.7 %fusion.7 = f32[2,256,2,512,1]{3,1,4,2,0:T(8,128)S(1)} fusion(bf16[1,2,112,256]{3,2,0,1:T(8,128)(2,1)S(1)} %get-tuple-element.33, bf16[1,2,112,256]{3,2,0,1:T(8,128)(2,1)S(1)} %get-tuple-element.32, bf16[1,2,112,256]{3,2,0,1:T(8,128)(2,1)S(1)} %get-tuple-element.31, bf16[1,2,112,512]{3,2,1,0:T(8,128)(2,1)S(1)} %bitcast.118, ...), kind=kOutput, calls=%fused_computation.23 | convolution fusion | flops 354041856 | bytes 3129344 | tf_op jit(solution)/shard_map/dot_general | solution.py:47
  20.2 5.3 %collective-permute-done.2 = bf16[2,112,512]{2,1,0:T(8,128)(2,1)S(1)} collective-permute-done((bf16[2,112,512]{2,1,0:T(8,128)(2,1)S(1)}, bf16[2,112,512]{2,1,0:T(8,128)(2,1)S(1)}, u32[]{:S(2)}, u32[]{:S(2)}) %collective-permute-start.2) | collective-permute-done | bytes 229408 | tf_op jit(solution)/shard_map/ppermute | solution.py:66
  25.5 0.5 %bitcast_add_fusion = f32[2,256,2,512]{3,1,2,0:T(8,128)S(1)} fusion(f32[2,256,2,512,1]{3,1,4,2,0:T(8,128)S(1)} %fusion.7, bf16[2,112,512]{2,1,0:T(8,128)(2,1)S(1)} %collective-permute-done.2, bf16[1,4,2,112,256]{4,3,2,1,0:T(8,128)(2,1)S(1)} %copy-done.1, s32[]{:T(128)S(6)} %select_n.90), kind=kOutput, calls=%fused_computation.8 | convolution fusion | flops 117964800 | bytes 4538372 | tf_op jit(solution)/shard_map/dot_general | solution.py:47
  26.0 0.2 fusion.18
  26.2 0.1 fusion.22
  26.2 0.1 collective-permute-start.3
  26.3 1.3 %collective-permute-start.4 = (bf16[2,64,512]{2,1,0:T(8,128)(2,1)S(1)}, bf16[2,64,512]{2,1,0:T(8,128)(2,1)S(1)}, u32[]{:S(2)}, u32[]{:S(2)}) collective-permute-start(bf16[2,64,512]{2,1,0:T(8,128)(2,1)S(1)} %get-tuple-element.27), channel_id=1, source_target_pairs={{0,2},{1,3},{2,0},{3,1},{4,6},{5,7},{6,4},{7,5},{8,10},{9,11},{10,... | collective-permute-start | bytes 393224 | tf_op jit(solution)/shard_map/ppermute | solution.py:90
  27.6 0.5 %collective-permute-start.5 = (bf16[2,64,512]{2,1,0:T(8,128)(2,1)S(1)}, bf16[2,64,512]{2,1,0:T(8,128)(2,1)S(1)}, u32[]{:S(2)}, u32[]{:S(2)}) collective-permute-start(bf16[2,64,512]{2,1,0:T(8,128)(2,1)S(1)} %get-tuple-element.28), channel_id=1, source_target_pairs={{0,3},{1,2},{2,1},{3,0},{4,7},{5,6},{6,5},{7,4},{8,11},{9,10},{10,... | collective-permute-start | bytes 393224 | tf_op jit(solution)/shard_map/ppermute | solution.py:90
  28.3 4.4 %collective-permute-done.4 = bf16[2,64,512]{2,1,0:T(8,128)(2,1)S(1)} collective-permute-done((bf16[2,64,512]{2,1,0:T(8,128)(2,1)S(1)}, bf16[2,64,512]{2,1,0:T(8,128)(2,1)S(1)}, u32[]{:S(2)}, u32[]{:S(2)}) %collective-permute-start.4) | collective-permute-done | bytes 131104 | tf_op jit(solution)/shard_map/ppermute | solution.py:90
  32.7 1.9 %collective-permute-done.5 = bf16[2,64,512]{2,1,0:T(8,128)(2,1)S(1)} collective-permute-done((bf16[2,64,512]{2,1,0:T(8,128)(2,1)S(1)}, bf16[2,64,512]{2,1,0:T(8,128)(2,1)S(1)}, u32[]{:S(2)}, u32[]{:S(2)}) %collective-permute-start.5) | collective-permute-done | bytes 131104 | tf_op jit(solution)/shard_map/ppermute | solution.py:90
  34.6 4.0 %subtract_select_fusion = f32[64,32,512]{2,1,0:T(8,128)} fusion(f32[32,512]{1,0:T(8,128)S(1)} %broadcast_in_dim.40, f32[64,512]{1,0:T(8,128)S(1)} %get-tuple-element.46, f32[32,512]{1,0:T(8,128)S(1)} %broadcast_in_dim.39, f32[64,512]{1,0:T(8,128)S(1)} %get-tuple-element.45, f32[32,512]{1,0:T(8,128)S(1)} %broadcast_in_dim.38, ...), kind=kLoop, calls=%fused_computation | loop fusion | flops 19922944 | bytes 6029312 | tf_op jit(solution)/shard_map/jit(_where)/select_n | solution.py:151
  (17 shorter events, 0.2 us)
Async XLA Ops:
  0.0 3.4 %copy-start = (bf16[1,1,2,2,112,512]{5,4,3,2,1,0:T(8,128)(2,1)S(1)}, bf16[1,1,2,2,112,512]{5,4,3,2,1,0:T(8,128)(2,1)}, u32[]{:S(2)}) copy-start(bf16[1,1,2,2,112,512]{5,4,3,2,1,0:T(8,128)(2,1)} %param.6) | copy-start | bytes 1376260
  3.3 6.4 %copy-start.2 = (s32[2,64,512]{2,1,0:T(8,128)S(1)}, s32[2,64,512]{2,1,0:T(8,128)}, u32[]{:S(2)}) copy-start(s32[2,64,512]{2,1,0:T(8,128)} %param.9) | copy-start | bytes 786436
  3.3 16.1 %copy-start.1 = (bf16[1,4,2,112,256]{4,3,2,1,0:T(8,128)(2,1)S(1)}, bf16[1,4,2,112,256]{4,3,2,1,0:T(8,128)(2,1)}, u32[]{:S(2)}) copy-start(bf16[1,4,2,112,256]{4,3,2,1,0:T(8,128)(2,1)} %param.7) | copy-start | bytes 1376260
  4.1 14.7 %collective-permute-start = (bf16[2,112,512]{2,1,0:T(8,128)(2,1)S(1)}, bf16[2,112,512]{2,1,0:T(8,128)(2,1)S(1)}, u32[]{:S(2)}, u32[]{:S(2)}) collective-permute-start(bf16[2,112,512]{2,1,0:T(8,128)(2,1)S(1)} %get-tuple-element.35), channel_id=1, source_target_pairs={{0,8},{8,0},{4,12},{12,4},{1,9},{9,1},{5,13},{13,5},{2,10},{10,2},... | collective-permute-start | bytes 688136 | tf_op jit(solution)/shard_map/ppermute | solution.py:64
  8.2 11.3 %collective-permute-start.1 = (bf16[2,112,512]{2,1,0:T(8,128)(2,1)S(1)}, bf16[2,112,512]{2,1,0:T(8,128)(2,1)S(1)}, u32[]{:S(2)}, u32[]{:S(2)}) collective-permute-start(bf16[2,112,512]{2,1,0:T(8,128)(2,1)S(1)} %get-tuple-element.36), channel_id=1, source_target_pairs={{0,4},{4,0},{8,12},{12,8},{1,5},{5,1},{9,13},{13,9},{2,6},{6,2},{1... | collective-permute-start | bytes 688136 | tf_op jit(solution)/shard_map/ppermute | solution.py:65
  18.8 6.7 %collective-permute-start.2 = (bf16[2,112,512]{2,1,0:T(8,128)(2,1)S(1)}, bf16[2,112,512]{2,1,0:T(8,128)(2,1)S(1)}, u32[]{:S(2)}, u32[]{:S(2)}) collective-permute-start(bf16[2,112,512]{2,1,0:T(8,128)(2,1)S(1)} %collective-permute-done), channel_id=1, source_target_pairs={{0,4},{4,0},{8,12},{12,8},{1,5},{5,1},{9,13},{13,9},{2,6},{6,2},{1... | collective-permute-start | bytes 688136 | tf_op jit(solution)/shard_map/ppermute | solution.py:66
  26.2 2.0 %collective-permute-start.3 = (bf16[2,64,512]{2,1,0:T(8,128)(2,1)S(1)}, bf16[2,64,512]{2,1,0:T(8,128)(2,1)S(1)}, u32[]{:S(2)}, u32[]{:S(2)}) collective-permute-start(bf16[2,64,512]{2,1,0:T(8,128)(2,1)S(1)} %get-tuple-element.26), channel_id=1, source_target_pairs={{0,1},{1,0},{2,3},{3,2},{4,5},{5,4},{6,7},{7,6},{8,9},{9,8},{10,11... | collective-permute-start | bytes 393224 | tf_op jit(solution)/shard_map/ppermute | solution.py:90
  26.3 6.4 %collective-permute-start.4 = (bf16[2,64,512]{2,1,0:T(8,128)(2,1)S(1)}, bf16[2,64,512]{2,1,0:T(8,128)(2,1)S(1)}, u32[]{:S(2)}, u32[]{:S(2)}) collective-permute-start(bf16[2,64,512]{2,1,0:T(8,128)(2,1)S(1)} %get-tuple-element.27), channel_id=1, source_target_pairs={{0,2},{1,3},{2,0},{3,1},{4,6},{5,7},{6,4},{7,5},{8,10},{9,11},{10,... | collective-permute-start | bytes 393224 | tf_op jit(solution)/shard_map/ppermute | solution.py:90
  27.6 7.0 %collective-permute-start.5 = (bf16[2,64,512]{2,1,0:T(8,128)(2,1)S(1)}, bf16[2,64,512]{2,1,0:T(8,128)(2,1)S(1)}, u32[]{:S(2)}, u32[]{:S(2)}) collective-permute-start(bf16[2,64,512]{2,1,0:T(8,128)(2,1)S(1)} %get-tuple-element.28), channel_id=1, source_target_pairs={{0,3},{1,2},{2,1},{3,0},{4,7},{5,6},{6,5},{7,4},{8,11},{9,10},{10,... | collective-permute-start | bytes 393224 | tf_op jit(solution)/shard_map/ppermute | solution.py:90

commit v16 on v14

--- a/solution.py
+++ b/solution.py
@@ -29,6 +29,7 @@
         ],
         axis=1,
     )
+    stacked = lax.optimization_barrier(stacked)
     x_both = x_local.reshape(x_local.shape[0] * x_local.shape[1], x_local.shape[2])
     products = lax.dot_general(
         stacked, x_both, (((3,), (0,)), ((), ())), preferred_element_type=jnp.float32

time: 38.1 us -> 39.5 us (1.037)
  other arithmetic: 5.26 us -> 6.37 us
  matrix products: 1.82 us -> 2.79 us
  waiting for transfers between devices: 20.6 us -> 20 us
    unnamed x7 -> x6, local copies, waits for them, and re-layouts: 1.15 us -> 0.02 us
    squeeze x1, local copies, waits for them, and re-layouts: 0.03 us -> 1.09 us  [column_products(): v_real, v_imag = (v_local[:, 0], v_local[:, 1])]
    neg x1, other arithmetic: 0.02 us -> 1.04 us  [column_products(): -v_imag]
    dot_general x2, matrix products: 1.18 us -> 2.15 us  [row_products(): lax.dot_general(u_part, blocks, (((0, 2), (0, 2)), ((), ())), preferred_e...]
    ppermute x1, waiting for transfers between devices: 4.8 us -> 4.05 us  [relay_exchange(): passed = lax.ppermute(across, 'tile', pairs)]
  transfers between devices with their start and end apart: 6 -> 6, of which waited for: 4 -> 4; matrix products, arithmetic and copies ran while one was open for 4% -> 6% of each run, Pallas kernels for 0% -> 0%
where the time goes in v16:
time: 39.5 us; the launch traced here: 39.3 us
  waiting for transfers between devices  20 us (51%)
  starting transfers between devices  8.06 us (20%)
  other arithmetic  6.37 us (16%)
  matrix products  2.79 us (7%)
  local copies, waits for them, and re-layouts  1.83 us (5%)
    ppermute x1, waiting for transfers between devices, relay_exchange(): across = lax.ppermute(other, 'tile', [(0, 2), (2, 0), (1, 3), (3, 1)])  9.68 us
    ppermute x3, waiting for transfers between devices, freq_exchange(): pieces.append((f ^ d, lax.ppermute(part, 'freq', pairs)))  6.27 us
    ppermute x1, waiting for transfers between devices, relay_exchange(): passed = lax.ppermute(across, 'tile', pairs)  4.05 us
    select_n x1, other arithmetic, per_device(): return jnp.where(inside, traces, jnp.float32(0.0))  3.96 us
    ppermute x1, starting transfers between devices, relay_exchange(): partner = lax.ppermute(mine, 'tile', pairs)  3.09 us
    ppermute x1, starting transfers between devices, relay_exchange(): across = lax.ppermute(other, 'tile', [(0, 2), (2, 0), (1, 3), (3, 1)])  2.59 us
    dot_general x2, matrix products, row_products(): lax.dot_general(u_part, blocks, (((0, 2), (0, 2)), ((), ())), preferred_e...  2.15 us
    ppermute x3, starting transfers between devices, freq_exchange(): pieces.append((f ^ d, lax.ppermute(part, 'freq', pairs)))  1.93 us
  transfers between devices with their start and end apart: 6, of which 4 were waited for; matrix products, arithmetic and copies ran while one was open for 6% of the time, Pallas kernels for 0%

profile of v16, /device:TPU:0, one launch (start us, length us, event | category | flops | bytes accessed | tf_op | source)
XLA Modules:
  0.0 39.3 jit_solution(15436657979399200051)
XLA Ops:
  0.0 1.0 %fusion.45 = bf16[2,112,512]{2,1,0:T(8,128)(2,1)S(1)} fusion(bf16[2,2,112,512]{3,2,1,0:T(8,128)(2,1)} %bitcast.93), kind=kLoop, calls=%fused_computation.95 | loop fusion | flops 114688 | bytes 458752 | tf_op jit(solution)/shard_map/neg | solution.py:27
  1.1 1.1 %slice_bitcast_fusion = (bf16[2,112,512]{2,1,0:T(8,128)(2,1)S(1)}, bf16[2,112,512]{2,1,0:T(8,128)(2,1)S(1)}) fusion(bf16[2,2,112,512]{3,2,1,0:T(8,128)(2,1)} %bitcast.94), kind=kLoop, calls=%fused_computation.34 | loop fusion | bytes 917504 | tf_op jit(solution)/shard_map/squeeze | solution.py:24
  2.1 0.0 copy-start.2
  2.2 0.8 %iota_compare_fusion.2 = pred[2,112]{1,0:T(4,128)(4,1)S(1)} fusion(s32[2]{0:T(128)} %bitcast.97), kind=kLoop, calls=%fused_computation.76 | loop fusion | flops 224 | bytes 232 | tf_op jit(solution)/shard_map/lt | solution.py:38
  2.9 0.1 maximum_bitcast_fusion
  3.0 0.0 copy-start.1
  3.0 0.1 pad_maximum_fusion
  3.2 0.6 %fusion.1 = bf16[2,2,112,512]{3,2,1,0:T(8,128)(2,1)S(1)} fusion(bf16[1024,512,1,1]{1,0,3,2:T(8,128)(2,1)S(1)} %bitcast.92, bf16[2,2,112,1024]{3,2,0,1:T(8,128)(2,1)S(1)} %pad_maximum_fusion, pred[2,112]{1,0:T(4,128)(4,1)S(1)} %iota_compare_fusion.2), kind=kOutput, calls=%fused_computation.6 | convolution fusion | flops 470220800 | bytes 2425056 | tf_op jit(solution)/shard_map/dot_general | solution.py:34
  3.8 3.1 %collective-permute-start.1 = (bf16[2,112,512]{2,1,0:T(8,128)(2,1)S(1)}, bf16[2,112,512]{2,1,0:T(8,128)(2,1)S(1)}, u32[]{:S(2)}, u32[]{:S(2)}) collective-permute-start(bf16[2,112,512]{2,1,0:T(8,128)(2,1)S(1)} %bitcast.95), channel_id=1, source_target_pairs={{0,4},{4,0},{8,12},{12,8},{1,5},{5,1},{9,13},{13,9},{2,6},{6,2},{1... | collective-permute-start | bytes 688136 | tf_op jit(solution)/shard_map/ppermute | solution.py:70
  6.9 2.6 %collective-permute-start = (bf16[2,112,512]{2,1,0:T(8,128)(2,1)S(1)}, bf16[2,112,512]{2,1,0:T(8,128)(2,1)}, u32[]{:S(2)}, u32[]{:S(2)}) collective-permute-start(bf16[2,112,512]{2,1,0:T(8,128)(2,1)S(1)} %get-tuple-element.30), channel_id=1, source_target_pairs={{0,8},{8,0},{4,12},{12,4},{1,9},{9,1},{5,13},{13,5},{2,10},{10,2},... | collective-permute-start | bytes 688136 | tf_op jit(solution)/shard_map/ppermute | solution.py:69
  9.6 0.1 fusion.26
  9.7 0.1 broadcast_in_dim.39
  9.8 0.1 broadcast_in_dim.37
  9.9 0.1 broadcast_in_dim.35
  9.9 0.1 broadcast_in_dim.33
  10.0 0.1 broadcast_in_dim.34
  10.1 0.1 broadcast_in_dim.36
  10.1 0.1 broadcast_in_dim.38
  10.2 0.1 broadcast_in_dim.40
  10.3 9.7 %collective-permute-done = bf16[2,112,512]{2,1,0:T(8,128)(2,1)} collective-permute-done((bf16[2,112,512]{2,1,0:T(8,128)(2,1)S(1)}, bf16[2,112,512]{2,1,0:T(8,128)(2,1)}, u32[]{:S(2)}, u32[]{:S(2)}) %collective-permute-start) | collective-permute-done | bytes 229408 | tf_op jit(solution)/shard_map/ppermute | solution.py:69
  20.0 0.4 %collective-permute-start.2 = (bf16[2,112,512]{2,1,0:T(8,128)(2,1)}, bf16[2,112,512]{2,1,0:T(8,128)(2,1)S(1)}, u32[]{:S(2)}, u32[]{:S(2)}) collective-permute-start(bf16[2,112,512]{2,1,0:T(8,128)(2,1)} %collective-permute-done), channel_id=1, source_target_pairs={{0,4},{4,0},{8,12},{12,8},{1,5},{5,1},{9,13},{13,9},{2,6},{6,2},{1... | collective-permute-start | bytes 688136 | tf_op jit(solution)/shard_map/ppermute | solution.py:71
  20.5 1.7 %fusion.3 = f32[2,256,2,512,1]{3,1,4,2,0:T(8,128)S(1)} fusion(bf16[1,2,112,256]{3,2,0,1:T(8,128)(2,1)S(1)} %get-tuple-element.29, bf16[1,2,112,256]{3,2,0,1:T(8,128)(2,1)S(1)} %get-tuple-element.28, bf16[1,2,112,256]{3,2,0,1:T(8,128)(2,1)S(1)} %get-tuple-element.27, bf16[1,2,112,512]{3,2,1,0:T(8,128)(2,1)S(1)} %bitcast.96, ...), kind=kOutput, calls=%fused_computation.18 | convolution fusion | flops 354041856 | bytes 3129344 | tf_op jit(solution)/shard_map/dot_general | solution.py:52
  22.2 4.1 %collective-permute-done.2 = bf16[2,112,512]{2,1,0:T(8,128)(2,1)S(1)} collective-permute-done((bf16[2,112,512]{2,1,0:T(8,128)(2,1)}, bf16[2,112,512]{2,1,0:T(8,128)(2,1)S(1)}, u32[]{:S(2)}, u32[]{:S(2)}) %collective-permute-start.2) | collective-permute-done | bytes 229408 | tf_op jit(solution)/shard_map/ppermute | solution.py:71
  26.2 0.5 %bitcast_add_fusion = f32[2,256,2,512]{3,1,2,0:T(8,128)S(1)} fusion(f32[2,256,2,512,1]{3,1,4,2,0:T(8,128)S(1)} %fusion.3, bf16[2,112,512]{2,1,0:T(8,128)(2,1)S(1)} %collective-permute-done.2, bf16[1,4,2,112,256]{4,3,2,1,0:T(8,128)(2,1)S(1)} %copy-done.1, s32[]{:T(128)S(6)} %select_n.89), kind=kOutput, calls=%fused_computation.4 | convolution fusion | flops 117964800 | bytes 4538372 | tf_op jit(solution)/shard_map/dot_general | solution.py:52
  26.7 0.2 fusion.13
  26.8 0.1 fusion.17
  26.9 0.1 collective-permute-start.3
  27.0 1.5 %collective-permute-start.4 = (bf16[2,64,512]{2,1,0:T(8,128)(2,1)S(1)}, bf16[2,64,512]{2,1,0:T(8,128)(2,1)S(1)}, u32[]{:S(2)}, u32[]{:S(2)}) collective-permute-start(bf16[2,64,512]{2,1,0:T(8,128)(2,1)S(1)} %get-tuple-element.25), channel_id=1, source_target_pairs={{0,2},{1,3},{2,0},{3,1},{4,6},{5,7},{6,4},{7,5},{8,10},{9,11},{10,... | collective-permute-start | bytes 393224 | tf_op jit(solution)/shard_map/ppermute | solution.py:95
  28.5 0.3 collective-permute-start.5
  28.9 4.4 %collective-permute-done.4 = bf16[2,64,512]{2,1,0:T(8,128)(2,1)S(1)} collective-permute-done((bf16[2,64,512]{2,1,0:T(8,128)(2,1)S(1)}, bf16[2,64,512]{2,1,0:T(8,128)(2,1)S(1)}, u32[]{:S(2)}, u32[]{:S(2)}) %collective-permute-start.4) | collective-permute-done | bytes 131104 | tf_op jit(solution)/shard_map/ppermute | solution.py:95
  33.4 1.9 %collective-permute-done.5 = bf16[2,64,512]{2,1,0:T(8,128)(2,1)S(1)} collective-permute-done((bf16[2,64,512]{2,1,0:T(8,128)(2,1)S(1)}, bf16[2,64,512]{2,1,0:T(8,128)(2,1)S(1)}, u32[]{:S(2)}, u32[]{:S(2)}) %collective-permute-start.5) | collective-permute-done | bytes 131104 | tf_op jit(solution)/shard_map/ppermute | solution.py:95
  35.3 4.0 %subtract_select_fusion = f32[64,32,512]{2,1,0:T(8,128)} fusion(f32[32,512]{1,0:T(8,128)S(1)} %broadcast_in_dim.40, f32[64,512]{1,0:T(8,128)S(1)} %get-tuple-element.43, f32[32,512]{1,0:T(8,128)S(1)} %broadcast_in_dim.39, f32[64,512]{1,0:T(8,128)S(1)} %get-tuple-element.42, f32[32,512]{1,0:T(8,128)S(1)} %broadcast_in_dim.38, ...), kind=kLoop, calls=%fused_computation | loop fusion | flops 19922944 | bytes 6029312 | tf_op jit(solution)/shard_map/jit(_where)/select_n | solution.py:156
  (18 shorter events, 0.2 us)
Async XLA Ops:
  0.0 3.1 %copy-start = (bf16[1,2,512,512]{3,2,1,0:T(8,128)(2,1)S(1)}, bf16[1,2,512,512]{3,2,1,0:T(8,128)(2,1)}, u32[]{:S(2)}) copy-start(bf16[1,2,512,512]{3,2,1,0:T(8,128)(2,1)} %param.5) | copy-start | bytes 3145732
  2.1 7.4 %copy-start.2 = (s32[2,64,512]{2,1,0:T(8,128)S(1)}, s32[2,64,512]{2,1,0:T(8,128)}, u32[]{:S(2)}) copy-start(s32[2,64,512]{2,1,0:T(8,128)} %param.9) | copy-start | bytes 786436
  3.0 17.4 %copy-start.1 = (bf16[1,4,2,112,256]{4,3,2,1,0:T(8,128)(2,1)S(1)}, bf16[1,4,2,112,256]{4,3,2,1,0:T(8,128)(2,1)}, u32[]{:S(2)}) copy-start(bf16[1,4,2,112,256]{4,3,2,1,0:T(8,128)(2,1)} %param.7) | copy-start | bytes 1376260
  3.8 16.6 %collective-permute-start.1 = (bf16[2,112,512]{2,1,0:T(8,128)(2,1)S(1)}, bf16[2,112,512]{2,1,0:T(8,128)(2,1)S(1)}, u32[]{:S(2)}, u32[]{:S(2)}) collective-permute-start(bf16[2,112,512]{2,1,0:T(8,128)(2,1)S(1)} %bitcast.95), channel_id=1, source_target_pairs={{0,4},{4,0},{8,12},{12,8},{1,5},{5,1},{9,13},{13,9},{2,6},{6,2},{1... | collective-permute-start | bytes 688136 | tf_op jit(solution)/shard_map/ppermute | solution.py:70
  6.9 13.0 %collective-permute-start = (bf16[2,112,512]{2,1,0:T(8,128)(2,1)S(1)}, bf16[2,112,512]{2,1,0:T(8,128)(2,1)}, u32[]{:S(2)}, u32[]{:S(2)}) collective-permute-start(bf16[2,112,512]{2,1,0:T(8,128)(2,1)S(1)} %get-tuple-element.30), channel_id=1, source_target_pairs={{0,8},{8,0},{4,12},{12,4},{1,9},{9,1},{5,13},{13,5},{2,10},{10,2},... | collective-permute-start | bytes 688136 | tf_op jit(solution)/shard_map/ppermute | solution.py:69
  20.0 6.2 %collective-permute-start.2 = (bf16[2,112,512]{2,1,0:T(8,128)(2,1)}, bf16[2,112,512]{2,1,0:T(8,128)(2,1)S(1)}, u32[]{:S(2)}, u32[]{:S(2)}) collective-permute-start(bf16[2,112,512]{2,1,0:T(8,128)(2,1)} %collective-permute-done), channel_id=1, source_target_pairs={{0,4},{4,0},{8,12},{12,8},{1,5},{5,1},{9,13},{13,9},{2,6},{6,2},{1... | collective-permute-start | bytes 688136 | tf_op jit(solution)/shard_map/ppermute | solution.py:71
  26.9 2.0 %collective-permute-start.3 = (bf16[2,64,512]{2,1,0:T(8,128)(2,1)S(1)}, bf16[2,64,512]{2,1,0:T(8,128)(2,1)S(1)}, u32[]{:S(2)}, u32[]{:S(2)}) collective-permute-start(bf16[2,64,512]{2,1,0:T(8,128)(2,1)S(1)} %get-tuple-element.24), channel_id=1, source_target_pairs={{0,1},{1,0},{2,3},{3,2},{4,5},{5,4},{6,7},{7,6},{8,9},{9,8},{10,11... | collective-permute-start | bytes 393224 | tf_op jit(solution)/shard_map/ppermute | solution.py:95
  27.0 6.4 %collective-permute-start.4 = (bf16[2,64,512]{2,1,0:T(8,128)(2,1)S(1)}, bf16[2,64,512]{2,1,0:T(8,128)(2,1)S(1)}, u32[]{:S(2)}, u32[]{:S(2)}) collective-permute-start(bf16[2,64,512]{2,1,0:T(8,128)(2,1)S(1)} %get-tuple-element.25), channel_id=1, source_target_pairs={{0,2},{1,3},{2,0},{3,1},{4,6},{5,7},{6,4},{7,5},{8,10},{9,11},{10,... | collective-permute-start | bytes 393224 | tf_op jit(solution)/shard_map/ppermute | solution.py:95
  28.5 6.7 %collective-permute-start.5 = (bf16[2,64,512]{2,1,0:T(8,128)(2,1)S(1)}, bf16[2,64,512]{2,1,0:T(8,128)(2,1)S(1)}, u32[]{:S(2)}, u32[]{:S(2)}) collective-permute-start(bf16[2,64,512]{2,1,0:T(8,128)(2,1)S(1)} %get-tuple-element.26), channel_id=1, source_target_pairs={{0,3},{1,2},{2,1},{3,0},{4,7},{5,6},{6,5},{7,4},{8,11},{9,10},{10,... | collective-permute-start | bytes 393224 | tf_op jit(solution)/shard_map/ppermute | solution.py:95

commit v17 on v15

--- a/solution.py
+++ b/solution.py
@@ -21,14 +21,11 @@
 
 
 def column_products(v_local, x_local, rank_local):
-    x_real, x_imag = x_local[0], x_local[1]
-    x_both = jnp.stack(
-        [jnp.stack([x_real, x_imag], axis=1), jnp.stack([-x_imag, x_real], axis=1)], axis=0
+    part_sign = jnp.array([1.0, -1.0], jnp.bfloat16)[None, :, None, None]
+    stacked = jnp.stack([v_local * part_sign, v_local[:, ::-1]], axis=1)
+    products = lax.dot_general(
+        stacked, x_local, (((2, 4), (0, 1)), ((), ())), preferred_element_type=jnp.float32
     )
-    products = lax.dot_general(
-        v_local, x_both, (((1, 3), (0, 1)), ((), ())), preferred_element_type=jnp.float32
-    )
-    products = products.transpose(0, 2, 1, 3)
     slot_index = jnp.arange(v_local.shape[2], dtype=jnp.int32)
     live_slots = slot_index[None, None, :, None] < rank_local[:, None, None, None]
     return jnp.where(live_slots, products, jnp.float32(0.0)).astype(jnp.bfloat16)

time: 38.8 us -> 39.4 us (1.015)
  matrix products: 1.82 us -> 2.79 us
    ppermute x1, starting transfers between devices: 1.58 us -> 3.11 us  [relay_exchange(): partner = lax.ppermute(mine, 'tile', pairs)]
    ppermute x1, starting transfers between devices: 4.1 us -> 2.59 us  [relay_exchange(): across = lax.ppermute(other, 'tile', [(0, 2), (2, 0), (1, 3), (3, 1)])]
    ppermute x1, waiting for transfers between devices: 8.29 us -> 9.68 us  [relay_exchange(): across = lax.ppermute(other, 'tile', [(0, 2), (2, 0), (1, 3), (3, 1)])]
    ppermute x1, waiting for transfers between devices: 5.34 us -> 4.05 us  [relay_exchange(): passed = lax.ppermute(across, 'tile', pairs)]
    neg x1 -> x0, other arithmetic: 1.13 us -> none  [column_products(): -x_imag]
    mul x0 -> x1, other arithmetic: none -> 1.12 us  [column_products(): stacked = jnp.stack([v_local * part_sign, v_local[:, ::-1]], axis=1)]
    dot_general x2, matrix products: 1.18 us -> 2.15 us  [row_products(): lax.dot_general(u_part, blocks, (((0, 2), (0, 2)), ((), ())), preferred_e...]
  transfers between devices with their start and end apart: 6 -> 6, of which waited for: 4 -> 4; matrix products, arithmetic and copies ran while one was open for 4% -> 6% of each run, Pallas kernels for 0% -> 0%
where the time goes in v17:
time: 39.4 us; the launch traced here: 39.2 us
  waiting for transfers between devices  20 us (51%)
  starting transfers between devices  8.08 us (21%)
  other arithmetic  6.36 us (16%)
  matrix products  2.79 us (7%)
  local copies, waits for them, and re-layouts  1.79 us (5%)
    ppermute x1, waiting for transfers between devices, relay_exchange(): across = lax.ppermute(other, 'tile', [(0, 2), (2, 0), (1, 3), (3, 1)])  9.68 us
    ppermute x3, waiting for transfers between devices, freq_exchange(): pieces.append((f ^ d, lax.ppermute(part, 'freq', pairs)))  6.27 us
    ppermute x1, waiting for transfers between devices, relay_exchange(): passed = lax.ppermute(across, 'tile', pairs)  4.05 us
    select_n x1, other arithmetic, per_device(): return jnp.where(inside, traces, jnp.float32(0.0))  3.96 us
    ppermute x1, starting transfers between devices, relay_exchange(): partner = lax.ppermute(mine, 'tile', pairs)  3.11 us
    ppermute x1, starting transfers between devices, relay_exchange(): across = lax.ppermute(other, 'tile', [(0, 2), (2, 0), (1, 3), (3, 1)])  2.59 us
    dot_general x2, matrix products, row_products(): lax.dot_general(u_part, blocks, (((0, 2), (0, 2)), ((), ())), preferred_e...  2.15 us
    ppermute x3, starting transfers between devices, freq_exchange(): pieces.append((f ^ d, lax.ppermute(part, 'freq', pairs)))  1.93 us
  transfers between devices with their start and end apart: 6, of which 4 were waited for; matrix products, arithmetic and copies ran while one was open for 6% of the time, Pallas kernels for 0%

profile of v17, /device:TPU:0, one launch (start us, length us, event | category | flops | bytes accessed | tf_op | source)
XLA Modules:
  0.0 39.2 jit_solution(963262051818718268)
XLA Ops:
  0.0 0.0 copy-start
  0.0 0.9 %iota_compare_fusion.2 = pred[2,112]{1,0:T(4,128)(4,1)S(1)} fusion(s32[2]{0:T(128)} %bitcast.95), kind=kLoop, calls=%fused_computation.77 | loop fusion | flops 224 | bytes 232 | tf_op jit(solution)/shard_map/lt | solution.py:30
  0.9 1.1 %bitcast_multiply_fusion = bf16[2,1,2,112,512]{4,3,2,1,0:T(8,128)(2,1)S(1)} fusion(bf16[1,1,2,2,112,512]{5,4,3,2,1,0:T(8,128)(2,1)} %param.7, bf16[2]{0:T(256)(128)(2,1)} %constant.93.clone), kind=kLoop, calls=%fused_computation.28 | loop fusion | flops 229376 | bytes 917508 | tf_op jit(solution)/shard_map/mul | solution.py:25
  2.0 1.1 %reverse_bitcast_fusion = bf16[2,1,2,112,512]{4,3,2,1,0:T(8,128)(2,1)S(1)} fusion(bf16[2,2,112,512]{3,2,1,0:T(8,128)(2,1)} %bitcast.92), kind=kLoop, calls=%fused_computation.29 | loop fusion | bytes 917504 | tf_op jit(solution)/shard_map/stack | solution.py:25
  3.1 0.6 %fusion.2 = bf16[2,2,112,512]{3,2,1,0:T(8,128)(2,1)S(1)} fusion(bf16[1,2,512,512]{3,2,1,0:T(8,128)(2,1)S(1)} %copy-done, bf16[2,1,2,112,512]{4,3,2,1,0:T(8,128)(2,1)S(1)} %reverse_bitcast_fusion, bf16[2,1,2,112,512]{4,3,2,1,0:T(8,128)(2,1)S(1)} %bitcast_multiply_fusion, pred[2,112]{1,0:T(4,128)(4,1)S(1)} %iota_compare_fusion.2), kind=kOutput, calls=%fused_computation.7 | convolution fusion | flops 470679552 | bytes 2425056 | tf_op jit(solution)/shard_map/dot_general | solution.py:26
  3.8 3.1 %collective-permute-start.1 = (bf16[2,112,512]{2,1,0:T(8,128)(2,1)S(1)}, bf16[2,112,512]{2,1,0:T(8,128)(2,1)S(1)}, u32[]{:S(2)}, u32[]{:S(2)}) collective-permute-start(bf16[2,112,512]{2,1,0:T(8,128)(2,1)S(1)} %bitcast.93), channel_id=1, source_target_pairs={{0,4},{4,0},{8,12},{12,8},{1,5},{5,1},{9,13},{13,9},{2,6},{6,2},{1... | collective-permute-start | bytes 688136 | tf_op jit(solution)/shard_map/ppermute | solution.py:62
  6.9 2.6 %collective-permute-start = (bf16[2,112,512]{2,1,0:T(8,128)(2,1)S(1)}, bf16[2,112,512]{2,1,0:T(8,128)(2,1)}, u32[]{:S(2)}, u32[]{:S(2)}) collective-permute-start(bf16[2,112,512]{2,1,0:T(8,128)(2,1)S(1)} %get-tuple-element.30), channel_id=1, source_target_pairs={{0,8},{8,0},{4,12},{12,4},{1,9},{9,1},{5,13},{13,5},{2,10},{10,2},... | collective-permute-start | bytes 688136 | tf_op jit(solution)/shard_map/ppermute | solution.py:61
  9.5 0.0 copy-done.2
  9.5 0.1 fusion.30
  9.6 0.1 broadcast_in_dim.39
  9.7 0.1 broadcast_in_dim.37
  9.8 0.1 broadcast_in_dim.35
  9.9 0.1 broadcast_in_dim.33
  9.9 0.1 broadcast_in_dim.34
  10.0 0.1 broadcast_in_dim.36
  10.1 0.1 broadcast_in_dim.38
  10.1 0.1 broadcast_in_dim.40
  10.2 9.7 %collective-permute-done = bf16[2,112,512]{2,1,0:T(8,128)(2,1)} collective-permute-done((bf16[2,112,512]{2,1,0:T(8,128)(2,1)S(1)}, bf16[2,112,512]{2,1,0:T(8,128)(2,1)}, u32[]{:S(2)}, u32[]{:S(2)}) %collective-permute-start) | collective-permute-done | bytes 229408 | tf_op jit(solution)/shard_map/ppermute | solution.py:61
  19.9 0.4 %collective-permute-start.2 = (bf16[2,112,512]{2,1,0:T(8,128)(2,1)}, bf16[2,112,512]{2,1,0:T(8,128)(2,1)S(1)}, u32[]{:S(2)}, u32[]{:S(2)}) collective-permute-start(bf16[2,112,512]{2,1,0:T(8,128)(2,1)} %collective-permute-done), channel_id=1, source_target_pairs={{0,4},{4,0},{8,12},{12,8},{1,5},{5,1},{9,13},{13,9},{2,6},{6,2},{1... | collective-permute-start | bytes 688136 | tf_op jit(solution)/shard_map/ppermute | solution.py:63
  20.4 0.0 collective-permute-done.1
  20.4 1.7 %fusion.7 = f32[2,256,2,512,1]{3,1,4,2,0:T(8,128)S(1)} fusion(bf16[1,2,112,256]{3,2,0,1:T(8,128)(2,1)S(1)} %get-tuple-element.29, bf16[1,2,112,256]{3,2,0,1:T(8,128)(2,1)S(1)} %get-tuple-element.28, bf16[1,2,112,256]{3,2,0,1:T(8,128)(2,1)S(1)} %get-tuple-element.27, bf16[1,2,112,512]{3,2,1,0:T(8,128)(2,1)S(1)} %bitcast.94, ...), kind=kOutput, calls=%fused_computation.21 | convolution fusion | flops 354041856 | bytes 3129344 | tf_op jit(solution)/shard_map/dot_general | solution.py:44
  22.1 4.0 %collective-permute-done.2 = bf16[2,112,512]{2,1,0:T(8,128)(2,1)S(1)} collective-permute-done((bf16[2,112,512]{2,1,0:T(8,128)(2,1)}, bf16[2,112,512]{2,1,0:T(8,128)(2,1)S(1)}, u32[]{:S(2)}, u32[]{:S(2)}) %collective-permute-start.2) | collective-permute-done | bytes 229408 | tf_op jit(solution)/shard_map/ppermute | solution.py:63
  26.1 0.5 %bitcast_add_fusion = f32[2,256,2,512]{3,1,2,0:T(8,128)S(1)} fusion(f32[2,256,2,512,1]{3,1,4,2,0:T(8,128)S(1)} %fusion.7, bf16[2,112,512]{2,1,0:T(8,128)(2,1)S(1)} %collective-permute-done.2, bf16[1,4,2,112,256]{4,3,2,1,0:T(8,128)(2,1)S(1)} %copy-done.1, s32[]{:T(128)S(6)} %select_n.89), kind=kOutput, calls=%fused_computation.4 | convolution fusion | flops 117964800 | bytes 4538372 | tf_op jit(solution)/shard_map/dot_general | solution.py:44
  26.6 0.2 fusion.17
  26.8 0.1 fusion.21
  26.8 0.1 collective-permute-start.3
  26.9 1.6 %collective-permute-start.4 = (bf16[2,64,512]{2,1,0:T(8,128)(2,1)S(1)}, bf16[2,64,512]{2,1,0:T(8,128)(2,1)S(1)}, u32[]{:S(2)}, u32[]{:S(2)}) collective-permute-start(bf16[2,64,512]{2,1,0:T(8,128)(2,1)S(1)} %get-tuple-element.25), channel_id=1, source_target_pairs={{0,2},{1,3},{2,0},{3,1},{4,6},{5,7},{6,4},{7,5},{8,10},{9,11},{10,... | collective-permute-start | bytes 393224 | tf_op jit(solution)/shard_map/ppermute | solution.py:87
  28.5 0.3 collective-permute-start.5
  28.8 0.0 collective-permute-done.3
  28.9 4.4 %collective-permute-done.4 = bf16[2,64,512]{2,1,0:T(8,128)(2,1)S(1)} collective-permute-done((bf16[2,64,512]{2,1,0:T(8,128)(2,1)S(1)}, bf16[2,64,512]{2,1,0:T(8,128)(2,1)S(1)}, u32[]{:S(2)}, u32[]{:S(2)}) %collective-permute-start.4) | collective-permute-done | bytes 131104 | tf_op jit(solution)/shard_map/ppermute | solution.py:87
  33.3 1.9 %collective-permute-done.5 = bf16[2,64,512]{2,1,0:T(8,128)(2,1)S(1)} collective-permute-done((bf16[2,64,512]{2,1,0:T(8,128)(2,1)S(1)}, bf16[2,64,512]{2,1,0:T(8,128)(2,1)S(1)}, u32[]{:S(2)}, u32[]{:S(2)}) %collective-permute-start.5) | collective-permute-done | bytes 131104 | tf_op jit(solution)/shard_map/ppermute | solution.py:87
  35.2 4.0 %subtract_select_fusion = f32[64,32,512]{2,1,0:T(8,128)} fusion(f32[32,512]{1,0:T(8,128)S(1)} %broadcast_in_dim.40, f32[64,512]{1,0:T(8,128)S(1)} %get-tuple-element.41, f32[32,512]{1,0:T(8,128)S(1)} %broadcast_in_dim.39, f32[64,512]{1,0:T(8,128)S(1)} %get-tuple-element.40, f32[32,512]{1,0:T(8,128)S(1)} %broadcast_in_dim.38, ...), kind=kLoop, calls=%fused_computation | loop fusion | flops 19922944 | bytes 6029312 | tf_op jit(solution)/shard_map/jit(_where)/select_n | solution.py:148
  (16 shorter events, 0.2 us)
Async XLA Ops:
  0.0 3.1 %copy-start = (bf16[1,2,512,512]{3,2,1,0:T(8,128)(2,1)S(1)}, bf16[1,2,512,512]{3,2,1,0:T(8,128)(2,1)}, u32[]{:S(2)}) copy-start(bf16[1,2,512,512]{3,2,1,0:T(8,128)(2,1)} %param.6) | copy-start | bytes 3145732
  0.0 9.5 %copy-start.2 = (s32[2,64,512]{2,1,0:T(8,128)S(1)}, s32[2,64,512]{2,1,0:T(8,128)}, u32[]{:S(2)}) copy-start(s32[2,64,512]{2,1,0:T(8,128)} %param.10) | copy-start | bytes 786436
  0.0 20.3 %copy-start.1 = (bf16[1,4,2,112,256]{4,3,2,1,0:T(8,128)(2,1)S(1)}, bf16[1,4,2,112,256]{4,3,2,1,0:T(8,128)(2,1)}, u32[]{:S(2)}) copy-start(bf16[1,4,2,112,256]{4,3,2,1,0:T(8,128)(2,1)} %param.8) | copy-start | bytes 1376260
  3.8 16.6 %collective-permute-start.1 = (bf16[2,112,512]{2,1,0:T(8,128)(2,1)S(1)}, bf16[2,112,512]{2,1,0:T(8,128)(2,1)S(1)}, u32[]{:S(2)}, u32[]{:S(2)}) collective-permute-start(bf16[2,112,512]{2,1,0:T(8,128)(2,1)S(1)} %bitcast.93), channel_id=1, source_target_pairs={{0,4},{4,0},{8,12},{12,8},{1,5},{5,1},{9,13},{13,9},{2,6},{6,2},{1... | collective-permute-start | bytes 688136 | tf_op jit(solution)/shard_map/ppermute | solution.py:62
  6.9 13.0 %collective-permute-start = (bf16[2,112,512]{2,1,0:T(8,128)(2,1)S(1)}, bf16[2,112,512]{2,1,0:T(8,128)(2,1)}, u32[]{:S(2)}, u32[]{:S(2)}) collective-permute-start(bf16[2,112,512]{2,1,0:T(8,128)(2,1)S(1)} %get-tuple-element.30), channel_id=1, source_target_pairs={{0,8},{8,0},{4,12},{12,4},{1,9},{9,1},{5,13},{13,5},{2,10},{10,2},... | collective-permute-start | bytes 688136 | tf_op jit(solution)/shard_map/ppermute | solution.py:61
  19.9 6.2 %collective-permute-start.2 = (bf16[2,112,512]{2,1,0:T(8,128)(2,1)}, bf16[2,112,512]{2,1,0:T(8,128)(2,1)S(1)}, u32[]{:S(2)}, u32[]{:S(2)}) collective-permute-start(bf16[2,112,512]{2,1,0:T(8,128)(2,1)} %collective-permute-done), channel_id=1, source_target_pairs={{0,4},{4,0},{8,12},{12,8},{1,5},{5,1},{9,13},{13,9},{2,6},{6,2},{1... | collective-permute-start | bytes 688136 | tf_op jit(solution)/shard_map/ppermute | solution.py:63
  26.8 2.0 %collective-permute-start.3 = (bf16[2,64,512]{2,1,0:T(8,128)(2,1)S(1)}, bf16[2,64,512]{2,1,0:T(8,128)(2,1)S(1)}, u32[]{:S(2)}, u32[]{:S(2)}) collective-permute-start(bf16[2,64,512]{2,1,0:T(8,128)(2,1)S(1)} %get-tuple-element.24), channel_id=1, source_target_pairs={{0,1},{1,0},{2,3},{3,2},{4,5},{5,4},{6,7},{7,6},{8,9},{9,8},{10,11... | collective-permute-start | bytes 393224 | tf_op jit(solution)/shard_map/ppermute | solution.py:87
  26.9 6.4 %collective-permute-start.4 = (bf16[2,64,512]{2,1,0:T(8,128)(2,1)S(1)}, bf16[2,64,512]{2,1,0:T(8,128)(2,1)S(1)}, u32[]{:S(2)}, u32[]{:S(2)}) collective-permute-start(bf16[2,64,512]{2,1,0:T(8,128)(2,1)S(1)} %get-tuple-element.25), channel_id=1, source_target_pairs={{0,2},{1,3},{2,0},{3,1},{4,6},{5,7},{6,4},{7,5},{8,10},{9,11},{10,... | collective-permute-start | bytes 393224 | tf_op jit(solution)/shard_map/ppermute | solution.py:87
  28.5 6.7 %collective-permute-start.5 = (bf16[2,64,512]{2,1,0:T(8,128)(2,1)S(1)}, bf16[2,64,512]{2,1,0:T(8,128)(2,1)S(1)}, u32[]{:S(2)}, u32[]{:S(2)}) collective-permute-start(bf16[2,64,512]{2,1,0:T(8,128)(2,1)S(1)} %get-tuple-element.26), channel_id=1, source_target_pairs={{0,3},{1,2},{2,1},{3,0},{4,7},{5,6},{6,5},{7,4},{8,11},{9,10},{10,... | collective-permute-start | bytes 393224 | tf_op jit(solution)/shard_map/ppermute | solution.py:87

commit v18 on v14

--- a/solution.py
+++ b/solution.py
@@ -21,7 +21,10 @@
 
 
 def column_products(v_local, x_local, rank_local):
-    v_real, v_imag = v_local[:, 0], v_local[:, 1]
+    slot_index = jnp.arange(v_local.shape[2], dtype=jnp.int32)
+    live_slots = slot_index[None, None, :, None] < rank_local[:, None, None, None]
+    v_live = jnp.where(live_slots, v_local, jnp.zeros((), v_local.dtype))
+    v_real, v_imag = v_live[:, 0], v_live[:, 1]
     stacked = jnp.stack(
         [
             jnp.concatenate([v_real, -v_imag], axis=-1),
@@ -33,9 +36,7 @@
     products = lax.dot_general(
         stacked, x_both, (((3,), (0,)), ((), ())), preferred_element_type=jnp.float32
     )
-    slot_index = jnp.arange(v_local.shape[2], dtype=jnp.int32)
-    live_slots = slot_index[None, None, :, None] < rank_local[:, None, None, None]
-    return jnp.where(live_slots, products, jnp.float32(0.0)).astype(jnp.bfloat16)
+    return products.astype(jnp.bfloat16)
 
 
 def row_spectrum(u_local, blocks):

time: 38.1 us -> 38.1 us (level)
  other arithmetic: 5.26 us -> 6.46 us
  local copies, waits for them, and re-layouts: 1.91 us -> 0.77 us
    select_n x0 -> x1, other arithmetic: none -> 1.16 us  [column_products(): v_live = jnp.where(live_slots, v_local, jnp.zeros((), v_local.dtype))]
    unnamed x7 -> x6, local copies, waits for them, and re-layouts: 1.15 us -> 0.01 us
where the time goes in v18:
time: 38.1 us; the launch traced here: 38 us
  waiting for transfers between devices  20.6 us (54%)
  starting transfers between devices  8.06 us (21%)
  other arithmetic  6.46 us (17%)
  matrix products  1.82 us (5%)
  local copies, waits for them, and re-layouts  0.77 us (2%)
    ppermute x1, waiting for transfers between devices, relay_exchange(): across = lax.ppermute(other, 'tile', [(0, 2), (2, 0), (1, 3), (3, 1)])  9.58 us
    ppermute x3, waiting for transfers between devices, freq_exchange(): pieces.append((f ^ d, lax.ppermute(part, 'freq', pairs)))  6.27 us
    ppermute x1, waiting for transfers between devices, relay_exchange(): passed = lax.ppermute(across, 'tile', pairs)  4.8 us
    select_n x1, other arithmetic, per_device(): return jnp.where(inside, traces, jnp.float32(0.0))  3.96 us
    ppermute x1, starting transfers between devices, relay_exchange(): partner = lax.ppermute(mine, 'tile', pairs)  3.09 us
    ppermute x1, starting transfers between devices, relay_exchange(): across = lax.ppermute(other, 'tile', [(0, 2), (2, 0), (1, 3), (3, 1)])  2.59 us
    ppermute x3, starting transfers between devices, freq_exchange(): pieces.append((f ^ d, lax.ppermute(part, 'freq', pairs)))  1.93 us
    dot_general x2, matrix products, row_products(): lax.dot_general(u_part, blocks, (((0, 2), (0, 2)), ((), ())), preferred_e...  1.18 us
  transfers between devices with their start and end apart: 6, of which 4 were waited for; matrix products, arithmetic and copies ran while one was open for 4% of the time, Pallas kernels for 0%

profile of v18, /device:TPU:0, one launch (start us, length us, event | category | flops | bytes accessed | tf_op | source)
XLA Modules:
  0.0 38.0 jit_solution(15994052945391183692)
XLA Ops:
  0.0 0.8 %iota_compare_fusion.2 = pred[2,112]{1,0:T(4,128)(4,1)S(1)} fusion(s32[2]{0:T(128)} %bitcast.97), kind=kLoop, calls=%fused_computation.77 | loop fusion | flops 224 | bytes 232 | tf_op jit(solution)/shard_map/lt | solution.py:25
  0.8 1.2 %bitcast_select_fusion = bf16[2,2,112,512]{3,2,0,1:T(8,128)(2,1)S(1)} fusion(bf16[1,1,2,2,112,512]{5,4,3,2,1,0:T(8,128)(2,1)} %param.6, pred[2,112]{1,0:T(4,128)(4,1)S(1)} %iota_compare_fusion.2), kind=kLoop, calls=%fused_computation.27 | loop fusion | flops 229376 | bytes 917728 | tf_op jit(solution)/shard_map/jit(_where)/select_n | solution.py:26
  2.0 0.0 copy-start.1
  2.1 0.1 maximum_bitcast_fusion
  2.2 0.6 %convolution_convert_fusion = bf16[2,2,112,512]{3,2,1,0:T(8,128)(2,1)S(1)} fusion(bf16[1024,512,1,1]{1,0,3,2:T(8,128)(2,1)S(1)} %bitcast.93, bf16[2,1,112,1024]{3,2,1,0:T(8,128)(2,1)S(1)} %get-tuple-element.45, bf16[2,1,112,1024]{3,2,1,0:T(8,128)(2,1)S(1)} %get-tuple-element.44), kind=kOutput, calls=%fused_computation.5 | convolution fusion | flops 470450176 | bytes 2424832 | tf_op jit(solution)/shard_map/dot_general | solution.py:36
  2.9 3.1 %collective-permute-start.1 = (bf16[2,112,512]{2,1,0:T(8,128)(2,1)S(1)}, bf16[2,112,512]{2,1,0:T(8,128)(2,1)S(1)}, u32[]{:S(2)}, u32[]{:S(2)}) collective-permute-start(bf16[2,112,512]{2,1,0:T(8,128)(2,1)S(1)} %bitcast.94), channel_id=1, source_target_pairs={{0,4},{4,0},{8,12},{12,8},{1,5},{5,1},{9,13},{13,9},{2,6},{6,2},{1... | collective-permute-start | bytes 688136 | tf_op jit(solution)/shard_map/ppermute | solution.py:70
  6.0 2.6 %collective-permute-start = (bf16[2,112,512]{2,1,0:T(8,128)(2,1)S(1)}, bf16[2,112,512]{2,1,0:T(8,128)(2,1)S(1)}, u32[]{:S(2)}, u32[]{:S(2)}) collective-permute-start(bf16[2,112,512]{2,1,0:T(8,128)(2,1)S(1)} %get-tuple-element.30), channel_id=1, source_target_pairs={{0,8},{8,0},{4,12},{12,4},{1,9},{9,1},{5,13},{13,5},{2,10},{10,2},... | collective-permute-start | bytes 688136 | tf_op jit(solution)/shard_map/ppermute | solution.py:69
  8.6 0.1 fusion.27
  8.7 0.1 broadcast_in_dim.39
  8.8 0.1 broadcast_in_dim.37
  8.9 0.1 broadcast_in_dim.35
  9.0 0.1 broadcast_in_dim.33
  9.0 0.1 broadcast_in_dim.34
  9.1 0.1 broadcast_in_dim.36
  9.2 0.1 broadcast_in_dim.38
  9.2 0.1 broadcast_in_dim.40
  9.3 9.6 %collective-permute-done = bf16[2,112,512]{2,1,0:T(8,128)(2,1)S(1)} collective-permute-done((bf16[2,112,512]{2,1,0:T(8,128)(2,1)S(1)}, bf16[2,112,512]{2,1,0:T(8,128)(2,1)S(1)}, u32[]{:S(2)}, u32[]{:S(2)}) %collective-permute-start) | collective-permute-done | bytes 229408 | tf_op jit(solution)/shard_map/ppermute | solution.py:69
  18.9 0.4 %collective-permute-start.2 = (bf16[2,112,512]{2,1,0:T(8,128)(2,1)S(1)}, bf16[2,112,512]{2,1,0:T(8,128)(2,1)S(1)}, u32[]{:S(2)}, u32[]{:S(2)}) collective-permute-start(bf16[2,112,512]{2,1,0:T(8,128)(2,1)S(1)} %collective-permute-done), channel_id=1, source_target_pairs={{0,4},{4,0},{8,12},{12,8},{1,5},{5,1},{9,13},{13,9},{2,6},{6,2},{1... | collective-permute-start | bytes 688136 | tf_op jit(solution)/shard_map/ppermute | solution.py:71
  19.3 0.0 copy-done.1
  19.4 0.0 collective-permute-done.1
  19.4 0.7 %fusion.4 = f32[2,256,2,512,1]{3,1,4,2,0:T(8,128)S(1)} fusion(bf16[1,2,112,256]{3,2,0,1:T(8,128)(2,1)S(1)} %get-tuple-element.29, bf16[1,2,112,256]{3,2,0,1:T(8,128)(2,1)S(1)} %get-tuple-element.28, bf16[1,2,112,256]{3,2,0,1:T(8,128)(2,1)S(1)} %get-tuple-element.27, bf16[1,2,112,512]{3,2,1,0:T(8,128)(2,1)S(1)} %bitcast.95, ...), kind=kOutput, calls=%fused_computation.18 | convolution fusion | flops 354041856 | bytes 3129344 | tf_op jit(solution)/shard_map/dot_general | solution.py:52
  20.1 4.8 %collective-permute-done.2 = bf16[2,112,512]{2,1,0:T(8,128)(2,1)S(1)} collective-permute-done((bf16[2,112,512]{2,1,0:T(8,128)(2,1)S(1)}, bf16[2,112,512]{2,1,0:T(8,128)(2,1)S(1)}, u32[]{:S(2)}, u32[]{:S(2)}) %collective-permute-start.2) | collective-permute-done | bytes 229408 | tf_op jit(solution)/shard_map/ppermute | solution.py:71
  24.9 0.5 %bitcast_add_fusion = f32[2,256,2,512]{3,1,2,0:T(8,128)S(1)} fusion(f32[2,256,2,512,1]{3,1,4,2,0:T(8,128)S(1)} %fusion.4, bf16[2,112,512]{2,1,0:T(8,128)(2,1)S(1)} %collective-permute-done.2, bf16[1,4,2,112,256]{4,3,2,1,0:T(8,128)(2,1)S(1)} %copy-done.1, s32[]{:T(128)S(6)} %select_n.89), kind=kOutput, calls=%fused_computation.4 | convolution fusion | flops 117964800 | bytes 4538372 | tf_op jit(solution)/shard_map/dot_general | solution.py:52
  25.4 0.2 fusion.14
  25.5 0.1 fusion.18
  25.6 0.1 collective-permute-start.3
  25.7 1.6 %collective-permute-start.4 = (bf16[2,64,512]{2,1,0:T(8,128)(2,1)S(1)}, bf16[2,64,512]{2,1,0:T(8,128)(2,1)S(1)}, u32[]{:S(2)}, u32[]{:S(2)}) collective-permute-start(bf16[2,64,512]{2,1,0:T(8,128)(2,1)S(1)} %get-tuple-element.25), channel_id=1, source_target_pairs={{0,2},{1,3},{2,0},{3,1},{4,6},{5,7},{6,4},{7,5},{8,10},{9,11},{10,... | collective-permute-start | bytes 393224 | tf_op jit(solution)/shard_map/ppermute | solution.py:95
  27.3 0.3 collective-permute-start.5
  27.6 0.0 collective-permute-done.3
  27.6 4.4 %collective-permute-done.4 = bf16[2,64,512]{2,1,0:T(8,128)(2,1)S(1)} collective-permute-done((bf16[2,64,512]{2,1,0:T(8,128)(2,1)S(1)}, bf16[2,64,512]{2,1,0:T(8,128)(2,1)S(1)}, u32[]{:S(2)}, u32[]{:S(2)}) %collective-permute-start.4) | collective-permute-done | bytes 131104 | tf_op jit(solution)/shard_map/ppermute | solution.py:95
  32.1 1.9 %collective-permute-done.5 = bf16[2,64,512]{2,1,0:T(8,128)(2,1)S(1)} collective-permute-done((bf16[2,64,512]{2,1,0:T(8,128)(2,1)S(1)}, bf16[2,64,512]{2,1,0:T(8,128)(2,1)S(1)}, u32[]{:S(2)}, u32[]{:S(2)}) %collective-permute-start.5) | collective-permute-done | bytes 131104 | tf_op jit(solution)/shard_map/ppermute | solution.py:95
  34.0 4.0 %subtract_select_fusion = f32[64,32,512]{2,1,0:T(8,128)} fusion(f32[32,512]{1,0:T(8,128)S(1)} %broadcast_in_dim.40, f32[64,512]{1,0:T(8,128)S(1)} %get-tuple-element.43, f32[32,512]{1,0:T(8,128)S(1)} %broadcast_in_dim.39, f32[64,512]{1,0:T(8,128)S(1)} %get-tuple-element.42, f32[32,512]{1,0:T(8,128)S(1)} %broadcast_in_dim.38, ...), kind=kLoop, calls=%fused_computation | loop fusion | flops 19922944 | bytes 6029312 | tf_op jit(solution)/shard_map/jit(_where)/select_n | solution.py:156
  (18 shorter events, 0.3 us)
Async XLA Ops:
  0.0 2.2 %copy-start = (bf16[1,2,512,512]{3,2,1,0:T(8,128)(2,1)S(1)}, bf16[1,2,512,512]{3,2,1,0:T(8,128)(2,1)}, u32[]{:S(2)}) copy-start(bf16[1,2,512,512]{3,2,1,0:T(8,128)(2,1)} %param.5) | copy-start | bytes 3145732
  0.8 7.7 %copy-start.2 = (s32[2,64,512]{2,1,0:T(8,128)S(1)}, s32[2,64,512]{2,1,0:T(8,128)}, u32[]{:S(2)}) copy-start(s32[2,64,512]{2,1,0:T(8,128)} %param.9) | copy-start | bytes 786436
  2.0 17.3 %copy-start.1 = (bf16[1,4,2,112,256]{4,3,2,1,0:T(8,128)(2,1)S(1)}, bf16[1,4,2,112,256]{4,3,2,1,0:T(8,128)(2,1)}, u32[]{:S(2)}) copy-start(bf16[1,4,2,112,256]{4,3,2,1,0:T(8,128)(2,1)} %param.7) | copy-start | bytes 1376260
  2.9 16.5 %collective-permute-start.1 = (bf16[2,112,512]{2,1,0:T(8,128)(2,1)S(1)}, bf16[2,112,512]{2,1,0:T(8,128)(2,1)S(1)}, u32[]{:S(2)}, u32[]{:S(2)}) collective-permute-start(bf16[2,112,512]{2,1,0:T(8,128)(2,1)S(1)} %bitcast.94), channel_id=1, source_target_pairs={{0,4},{4,0},{8,12},{12,8},{1,5},{5,1},{9,13},{13,9},{2,6},{6,2},{1... | collective-permute-start | bytes 688136 | tf_op jit(solution)/shard_map/ppermute | solution.py:70
  6.0 12.9 %collective-permute-start = (bf16[2,112,512]{2,1,0:T(8,128)(2,1)S(1)}, bf16[2,112,512]{2,1,0:T(8,128)(2,1)S(1)}, u32[]{:S(2)}, u32[]{:S(2)}) collective-permute-start(bf16[2,112,512]{2,1,0:T(8,128)(2,1)S(1)} %get-tuple-element.30), channel_id=1, source_target_pairs={{0,8},{8,0},{4,12},{12,4},{1,9},{9,1},{5,13},{13,5},{2,10},{10,2},... | collective-permute-start | bytes 688136 | tf_op jit(solution)/shard_map/ppermute | solution.py:69
  18.9 6.0 %collective-permute-start.2 = (bf16[2,112,512]{2,1,0:T(8,128)(2,1)S(1)}, bf16[2,112,512]{2,1,0:T(8,128)(2,1)S(1)}, u32[]{:S(2)}, u32[]{:S(2)}) collective-permute-start(bf16[2,112,512]{2,1,0:T(8,128)(2,1)S(1)} %collective-permute-done), channel_id=1, source_target_pairs={{0,4},{4,0},{8,12},{12,8},{1,5},{5,1},{9,13},{13,9},{2,6},{6,2},{1... | collective-permute-start | bytes 688136 | tf_op jit(solution)/shard_map/ppermute | solution.py:71
  25.6 2.0 %collective-permute-start.3 = (bf16[2,64,512]{2,1,0:T(8,128)(2,1)S(1)}, bf16[2,64,512]{2,1,0:T(8,128)(2,1)S(1)}, u32[]{:S(2)}, u32[]{:S(2)}) collective-permute-start(bf16[2,64,512]{2,1,0:T(8,128)(2,1)S(1)} %get-tuple-element.24), channel_id=1, source_target_pairs={{0,1},{1,0},{2,3},{3,2},{4,5},{5,4},{6,7},{7,6},{8,9},{9,8},{10,11... | collective-permute-start | bytes 393224 | tf_op jit(solution)/shard_map/ppermute | solution.py:95
  25.7 6.4 %collective-permute-start.4 = (bf16[2,64,512]{2,1,0:T(8,128)(2,1)S(1)}, bf16[2,64,512]{2,1,0:T(8,128)(2,1)S(1)}, u32[]{:S(2)}, u32[]{:S(2)}) collective-permute-start(bf16[2,64,512]{2,1,0:T(8,128)(2,1)S(1)} %get-tuple-element.25), channel_id=1, source_target_pairs={{0,2},{1,3},{2,0},{3,1},{4,6},{5,7},{6,4},{7,5},{8,10},{9,11},{10,... | collective-permute-start | bytes 393224 | tf_op jit(solution)/shard_map/ppermute | solution.py:95
  27.3 6.7 %collective-permute-start.5 = (bf16[2,64,512]{2,1,0:T(8,128)(2,1)S(1)}, bf16[2,64,512]{2,1,0:T(8,128)(2,1)S(1)}, u32[]{:S(2)}, u32[]{:S(2)}) collective-permute-start(bf16[2,64,512]{2,1,0:T(8,128)(2,1)S(1)} %get-tuple-element.26), channel_id=1, source_target_pairs={{0,3},{1,2},{2,1},{3,0},{4,7},{5,6},{6,5},{7,4},{8,11},{9,10},{10,... | collective-permute-start | bytes 393224 | tf_op jit(solution)/shard_map/ppermute | solution.py:95

commit v19 on v14

--- a/solution.py
+++ b/solution.py
@@ -73,8 +73,14 @@
     early = row_products(
         jnp.stack(u_order[:3], axis=0), jnp.stack([mine, across, partner], axis=0)
     )
-    late = row_products(u_order[3][None], passed[None])
-    return finish_spectrum(early + late)
+    last_u = u_order[3]
+
+    def spectrum_of(start, width):
+        u_part = lax.dynamic_slice_in_dim(last_u, start, width, axis=2)
+        late = row_products(u_part[None], passed[None])
+        return finish_spectrum(lax.dynamic_slice_in_dim(early, start, width, axis=1) + late)
+
+    return spectrum_of
 
 
 def gather_exchange(own, u_local, n_tile):
@@ -84,14 +90,16 @@
     return row_spectrum(u_local, received)
 
 
-def freq_exchange(spectrum, n_freq):
+def freq_exchange(spectrum_of, count_rec, n_freq):
     f = lax.axis_index("freq")
-    width = spectrum.shape[1] // n_freq
-    pieces = [(f, lax.dynamic_slice_in_dim(spectrum, f * width, width, axis=1))]
-    for d in range(1, n_freq):
-        part = lax.dynamic_slice_in_dim(spectrum, (f ^ d) * width, width, axis=1)
+    width = count_rec // n_freq
+    sent = {}
+    for d in reversed(range(1, n_freq)):
+        part = spectrum_of((f ^ d) * width, width)
         pairs = [(i, i ^ d) for i in range(n_freq)]
-        pieces.append((f ^ d, lax.ppermute(part, "freq", pairs)))
+        sent[d] = lax.ppermute(part, "freq", pairs)
+    pieces = [(f, spectrum_of(f * width, width))]
+    pieces += [(f ^ d, sent[d]) for d in range(1, n_freq)]
     return pieces
 
 
@@ -112,12 +120,16 @@
             x_part = x_local[:, :, c * width:(c + 1) * width]
             own = column_products(v_local, x_part, rank_local)
             if use_relay:
-                spectrum = relay_exchange(own, u_local)
+                spectrum_of = relay_exchange(own, u_local)
             else:
                 spectrum = gather_exchange(own, u_local, n_tile)
+                spectrum_of = lambda start, width, spectrum=spectrum: (
+                    lax.dynamic_slice_in_dim(spectrum, start, width, axis=1)
+                )
             if use_swaps:
-                received_parts.append(freq_exchange(spectrum, n_freq))
+                received_parts.append(freq_exchange(spectrum_of, u_local.shape[3], n_freq))
             else:
+                spectrum = spectrum_of(0, u_local.shape[3])
                 received = lax.all_to_all(
                     spectrum[None], "freq", split_axis=2, concat_axis=0, tiled=True
                 )

time: 38.1 us -> 38.1 us (level)
  waiting for transfers between devices: 20.6 us -> 19.6 us
  matrix products: 1.82 us -> 2.68 us
    ppermute x3, waiting for transfers between devices: 6.27 us -> 5.32 us  [freq_exchange(): sent[d] = lax.ppermute(part, 'freq', pairs)]
    dot_general x2 -> x5, matrix products: 1.18 us -> 2.04 us  [row_products(): lax.dot_general(u_part, blocks, (((0, 2), (0, 2)), ((), ())), preferred_e...]
    ppermute x1, waiting for transfers between devices: 4.8 us -> 4.14 us  [relay_exchange(): passed = lax.ppermute(across, 'tile', pairs)]
    ppermute x1, waiting for transfers between devices: 9.58 us -> 10.2 us  [relay_exchange(): across = lax.ppermute(other, 'tile', [(0, 2), (2, 0), (1, 3), (3, 1)])]
  transfers between devices with their start and end apart: 6 -> 6, of which waited for: 4 -> 4; matrix products, arithmetic and copies ran while one was open for 4% -> 7% of each run, Pallas kernels for 0% -> 0%
where the time goes in v19:
time: 38.1 us; the launch traced here: 38 us
  waiting for transfers between devices  19.6 us (51%)
  starting transfers between devices  8.17 us (21%)
  other arithmetic  5.25 us (14%)
  matrix products  2.68 us (7%)
  local copies, waits for them, and re-layouts  1.93 us (5%)
    ppermute x1, waiting for transfers between devices, relay_exchange(): across = lax.ppermute(other, 'tile', [(0, 2), (2, 0), (1, 3), (3, 1)])  10.2 us
    ppermute x3, waiting for transfers between devices, freq_exchange(): sent[d] = lax.ppermute(part, 'freq', pairs)  5.32 us
    ppermute x1, waiting for transfers between devices, relay_exchange(): passed = lax.ppermute(across, 'tile', pairs)  4.14 us
    select_n x1, other arithmetic, per_device(): return jnp.where(inside, traces, jnp.float32(0.0))  3.96 us
    ppermute x1, starting transfers between devices, relay_exchange(): partner = lax.ppermute(mine, 'tile', pairs)  3.09 us
    ppermute x1, starting transfers between devices, relay_exchange(): across = lax.ppermute(other, 'tile', [(0, 2), (2, 0), (1, 3), (3, 1)])  2.59 us
    dot_general x5, matrix products, row_products(): lax.dot_general(u_part, blocks, (((0, 2), (0, 2)), ((), ())), preferred_e...  2.04 us
    ppermute x3, starting transfers between devices, freq_exchange(): sent[d] = lax.ppermute(part, 'freq', pairs)  2.04 us
  transfers between devices with their start and end apart: 6, of which 4 were waited for; matrix products, arithmetic and copies ran while one was open for 7% of the time, Pallas kernels for 0%

profile of v19, /device:TPU:0, one launch (start us, length us, event | category | flops | bytes accessed | tf_op | source)
XLA Modules:
  0.0 38.0 jit_solution(1584745682533289749)
XLA Ops:
  0.0 1.1 %copy.25 = bf16[1,1,2,2,112,512]{5,4,2,3,1,0:T(8,128)(2,1)S(1)} copy(bf16[1,1,2,2,112,512]{5,4,3,2,1,0:T(8,128)(2,1)} %param.6) | data formatting | bytes 917504 | tf_op args[1]
  1.1 0.0 copy-start.2
  1.2 0.0 copy-start.1
  1.2 0.8 %iota_compare_fusion.2 = pred[2,112]{1,0:T(4,128)(4,1)S(1)} fusion(s32[2]{0:T(128)} %bitcast.143), kind=kLoop, calls=%fused_computation.102 | loop fusion | flops 224 | bytes 232 | tf_op jit(solution)/shard_map/lt | solution.py:37
  2.0 0.1 maximum_bitcast_fusion
  2.1 0.6 %fusion.1 = bf16[2,2,112,512]{3,2,1,0:T(8,128)(2,1)S(1)} fusion(bf16[1024,512,1,1]{1,0,3,2:T(8,128)(2,1)S(1)} %bitcast.137, bf16[2,1,112,1024]{3,2,1,0:T(8,128)(2,1)S(1)} %get-tuple-element.47, bf16[2,1,112,1024]{3,2,1,0:T(8,128)(2,1)S(1)} %get-tuple-element.46, pred[2,112]{1,0:T(4,128)(4,1)S(1)} %iota_compare_fusion.2), kind=kOutput, calls=%fused_computation.6 | convolution fusion | flops 470679552 | bytes 2425056 | tf_op jit(solution)/shard_map/dot_general | solution.py:33
  2.8 3.1 %collective-permute-start.1 = (bf16[2,112,512]{2,1,0:T(8,128)(2,1)S(1)}, bf16[2,112,512]{2,1,0:T(8,128)(2,1)S(1)}, u32[]{:S(2)}, u32[]{:S(2)}) collective-permute-start(bf16[2,112,512]{2,1,0:T(8,128)(2,1)S(1)} %bitcast.140), channel_id=1, source_target_pairs={{0,4},{4,0},{8,12},{12,8},{1,5},{5,1},{9,13},{13,9},{2,6},{6,2},{1... | collective-permute-start | bytes 688136 | tf_op jit(solution)/shard_map/ppermute | solution.py:69
  5.9 2.6 %collective-permute-start = (bf16[2,112,512]{2,1,0:T(8,128)(2,1)S(1)}, bf16[2,112,512]{2,1,0:T(8,128)(2,1)S(1)}, u32[]{:S(2)}, u32[]{:S(2)}) collective-permute-start(bf16[2,112,512]{2,1,0:T(8,128)(2,1)S(1)} %get-tuple-element.32), channel_id=1, source_target_pairs={{0,8},{8,0},{4,12},{12,4},{1,9},{9,1},{5,13},{13,5},{2,10},{10,2},... | collective-permute-start | bytes 688136 | tf_op jit(solution)/shard_map/ppermute | solution.py:68
  8.5 0.1 fusion.46
  8.7 10.2 %collective-permute-done = bf16[2,112,512]{2,1,0:T(8,128)(2,1)S(1)} collective-permute-done((bf16[2,112,512]{2,1,0:T(8,128)(2,1)S(1)}, bf16[2,112,512]{2,1,0:T(8,128)(2,1)S(1)}, u32[]{:S(2)}, u32[]{:S(2)}) %collective-permute-start) | collective-permute-done | bytes 229408 | tf_op jit(solution)/shard_map/ppermute | solution.py:68
  18.8 0.4 %collective-permute-start.2 = (bf16[2,112,512]{2,1,0:T(8,128)(2,1)S(1)}, bf16[2,112,512]{2,1,0:T(8,128)(2,1)S(1)}, u32[]{:S(2)}, u32[]{:S(2)}) collective-permute-start(bf16[2,112,512]{2,1,0:T(8,128)(2,1)S(1)} %collective-permute-done), channel_id=1, source_target_pairs={{0,4},{4,0},{8,12},{12,8},{1,5},{5,1},{9,13},{13,9},{2,6},{6,2},{1... | collective-permute-start | bytes 688136 | tf_op jit(solution)/shard_map/ppermute | solution.py:70
  19.4 0.1 broadcast_in_dim.39
  19.4 0.1 broadcast_in_dim.37
  19.5 0.1 broadcast_in_dim.35
  19.6 0.1 broadcast_in_dim.33
  19.6 0.1 broadcast_in_dim.34
  19.7 0.1 broadcast_in_dim.36
  19.8 0.1 broadcast_in_dim.38
  19.9 0.1 broadcast_in_dim.40
  20.0 0.0 collective-permute-done.1
  20.0 0.7 %convolution_bitcast_fusion = f32[2,256,2,512]{3,1,2,0:T(8,128)S(1)} fusion(bf16[1,2,112,256]{3,2,0,1:T(8,128)(2,1)S(1)} %get-tuple-element.30, bf16[1,2,112,256]{3,2,0,1:T(8,128)(2,1)S(1)} %get-tuple-element.31, bf16[1,2,112,256]{3,2,0,1:T(8,128)(2,1)S(1)} %get-tuple-element.29, bf16[1,2,112,512]{3,2,1,0:T(8,128)(2,1)S(1)} %bitcast.141, ...), kind=kOutput, calls=%fused_computation.4 | convolution fusion | flops 354041856 | bytes 3129344 | tf_op jit(solution)/shard_map/dot_general | solution.py:51
  20.7 4.1 %collective-permute-done.2 = bf16[2,112,512]{2,1,0:T(8,128)(2,1)S(1)} collective-permute-done((bf16[2,112,512]{2,1,0:T(8,128)(2,1)S(1)}, bf16[2,112,512]{2,1,0:T(8,128)(2,1)S(1)}, u32[]{:S(2)}, u32[]{:S(2)}) %collective-permute-start.2) | collective-permute-done | bytes 229408 | tf_op jit(solution)/shard_map/ppermute | solution.py:70
  24.9 0.3 convolution_add_fusion
  25.3 0.1 collective-permute-start.5
  25.3 0.3 convolution_add_fusion.1
  25.7 1.6 %collective-permute-start.4 = (bf16[2,64,512]{2,1,0:T(8,128)(2,1)S(1)}, bf16[2,64,512]{2,1,0:T(8,128)(2,1)S(1)}, u32[]{:S(2)}, u32[]{:S(2)}) collective-permute-start(bf16[2,64,512]{2,1,0:T(8,128)(2,1)S(1)} %pad_maximum_fusion.2), channel_id=1, source_target_pairs={{0,2},{1,3},{2,0},{3,1},{4,6},{5,7},{6,4},{7,5},{8,10},{9,11},{10,... | collective-permute-start | bytes 393224 | tf_op jit(solution)/shard_map/ppermute | solution.py:100
  27.3 0.3 convolution_add_fusion.3
  27.7 0.3 convolution_add_fusion.2
  28.1 0.4 %collective-permute-start.3 = (bf16[2,64,512]{2,1,0:T(8,128)(2,1)S(1)}, bf16[2,64,512]{2,1,0:T(8,128)(2,1)S(1)}, u32[]{:S(2)}, u32[]{:S(2)}) collective-permute-start(bf16[2,64,512]{2,1,0:T(8,128)(2,1)S(1)} %pad_maximum_fusion.1), channel_id=1, source_target_pairs={{0,1},{1,0},{2,3},{3,2},{4,5},{5,4},{6,7},{7,6},{8,9},{9,8},{10,11... | collective-permute-start | bytes 393224 | tf_op jit(solution)/shard_map/ppermute | solution.py:100
  28.6 2.5 %collective-permute-done.5 = bf16[2,64,512]{2,1,0:T(8,128)(2,1)S(1)} collective-permute-done((bf16[2,64,512]{2,1,0:T(8,128)(2,1)S(1)}, bf16[2,64,512]{2,1,0:T(8,128)(2,1)S(1)}, u32[]{:S(2)}, u32[]{:S(2)}) %collective-permute-start.5) | collective-permute-done | bytes 131104 | tf_op jit(solution)/shard_map/ppermute | solution.py:100
  31.1 2.8 %collective-permute-done.4 = bf16[2,64,512]{2,1,0:T(8,128)(2,1)S(1)} collective-permute-done((bf16[2,64,512]{2,1,0:T(8,128)(2,1)S(1)}, bf16[2,64,512]{2,1,0:T(8,128)(2,1)S(1)}, u32[]{:S(2)}, u32[]{:S(2)}) %collective-permute-start.4) | collective-permute-done | bytes 131104 | tf_op jit(solution)/shard_map/ppermute | solution.py:100
  34.0 4.0 %subtract_select_fusion = f32[64,32,512]{2,1,0:T(8,128)} fusion(f32[32,512]{1,0:T(8,128)S(1)} %broadcast_in_dim.40, f32[64,512]{1,0:T(8,128)S(1)} %get-tuple-element.45, f32[32,512]{1,0:T(8,128)S(1)} %broadcast_in_dim.39, f32[64,512]{1,0:T(8,128)S(1)} %get-tuple-element.44, f32[32,512]{1,0:T(8,128)S(1)} %broadcast_in_dim.38, ...), kind=kLoop, calls=%fused_computation | loop fusion | flops 19922944 | bytes 6029312 | tf_op jit(solution)/shard_map/jit(_where)/select_n | solution.py:167
  (27 shorter events, 0.5 us)
Async XLA Ops:
  0.0 2.1 %copy-start = (bf16[1,2,512,512]{3,2,1,0:T(8,128)(2,1)S(1)}, bf16[1,2,512,512]{3,2,1,0:T(8,128)(2,1)}, u32[]{:S(2)}) copy-start(bf16[1,2,512,512]{3,2,1,0:T(8,128)(2,1)} %param.5) | copy-start | bytes 3145732
  1.1 7.5 %copy-start.2 = (s32[2,64,512]{2,1,0:T(8,128)S(1)}, s32[2,64,512]{2,1,0:T(8,128)}, u32[]{:S(2)}) copy-start(s32[2,64,512]{2,1,0:T(8,128)} %param.9) | copy-start | bytes 786436
  1.2 18.8 %copy-start.1 = (bf16[1,4,2,112,256]{4,3,2,1,0:T(8,128)(2,1)S(1)}, bf16[1,4,2,112,256]{4,3,2,1,0:T(8,128)(2,1)}, u32[]{:S(2)}) copy-start(bf16[1,4,2,112,256]{4,3,2,1,0:T(8,128)(2,1)} %param.7) | copy-start | bytes 1376260
  2.8 17.2 %collective-permute-start.1 = (bf16[2,112,512]{2,1,0:T(8,128)(2,1)S(1)}, bf16[2,112,512]{2,1,0:T(8,128)(2,1)S(1)}, u32[]{:S(2)}, u32[]{:S(2)}) collective-permute-start(bf16[2,112,512]{2,1,0:T(8,128)(2,1)S(1)} %bitcast.140), channel_id=1, source_target_pairs={{0,4},{4,0},{8,12},{12,8},{1,5},{5,1},{9,13},{13,9},{2,6},{6,2},{1... | collective-permute-start | bytes 688136 | tf_op jit(solution)/shard_map/ppermute | solution.py:69
  5.9 12.9 %collective-permute-start = (bf16[2,112,512]{2,1,0:T(8,128)(2,1)S(1)}, bf16[2,112,512]{2,1,0:T(8,128)(2,1)S(1)}, u32[]{:S(2)}, u32[]{:S(2)}) collective-permute-start(bf16[2,112,512]{2,1,0:T(8,128)(2,1)S(1)} %get-tuple-element.32), channel_id=1, source_target_pairs={{0,8},{8,0},{4,12},{12,4},{1,9},{9,1},{5,13},{13,5},{2,10},{10,2},... | collective-permute-start | bytes 688136 | tf_op jit(solution)/shard_map/ppermute | solution.py:68
  18.8 6.0 %collective-permute-start.2 = (bf16[2,112,512]{2,1,0:T(8,128)(2,1)S(1)}, bf16[2,112,512]{2,1,0:T(8,128)(2,1)S(1)}, u32[]{:S(2)}, u32[]{:S(2)}) collective-permute-start(bf16[2,112,512]{2,1,0:T(8,128)(2,1)S(1)} %collective-permute-done), channel_id=1, source_target_pairs={{0,4},{4,0},{8,12},{12,8},{1,5},{5,1},{9,13},{13,9},{2,6},{6,2},{1... | collective-permute-start | bytes 688136 | tf_op jit(solution)/shard_map/ppermute | solution.py:70
  25.3 5.8 %collective-permute-start.5 = (bf16[2,64,512]{2,1,0:T(8,128)(2,1)S(1)}, bf16[2,64,512]{2,1,0:T(8,128)(2,1)S(1)}, u32[]{:S(2)}, u32[]{:S(2)}) collective-permute-start(bf16[2,64,512]{2,1,0:T(8,128)(2,1)S(1)} %pad_maximum_fusion.3), channel_id=1, source_target_pairs={{0,3},{1,2},{2,1},{3,0},{4,7},{5,6},{6,5},{7,4},{8,11},{9,10},{10,... | collective-permute-start | bytes 393224 | tf_op jit(solution)/shard_map/ppermute | solution.py:100
  25.7 8.2 %collective-permute-start.4 = (bf16[2,64,512]{2,1,0:T(8,128)(2,1)S(1)}, bf16[2,64,512]{2,1,0:T(8,128)(2,1)S(1)}, u32[]{:S(2)}, u32[]{:S(2)}) collective-permute-start(bf16[2,64,512]{2,1,0:T(8,128)(2,1)S(1)} %pad_maximum_fusion.2), channel_id=1, source_target_pairs={{0,2},{1,3},{2,0},{3,1},{4,6},{5,7},{6,4},{7,5},{8,10},{9,11},{10,... | collective-permute-start | bytes 393224 | tf_op jit(solution)/shard_map/ppermute | solution.py:100
  28.1 5.9 %collective-permute-start.3 = (bf16[2,64,512]{2,1,0:T(8,128)(2,1)S(1)}, bf16[2,64,512]{2,1,0:T(8,128)(2,1)S(1)}, u32[]{:S(2)}, u32[]{:S(2)}) collective-permute-start(bf16[2,64,512]{2,1,0:T(8,128)(2,1)S(1)} %pad_maximum_fusion.1), channel_id=1, source_target_pairs={{0,1},{1,0},{2,3},{3,2},{4,5},{5,4},{6,7},{7,6},{8,9},{9,8},{10,11... | collective-permute-start | bytes 393224 | tf_op jit(solution)/shard_map/ppermute | solution.py:100
